TPU v7x, 32 devices: a whole 2x2x4 slice. The times are simulated.
32 devices in a mesh: grp: 2 (over y), rot: 4 (over z), sub: 2 (over x), ref: 2 (over core).
Axes of the slice: x: 2, y: 2, z: 4, core: 2. Of those that a mesh axis runs over, the one named last changes fastest.
Arguments:
- ligand: bfloat16 [16, 4, 64, 64, 64], P(('grp', 'rot', 'ref'), None, 'sub'), parts along dimension 0, may hold values from -6 to 6
- receptor: float32 [4, 4, 64, 64, 64], P('grp', None, 'rot', 'sub'), parts along dimension 0, may hold values from -6 to 6
- tile_list: int32 [8, 2, 2, 8], P(('grp', 'rot'), 'sub', 'ref'), parts along dimension 0, may hold values from 0 to 255
- tile_owner: int32 [8, 2, 2, 8, 1], P(('grp', 'rot'), 'sub', 'ref'), parts along dimension 0, may hold values from 0 to 7; in each aligned block of 8 rows (0 to 7, 8 to 15, ..., all dimensions but the last counted through in order) at most 2 rows name the same one
- refine_weight: float32 [512, 512], replicated, may hold values from -0.25 to 0.25
Outputs:
- scores: float32 [16, 64, 64, 64], P(('grp', 'rot', 'ref'), 'sub'), parts along dimension 0
- refined: float32 [16, 2, 8, 2, 512], P(('grp', 'rot', 'ref'), 'sub'), parts along dimension 0
There are 2 independent parts, one for each index of `grp`. A program takes and returns all parts, laid end to end along the dimension named above; an argument that names none is the same for every part. Nothing has to cross between parts.
Inputs may be any that keep to these rules, and one draw needn't show every extreme that they name: `tile_owner`: in one device's list no owner is named more than 2 times, and in every draw some device names one owner exactly 2 times.
All inputs are finite; a program needn't handle non-finite values.
Results may differ from a plain program's by a relative error of at most 0.004.
Values may be sent and summed in bfloat16 or wider, within the bound.
No kernel may reach another device: no remote copies, remote signals or barrier semaphores. Data moves between devices by JAX's collectives and lax.ppermute only.
A program may use at most 128 MiB of HBM per device.

v0:
```python
import functools
import math

import jax
import jax.numpy as jnp
from jax import lax
from jax.experimental import pallas as pl
from jax.experimental.pallas import tpu as pltpu
from jax.sharding import PartitionSpec as P

CAP = 2


highest = lax.Precision.HIGH


def make_tables(length):
    counter = jnp.arange(length, dtype=jnp.int32)
    phases = counter[:, None] * counter[None, :] % length
    angles = phases.astype(jnp.float32) * (2.0 * math.pi / length)
    return (jnp.cos(angles), jnp.sin(angles))


def combine_kernel(in_ref, out_ref, *, first, second):
    batch, _, rows, lanes = in_ref.shape
    split = out_ref.shape[0]
    part = rows // split
    half = lanes // 2
    cos_part = in_ref[:, 0].reshape(batch * rows, lanes)
    sin_part = in_ref[:, 1].reshape(batch * rows, lanes)
    low = lax.broadcasted_iota(jnp.int32, cos_part.shape, 1) < half
    signs = jnp.where(low, first, second).astype(jnp.float32)
    result = (cos_part + pltpu.roll(sin_part, half, 1) * signs).reshape(batch, rows, lanes)
    for piece in range(split):
        out_ref[piece] = result[:, piece * part:(piece + 1) * part].astype(out_ref.dtype)


def combine_call(stacked, first, second, split, dtype):
    batch, _, rows, lanes = stacked.shape
    block = max(b for b in range(1, 17) if batch % b == 0)
    part = rows // split
    return pl.pallas_call(
        functools.partial(combine_kernel, first=first, second=second),
        grid=(batch // block,),
        in_specs=[pl.BlockSpec((block, 2, rows, lanes), lambda i: (i, 0, 0, 0))],
        out_specs=pl.BlockSpec((split, block, part, lanes), lambda i: (0, i, 0, 0)),
        out_shape=jax.ShapeDtypeStruct((split, batch, part, lanes), dtype),
        cost_estimate=pl.CostEstimate(
            flops=3 * batch * rows * lanes,
            bytes_accessed=(8 + jnp.dtype(dtype).itemsize) * batch * rows * lanes,
            transcendentals=0,
        ),
    )(stacked)


def gather_by_shifts(piece, axis):
    count = lax.axis_size(axis)
    me = lax.axis_index(axis)
    pieces = [piece]
    for shift in range(1, count):
        pairs = [(k, (k + shift) % count) for k in range(count)]
        pieces.append(lax.ppermute(piece, axis, pairs))
    doubled = jnp.stack(pieces[::-1] * 2)
    return lax.dynamic_slice_in_dim(doubled, (count - 1 - me) % count, count, axis=0)


def gather_receptor(receptor):
    _, terms, kx_local, ky_local, kz = receptor.shape
    n_ref = lax.axis_size("ref")
    n_rot = lax.axis_size("rot")
    rows = ky_local // n_ref
    block = lax.dynamic_slice_in_dim(receptor, lax.axis_index("ref") * rows, rows, axis=3)
    mine = jnp.concatenate([block[0], block[1]], axis=-1).astype(jnp.bfloat16)
    mine = jnp.swapaxes(mine, 1, 2)
    along_rot = gather_by_shifts(mine, "rot")
    both = gather_by_shifts(along_rot, "ref")
    both = jnp.transpose(both, (2, 0, 3, 1, 4, 5))
    return both.reshape(terms, ky_local, n_rot * kx_local, 2 * kz)


def product_kernel(*refs):
    *spec_refs, rec_ref, out_ref = refs
    lanes = out_ref.shape[-1]
    half = lanes // 2
    total = None
    term = 0
    for spec_ref in spec_refs:
        for inner in range(spec_ref.shape[0]):
            spec = spec_ref[inner].astype(jnp.float32)
            rec = rec_ref[term].astype(jnp.float32)
            term += 1
            low = lax.broadcasted_iota(jnp.int32, rec.shape, 1) < half
            rec_turned = pltpu.roll(rec, half, 1)
            rec_real = jnp.where(low, rec, rec_turned)
            rec_imag = jnp.where(low, rec_turned, -rec)
            part = rec_real * spec + rec_imag * pltpu.roll(spec, half, 1)
            total = part if total is None else total + part
    out_ref[...] = total


def correlate(spectra, receptor):
    rots, _, kx, ky, lanes = spectra[0].shape
    terms = receptor.shape[0]
    rows = kx * ky
    block = min(rows, 512)
    specs = [part.reshape(rots, part.shape[1], rows, lanes) for part in spectra]
    rec = receptor.reshape(terms, rows, lanes)
    out = pl.pallas_call(
        product_kernel,
        grid=(rots, rows // block),
        in_specs=[
            pl.BlockSpec((None, part.shape[1], block, lanes), lambda r, i: (r, 0, i, 0))
            for part in specs
        ]
        + [pl.BlockSpec((terms, block, lanes), lambda r, i: (0, i, 0))],
        out_specs=pl.BlockSpec((None, block, lanes), lambda r, i: (r, i, 0)),
        out_shape=jax.ShapeDtypeStruct((rots, rows, lanes), jnp.float32),
        cost_estimate=pl.CostEstimate(
            flops=8 * rots * terms * rows * lanes,
            bytes_accessed=2 * (rots + 1) * terms * rows * lanes + 4 * rots * rows * lanes,
            transcendentals=0,
        ),
    )(*specs, rec)
    return out.reshape(rots, kx, ky, lanes)


def local(ligand, receptor, tile_list, tile_owner, refine_weight):
    rots, terms, x_local, ny, nz = ligand.shape
    length = nz
    n_sub = lax.axis_size("sub")
    y_local = ny // n_sub
    cos_table, sin_table = make_tables(length)
    pair = jnp.stack([cos_table, sin_table])

    chunks = 2 if terms % 2 == 0 else 1
    part_terms = terms // chunks
    pair_x = pair.reshape(2, length, n_sub, x_local)
    z_table = jnp.concatenate([cos_table, -sin_table], axis=1)
    values = ligand.astype(jnp.float32)
    spectra = []
    for chunk in range(chunks):
        part = values[:, chunk * part_terms:(chunk + 1) * part_terms]
        along_z = jnp.einsum("rtxyz,zl->rtxyl", part, z_table, precision=highest)
        along_y = jnp.einsum("ejy,rtxyl->rtxejl", pair, along_z, precision=highest)
        sending = combine_call(
            along_y.reshape(-1, 2, ny, 2 * length), 1.0, -1.0, n_sub, jnp.bfloat16
        ).reshape(n_sub, rots, part_terms, x_local, y_local, 2 * length)
        turned = lax.all_to_all(sending, "sub", split_axis=0, concat_axis=0, tiled=True)
        turned = turned.astype(jnp.float32)
        along_x = sum(
            jnp.einsum("ekx,rtxjl->rtjekl", pair_x[:, :, s], turned[s], precision=highest)
            for s in range(n_sub)
        )
        spectrum = combine_call(
            along_x.reshape(-1, 2, length, 2 * length), 1.0, -1.0, 1, jnp.bfloat16
        )
        spectra.append(spectrum.reshape(rots, part_terms, y_local, length, 2 * length))

    whole_receptor = gather_receptor(receptor)
    product = correlate(spectra, whole_receptor)

    back_x = jnp.einsum("exk,rjkl->xrejl", pair, product, precision=highest)
    back_x = combine_call(back_x.reshape(-1, 2, y_local, 2 * length), -1.0, 1.0, 1, jnp.float32)
    back_x = back_x.reshape(n_sub, x_local, rots, y_local, 2 * length)
    returned = lax.all_to_all(back_x, "sub", split_axis=0, concat_axis=0, tiled=True)
    pair_y = pair.reshape(2, length, n_sub, y_local)
    back_y = sum(
        jnp.einsum("eyj,xrjl->rxeyl", pair_y[:, :, s], returned[s], precision=highest)
        for s in range(n_sub)
    )
    back_y = combine_call(back_y.reshape(-1, 2, ny, 2 * length), -1.0, 1.0, 1, jnp.float32)
    back_y = back_y.reshape(rots, x_local, ny, 2 * length)
    last_table = jnp.concatenate([cos_table, -sin_table], axis=0)
    scores = jnp.einsum("rxyl,lz->rxyz", back_y, last_table, precision=highest) / float(length**3)

    tile_cells = 8 * length
    tile_rows = scores.reshape(-1, tile_cells)
    listing = tile_list.reshape(-1)
    owners = tile_owner.reshape(-1)
    listed = listing.shape[0]
    chosen = tile_rows[listing]
    owner_count = lax.axis_size(("rot", "ref"))
    order = jnp.arange(listed, dtype=jnp.int32)
    earlier = (owners[:, None] == owners[None, :]) & (order[None, :] < order[:, None])
    slot = jnp.sum(earlier.astype(jnp.int32), axis=1)
    target = owners * CAP + slot
    placing = (jnp.arange(owner_count * CAP, dtype=jnp.int32)[:, None] == target[None, :]).astype(
        jnp.float32
    )
    done = jnp.dot(chosen, refine_weight, precision=highest)
    packed = jnp.dot(placing, done, precision=highest).reshape(owner_count, CAP, tile_cells)
    refined = lax.all_to_all(packed, ("rot", "ref"), split_axis=0, concat_axis=0, tiled=True)
    return (scores, refined.reshape(1, 1, owner_count, CAP, tile_cells))


def solution(mesh):
    in_specs = (
        P(("grp", "rot", "ref"), None, "sub", None, None),
        P("grp", None, "rot", "sub", None),
        P(("grp", "rot"), "sub", "ref", None),
        P(("grp", "rot"), "sub", "ref", None, None),
        P(),
    )
    out_specs = (
        P(("grp", "rot", "ref"), "sub", None, None),
        P(("grp", "rot", "ref"), "sub", None, None, None),
    )
    return jax.shard_map(local, mesh=mesh, in_specs=in_specs, out_specs=out_specs, check_vma=False)
```

profile of v0, /device:TPU:0, one launch (start us, length us, event | category | flops | bytes accessed | tf_op | source)
XLA Modules:
  0.0 126.2 jit_solution(12219923954127657667)
XLA Ops:
  0.7 1.6 %copy-done = f32[2,4,16,32,64]{4,3,2,1,0:T(8,128)S(1)} copy-done((f32[2,4,16,32,64]{4,3,2,1,0:T(8,128)S(1)}, f32[2,4,16,32,64]{4,3,2,1,0:T(8,128)}, u32[]{:S(2)}) %copy-start) | copy-done | bytes 1048600
  3.3 5.0 %collective-permute-start = (bf16[4,16,16,128]{3,1,2,0:T(8,128)(2,1)}, bf16[4,16,16,128]{3,1,2,0:T(8,128)(2,1)S(1)}, u32[]{:S(2)}, u32[]{:S(2)}) collective-permute-start(bf16[4,16,16,128]{3,1,2,0:T(8,128)(2,1)} %fusion.67), channel_id=1, source_target_pairs={{0,12},{4,0},{8,4},{12,8},{1,13},{5,1},{9,5},{13,9},{2,14},{6,2},{... | collective-permute-start | bytes 786440 | tf_op jit(solution)/shard_map/ppermute | solution.py:62
  10.4 3.7 %fusion.6 = f32[2,32,128,2,64]{2,4,3,1,0:T(8,128)} fusion(f32[128,2,32,64]{0,3,2,1:T(8,128)S(1)} %fusion.11, f32[1,64,64]{2,1,0:T(8,128)S(1)} %get-tuple-element.8, f32[1,64,64]{2,1,0:T(8,128)S(1)} %get-tuple-element.9), kind=kOutput, calls=%fused_computation.13 | convolution fusion | flops 402661376 | bytes 6324224 | tf_op jit(solution)/shard_map/ejy,rtxyl->rtxejl/dot_general | solution.py:144
  14.1 4.3 %shard_map.68 = bf16[2,64,32,128]{3,2,1,0:T(8,128)(2,1)} custom-call(f32[64,2,64,128]{3,2,1,0:T(8,128)} %bitcast.193), custom_call_target="tpu_custom_call" | custom-call | flops 1572864 | bytes 5242880 | tf_op jit(solution)/shard_map/pallas_call | solution.py:42
  18.5 2.6 %copy.12 = bf16[2,1,2,32,32,128]{5,3,4,2,1,0:T(8,128)(2,1)} copy(bf16[2,1,2,32,32,128]{5,4,3,2,0,1:T(8,128)(2,1)} %bitcast.200) | data formatting | bytes 2097152 | tf_op jit(solution)/shard_map/reshape | solution.py:147
  21.1 3.6 %all-to-all-start = ((bf16[2,1,2,32,32,128]{5,3,4,2,1,0:T(8,128)(2,1)}), bf16[2,1,2,32,32,128]{5,3,4,2,1,0:T(8,128)(2,1)S(1)}, u32[]{:S(2)}, u32[]{:S(2)}) async-start(bf16[2,1,2,32,32,128]{5,3,4,2,1,0:T(8,128)(2,1)} %copy.12), calls=%async_computation | async-start | bytes 2097152 | tf_op jit(solution)/shard_map/all_to_all | solution.py:148
  24.6 1.9 %fusion.9 = f32[128,2,32,64]{0,3,2,1:T(8,128)S(1)} fusion(bf16[1,4,32,64,64]{4,3,2,1,0:T(8,128)(2,1)} %param.5, f32[64,64]{0,1:T(8,128)S(1)} %get-tuple-element.6, f32[64,64]{0,1:T(8,128)S(1)} %get-tuple-element.7), kind=kOutput, calls=%fused_computation.19 | convolution fusion | flops 201334784 | bytes 3178496 | tf_op jit(solution)/shard_map/rtxyz,zl->rtxyl/dot_general | solution.py:143
  26.6 3.7 %fusion.4 = f32[2,32,128,2,64]{2,4,3,1,0:T(8,128)} fusion(f32[128,2,32,64]{0,3,2,1:T(8,128)S(1)} %fusion.9, f32[1,64,64]{2,1,0:T(8,128)S(1)} %get-tuple-element.8, f32[1,64,64]{2,1,0:T(8,128)S(1)} %get-tuple-element.9), kind=kOutput, calls=%fused_computation.11 | convolution fusion | flops 402661376 | bytes 6324224 | tf_op jit(solution)/shard_map/ejy,rtxyl->rtxejl/dot_general | solution.py:144
  30.6 4.3 %shard_map.70 = bf16[2,64,32,128]{3,2,1,0:T(8,128)(2,1)} custom-call(f32[64,2,64,128]{3,2,1,0:T(8,128)} %bitcast.192), custom_call_target="tpu_custom_call" | custom-call | flops 1572864 | bytes 5242880 | tf_op jit(solution)/shard_map/pallas_call | solution.py:42
  34.9 2.7 %copy.13 = bf16[2,1,2,32,32,128]{5,3,4,2,1,0:T(8,128)(2,1)} copy(bf16[2,1,2,32,32,128]{5,4,3,2,0,1:T(8,128)(2,1)} %bitcast.201) | data formatting | bytes 2097152 | tf_op jit(solution)/shard_map/reshape | solution.py:147
  39.6 3.8 %all-to-all-start.1 = ((bf16[2,1,2,32,32,128]{5,3,4,2,1,0:T(8,128)(2,1)}), bf16[2,1,2,32,32,128]{5,3,4,2,1,0:T(8,128)(2,1)S(1)}, u32[]{:S(2)}, u32[]{:S(2)}) async-start(bf16[2,1,2,32,32,128]{5,3,4,2,1,0:T(8,128)(2,1)} %copy.13), calls=%async_computation.1 | async-start | bytes 2097152 | tf_op jit(solution)/shard_map/all_to_all | solution.py:148
  43.4 1.3 %fusion.17 = f32[2,32,128,2,64]{2,4,3,1,0:T(8,128)S(1)} fusion(bf16[2,1,2,32,32,128]{5,3,4,2,1,0:T(8,128)(2,1)S(1)} %all-to-all-done, f32[1,64,2,32]{1,3,0,2:T(8,128)S(1)} %get-tuple-element.5, f32[1,64,2,32]{1,3,0,2:T(8,128)S(1)} %get-tuple-element.4), kind=kOutput, calls=%fused_computation.34 | convolution fusion | flops 201330688 | bytes 4784128 | tf_op jit(solution)/shard_map/ekx,rtxjl->rtjekl/dot_general | solution.py:151
  44.7 3.6 %convolution_add_fusion.1 = f32[2,32,128,2,64]{2,4,3,1,0:T(8,128)} fusion(f32[2,32,128,2,64]{2,4,3,1,0:T(8,128)S(1)} %fusion.17, bf16[2,1,2,32,32,128]{5,3,4,2,1,0:T(8,128)(2,1)S(1)} %all-to-all-done, f32[1,64,2,32]{1,3,0,2:T(8,128)S(1)} %get-tuple-element.4, f32[1,64,2,32]{1,3,0,2:T(8,128)S(1)} %get-tuple-element.5), kind=kOutput, calls=%fused_computation.6 | convolution fusion | flops 202379264 | bytes 8978432 | tf_op jit(solution)/shard_map/ekx,rtxjl->rtjekl/dot_general | solution.py:151
  48.3 4.3 %shard_map.69 = bf16[1,64,64,128]{3,2,1,0:T(8,128)(2,1)} custom-call(f32[64,2,64,128]{3,2,1,0:T(8,128)} %bitcast.190), custom_call_target="tpu_custom_call" | custom-call | flops 1572864 | bytes 5242880 | tf_op jit(solution)/shard_map/pallas_call | solution.py:42
  52.7 5.5 %all-to-all-done.1 = bf16[2,1,2,32,32,128]{5,3,4,2,1,0:T(8,128)(2,1)S(1)} async-done(((bf16[2,1,2,32,32,128]{5,3,4,2,1,0:T(8,128)(2,1)}), bf16[2,1,2,32,32,128]{5,3,4,2,1,0:T(8,128)(2,1)S(1)}, u32[]{:S(2)}, u32[]{:S(2)}) %all-to-all-start.1) | async-done | bytes 1048608 | tf_op jit(solution)/shard_map/all_to_all | solution.py:148
  58.2 1.3 %fusion.16 = f32[2,32,128,2,64]{2,4,3,1,0:T(8,128)S(1)} fusion(bf16[2,1,2,32,32,128]{5,3,4,2,1,0:T(8,128)(2,1)S(1)} %all-to-all-done.1, f32[1,64,2,32]{1,3,0,2:T(8,128)S(1)} %get-tuple-element.5, f32[1,64,2,32]{1,3,0,2:T(8,128)S(1)} %get-tuple-element.4), kind=kOutput, calls=%fused_computation.31 | convolution fusion | flops 201330688 | bytes 4784128 | tf_op jit(solution)/shard_map/ekx,rtxjl->rtjekl/dot_general | solution.py:151
  59.5 3.6 %convolution_add_fusion = f32[2,32,128,2,64]{2,4,3,1,0:T(8,128)} fusion(f32[2,32,128,2,64]{2,4,3,1,0:T(8,128)S(1)} %fusion.16, bf16[2,1,2,32,32,128]{5,3,4,2,1,0:T(8,128)(2,1)S(1)} %all-to-all-done.1, f32[1,64,2,32]{1,3,0,2:T(8,128)S(1)} %get-tuple-element.4, f32[1,64,2,32]{1,3,0,2:T(8,128)S(1)} %get-tuple-element.5), kind=kOutput, calls=%fused_computation.5 | convolution fusion | flops 202379264 | bytes 8978432 | tf_op jit(solution)/shard_map/ekx,rtxjl->rtjekl/dot_general | solution.py:151
  63.1 4.3 %shard_map.71 = bf16[1,64,64,128]{3,2,1,0:T(8,128)(2,1)} custom-call(f32[64,2,64,128]{3,2,1,0:T(8,128)} %bitcast.191), custom_call_target="tpu_custom_call" | custom-call | flops 1572864 | bytes 5242880 | tf_op jit(solution)/shard_map/pallas_call | solution.py:42
  67.5 2.7 %fusion.3 = bf16[4,2,16,4,16,128]{5,2,4,0,3,1:T(8,128)(2,1)S(1)} fusion(s32[]{:T(128)S(6)} %select_n.79, bf16[1,4,4,16,16,128]{5,3,4,2,1,0:T(8,128)(2,1)} %bitcast.59, bf16[1,4,4,16,16,128]{5,3,4,2,1,0:T(8,128)(2,1)S(1)} %fusion.73), kind=kLoop, calls=%fused_computation.10 | loop fusion | flops 3145728 | bytes 4194308 | tf_op jit(solution)/shard_map/transpose | solution.py:77
  70.2 1.9 %copy.14 = bf16[4,2,16,4,16,128]{5,4,3,2,1,0:T(8,128)(2,1)} copy(bf16[4,2,16,4,16,128]{5,2,4,0,3,1:T(8,128)(2,1)S(1)} %fusion.3) | data formatting | bytes 4194304 | tf_op jit(solution)/shard_map/transpose | solution.py:77
  72.0 4.9 %shard_map.72 = f32[1,2048,128]{2,1,0:T(8,128)} custom-call(bf16[1,2,2048,128]{3,2,1,0:T(8,128)(2,1)} %bitcast.196, bf16[1,2,2048,128]{3,2,1,0:T(8,128)(2,1)} %bitcast.197, bf16[4,2048,128]{2,1,0:T(8,128)(2,1)} %bitcast.194), custom_call_target="tpu_custom_call" | custom-call | flops 8388608 | bytes 5242880 | tf_op jit(solution)/shard_map/pallas_call | solution.py:108
  77.0 2.2 %fusion.18 = f32[32,128,2,64]{1,3,2,0:T(8,128)S(1)} fusion(f32[32,64,128,1]{2,1,3,0:T(8,128)} %bitcast.198, f32[1,64,64]{2,1,0:T(8,128)S(1)} %copy-done.5, f32[1,64,64]{2,1,0:T(8,128)S(1)} %copy-done.7), kind=kOutput, calls=%fused_computation.50 | convolution fusion | flops 201334784 | bytes 3178496 | tf_op jit(solution)/shard_map/exk,rjkl->xrejl/dot_general | solution.py:162
  79.2 2.5 %copy.31 = f32[32,128,2,64]{1,0,2,3:T(8,128)} copy(f32[32,128,2,64]{1,3,2,0:T(8,128)S(1)} %fusion.18) | data formatting | bytes 4194304 | tf_op jit(solution)/shard_map/exk,rjkl->xrejl/dot_general | solution.py:162
  81.7 3.8 %shard_map.73 = f32[1,64,32,128]{3,2,1,0:T(8,128)} custom-call(f32[64,2,32,128]{3,2,1,0:T(8,128)} %bitcast.195), custom_call_target="tpu_custom_call" | custom-call | flops 786432 | bytes 3145728 | tf_op jit(solution)/shard_map/pallas_call | solution.py:42
  85.6 3.8 %all-to-all-start.2 = ((f32[2,32,1,32,128]{4,3,1,2,0:T(8,128)}), f32[2,32,1,32,128]{4,3,1,2,0:T(8,128)S(1)}, u32[]{:S(2)}, u32[]{:S(2)}) async-start(f32[2,32,1,32,128]{4,3,1,2,0:T(8,128)} %bitcast.199), calls=%async_computation.2 | async-start | bytes 2097152 | tf_op jit(solution)/shard_map/all_to_all | solution.py:165
  89.6 13.9 %all-to-all-done.2 = f32[2,32,1,32,128]{4,3,1,2,0:T(8,128)S(1)} async-done(((f32[2,32,1,32,128]{4,3,1,2,0:T(8,128)}), f32[2,32,1,32,128]{4,3,1,2,0:T(8,128)S(1)}, u32[]{:S(2)}, u32[]{:S(2)}) %all-to-all-start.2) | async-done | bytes 1048608 | tf_op jit(solution)/shard_map/all_to_all | solution.py:165
  104.5 2.4 %add_bitcast_fusion.in_ref = f32[32,2,64,128]{3,2,1,0:T(8,128)} fusion(f32[32,128,2,64]{1,3,2,0:T(8,128)S(1)} %fusion.15, f32[2,32,1,32,128]{4,3,1,2,0:T(8,128)S(1)} %all-to-all-done.2, f32[1,64,2,32]{1,3,0,2:T(8,128)S(1)} %get-tuple-element.4, f32[1,64,2,32]{1,3,0,2:T(8,128)S(1)} %get-tuple-element.5), kind=kOutput, calls=%fused_computation.16 | convolution fusion | flops 101191680 | bytes 4784128 | tf_op jit(solution)/shard_map/eyj,xrjl->rxeyl/dot_general | solution.py:168
  106.8 2.7 %shard_map.74 = f32[1,32,64,128]{3,2,1,0:T(8,128)} custom-call(f32[32,2,64,128]{3,2,1,0:T(8,128)} %add_bitcast_fusion.in_ref), custom_call_target="tpu_custom_call" | custom-call | flops 786432 | bytes 3145728 | tf_op jit(solution)/shard_map/pallas_call | solution.py:42
  109.5 1.9 %convolution_multiply_fusion = f32[32,64,64]{2,1,0:T(8,128)S(1)} fusion(f32[1,32,64,128]{3,2,1,0:T(8,128)} %shard_map.74, f32[64,64]{0,1:T(8,128)S(1)} %get-tuple-element.6, f32[64,64]{0,1:T(8,128)S(1)} %get-tuple-element.7), kind=kOutput, calls=%fused_computation.17 | convolution fusion | flops 100802560 | bytes 1605632 | tf_op jit(solution)/shard_map/rxyl,lz->rxyz/dot_general | solution.py:174
  112.6 1.6 %gather_fusion = f32[8,512]{1,0:T(8,128)S(1)} fusion(f32[256,512]{1,0:T(8,128)} %reshape.306, s32[1024]{0:T(1024)S(1)} %pad_clamp_fusion), kind=kCustom, calls=%fused_computation | custom fusion | bytes 32800 | tf_op jit(solution)/shard_map/gather | solution.py:181
  114.2 1.6 %fusion.68 = f32[8,512]{1,0:T(8,128)S(1)} fusion(f32[8,512]{1,0:T(8,128)S(1)} %gather_fusion, f32[512,512]{1,0:T(8,128)} %param.9), kind=kOutput, calls=%fused_computation.117 | convolution fusion | flops 12582912 | bytes 1081344 | tf_op jit(solution)/shard_map/dot_general | solution.py:190
  115.9 9.6 %all_to_all.20 = f32[8,2,512]{2,1,0:T(2,128)S(1)} all-to-all(f32[8,2,512]{2,1,0:T(2,128)S(1)} %reshape.308), channel_id=1, replica_groups=mesh['grp'=2,'rot'=4,'sub'=2,'ref'=2] {'rot','ref'}, dimensions={0} | all-to-all | bytes 65536 | tf_op jit(solution)/shard_map/all_to_all | solution.py:192
  (54 shorter events, 8.4 us)
Async XLA Ops:
  0.6 1.6 %copy-start = (f32[2,4,16,32,64]{4,3,2,1,0:T(8,128)S(1)}, f32[2,4,16,32,64]{4,3,2,1,0:T(8,128)}, u32[]{:S(2)}) copy-start(f32[2,4,16,32,64]{4,3,2,1,0:T(8,128)} %param.6) | copy-start | bytes 3145732
  2.2 7.4 %copy-start.3 = (bf16[1,4,32,64,64]{4,3,2,1,0:T(8,128)(2,1)S(1)}, bf16[1,4,32,64,64]{4,3,2,1,0:T(8,128)(2,1)}, u32[]{:S(2)}) copy-start(bf16[1,4,32,64,64]{4,3,2,1,0:T(8,128)(2,1)} %param.5) | copy-start | bytes 3145732
  3.3 34.4 %collective-permute-start = (bf16[4,16,16,128]{3,1,2,0:T(8,128)(2,1)}, bf16[4,16,16,128]{3,1,2,0:T(8,128)(2,1)S(1)}, u32[]{:S(2)}, u32[]{:S(2)}) collective-permute-start(bf16[4,16,16,128]{3,1,2,0:T(8,128)(2,1)} %fusion.67), channel_id=1, source_target_pairs={{0,12},{4,0},{8,4},{12,8},{1,13},{5,1},{9,5},{13,9},{2,14},{6,2},{... | collective-permute-start | bytes 786440 | tf_op jit(solution)/shard_map/ppermute | solution.py:62
  8.3 29.3 %collective-permute-start.1 = (bf16[4,16,16,128]{3,1,2,0:T(8,128)(2,1)}, bf16[4,16,16,128]{3,1,2,0:T(8,128)(2,1)S(1)}, u32[]{:S(2)}, u32[]{:S(2)}) collective-permute-start(bf16[4,16,16,128]{3,1,2,0:T(8,128)(2,1)} %fusion.67), channel_id=1, source_target_pairs={{0,8},{4,12},{8,0},{12,4},{1,9},{5,13},{9,1},{13,5},{2,10},{6,14},... | collective-permute-start | bytes 786440 | tf_op jit(solution)/shard_map/ppermute | solution.py:62
  8.3 29.4 %collective-permute-start.2 = (bf16[4,16,16,128]{3,1,2,0:T(8,128)(2,1)}, bf16[4,16,16,128]{3,1,2,0:T(8,128)(2,1)S(1)}, u32[]{:S(2)}, u32[]{:S(2)}) collective-permute-start(bf16[4,16,16,128]{3,1,2,0:T(8,128)(2,1)} %fusion.67), channel_id=1, source_target_pairs={{0,4},{4,8},{8,12},{12,0},{1,5},{5,9},{9,13},{13,1},{2,6},{6,10},{... | collective-permute-start | bytes 786440 | tf_op jit(solution)/shard_map/ppermute | solution.py:62
  9.6 17.0 %copy-start.4 = (f32[1,64,64]{2,1,0:T(8,128)}, f32[1,64,64]{2,1,0:T(8,128)S(1)}, u32[]{:S(2)}) copy-start(f32[1,64,64]{2,1,0:T(8,128)S(1)} %get-tuple-element.8) | copy-start | bytes 49156
  9.6 17.0 %copy-start.6 = (f32[1,64,64]{2,1,0:T(8,128)}, f32[1,64,64]{2,1,0:T(8,128)S(1)}, u32[]{:S(2)}) copy-start(f32[1,64,64]{2,1,0:T(8,128)S(1)} %get-tuple-element.9) | copy-start | bytes 49156
  21.1 18.6 %all-to-all-start = ((bf16[2,1,2,32,32,128]{5,3,4,2,1,0:T(8,128)(2,1)}), bf16[2,1,2,32,32,128]{5,3,4,2,1,0:T(8,128)(2,1)S(1)}, u32[]{:S(2)}, u32[]{:S(2)}) async-start(bf16[2,1,2,32,32,128]{5,3,4,2,1,0:T(8,128)(2,1)} %copy.12), calls=%async_computation | async-start | bytes 2097152 | tf_op jit(solution)/shard_map/all_to_all | solution.py:148
  39.4 28.0 %collective-permute-start.3 = (bf16[4,4,16,16,128]{4,2,3,1,0:T(8,128)(2,1)}, bf16[4,4,16,16,128]{4,2,3,1,0:T(8,128)(2,1)}, u32[]{:S(2)}, u32[]{:S(2)}) collective-permute-start(bf16[4,4,16,16,128]{4,2,3,1,0:T(8,128)(2,1)} %constant_dynamic-slice_fusion), channel_id=1, source_target_pairs={{0,1},{1,0},{2,3},{3,2},{4,5},{5,4},{6,7},{7,6},{8,9},{9,8},{10,11... | collective-permute-start | bytes 3145736 | tf_op jit(solution)/shard_map/ppermute | solution.py:62
  39.6 18.6 %all-to-all-start.1 = ((bf16[2,1,2,32,32,128]{5,3,4,2,1,0:T(8,128)(2,1)}), bf16[2,1,2,32,32,128]{5,3,4,2,1,0:T(8,128)(2,1)S(1)}, u32[]{:S(2)}, u32[]{:S(2)}) async-start(bf16[2,1,2,32,32,128]{5,3,4,2,1,0:T(8,128)(2,1)} %copy.13), calls=%async_computation.1 | async-start | bytes 2097152 | tf_op jit(solution)/shard_map/all_to_all | solution.py:148
  72.0 4.9 %copy-start.5 = (f32[1,64,64]{2,1,0:T(8,128)S(1)}, f32[1,64,64]{2,1,0:T(8,128)}, u32[]{:S(2)}) copy-start(f32[1,64,64]{2,1,0:T(8,128)} %copy-done.4) | copy-start | bytes 49156
  72.0 4.9 %copy-start.7 = (f32[1,64,64]{2,1,0:T(8,128)S(1)}, f32[1,64,64]{2,1,0:T(8,128)}, u32[]{:S(2)}) copy-start(f32[1,64,64]{2,1,0:T(8,128)} %copy-done.6) | copy-start | bytes 49156
  81.7 7.6 %copy-start.8 = (s32[1,1,1,8]{3,2,1,0:T(1,128)S(1)}, s32[1,1,1,8]{3,2,1,0:T(1,128)}, u32[]{:S(2)}) copy-start(s32[1,1,1,8]{3,2,1,0:T(1,128)} %param.7) | copy-start | bytes 100
  81.7 7.7 %copy-start.9 = (s32[1,1,1,8,1]{3,4,2,1,0:T(1,128)S(1)}, s32[1,1,1,8,1]{3,4,2,1,0:T(1,128)}, u32[]{:S(2)}) copy-start(s32[1,1,1,8,1]{3,4,2,1,0:T(1,128)} %param.8) | copy-start | bytes 100
  85.6 17.9 %all-to-all-start.2 = ((f32[2,32,1,32,128]{4,3,1,2,0:T(8,128)}), f32[2,32,1,32,128]{4,3,1,2,0:T(8,128)S(1)}, u32[]{:S(2)}, u32[]{:S(2)}) async-start(f32[2,32,1,32,128]{4,3,1,2,0:T(8,128)} %bitcast.199), calls=%async_computation.2 | async-start | bytes 2097152 | tf_op jit(solution)/shard_map/all_to_all | solution.py:165
  106.8 19.3 %copy-start.1 = (f32[2,4,16,32,64]{4,3,2,1,0:T(8,128)S(1)}, f32[2,4,16,32,64]{4,3,2,1,0:T(8,128)}, u32[]{:S(2)}) copy-start(f32[2,4,16,32,64]{4,3,2,1,0:T(8,128)} %param.6) | copy-start | bytes 3145732
  111.4 14.8 %copy-start.2 = (f32[32,64,64]{2,1,0:T(8,128)}, f32[32,64,64]{2,1,0:T(8,128)S(1)}, u32[]{:S(2)}) copy-start(f32[32,64,64]{2,1,0:T(8,128)S(1)} %convolution_multiply_fusion) | copy-start | bytes 1572868
where the time goes:
time: 127 us; the launch traced here: 126 us
  matrix products  29 us (23%)
  Pallas kernels  28.8 us (23%)
  waiting for transfers between devices  19.4 us (15%)
  starting transfers between devices  17.2 us (14%)
  local copies, waits for them, and re-layouts  16.4 us (13%)
  blocking collectives  9.63 us (8%)
  other arithmetic  4.63 us (4%)
    pallas_call x6, Pallas kernels, combine_call(): pl.pallas_call(functools.partial(combine_kernel, first=first, second=seco...  23.9 us
    all_to_all x1, waiting for transfers between devices, local(): lax.all_to_all(back_x, 'sub', split_axis=0, concat_axis=0, tiled=True)  13.9 us
    dot_general x4, matrix products, local(): jnp.einsum('ekx,rtxjl->rtjekl', pair_x[:, :, s], turned[s], precision=hig...  9.8 us
    all_to_all x1, blocking collectives, local(): lax.all_to_all(packed, ('rot', 'ref'), split_axis=0, concat_axis=0, tiled...  9.63 us
    dot_general x2, matrix products, local(): along_y = jnp.einsum('ejy,rtxyl->rtxejl', pair, along_z, precision=highest)  7.45 us
    all_to_all x2, starting transfers between devices, local(): lax.all_to_all(sending, 'sub', split_axis=0, concat_axis=0, tiled=True)  7.35 us
    ppermute x4, starting transfers between devices, gather_by_shifts(): pieces.append(lax.ppermute(piece, axis, pairs))  6.06 us
    all_to_all x2, waiting for transfers between devices, local(): lax.all_to_all(sending, 'sub', split_axis=0, concat_axis=0, tiled=True)  5.54 us
  transfers between devices with their start and end apart: 7, of which 2 were waited for; matrix products, arithmetic and copies ran while one was open for 22% of the time, Pallas kernels for 14%

commit v1 on v0

--- a/solution.py
+++ b/solution.py
@@ -28,7 +28,7 @@
     half = lanes // 2
     cos_part = in_ref[:, 0].reshape(batch * rows, lanes)
     sin_part = in_ref[:, 1].reshape(batch * rows, lanes)
-    low = lax.broadcasted_iota(jnp.int32, cos_part.shape, 1) < half
+    low = lax.broadcasted_iota(jnp.int32, (1, lanes), 1) < half
     signs = jnp.where(low, first, second).astype(jnp.float32)
     result = (cos_part + pltpu.roll(sin_part, half, 1) * signs).reshape(batch, rows, lanes)
     for piece in range(split):
@@ -37,7 +37,7 @@
 
 def combine_call(stacked, first, second, split, dtype):
     batch, _, rows, lanes = stacked.shape
-    block = max(b for b in range(1, 17) if batch % b == 0)
+    block = max(b for b in range(1, 33) if batch % b == 0)
     part = rows // split
     return pl.pallas_call(
         functools.partial(combine_kernel, first=first, second=second),
@@ -89,7 +89,7 @@
             spec = spec_ref[inner].astype(jnp.float32)
             rec = rec_ref[term].astype(jnp.float32)
             term += 1
-            low = lax.broadcasted_iota(jnp.int32, rec.shape, 1) < half
+            low = lax.broadcasted_iota(jnp.int32, (1, lanes), 1) < half
             rec_turned = pltpu.roll(rec, half, 1)
             rec_real = jnp.where(low, rec, rec_turned)
             rec_imag = jnp.where(low, rec_turned, -rec)

time: 127 us -> 123 us (0.969)
  Pallas kernels: 28.8 us -> 24 us
    pallas_call x6, Pallas kernels: 23.9 us -> 19 us  [combine_call(): pl.pallas_call(functools.partial(combine_kernel, first=first, second=seco...]
  transfers between devices with their start and end apart: 7 -> 7, of which waited for: 2 -> 2; matrix products, arithmetic and copies ran while one was open for 22% -> 23% of each run, Pallas kernels for 14% -> 11%
where the time goes in v1:
time: 123 us; the launch traced here: 122 us
  matrix products  29.1 us (24%)
  Pallas kernels  24 us (20%)
  waiting for transfers between devices  20.4 us (17%)
  starting transfers between devices  17.2 us (14%)
  local copies, waits for them, and re-layouts  16.4 us (13%)
  blocking collectives  9.63 us (8%)
  other arithmetic  4.63 us (4%)
    pallas_call x6, Pallas kernels, combine_call(): pl.pallas_call(functools.partial(combine_kernel, first=first, second=seco...  19 us
    all_to_all x1, waiting for transfers between devices, local(): lax.all_to_all(back_x, 'sub', split_axis=0, concat_axis=0, tiled=True)  13.9 us
    dot_general x4, matrix products, local(): jnp.einsum('ekx,rtxjl->rtjekl', pair_x[:, :, s], turned[s], precision=hig...  9.8 us
    all_to_all x1, blocking collectives, local(): lax.all_to_all(packed, ('rot', 'ref'), split_axis=0, concat_axis=0, tiled...  9.63 us
    dot_general x2, matrix products, local(): along_y = jnp.einsum('ejy,rtxyl->rtxejl', pair, along_z, precision=highest)  7.45 us
    all_to_all x2, starting transfers between devices, local(): lax.all_to_all(sending, 'sub', split_axis=0, concat_axis=0, tiled=True)  7.35 us
    all_to_all x2, waiting for transfers between devices, local(): lax.all_to_all(sending, 'sub', split_axis=0, concat_axis=0, tiled=True)  6.53 us
    ppermute x4, starting transfers between devices, gather_by_shifts(): pieces.append(lax.ppermute(piece, axis, pairs))  6.06 us
  transfers between devices with their start and end apart: 7, of which 2 were waited for; matrix products, arithmetic and copies ran while one was open for 23% of the time, Pallas kernels for 11%

profile of v1, /device:TPU:0, one launch (start us, length us, event | category | flops | bytes accessed | tf_op | source)
XLA Modules:
  0.0 122.3 jit_solution(15970066547798460689)
XLA Ops:
  0.7 1.6 %copy-done = f32[2,4,16,32,64]{4,3,2,1,0:T(8,128)S(1)} copy-done((f32[2,4,16,32,64]{4,3,2,1,0:T(8,128)S(1)}, f32[2,4,16,32,64]{4,3,2,1,0:T(8,128)}, u32[]{:S(2)}) %copy-start) | copy-done | bytes 1048600
  3.3 5.0 %collective-permute-start = (bf16[4,16,16,128]{3,1,2,0:T(8,128)(2,1)}, bf16[4,16,16,128]{3,1,2,0:T(8,128)(2,1)S(1)}, u32[]{:S(2)}, u32[]{:S(2)}) collective-permute-start(bf16[4,16,16,128]{3,1,2,0:T(8,128)(2,1)} %fusion.67), channel_id=1, source_target_pairs={{0,12},{4,0},{8,4},{12,8},{1,13},{5,1},{9,5},{13,9},{2,14},{6,2},{... | collective-permute-start | bytes 786440 | tf_op jit(solution)/shard_map/ppermute | solution.py:62
  10.4 3.7 %fusion.6 = f32[2,32,128,2,64]{2,4,3,1,0:T(8,128)} fusion(f32[128,2,32,64]{0,3,2,1:T(8,128)S(1)} %fusion.11, f32[1,64,64]{2,1,0:T(8,128)S(1)} %get-tuple-element.8, f32[1,64,64]{2,1,0:T(8,128)S(1)} %get-tuple-element.9), kind=kOutput, calls=%fused_computation.13 | convolution fusion | flops 402661376 | bytes 6324224 | tf_op jit(solution)/shard_map/ejy,rtxyl->rtxejl/dot_general | solution.py:144
  14.1 3.4 %shard_map.68 = bf16[2,64,32,128]{3,2,1,0:T(8,128)(2,1)} custom-call(f32[64,2,64,128]{3,2,1,0:T(8,128)} %bitcast.193), custom_call_target="tpu_custom_call" | custom-call | flops 1572864 | bytes 5242880 | tf_op jit(solution)/shard_map/pallas_call | solution.py:42
  17.5 2.6 %copy.12 = bf16[2,1,2,32,32,128]{5,3,4,2,1,0:T(8,128)(2,1)} copy(bf16[2,1,2,32,32,128]{5,4,3,2,0,1:T(8,128)(2,1)} %bitcast.200) | data formatting | bytes 2097152 | tf_op jit(solution)/shard_map/reshape | solution.py:147
  20.1 3.6 %all-to-all-start = ((bf16[2,1,2,32,32,128]{5,3,4,2,1,0:T(8,128)(2,1)}), bf16[2,1,2,32,32,128]{5,3,4,2,1,0:T(8,128)(2,1)S(1)}, u32[]{:S(2)}, u32[]{:S(2)}) async-start(bf16[2,1,2,32,32,128]{5,3,4,2,1,0:T(8,128)(2,1)} %copy.12), calls=%async_computation | async-start | bytes 2097152 | tf_op jit(solution)/shard_map/all_to_all | solution.py:148
  23.7 1.9 %fusion.9 = f32[128,2,32,64]{0,3,2,1:T(8,128)S(1)} fusion(bf16[1,4,32,64,64]{4,3,2,1,0:T(8,128)(2,1)} %param.5, f32[64,64]{0,1:T(8,128)S(1)} %get-tuple-element.6, f32[64,64]{0,1:T(8,128)S(1)} %get-tuple-element.7), kind=kOutput, calls=%fused_computation.19 | convolution fusion | flops 201334784 | bytes 3178496 | tf_op jit(solution)/shard_map/rtxyz,zl->rtxyl/dot_general | solution.py:143
  25.6 3.7 %fusion.4 = f32[2,32,128,2,64]{2,4,3,1,0:T(8,128)} fusion(f32[128,2,32,64]{0,3,2,1:T(8,128)S(1)} %fusion.9, f32[1,64,64]{2,1,0:T(8,128)S(1)} %get-tuple-element.8, f32[1,64,64]{2,1,0:T(8,128)S(1)} %get-tuple-element.9), kind=kOutput, calls=%fused_computation.11 | convolution fusion | flops 402661376 | bytes 6324224 | tf_op jit(solution)/shard_map/ejy,rtxyl->rtxejl/dot_general | solution.py:144
  29.6 3.4 %shard_map.70 = bf16[2,64,32,128]{3,2,1,0:T(8,128)(2,1)} custom-call(f32[64,2,64,128]{3,2,1,0:T(8,128)} %bitcast.192), custom_call_target="tpu_custom_call" | custom-call | flops 1572864 | bytes 5242880 | tf_op jit(solution)/shard_map/pallas_call | solution.py:42
  33.0 2.7 %copy.13 = bf16[2,1,2,32,32,128]{5,3,4,2,1,0:T(8,128)(2,1)} copy(bf16[2,1,2,32,32,128]{5,4,3,2,0,1:T(8,128)(2,1)} %bitcast.201) | data formatting | bytes 2097152 | tf_op jit(solution)/shard_map/reshape | solution.py:147
  37.7 3.8 %all-to-all-start.1 = ((bf16[2,1,2,32,32,128]{5,3,4,2,1,0:T(8,128)(2,1)}), bf16[2,1,2,32,32,128]{5,3,4,2,1,0:T(8,128)(2,1)S(1)}, u32[]{:S(2)}, u32[]{:S(2)}) async-start(bf16[2,1,2,32,32,128]{5,3,4,2,1,0:T(8,128)(2,1)} %copy.13), calls=%async_computation.1 | async-start | bytes 2097152 | tf_op jit(solution)/shard_map/all_to_all | solution.py:148
  41.5 1.3 %fusion.17 = f32[2,32,128,2,64]{2,4,3,1,0:T(8,128)S(1)} fusion(bf16[2,1,2,32,32,128]{5,3,4,2,1,0:T(8,128)(2,1)S(1)} %all-to-all-done, f32[1,64,2,32]{1,3,0,2:T(8,128)S(1)} %get-tuple-element.5, f32[1,64,2,32]{1,3,0,2:T(8,128)S(1)} %get-tuple-element.4), kind=kOutput, calls=%fused_computation.34 | convolution fusion | flops 201330688 | bytes 4784128 | tf_op jit(solution)/shard_map/ekx,rtxjl->rtjekl/dot_general | solution.py:151
  42.8 3.6 %convolution_add_fusion.1 = f32[2,32,128,2,64]{2,4,3,1,0:T(8,128)} fusion(f32[2,32,128,2,64]{2,4,3,1,0:T(8,128)S(1)} %fusion.17, bf16[2,1,2,32,32,128]{5,3,4,2,1,0:T(8,128)(2,1)S(1)} %all-to-all-done, f32[1,64,2,32]{1,3,0,2:T(8,128)S(1)} %get-tuple-element.4, f32[1,64,2,32]{1,3,0,2:T(8,128)S(1)} %get-tuple-element.5), kind=kOutput, calls=%fused_computation.6 | convolution fusion | flops 202379264 | bytes 8978432 | tf_op jit(solution)/shard_map/ekx,rtxjl->rtjekl/dot_general | solution.py:151
  46.4 3.4 %shard_map.69 = bf16[1,64,64,128]{3,2,1,0:T(8,128)(2,1)} custom-call(f32[64,2,64,128]{3,2,1,0:T(8,128)} %bitcast.190), custom_call_target="tpu_custom_call" | custom-call | flops 1572864 | bytes 5242880 | tf_op jit(solution)/shard_map/pallas_call | solution.py:42
  49.7 6.5 %all-to-all-done.1 = bf16[2,1,2,32,32,128]{5,3,4,2,1,0:T(8,128)(2,1)S(1)} async-done(((bf16[2,1,2,32,32,128]{5,3,4,2,1,0:T(8,128)(2,1)}), bf16[2,1,2,32,32,128]{5,3,4,2,1,0:T(8,128)(2,1)S(1)}, u32[]{:S(2)}, u32[]{:S(2)}) %all-to-all-start.1) | async-done | bytes 1048608 | tf_op jit(solution)/shard_map/all_to_all | solution.py:148
  56.3 1.3 %fusion.16 = f32[2,32,128,2,64]{2,4,3,1,0:T(8,128)S(1)} fusion(bf16[2,1,2,32,32,128]{5,3,4,2,1,0:T(8,128)(2,1)S(1)} %all-to-all-done.1, f32[1,64,2,32]{1,3,0,2:T(8,128)S(1)} %get-tuple-element.5, f32[1,64,2,32]{1,3,0,2:T(8,128)S(1)} %get-tuple-element.4), kind=kOutput, calls=%fused_computation.31 | convolution fusion | flops 201330688 | bytes 4784128 | tf_op jit(solution)/shard_map/ekx,rtxjl->rtjekl/dot_general | solution.py:151
  57.6 3.6 %convolution_add_fusion = f32[2,32,128,2,64]{2,4,3,1,0:T(8,128)} fusion(f32[2,32,128,2,64]{2,4,3,1,0:T(8,128)S(1)} %fusion.16, bf16[2,1,2,32,32,128]{5,3,4,2,1,0:T(8,128)(2,1)S(1)} %all-to-all-done.1, f32[1,64,2,32]{1,3,0,2:T(8,128)S(1)} %get-tuple-element.4, f32[1,64,2,32]{1,3,0,2:T(8,128)S(1)} %get-tuple-element.5), kind=kOutput, calls=%fused_computation.5 | convolution fusion | flops 202379264 | bytes 8978432 | tf_op jit(solution)/shard_map/ekx,rtxjl->rtjekl/dot_general | solution.py:151
  61.2 3.4 %shard_map.71 = bf16[1,64,64,128]{3,2,1,0:T(8,128)(2,1)} custom-call(f32[64,2,64,128]{3,2,1,0:T(8,128)} %bitcast.191), custom_call_target="tpu_custom_call" | custom-call | flops 1572864 | bytes 5242880 | tf_op jit(solution)/shard_map/pallas_call | solution.py:42
  64.5 2.7 %fusion.3 = bf16[4,2,16,4,16,128]{5,2,4,0,3,1:T(8,128)(2,1)S(1)} fusion(s32[]{:T(128)S(6)} %select_n.79, bf16[1,4,4,16,16,128]{5,3,4,2,1,0:T(8,128)(2,1)} %bitcast.59, bf16[1,4,4,16,16,128]{5,3,4,2,1,0:T(8,128)(2,1)S(1)} %fusion.73), kind=kLoop, calls=%fused_computation.10 | loop fusion | flops 3145728 | bytes 4194308 | tf_op jit(solution)/shard_map/transpose | solution.py:77
  67.2 1.9 %copy.14 = bf16[4,2,16,4,16,128]{5,4,3,2,1,0:T(8,128)(2,1)} copy(bf16[4,2,16,4,16,128]{5,2,4,0,3,1:T(8,128)(2,1)S(1)} %fusion.3) | data formatting | bytes 4194304 | tf_op jit(solution)/shard_map/transpose | solution.py:77
  69.1 4.9 %shard_map.72 = f32[1,2048,128]{2,1,0:T(8,128)} custom-call(bf16[1,2,2048,128]{3,2,1,0:T(8,128)(2,1)} %bitcast.196, bf16[1,2,2048,128]{3,2,1,0:T(8,128)(2,1)} %bitcast.197, bf16[4,2048,128]{2,1,0:T(8,128)(2,1)} %bitcast.194), custom_call_target="tpu_custom_call" | custom-call | flops 8388608 | bytes 5242880 | tf_op jit(solution)/shard_map/pallas_call | solution.py:108
  74.0 2.2 %fusion.18 = f32[32,128,2,64]{1,3,2,0:T(8,128)S(1)} fusion(f32[32,64,128,1]{2,1,3,0:T(8,128)} %bitcast.198, f32[1,64,64]{2,1,0:T(8,128)S(1)} %copy-done.5, f32[1,64,64]{2,1,0:T(8,128)S(1)} %copy-done.7), kind=kOutput, calls=%fused_computation.50 | convolution fusion | flops 201334784 | bytes 3178496 | tf_op jit(solution)/shard_map/exk,rjkl->xrejl/dot_general | solution.py:162
  76.2 2.5 %copy.31 = f32[32,128,2,64]{1,0,2,3:T(8,128)} copy(f32[32,128,2,64]{1,3,2,0:T(8,128)S(1)} %fusion.18) | data formatting | bytes 4194304 | tf_op jit(solution)/shard_map/exk,rjkl->xrejl/dot_general | solution.py:162
  78.8 2.6 %shard_map.73 = f32[1,64,32,128]{3,2,1,0:T(8,128)} custom-call(f32[64,2,32,128]{3,2,1,0:T(8,128)} %bitcast.195), custom_call_target="tpu_custom_call" | custom-call | flops 786432 | bytes 3145728 | tf_op jit(solution)/shard_map/pallas_call | solution.py:42
  81.3 3.8 %all-to-all-start.2 = ((f32[2,32,1,32,128]{4,3,1,2,0:T(8,128)}), f32[2,32,1,32,128]{4,3,1,2,0:T(8,128)S(1)}, u32[]{:S(2)}, u32[]{:S(2)}) async-start(f32[2,32,1,32,128]{4,3,1,2,0:T(8,128)} %bitcast.199), calls=%async_computation.2 | async-start | bytes 2097152 | tf_op jit(solution)/shard_map/all_to_all | solution.py:165
  85.4 13.9 %all-to-all-done.2 = f32[2,32,1,32,128]{4,3,1,2,0:T(8,128)S(1)} async-done(((f32[2,32,1,32,128]{4,3,1,2,0:T(8,128)}), f32[2,32,1,32,128]{4,3,1,2,0:T(8,128)S(1)}, u32[]{:S(2)}, u32[]{:S(2)}) %all-to-all-start.2) | async-done | bytes 1048608 | tf_op jit(solution)/shard_map/all_to_all | solution.py:165
  100.3 2.4 %add_bitcast_fusion.in_ref = f32[32,2,64,128]{3,2,1,0:T(8,128)} fusion(f32[32,128,2,64]{1,3,2,0:T(8,128)S(1)} %fusion.15, f32[2,32,1,32,128]{4,3,1,2,0:T(8,128)S(1)} %all-to-all-done.2, f32[1,64,2,32]{1,3,0,2:T(8,128)S(1)} %get-tuple-element.4, f32[1,64,2,32]{1,3,0,2:T(8,128)S(1)} %get-tuple-element.5), kind=kOutput, calls=%fused_computation.16 | convolution fusion | flops 101191680 | bytes 4784128 | tf_op jit(solution)/shard_map/eyj,xrjl->rxeyl/dot_general | solution.py:168
  102.6 3.0 %shard_map.74 = f32[1,32,64,128]{3,2,1,0:T(8,128)} custom-call(f32[32,2,64,128]{3,2,1,0:T(8,128)} %add_bitcast_fusion.in_ref), custom_call_target="tpu_custom_call" | custom-call | flops 786432 | bytes 3145728 | tf_op jit(solution)/shard_map/pallas_call | solution.py:42
  105.7 1.9 %convolution_multiply_fusion = f32[32,64,64]{2,1,0:T(8,128)S(1)} fusion(f32[1,32,64,128]{3,2,1,0:T(8,128)} %shard_map.74, f32[64,64]{0,1:T(8,128)S(1)} %get-tuple-element.6, f32[64,64]{0,1:T(8,128)S(1)} %get-tuple-element.7), kind=kOutput, calls=%fused_computation.17 | convolution fusion | flops 100802560 | bytes 1605632 | tf_op jit(solution)/shard_map/rxyl,lz->rxyz/dot_general | solution.py:174
  108.7 1.6 %gather_fusion = f32[8,512]{1,0:T(8,128)S(1)} fusion(f32[256,512]{1,0:T(8,128)} %reshape.306, s32[1024]{0:T(1024)S(1)} %pad_clamp_fusion), kind=kCustom, calls=%fused_computation | custom fusion | bytes 32800 | tf_op jit(solution)/shard_map/gather | solution.py:181
  110.3 1.6 %fusion.68 = f32[8,512]{1,0:T(8,128)S(1)} fusion(f32[8,512]{1,0:T(8,128)S(1)} %gather_fusion, f32[512,512]{1,0:T(8,128)} %param.9), kind=kOutput, calls=%fused_computation.117 | convolution fusion | flops 12582912 | bytes 1081344 | tf_op jit(solution)/shard_map/dot_general | solution.py:190
  112.1 9.6 %all_to_all.20 = f32[8,2,512]{2,1,0:T(2,128)S(1)} all-to-all(f32[8,2,512]{2,1,0:T(2,128)S(1)} %reshape.308), channel_id=1, replica_groups=mesh['grp'=2,'rot'=4,'sub'=2,'ref'=2] {'rot','ref'}, dimensions={0} | all-to-all | bytes 65536 | tf_op jit(solution)/shard_map/all_to_all | solution.py:192
  (54 shorter events, 8.4 us)
Async XLA Ops:
  0.6 1.6 %copy-start = (f32[2,4,16,32,64]{4,3,2,1,0:T(8,128)S(1)}, f32[2,4,16,32,64]{4,3,2,1,0:T(8,128)}, u32[]{:S(2)}) copy-start(f32[2,4,16,32,64]{4,3,2,1,0:T(8,128)} %param.6) | copy-start | bytes 3145732
  2.2 7.4 %copy-start.3 = (bf16[1,4,32,64,64]{4,3,2,1,0:T(8,128)(2,1)S(1)}, bf16[1,4,32,64,64]{4,3,2,1,0:T(8,128)(2,1)}, u32[]{:S(2)}) copy-start(bf16[1,4,32,64,64]{4,3,2,1,0:T(8,128)(2,1)} %param.5) | copy-start | bytes 3145732
  3.3 32.4 %collective-permute-start = (bf16[4,16,16,128]{3,1,2,0:T(8,128)(2,1)}, bf16[4,16,16,128]{3,1,2,0:T(8,128)(2,1)S(1)}, u32[]{:S(2)}, u32[]{:S(2)}) collective-permute-start(bf16[4,16,16,128]{3,1,2,0:T(8,128)(2,1)} %fusion.67), channel_id=1, source_target_pairs={{0,12},{4,0},{8,4},{12,8},{1,13},{5,1},{9,5},{13,9},{2,14},{6,2},{... | collective-permute-start | bytes 786440 | tf_op jit(solution)/shard_map/ppermute | solution.py:62
  8.3 27.4 %collective-permute-start.1 = (bf16[4,16,16,128]{3,1,2,0:T(8,128)(2,1)}, bf16[4,16,16,128]{3,1,2,0:T(8,128)(2,1)S(1)}, u32[]{:S(2)}, u32[]{:S(2)}) collective-permute-start(bf16[4,16,16,128]{3,1,2,0:T(8,128)(2,1)} %fusion.67), channel_id=1, source_target_pairs={{0,8},{4,12},{8,0},{12,4},{1,9},{5,13},{9,1},{13,5},{2,10},{6,14},... | collective-permute-start | bytes 786440 | tf_op jit(solution)/shard_map/ppermute | solution.py:62
  8.3 27.4 %collective-permute-start.2 = (bf16[4,16,16,128]{3,1,2,0:T(8,128)(2,1)}, bf16[4,16,16,128]{3,1,2,0:T(8,128)(2,1)S(1)}, u32[]{:S(2)}, u32[]{:S(2)}) collective-permute-start(bf16[4,16,16,128]{3,1,2,0:T(8,128)(2,1)} %fusion.67), channel_id=1, source_target_pairs={{0,4},{4,8},{8,12},{12,0},{1,5},{5,9},{9,13},{13,1},{2,6},{6,10},{... | collective-permute-start | bytes 786440 | tf_op jit(solution)/shard_map/ppermute | solution.py:62
  9.6 16.0 %copy-start.4 = (f32[1,64,64]{2,1,0:T(8,128)}, f32[1,64,64]{2,1,0:T(8,128)S(1)}, u32[]{:S(2)}) copy-start(f32[1,64,64]{2,1,0:T(8,128)S(1)} %get-tuple-element.8) | copy-start | bytes 49156
  9.6 16.0 %copy-start.6 = (f32[1,64,64]{2,1,0:T(8,128)}, f32[1,64,64]{2,1,0:T(8,128)S(1)}, u32[]{:S(2)}) copy-start(f32[1,64,64]{2,1,0:T(8,128)S(1)} %get-tuple-element.9) | copy-start | bytes 49156
  20.1 17.6 %all-to-all-start = ((bf16[2,1,2,32,32,128]{5,3,4,2,1,0:T(8,128)(2,1)}), bf16[2,1,2,32,32,128]{5,3,4,2,1,0:T(8,128)(2,1)S(1)}, u32[]{:S(2)}, u32[]{:S(2)}) async-start(bf16[2,1,2,32,32,128]{5,3,4,2,1,0:T(8,128)(2,1)} %copy.12), calls=%async_computation | async-start | bytes 2097152 | tf_op jit(solution)/shard_map/all_to_all | solution.py:148
  37.5 27.0 %collective-permute-start.3 = (bf16[4,4,16,16,128]{4,2,3,1,0:T(8,128)(2,1)}, bf16[4,4,16,16,128]{4,2,3,1,0:T(8,128)(2,1)}, u32[]{:S(2)}, u32[]{:S(2)}) collective-permute-start(bf16[4,4,16,16,128]{4,2,3,1,0:T(8,128)(2,1)} %constant_dynamic-slice_fusion), channel_id=1, source_target_pairs={{0,1},{1,0},{2,3},{3,2},{4,5},{5,4},{6,7},{7,6},{8,9},{9,8},{10,11... | collective-permute-start | bytes 3145736 | tf_op jit(solution)/shard_map/ppermute | solution.py:62
  37.7 18.6 %all-to-all-start.1 = ((bf16[2,1,2,32,32,128]{5,3,4,2,1,0:T(8,128)(2,1)}), bf16[2,1,2,32,32,128]{5,3,4,2,1,0:T(8,128)(2,1)S(1)}, u32[]{:S(2)}, u32[]{:S(2)}) async-start(bf16[2,1,2,32,32,128]{5,3,4,2,1,0:T(8,128)(2,1)} %copy.13), calls=%async_computation.1 | async-start | bytes 2097152 | tf_op jit(solution)/shard_map/all_to_all | solution.py:148
  69.1 4.9 %copy-start.5 = (f32[1,64,64]{2,1,0:T(8,128)S(1)}, f32[1,64,64]{2,1,0:T(8,128)}, u32[]{:S(2)}) copy-start(f32[1,64,64]{2,1,0:T(8,128)} %copy-done.4) | copy-start | bytes 49156
  69.1 4.9 %copy-start.7 = (f32[1,64,64]{2,1,0:T(8,128)S(1)}, f32[1,64,64]{2,1,0:T(8,128)}, u32[]{:S(2)}) copy-start(f32[1,64,64]{2,1,0:T(8,128)} %copy-done.6) | copy-start | bytes 49156
  78.8 6.4 %copy-start.8 = (s32[1,1,1,8]{3,2,1,0:T(1,128)S(1)}, s32[1,1,1,8]{3,2,1,0:T(1,128)}, u32[]{:S(2)}) copy-start(s32[1,1,1,8]{3,2,1,0:T(1,128)} %param.7) | copy-start | bytes 100
  78.8 6.4 %copy-start.9 = (s32[1,1,1,8,1]{3,4,2,1,0:T(1,128)S(1)}, s32[1,1,1,8,1]{3,4,2,1,0:T(1,128)}, u32[]{:S(2)}) copy-start(s32[1,1,1,8,1]{3,4,2,1,0:T(1,128)} %param.8) | copy-start | bytes 100
  81.3 17.9 %all-to-all-start.2 = ((f32[2,32,1,32,128]{4,3,1,2,0:T(8,128)}), f32[2,32,1,32,128]{4,3,1,2,0:T(8,128)S(1)}, u32[]{:S(2)}, u32[]{:S(2)}) async-start(f32[2,32,1,32,128]{4,3,1,2,0:T(8,128)} %bitcast.199), calls=%async_computation.2 | async-start | bytes 2097152 | tf_op jit(solution)/shard_map/all_to_all | solution.py:165
  102.6 19.7 %copy-start.1 = (f32[2,4,16,32,64]{4,3,2,1,0:T(8,128)S(1)}, f32[2,4,16,32,64]{4,3,2,1,0:T(8,128)}, u32[]{:S(2)}) copy-start(f32[2,4,16,32,64]{4,3,2,1,0:T(8,128)} %param.6) | copy-start | bytes 3145732
  107.6 14.8 %copy-start.2 = (f32[32,64,64]{2,1,0:T(8,128)}, f32[32,64,64]{2,1,0:T(8,128)S(1)}, u32[]{:S(2)}) copy-start(f32[32,64,64]{2,1,0:T(8,128)S(1)} %convolution_multiply_fusion) | copy-start | bytes 1572868

commit v2 on v1

--- a/solution.py
+++ b/solution.py
@@ -159,15 +159,22 @@
     whole_receptor = gather_receptor(receptor)
     product = correlate(spectra, whole_receptor)
 
-    back_x = jnp.einsum("exk,rjkl->xrejl", pair, product, precision=highest)
-    back_x = combine_call(back_x.reshape(-1, 2, y_local, 2 * length), -1.0, 1.0, 1, jnp.float32)
-    back_x = back_x.reshape(n_sub, x_local, rots, y_local, 2 * length)
-    returned = lax.all_to_all(back_x, "sub", split_axis=0, concat_axis=0, tiled=True)
+    halves = 2 if y_local % 16 == 0 else 1
+    rows_half = y_local // halves
     pair_y = pair.reshape(2, length, n_sub, y_local)
-    back_y = sum(
-        jnp.einsum("eyj,xrjl->rxeyl", pair_y[:, :, s], returned[s], precision=highest)
-        for s in range(n_sub)
-    )
+    back_y = 0.0
+    for h in range(halves):
+        rows = slice(h * rows_half, (h + 1) * rows_half)
+        back_x = jnp.einsum("exk,rjkl->xrejl", pair, product[:, rows], precision=highest)
+        back_x = combine_call(
+            back_x.reshape(-1, 2, rows_half, 2 * length), -1.0, 1.0, 1, jnp.float32
+        )
+        back_x = back_x.reshape(n_sub, x_local, rots, rows_half, 2 * length)
+        returned = lax.all_to_all(back_x, "sub", split_axis=0, concat_axis=0, tiled=True)
+        back_y = back_y + sum(
+            jnp.einsum("eyj,xrjl->rxeyl", pair_y[:, :, s, rows], returned[s], precision=highest)
+            for s in range(n_sub)
+        )
     back_y = combine_call(back_y.reshape(-1, 2, ny, 2 * length), -1.0, 1.0, 1, jnp.float32)
     back_y = back_y.reshape(rots, x_local, ny, 2 * length)
     last_table = jnp.concatenate([cos_table, -sin_table], axis=0)

time: 123 us -> 128 us (1.041)
  waiting for transfers between devices: 20.4 us -> 15.3 us
  matrix products: 29.1 us -> 32.8 us
  starting transfers between devices: 17.2 us -> 20.6 us
  Pallas kernels: 24 us -> 25.5 us
  local copies, waits for them, and re-layouts: 16.4 us -> 17.7 us
    all_to_all x1 -> x2, waiting for transfers between devices: 13.9 us -> 8.75 us  [local(): lax.all_to_all(back_x, 'sub', split_axis=0, concat_axis=0, tiled=True)]
    dot_general x3 -> x6, matrix products: 5.57 us -> 9.31 us  [the longest x4 7.16 us: local(): jnp.einsum('eyj,xrjl->rxeyl', pair_y[:, :, s, rows], returned[s], precisi...]
    all_to_all x1 -> x2, starting transfers between devices: 3.8 us -> 7.19 us  [local(): lax.all_to_all(back_x, 'sub', split_axis=0, concat_axis=0, tiled=True)]
    pallas_call x6 -> x7, Pallas kernels: 19 us -> 20.6 us  [combine_call(): pl.pallas_call(functools.partial(combine_kernel, first=first, second=seco...]
    dot_general x1 -> x2, local copies, waits for them, and re-layouts: 2.55 us -> 3.16 us  [local(): jnp.einsum('exk,rjkl->xrejl', pair, product[:, rows], precision=highest)]
    unnamed x27 -> x31, local copies, waits for them, and re-layouts: 2.44 us -> 3.02 us
  transfers between devices with their start and end apart: 7 -> 8, of which waited for: 2 -> 3; matrix products, arithmetic and copies ran while one was open for 23% -> 26% of each run, Pallas kernels for 11% -> 12%
where the time goes in v2:
time: 128 us; the launch traced here: 127 us
  matrix products  32.8 us (26%)
  Pallas kernels  25.5 us (20%)
  starting transfers between devices  20.6 us (16%)
  local copies, waits for them, and re-layouts  17.7 us (14%)
  waiting for transfers between devices  15.3 us (12%)
  blocking collectives  9.63 us (8%)
  other arithmetic  4.62 us (4%)
    pallas_call x7, Pallas kernels, combine_call(): pl.pallas_call(functools.partial(combine_kernel, first=first, second=seco...  20.6 us
    dot_general x4, matrix products, local(): jnp.einsum('ekx,rtxjl->rtjekl', pair_x[:, :, s], turned[s], precision=hig...  9.8 us
    all_to_all x1, blocking collectives, local(): lax.all_to_all(packed, ('rot', 'ref'), split_axis=0, concat_axis=0, tiled...  9.63 us
    all_to_all x2, waiting for transfers between devices, local(): lax.all_to_all(back_x, 'sub', split_axis=0, concat_axis=0, tiled=True)  8.75 us
    dot_general x2, matrix products, local(): along_y = jnp.einsum('ejy,rtxyl->rtxejl', pair, along_z, precision=highest)  7.46 us
    all_to_all x2, starting transfers between devices, local(): lax.all_to_all(sending, 'sub', split_axis=0, concat_axis=0, tiled=True)  7.35 us
    all_to_all x2, starting transfers between devices, local(): lax.all_to_all(back_x, 'sub', split_axis=0, concat_axis=0, tiled=True)  7.19 us
    dot_general x4, matrix products, local(): jnp.einsum('eyj,xrjl->rxeyl', pair_y[:, :, s, rows], returned[s], precisi...  7.16 us
  transfers between devices with their start and end apart: 8, of which 3 were waited for; matrix products, arithmetic and copies ran while one was open for 26% of the time, Pallas kernels for 12%

profile of v2, /device:TPU:0, one launch (start us, length us, event | category | flops | bytes accessed | tf_op | source)
XLA Modules:
  0.0 127.1 jit_solution(13323187026169007903)
XLA Ops:
  3.3 5.0 %collective-permute-start = (bf16[4,16,16,128]{3,1,2,0:T(8,128)(2,1)}, bf16[4,16,16,128]{3,1,2,0:T(8,128)(2,1)S(1)}, u32[]{:S(2)}, u32[]{:S(2)}) collective-permute-start(bf16[4,16,16,128]{3,1,2,0:T(8,128)(2,1)} %fusion.90), channel_id=1, source_target_pairs={{0,12},{4,0},{8,4},{12,8},{1,13},{5,1},{9,5},{13,9},{2,14},{6,2},{... | collective-permute-start | bytes 786440 | tf_op jit(solution)/shard_map/ppermute | solution.py:62
  10.4 3.7 %fusion.6 = f32[2,32,128,2,64]{2,4,3,1,0:T(8,128)} fusion(f32[128,2,32,64]{0,3,2,1:T(8,128)S(1)} %fusion.11, f32[1,64,64]{2,1,0:T(8,128)S(1)} %get-tuple-element.8, f32[1,64,64]{2,1,0:T(8,128)S(1)} %get-tuple-element.9), kind=kOutput, calls=%fused_computation.13 | convolution fusion | flops 402661376 | bytes 6324224 | tf_op jit(solution)/shard_map/ejy,rtxyl->rtxejl/dot_general | solution.py:144
  14.1 3.4 %shard_map.68 = bf16[2,64,32,128]{3,2,1,0:T(8,128)(2,1)} custom-call(f32[64,2,64,128]{3,2,1,0:T(8,128)} %bitcast.234), custom_call_target="tpu_custom_call" | custom-call | flops 1572864 | bytes 5242880 | tf_op jit(solution)/shard_map/pallas_call | solution.py:42
  17.5 2.6 %copy.14 = bf16[2,1,2,32,32,128]{5,3,4,2,1,0:T(8,128)(2,1)} copy(bf16[2,1,2,32,32,128]{5,4,3,2,0,1:T(8,128)(2,1)} %bitcast.240) | data formatting | bytes 2097152 | tf_op jit(solution)/shard_map/reshape | solution.py:147
  20.1 3.6 %all-to-all-start = ((bf16[2,1,2,32,32,128]{5,3,4,2,1,0:T(8,128)(2,1)}), bf16[2,1,2,32,32,128]{5,3,4,2,1,0:T(8,128)(2,1)S(1)}, u32[]{:S(2)}, u32[]{:S(2)}) async-start(bf16[2,1,2,32,32,128]{5,3,4,2,1,0:T(8,128)(2,1)} %copy.14), calls=%async_computation | async-start | bytes 2097152 | tf_op jit(solution)/shard_map/all_to_all | solution.py:148
  23.7 1.9 %fusion.9 = f32[128,2,32,64]{0,3,2,1:T(8,128)S(1)} fusion(bf16[1,4,32,64,64]{4,3,2,1,0:T(8,128)(2,1)} %param.5, f32[64,64]{0,1:T(8,128)S(1)} %get-tuple-element.6, f32[64,64]{0,1:T(8,128)S(1)} %get-tuple-element.7), kind=kOutput, calls=%fused_computation.18 | convolution fusion | flops 201334784 | bytes 3178496 | tf_op jit(solution)/shard_map/rtxyz,zl->rtxyl/dot_general | solution.py:143
  25.9 3.7 %fusion.4 = f32[2,32,128,2,64]{2,4,3,1,0:T(8,128)} fusion(f32[128,2,32,64]{0,3,2,1:T(8,128)S(1)} %fusion.9, f32[1,64,64]{2,1,0:T(8,128)S(1)} %get-tuple-element.8, f32[1,64,64]{2,1,0:T(8,128)S(1)} %get-tuple-element.9), kind=kOutput, calls=%fused_computation.11 | convolution fusion | flops 402661376 | bytes 6324224 | tf_op jit(solution)/shard_map/ejy,rtxyl->rtxejl/dot_general | solution.py:144
  29.8 3.4 %shard_map.70 = bf16[2,64,32,128]{3,2,1,0:T(8,128)(2,1)} custom-call(f32[64,2,64,128]{3,2,1,0:T(8,128)} %bitcast.233), custom_call_target="tpu_custom_call" | custom-call | flops 1572864 | bytes 5242880 | tf_op jit(solution)/shard_map/pallas_call | solution.py:42
  33.2 2.7 %copy.15 = bf16[2,1,2,32,32,128]{5,3,4,2,1,0:T(8,128)(2,1)} copy(bf16[2,1,2,32,32,128]{5,4,3,2,0,1:T(8,128)(2,1)} %bitcast.241) | data formatting | bytes 2097152 | tf_op jit(solution)/shard_map/reshape | solution.py:147
  38.0 3.8 %all-to-all-start.1 = ((bf16[2,1,2,32,32,128]{5,3,4,2,1,0:T(8,128)(2,1)}), bf16[2,1,2,32,32,128]{5,3,4,2,1,0:T(8,128)(2,1)S(1)}, u32[]{:S(2)}, u32[]{:S(2)}) async-start(bf16[2,1,2,32,32,128]{5,3,4,2,1,0:T(8,128)(2,1)} %copy.15), calls=%async_computation.1 | async-start | bytes 2097152 | tf_op jit(solution)/shard_map/all_to_all | solution.py:148
  43.1 3.6 %convolution_add_fusion.1 = f32[2,32,128,2,64]{2,4,3,1,0:T(8,128)} fusion(f32[2,32,128,2,64]{2,4,3,1,0:T(8,128)S(1)} %fusion.18, bf16[2,1,2,32,32,128]{5,3,4,2,1,0:T(8,128)(2,1)S(1)} %all-to-all-done, f32[1,64,2,32]{1,3,0,2:T(8,128)S(1)} %get-tuple-element.5, f32[1,64,2,32]{1,3,0,2:T(8,128)S(1)} %get-tuple-element.4), kind=kOutput, calls=%fused_computation.6 | convolution fusion | flops 202379264 | bytes 8978432 | tf_op jit(solution)/shard_map/ekx,rtxjl->rtjekl/dot_general | solution.py:151
  46.7 3.4 %shard_map.69 = bf16[1,64,64,128]{3,2,1,0:T(8,128)(2,1)} custom-call(f32[64,2,64,128]{3,2,1,0:T(8,128)} %bitcast.231), custom_call_target="tpu_custom_call" | custom-call | flops 1572864 | bytes 5242880 | tf_op jit(solution)/shard_map/pallas_call | solution.py:42
  50.0 6.5 %all-to-all-done.1 = bf16[2,1,2,32,32,128]{5,3,4,2,1,0:T(8,128)(2,1)S(1)} async-done(((bf16[2,1,2,32,32,128]{5,3,4,2,1,0:T(8,128)(2,1)}), bf16[2,1,2,32,32,128]{5,3,4,2,1,0:T(8,128)(2,1)S(1)}, u32[]{:S(2)}, u32[]{:S(2)}) %all-to-all-start.1) | async-done | bytes 1048608 | tf_op jit(solution)/shard_map/all_to_all | solution.py:148
  57.8 3.6 %convolution_add_fusion = f32[2,32,128,2,64]{2,4,3,1,0:T(8,128)} fusion(f32[2,32,128,2,64]{2,4,3,1,0:T(8,128)S(1)} %fusion.17, bf16[2,1,2,32,32,128]{5,3,4,2,1,0:T(8,128)(2,1)S(1)} %all-to-all-done.1, f32[1,64,2,32]{1,3,0,2:T(8,128)S(1)} %get-tuple-element.5, f32[1,64,2,32]{1,3,0,2:T(8,128)S(1)} %get-tuple-element.4), kind=kOutput, calls=%fused_computation.5 | convolution fusion | flops 202379264 | bytes 8978432 | tf_op jit(solution)/shard_map/ekx,rtxjl->rtjekl/dot_general | solution.py:151
  61.4 3.4 %shard_map.71 = bf16[1,64,64,128]{3,2,1,0:T(8,128)(2,1)} custom-call(f32[64,2,64,128]{3,2,1,0:T(8,128)} %bitcast.232), custom_call_target="tpu_custom_call" | custom-call | flops 1572864 | bytes 5242880 | tf_op jit(solution)/shard_map/pallas_call | solution.py:42
  64.8 2.7 %fusion.3 = bf16[4,2,16,4,16,128]{5,2,4,0,3,1:T(8,128)(2,1)S(1)} fusion(s32[]{:T(128)S(6)} %select_n.79, bf16[1,4,4,16,16,128]{5,3,4,2,1,0:T(8,128)(2,1)} %bitcast.59, bf16[1,4,4,16,16,128]{5,3,4,2,1,0:T(8,128)(2,1)S(1)} %fusion.95), kind=kLoop, calls=%fused_computation.10 | loop fusion | flops 3145728 | bytes 4194308 | tf_op jit(solution)/shard_map/transpose | solution.py:77
  67.5 1.9 %copy.16 = bf16[4,2,16,4,16,128]{5,4,3,2,1,0:T(8,128)(2,1)} copy(bf16[4,2,16,4,16,128]{5,2,4,0,3,1:T(8,128)(2,1)S(1)} %fusion.3) | data formatting | bytes 4194304 | tf_op jit(solution)/shard_map/transpose | solution.py:77
  69.3 4.9 %shard_map.72 = f32[1,2048,128]{2,1,0:T(8,128)} custom-call(bf16[1,2,2048,128]{3,2,1,0:T(8,128)(2,1)} %bitcast.236, bf16[1,2,2048,128]{3,2,1,0:T(8,128)(2,1)} %bitcast.239, bf16[4,2048,128]{2,1,0:T(8,128)(2,1)} %bitcast.235), custom_call_target="tpu_custom_call" | custom-call | flops 8388608 | bytes 5242880 | tf_op jit(solution)/shard_map/pallas_call | solution.py:108
  74.3 1.6 %fusion.16 = f32[16,128,2,64]{1,3,2,0:T(8,128)S(1)} fusion(f32[1,32,64,128]{3,2,1,0:T(8,128)} %bitcast.237, f32[1,64,64]{2,1,0:T(8,128)S(1)} %get-tuple-element.8, f32[1,64,64]{2,1,0:T(8,128)S(1)} %get-tuple-element.9), kind=kOutput, calls=%fused_computation.30 | convolution fusion | flops 100671488 | bytes 1605632 | tf_op jit(solution)/shard_map/exk,rjkl->xrejl/dot_general | solution.py:168
  75.9 1.6 %copy.40 = f32[16,128,2,64]{1,0,2,3:T(8,128)} copy(f32[16,128,2,64]{1,3,2,0:T(8,128)S(1)} %fusion.16) | data formatting | bytes 2097152 | tf_op jit(solution)/shard_map/exk,rjkl->xrejl/dot_general | solution.py:168
  77.5 2.0 %shard_map.73 = f32[1,64,16,128]{3,2,1,0:T(8,128)} custom-call(f32[64,2,16,128]{3,2,1,0:T(8,128)} %bitcast.243), custom_call_target="tpu_custom_call" | custom-call | flops 393216 | bytes 1572864 | tf_op jit(solution)/shard_map/pallas_call | solution.py:42
  79.5 3.5 %all-to-all-start.2 = ((f32[2,32,1,16,128]{4,3,1,2,0:T(8,128)}), f32[2,32,1,16,128]{4,3,1,2,0:T(8,128)S(1)}, u32[]{:S(2)}, u32[]{:S(2)}) async-start(f32[2,32,1,16,128]{4,3,1,2,0:T(8,128)} %bitcast.245), calls=%async_computation.2 | async-start | bytes 1048576 | tf_op jit(solution)/shard_map/all_to_all | solution.py:173
  85.2 2.0 %shard_map.74 = f32[1,64,16,128]{3,2,1,0:T(8,128)} custom-call(f32[64,2,16,128]{3,2,1,0:T(8,128)} %bitcast.244), custom_call_target="tpu_custom_call" | custom-call | flops 393216 | bytes 1572864 | tf_op jit(solution)/shard_map/pallas_call | solution.py:42
  87.2 4.5 %all-to-all-done.2 = f32[2,32,1,16,128]{4,3,1,2,0:T(8,128)S(1)} async-done(((f32[2,32,1,16,128]{4,3,1,2,0:T(8,128)}), f32[2,32,1,16,128]{4,3,1,2,0:T(8,128)S(1)}, u32[]{:S(2)}, u32[]{:S(2)}) %all-to-all-start.2) | async-done | bytes 524320 | tf_op jit(solution)/shard_map/all_to_all | solution.py:173
  91.7 3.7 %all-to-all-start.3 = ((f32[2,32,1,16,128]{4,3,1,2,0:T(8,128)}), f32[2,32,1,16,128]{4,3,1,2,0:T(8,128)S(1)}, u32[]{:S(2)}, u32[]{:S(2)}) async-start(f32[2,32,1,16,128]{4,3,1,2,0:T(8,128)} %bitcast.246), calls=%async_computation.3 | async-start | bytes 1048576 | tf_op jit(solution)/shard_map/all_to_all | solution.py:173
  96.4 2.4 %fusion.20 = f32[32,128,2,64]{1,3,2,0:T(8,128)} fusion(f32[2,32,1,16,128]{4,3,1,2,0:T(8,128)S(1)} %all-to-all-done.2, f32[1,64,2,32]{1,3,0,2:T(8,128)S(1)} %get-tuple-element.5, f32[1,64,2,32]{1,3,0,2:T(8,128)S(1)} %get-tuple-element.4), kind=kOutput, calls=%fused_computation.41 | convolution fusion | flops 50333696 | bytes 2424832 | tf_op jit(solution)/shard_map/eyj,xrjl->rxeyl/dot_general | solution.py:175
  98.8 4.3 %all-to-all-done.3 = f32[2,32,1,16,128]{4,3,1,2,0:T(8,128)S(1)} async-done(((f32[2,32,1,16,128]{4,3,1,2,0:T(8,128)}), f32[2,32,1,16,128]{4,3,1,2,0:T(8,128)S(1)}, u32[]{:S(2)}, u32[]{:S(2)}) %all-to-all-start.3) | async-done | bytes 524320 | tf_op jit(solution)/shard_map/all_to_all | solution.py:173
  104.6 2.8 %add_bitcast_fusion.in_ref = f32[32,2,64,128]{3,2,1,0:T(8,128)} fusion(f32[32,128,2,64]{1,3,2,0:T(8,128)S(1)} %fusion.19, f32[32,128,2,64]{1,3,2,0:T(8,128)S(1)} %fusion.21, f32[32,128,2,64]{1,3,2,0:T(8,128)S(1)} %copy-done.2, f32[2,32,1,16,128]{4,3,1,2,0:T(8,128)S(1)} %all-to-all-done.3, f32[1,64,2,32]{1,3,0,2:T(8,128)S(1)} %get-tuple-element.4, ...), kind=kOutput, calls=%fused_computation.15 | convolution fusion | flops 51906560 | bytes 8716288 | tf_op jit(solution)/shard_map/eyj,xrjl->rxeyl/dot_general | solution.py:175
  107.4 3.0 %shard_map.75 = f32[1,32,64,128]{3,2,1,0:T(8,128)} custom-call(f32[32,2,64,128]{3,2,1,0:T(8,128)} %add_bitcast_fusion.in_ref), custom_call_target="tpu_custom_call" | custom-call | flops 786432 | bytes 3145728 | tf_op jit(solution)/shard_map/pallas_call | solution.py:42
  110.5 1.9 %convolution_multiply_fusion = f32[32,64,64]{2,1,0:T(8,128)S(1)} fusion(f32[1,32,64,128]{3,2,1,0:T(8,128)} %shard_map.75, f32[64,64]{0,1:T(8,128)S(1)} %copy-done.7, f32[64,64]{0,1:T(8,128)S(1)} %copy-done.9), kind=kOutput, calls=%fused_computation.16 | convolution fusion | flops 100802560 | bytes 1605632 | tf_op jit(solution)/shard_map/rxyl,lz->rxyz/dot_general | solution.py:181
  113.5 1.6 %gather_fusion = f32[8,512]{1,0:T(8,128)S(1)} fusion(f32[256,512]{1,0:T(8,128)} %reshape.335, s32[1024]{0:T(1024)S(1)} %pad_clamp_fusion), kind=kCustom, calls=%fused_computation | custom fusion | bytes 32800 | tf_op jit(solution)/shard_map/gather | solution.py:188
  116.8 9.6 %all_to_all.25 = f32[8,2,512]{2,1,0:T(2,128)S(1)} all-to-all(f32[8,2,512]{2,1,0:T(2,128)S(1)} %reshape.337), channel_id=1, replica_groups=mesh['grp'=2,'rot'=4,'sub'=2,'ref'=2] {'rot','ref'}, dimensions={0} | all-to-all | bytes 65536 | tf_op jit(solution)/shard_map/all_to_all | solution.py:199
  (65 shorter events, 17.9 us)
Async XLA Ops:
  0.6 1.6 %copy-start = (f32[2,4,16,32,64]{4,3,2,1,0:T(8,128)S(1)}, f32[2,4,16,32,64]{4,3,2,1,0:T(8,128)}, u32[]{:S(2)}) copy-start(f32[2,4,16,32,64]{4,3,2,1,0:T(8,128)} %param.6) | copy-start | bytes 3145732
  2.2 7.4 %copy-start.5 = (bf16[1,4,32,64,64]{4,3,2,1,0:T(8,128)(2,1)S(1)}, bf16[1,4,32,64,64]{4,3,2,1,0:T(8,128)(2,1)}, u32[]{:S(2)}) copy-start(bf16[1,4,32,64,64]{4,3,2,1,0:T(8,128)(2,1)} %param.5) | copy-start | bytes 3145732
  3.3 32.7 %collective-permute-start = (bf16[4,16,16,128]{3,1,2,0:T(8,128)(2,1)}, bf16[4,16,16,128]{3,1,2,0:T(8,128)(2,1)S(1)}, u32[]{:S(2)}, u32[]{:S(2)}) collective-permute-start(bf16[4,16,16,128]{3,1,2,0:T(8,128)(2,1)} %fusion.90), channel_id=1, source_target_pairs={{0,12},{4,0},{8,4},{12,8},{1,13},{5,1},{9,5},{13,9},{2,14},{6,2},{... | collective-permute-start | bytes 786440 | tf_op jit(solution)/shard_map/ppermute | solution.py:62
  8.3 27.6 %collective-permute-start.1 = (bf16[4,16,16,128]{3,1,2,0:T(8,128)(2,1)}, bf16[4,16,16,128]{3,1,2,0:T(8,128)(2,1)S(1)}, u32[]{:S(2)}, u32[]{:S(2)}) collective-permute-start(bf16[4,16,16,128]{3,1,2,0:T(8,128)(2,1)} %fusion.90), channel_id=1, source_target_pairs={{0,8},{4,12},{8,0},{12,4},{1,9},{5,13},{9,1},{13,5},{2,10},{6,14},... | collective-permute-start | bytes 786440 | tf_op jit(solution)/shard_map/ppermute | solution.py:62
  8.3 27.7 %collective-permute-start.2 = (bf16[4,16,16,128]{3,1,2,0:T(8,128)(2,1)}, bf16[4,16,16,128]{3,1,2,0:T(8,128)(2,1)S(1)}, u32[]{:S(2)}, u32[]{:S(2)}) collective-permute-start(bf16[4,16,16,128]{3,1,2,0:T(8,128)(2,1)} %fusion.90), channel_id=1, source_target_pairs={{0,4},{4,8},{8,12},{12,0},{1,5},{5,9},{9,13},{13,1},{2,6},{6,10},{... | collective-permute-start | bytes 786440 | tf_op jit(solution)/shard_map/ppermute | solution.py:62
  9.5 14.2 %copy-start.6 = (f32[64,64]{0,1:T(8,128)}, f32[64,64]{0,1:T(8,128)S(1)}, u32[]{:S(2)}) copy-start(f32[64,64]{0,1:T(8,128)S(1)} %get-tuple-element.6) | copy-start | bytes 49156
  9.5 14.2 %copy-start.8 = (f32[64,64]{0,1:T(8,128)}, f32[64,64]{0,1:T(8,128)S(1)}, u32[]{:S(2)}) copy-start(f32[64,64]{0,1:T(8,128)S(1)} %get-tuple-element.7) | copy-start | bytes 49156
  20.1 17.9 %all-to-all-start = ((bf16[2,1,2,32,32,128]{5,3,4,2,1,0:T(8,128)(2,1)}), bf16[2,1,2,32,32,128]{5,3,4,2,1,0:T(8,128)(2,1)S(1)}, u32[]{:S(2)}, u32[]{:S(2)}) async-start(bf16[2,1,2,32,32,128]{5,3,4,2,1,0:T(8,128)(2,1)} %copy.14), calls=%async_computation | async-start | bytes 2097152 | tf_op jit(solution)/shard_map/all_to_all | solution.py:148
  25.8 3.8 %copy-start.10 = (s32[1,1,1,8,1]{3,4,2,1,0:T(1,128)S(1)}, s32[1,1,1,8,1]{3,4,2,1,0:T(1,128)}, u32[]{:S(2)}) copy-start(s32[1,1,1,8,1]{3,4,2,1,0:T(1,128)} %param.8) | copy-start | bytes 100
  25.9 3.9 %copy-start.11 = (s32[1,1,1,8]{3,2,1,0:T(1,128)S(1)}, s32[1,1,1,8]{3,2,1,0:T(1,128)}, u32[]{:S(2)}) copy-start(s32[1,1,1,8]{3,2,1,0:T(1,128)} %param.7) | copy-start | bytes 100
  37.8 27.0 %collective-permute-start.3 = (bf16[4,4,16,16,128]{4,2,3,1,0:T(8,128)(2,1)}, bf16[4,4,16,16,128]{4,2,3,1,0:T(8,128)(2,1)}, u32[]{:S(2)}, u32[]{:S(2)}) collective-permute-start(bf16[4,4,16,16,128]{4,2,3,1,0:T(8,128)(2,1)} %constant_dynamic-slice_fusion), channel_id=1, source_target_pairs={{0,1},{1,0},{2,3},{3,2},{4,5},{5,4},{6,7},{7,6},{8,9},{9,8},{10,11... | collective-permute-start | bytes 3145736 | tf_op jit(solution)/shard_map/ppermute | solution.py:62
  38.0 18.5 %all-to-all-start.1 = ((bf16[2,1,2,32,32,128]{5,3,4,2,1,0:T(8,128)(2,1)}), bf16[2,1,2,32,32,128]{5,3,4,2,1,0:T(8,128)(2,1)S(1)}, u32[]{:S(2)}, u32[]{:S(2)}) async-start(bf16[2,1,2,32,32,128]{5,3,4,2,1,0:T(8,128)(2,1)} %copy.15), calls=%async_computation.1 | async-start | bytes 2097152 | tf_op jit(solution)/shard_map/all_to_all | solution.py:148
  75.9 7.1 %copy-start.3 = (f32[1,2048,128]{2,1,0:T(8,128)S(1)}, f32[1,2048,128]{2,1,0:T(8,128)}, u32[]{:S(2)}) copy-start(f32[1,2048,128]{2,1,0:T(8,128)} %shard_map.72) | copy-start | bytes 3145732
  79.5 12.2 %all-to-all-start.2 = ((f32[2,32,1,16,128]{4,3,1,2,0:T(8,128)}), f32[2,32,1,16,128]{4,3,1,2,0:T(8,128)S(1)}, u32[]{:S(2)}, u32[]{:S(2)}) async-start(f32[2,32,1,16,128]{4,3,1,2,0:T(8,128)} %bitcast.245), calls=%async_computation.2 | async-start | bytes 1048576 | tf_op jit(solution)/shard_map/all_to_all | solution.py:173
  91.7 11.4 %all-to-all-start.3 = ((f32[2,32,1,16,128]{4,3,1,2,0:T(8,128)}), f32[2,32,1,16,128]{4,3,1,2,0:T(8,128)S(1)}, u32[]{:S(2)}, u32[]{:S(2)}) async-start(f32[2,32,1,16,128]{4,3,1,2,0:T(8,128)} %bitcast.246), calls=%async_computation.3 | async-start | bytes 1048576 | tf_op jit(solution)/shard_map/all_to_all | solution.py:173
  103.0 1.6 %copy-start.2 = (f32[32,128,2,64]{1,3,2,0:T(8,128)S(1)}, f32[32,128,2,64]{1,3,2,0:T(8,128)}, u32[]{:S(2)}) copy-start(f32[32,128,2,64]{1,3,2,0:T(8,128)} %fusion.20) | copy-start | bytes 6291460
  107.4 3.1 %copy-start.7 = (f32[64,64]{0,1:T(8,128)S(1)}, f32[64,64]{0,1:T(8,128)}, u32[]{:S(2)}) copy-start(f32[64,64]{0,1:T(8,128)} %copy-done.6) | copy-start | bytes 49156
  107.4 3.1 %copy-start.9 = (f32[64,64]{0,1:T(8,128)S(1)}, f32[64,64]{0,1:T(8,128)}, u32[]{:S(2)}) copy-start(f32[64,64]{0,1:T(8,128)} %copy-done.8) | copy-start | bytes 49156
  107.4 19.7 %copy-start.1 = (f32[2,4,16,32,64]{4,3,2,1,0:T(8,128)S(1)}, f32[2,4,16,32,64]{4,3,2,1,0:T(8,128)}, u32[]{:S(2)}) copy-start(f32[2,4,16,32,64]{4,3,2,1,0:T(8,128)} %param.6) | copy-start | bytes 3145732
  112.3 14.8 %copy-start.4 = (f32[32,64,64]{2,1,0:T(8,128)}, f32[32,64,64]{2,1,0:T(8,128)S(1)}, u32[]{:S(2)}) copy-start(f32[32,64,64]{2,1,0:T(8,128)S(1)} %convolution_multiply_fusion) | copy-start | bytes 1572868

commit v3 on v1

--- a/solution.py
+++ b/solution.py
@@ -62,6 +62,17 @@
         pieces.append(lax.ppermute(piece, axis, pairs))
     doubled = jnp.stack(pieces[::-1] * 2)
     return lax.dynamic_slice_in_dim(doubled, (count - 1 - me) % count, count, axis=0)
+
+
+def exchange(sending, axis):
+    count = lax.axis_size(axis)
+    me = lax.axis_index(axis)
+    pieces = [(me, lax.dynamic_index_in_dim(sending, me, axis=0, keepdims=False))]
+    for shift in range(1, count):
+        piece = lax.dynamic_index_in_dim(sending, (me + shift) % count, axis=0, keepdims=False)
+        pairs = [(k, (k + shift) % count) for k in range(count)]
+        pieces.append(((me - shift) % count, lax.ppermute(piece, axis, pairs)))
+    return pieces
 
 
 def gather_receptor(receptor):
@@ -145,11 +156,14 @@
         sending = combine_call(
             along_y.reshape(-1, 2, ny, 2 * length), 1.0, -1.0, n_sub, jnp.bfloat16
         ).reshape(n_sub, rots, part_terms, x_local, y_local, 2 * length)
-        turned = lax.all_to_all(sending, "sub", split_axis=0, concat_axis=0, tiled=True)
-        turned = turned.astype(jnp.float32)
         along_x = sum(
-            jnp.einsum("ekx,rtxjl->rtjekl", pair_x[:, :, s], turned[s], precision=highest)
-            for s in range(n_sub)
+            jnp.einsum(
+                "ekx,rtxjl->rtjekl",
+                lax.dynamic_index_in_dim(pair_x, source, axis=2, keepdims=False),
+                piece.astype(jnp.float32),
+                precision=highest,
+            )
+            for source, piece in exchange(sending, "sub")
         )
         spectrum = combine_call(
             along_x.reshape(-1, 2, length, 2 * length), 1.0, -1.0, 1, jnp.bfloat16
@@ -162,11 +176,15 @@
     back_x = jnp.einsum("exk,rjkl->xrejl", pair, product, precision=highest)
     back_x = combine_call(back_x.reshape(-1, 2, y_local, 2 * length), -1.0, 1.0, 1, jnp.float32)
     back_x = back_x.reshape(n_sub, x_local, rots, y_local, 2 * length)
-    returned = lax.all_to_all(back_x, "sub", split_axis=0, concat_axis=0, tiled=True)
     pair_y = pair.reshape(2, length, n_sub, y_local)
     back_y = sum(
-        jnp.einsum("eyj,xrjl->rxeyl", pair_y[:, :, s], returned[s], precision=highest)
-        for s in range(n_sub)
+        jnp.einsum(
+            "eyj,xrjl->rxeyl",
+            lax.dynamic_index_in_dim(pair_y, source, axis=2, keepdims=False),
+            piece,
+            precision=highest,
+        )
+        for source, piece in exchange(back_x, "sub")
     )
     back_y = combine_call(back_y.reshape(-1, 2, ny, 2 * length), -1.0, 1.0, 1, jnp.float32)
     back_y = back_y.reshape(rots, x_local, ny, 2 * length)

time: 123 us -> 121 us (0.984)
  matrix products: 29.1 us -> 38.9 us
  waiting for transfers between devices: 20.4 us -> 11.1 us
  starting transfers between devices: 17.2 us -> 9.65 us
  local copies, waits for them, and re-layouts: 16.4 us -> 19.5 us
  other arithmetic: 4.63 us -> 6.64 us
    all_to_all x3 -> x0, waiting for transfers between devices: 20.4 us -> none  [the longest x1 13.9 us: local(): lax.all_to_all(back_x, 'sub', split_axis=0, concat_axis=0, tiled=True)]
    all_to_all x3 -> x0, starting transfers between devices: 11.2 us -> none  [the longest x2 7.35 us: local(): lax.all_to_all(sending, 'sub', split_axis=0, concat_axis=0, tiled=True)]
    ppermute x0 -> x3, waiting for transfers between devices: none -> 11.1 us  [exchange(): pieces.append(((me - shift) % count, lax.ppermute(piece, axis, pairs)))]
    dot_general x6, matrix products: 13.2 us -> 21.8 us  [the longest x4 17.4 us: local(): jnp.einsum('ekx,rtxjl->rtjekl', lax.dynamic_index_in_dim(pair_x, source,...]
    reshape x2 -> x0, local copies, waits for them, and re-layouts: 5.3 us -> none  [local(): sending = combine_call(along_y.reshape(-1, 2, ny, 2 * length), 1.0, -1.0,...]
    dynamic_slice x0 -> x4, local copies, waits for them, and re-layouts: none -> 4.64 us  [exchange(): lax.dynamic_index_in_dim(sending, (me + shift) % count, axis=0, keepdims=...]
    ppermute x0 -> x3, starting transfers between devices: none -> 3.58 us  [exchange(): pieces.append(((me - shift) % count, lax.ppermute(piece, axis, pairs)))]
    another operation x0 -> x1, other arithmetic: none -> 1.39 us  [local(): pair = jnp.stack([cos_table, sin_table])]
  transfers between devices with their start and end apart: 7 -> 7, of which waited for: 2 -> 1; matrix products, arithmetic and copies ran while one was open for 23% -> 34% of each run, Pallas kernels for 11% -> 11%
where the time goes in v3:
time: 121 us; the launch traced here: 120 us
  matrix products  38.9 us (32%)
  Pallas kernels  23.9 us (20%)
  local copies, waits for them, and re-layouts  19.5 us (16%)
  waiting for transfers between devices  11.1 us (9%)
  starting transfers between devices  9.65 us (8%)
  blocking collectives  9.63 us (8%)
  other arithmetic  6.64 us (5%)
    pallas_call x6, Pallas kernels, combine_call(): pl.pallas_call(functools.partial(combine_kernel, first=first, second=seco...  19 us
    dot_general x4, matrix products, local(): jnp.einsum('ekx,rtxjl->rtjekl', lax.dynamic_index_in_dim(pair_x, source,...  17.4 us
    ppermute x3, waiting for transfers between devices, exchange(): pieces.append(((me - shift) % count, lax.ppermute(piece, axis, pairs)))  11.1 us
    all_to_all x1, blocking collectives, local(): lax.all_to_all(packed, ('rot', 'ref'), split_axis=0, concat_axis=0, tiled...  9.63 us
    dot_general x2, matrix products, local(): along_y = jnp.einsum('ejy,rtxyl->rtxejl', pair, along_z, precision=highest)  7.46 us
    ppermute x4, starting transfers between devices, gather_by_shifts(): pieces.append(lax.ppermute(piece, axis, pairs))  6.06 us
    pallas_call x1, Pallas kernels, correlate(): pl.pallas_call(product_kernel, grid=(rots, rows // block), in_specs=[pl.B...  4.92 us
    dynamic_slice x4, local copies, waits for them, and re-layouts, exchange(): lax.dynamic_index_in_dim(sending, (me + shift) % count, axis=0, keepdims=...  4.64 us
  transfers between devices with their start and end apart: 7, of which 1 were waited for; matrix products, arithmetic and copies ran while one was open for 34% of the time, Pallas kernels for 11%

profile of v3, /device:TPU:0, one launch (start us, length us, event | category | flops | bytes accessed | tf_op | source)
XLA Modules:
  0.0 120.3 jit_solution(9267267270396109436)
XLA Ops:
  0.7 1.6 %copy-done = f32[2,4,16,32,64]{4,3,2,1,0:T(8,128)S(1)} copy-done((f32[2,4,16,32,64]{4,3,2,1,0:T(8,128)S(1)}, f32[2,4,16,32,64]{4,3,2,1,0:T(8,128)}, u32[]{:S(2)}) %copy-start) | copy-done | bytes 1048600
  3.3 5.0 %collective-permute-start.2 = (bf16[4,16,16,128]{3,1,2,0:T(8,128)(2,1)}, bf16[4,16,16,128]{3,1,2,0:T(8,128)(2,1)S(1)}, u32[]{:S(2)}, u32[]{:S(2)}) collective-permute-start(bf16[4,16,16,128]{3,1,2,0:T(8,128)(2,1)} %fusion.75), channel_id=1, source_target_pairs={{0,12},{4,0},{8,4},{12,8},{1,13},{5,1},{9,5},{13,9},{2,14},{6,2},{... | collective-permute-start | bytes 786440 | tf_op jit(solution)/shard_map/ppermute | solution.py:62
  9.6 1.9 %fusion.11 = f32[128,2,32,64]{0,3,2,1:T(8,128)S(1)} fusion(bf16[1,4,32,64,64]{4,3,2,1,0:T(8,128)(2,1)} %param.5, f32[64,64]{0,1:T(8,128)S(1)} %get-tuple-element.12, f32[64,64]{0,1:T(8,128)S(1)} %get-tuple-element.13), kind=kOutput, calls=%fused_computation.21 | convolution fusion | flops 201334784 | bytes 3178496 | tf_op jit(solution)/shard_map/rtxyz,zl->rtxyl/dot_general | solution.py:154
  11.6 3.7 %fusion.6 = f32[2,32,128,2,64]{2,4,3,1,0:T(8,128)} fusion(f32[128,2,32,64]{0,3,2,1:T(8,128)S(1)} %fusion.11, f32[1,64,64]{2,1,0:T(8,128)S(1)} %get-tuple-element.14, f32[1,64,64]{2,1,0:T(8,128)S(1)} %get-tuple-element.15), kind=kOutput, calls=%fused_computation.13 | convolution fusion | flops 402661376 | bytes 6324224 | tf_op jit(solution)/shard_map/ejy,rtxyl->rtxejl/dot_general | solution.py:155
  15.3 3.4 %shard_map.68 = bf16[2,64,32,128]{3,2,1,0:T(8,128)(2,1)} custom-call(f32[64,2,64,128]{3,2,1,0:T(8,128)} %bitcast.195), custom_call_target="tpu_custom_call" | custom-call | flops 1572864 | bytes 5242880 | tf_op jit(solution)/shard_map/pallas_call | solution.py:42
  21.0 1.5 %collective-permute-start = (bf16[1,2,32,32,128]{4,2,3,1,0:T(8,128)(2,1)}, bf16[1,2,32,32,128]{4,2,3,1,0:T(8,128)(2,1)S(1)}, u32[]{:S(2)}, u32[]{:S(2)}) collective-permute-start(bf16[1,2,32,32,128]{4,2,3,1,0:T(8,128)(2,1)} %bitcast.192), channel_id=1, source_target_pairs={{0,2},{2,0},{1,3},{3,1},{4,6},{6,4},{5,7},{7,5},{8,10},{10,8},{9,1... | collective-permute-start | bytes 1572872 | tf_op jit(solution)/shard_map/ppermute | solution.py:74
  22.5 1.9 %fusion.9 = f32[128,2,32,64]{0,3,2,1:T(8,128)S(1)} fusion(bf16[1,4,32,64,64]{4,3,2,1,0:T(8,128)(2,1)} %param.5, f32[64,64]{0,1:T(8,128)S(1)} %get-tuple-element.12, f32[64,64]{0,1:T(8,128)S(1)} %get-tuple-element.13), kind=kOutput, calls=%fused_computation.19 | convolution fusion | flops 201334784 | bytes 3178496 | tf_op jit(solution)/shard_map/rtxyz,zl->rtxyl/dot_general | solution.py:154
  24.4 3.7 %fusion.4 = f32[2,32,128,2,64]{2,4,3,1,0:T(8,128)} fusion(f32[128,2,32,64]{0,3,2,1:T(8,128)S(1)} %fusion.9, f32[1,64,64]{2,1,0:T(8,128)S(1)} %get-tuple-element.14, f32[1,64,64]{2,1,0:T(8,128)S(1)} %get-tuple-element.15), kind=kOutput, calls=%fused_computation.11 | convolution fusion | flops 402661376 | bytes 6324224 | tf_op jit(solution)/shard_map/ejy,rtxyl->rtxejl/dot_general | solution.py:155
  28.2 3.4 %shard_map.70 = bf16[2,64,32,128]{3,2,1,0:T(8,128)(2,1)} custom-call(f32[64,2,64,128]{3,2,1,0:T(8,128)} %bitcast.196), custom_call_target="tpu_custom_call" | custom-call | flops 1572864 | bytes 5242880 | tf_op jit(solution)/shard_map/pallas_call | solution.py:42
  35.2 1.4 %fusion.40 = (f32[2,64,1,32]{1,3,0,2:T(8,128)}, f32[2,64,1,32]{1,3,0,2:T(8,128)S(1)}) fusion(s32[]{:T(128)S(6)} %select_n.116, f32[1,64,2,32]{1,3,0,2:T(8,128)} %get-tuple-element.11, f32[1,64,2,32]{1,3,0,2:T(8,128)} %get-tuple-element.10, s32[]{:T(128)S(6)} %select_n.111), kind=kLoop, calls=%fused_computation.80 | loop fusion | flops 8192 | bytes 65544 | tf_op jit(solution)/shard_map/stack | solution.py:144
  36.6 3.3 %fusion.22 = f32[2,32,128,2,64]{2,4,3,1,0:T(8,128)} fusion(bf16[1,1,2,32,32,128]{5,4,3,2,0,1:T(8,128)(2,1)S(1)} %get-tuple-element.5, f32[2,64,1,32]{1,3,0,2:T(8,128)S(1)} %get-tuple-element.9), kind=kOutput, calls=%fused_computation.33 | convolution fusion | flops 201326592 | bytes 4734976 | tf_op jit(solution)/shard_map/ekx,rtxjl->rtjekl/dot_general | solution.py:160
  39.9 3.2 %fusion.19 = f32[2,32,128,2,64]{2,4,3,1,0:T(8,128)} fusion(bf16[1,1,2,32,32,128]{5,4,3,2,0,1:T(8,128)(2,1)S(1)} %get-tuple-element.3, f32[2,64,1,32]{1,3,0,2:T(8,128)S(1)} %get-tuple-element.9), kind=kOutput, calls=%fused_computation.30 | convolution fusion | flops 201326592 | bytes 4734976 | tf_op jit(solution)/shard_map/ekx,rtxjl->rtjekl/dot_general | solution.py:160
  46.6 1.5 %fusion.81 = bf16[1,4,4,16,16,128]{5,3,4,2,1,0:T(8,128)(2,1)S(1)} fusion(bf16[8,4,16,16,128]{4,2,3,1,0:T(8,128)(2,1)} %copy-done.3, s32[]{:T(128)S(6)} %select_n.119), kind=kLoop, calls=%fused_computation.131 | loop fusion | bytes 2097156 | tf_op jit(solution)/shard_map/stack | solution.py:63
  48.1 5.5 %convolution_add_fusion.1 = f32[2,32,128,2,64]{2,4,3,1,0:T(8,128)} fusion(f32[2,32,128,2,64]{2,4,3,1,0:T(8,128)} %fusion.22, bf16[1,2,32,32,128]{4,2,3,1,0:T(8,128)(2,1)S(1)} %collective-permute-done, f32[2,64,1,32]{1,3,0,2:T(8,128)S(1)} %copy-done.4), kind=kOutput, calls=%fused_computation.6 | convolution fusion | flops 202375168 | bytes 8929280 | tf_op jit(solution)/shard_map/ekx,rtxjl->rtjekl/dot_general | solution.py:160
  53.5 3.4 %shard_map.69 = bf16[1,64,64,128]{3,2,1,0:T(8,128)(2,1)} custom-call(f32[64,2,64,128]{3,2,1,0:T(8,128)} %bitcast.193), custom_call_target="tpu_custom_call" | custom-call | flops 1572864 | bytes 5242880 | tf_op jit(solution)/shard_map/pallas_call | solution.py:42
  56.9 5.4 %convolution_add_fusion = f32[2,32,128,2,64]{2,4,3,1,0:T(8,128)} fusion(f32[2,32,128,2,64]{2,4,3,1,0:T(8,128)} %fusion.19, bf16[1,2,32,32,128]{4,2,3,1,0:T(8,128)(2,1)S(1)} %collective-permute-done.1, f32[2,64,1,32]{1,3,0,2:T(8,128)S(1)} %copy-done.4), kind=kOutput, calls=%fused_computation.5 | convolution fusion | flops 202375168 | bytes 8929280 | tf_op jit(solution)/shard_map/ekx,rtxjl->rtjekl/dot_general | solution.py:160
  62.3 3.4 %shard_map.71 = bf16[1,64,64,128]{3,2,1,0:T(8,128)(2,1)} custom-call(f32[64,2,64,128]{3,2,1,0:T(8,128)} %bitcast.194), custom_call_target="tpu_custom_call" | custom-call | flops 1572864 | bytes 5242880 | tf_op jit(solution)/shard_map/pallas_call | solution.py:42
  65.7 2.7 %fusion.3 = bf16[4,2,16,4,16,128]{5,2,4,0,3,1:T(8,128)(2,1)S(1)} fusion(s32[]{:T(128)S(6)} %select_n.121, bf16[1,4,4,16,16,128]{5,3,4,2,1,0:T(8,128)(2,1)} %bitcast.61, bf16[1,4,4,16,16,128]{5,3,4,2,1,0:T(8,128)(2,1)S(1)} %fusion.81), kind=kLoop, calls=%fused_computation.10 | loop fusion | flops 3145728 | bytes 4194308 | tf_op jit(solution)/shard_map/transpose | solution.py:88
  68.4 1.9 %copy.17 = bf16[4,2,16,4,16,128]{5,4,3,2,1,0:T(8,128)(2,1)} copy(bf16[4,2,16,4,16,128]{5,2,4,0,3,1:T(8,128)(2,1)S(1)} %fusion.3) | data formatting | bytes 4194304 | tf_op jit(solution)/shard_map/transpose | solution.py:88
  70.2 4.9 %shard_map.72 = f32[1,2048,128]{2,1,0:T(8,128)} custom-call(bf16[1,2,2048,128]{3,2,1,0:T(8,128)(2,1)} %bitcast.199, bf16[1,2,2048,128]{3,2,1,0:T(8,128)(2,1)} %bitcast.200, bf16[4,2048,128]{2,1,0:T(8,128)(2,1)} %bitcast.197), custom_call_target="tpu_custom_call" | custom-call | flops 8388608 | bytes 5242880 | tf_op jit(solution)/shard_map/pallas_call | solution.py:119
  75.2 2.2 %fusion.27 = f32[32,128,2,64]{1,3,2,0:T(8,128)S(1)} fusion(f32[32,64,128,1]{2,1,3,0:T(8,128)} %bitcast.201, f32[1,64,64]{2,1,0:T(8,128)S(1)} %get-tuple-element.14, f32[1,64,64]{2,1,0:T(8,128)S(1)} %get-tuple-element.15), kind=kOutput, calls=%fused_computation.58 | convolution fusion | flops 201334784 | bytes 3178496 | tf_op jit(solution)/shard_map/exk,rjkl->xrejl/dot_general | solution.py:176
  77.4 2.6 %copy.43 = f32[32,128,2,64]{1,0,2,3:T(8,128)} copy(f32[32,128,2,64]{1,3,2,0:T(8,128)S(1)} %fusion.27) | data formatting | bytes 4194304 | tf_op jit(solution)/shard_map/exk,rjkl->xrejl/dot_general | solution.py:176
  79.9 2.5 %shard_map.73 = f32[1,64,32,128]{3,2,1,0:T(8,128)} custom-call(f32[64,2,32,128]{3,2,1,0:T(8,128)} %bitcast.198), custom_call_target="tpu_custom_call" | custom-call | flops 786432 | bytes 3145728 | tf_op jit(solution)/shard_map/pallas_call | solution.py:42
  83.5 1.6 %collective-permute-start.6 = (f32[32,1,32,128]{3,2,0,1:T(8,128)S(1)}, f32[32,1,32,128]{3,2,0,1:T(8,128)S(1)}, u32[]{:S(2)}, u32[]{:S(2)}) collective-permute-start(f32[32,1,32,128]{3,2,0,1:T(8,128)S(1)} %dynamic-slice_bitcast_fusion), channel_id=1, source_target_pairs={{0,2},{2,0},{1,3},{3,1},{4,6},{6,4},{5,7},{7,5},{8,10},{10,8},{9,1... | collective-permute-start | bytes 1572872 | tf_op jit(solution)/shard_map/ppermute | solution.py:74
  85.1 2.1 %fusion.16 = f32[32,128,2,64]{1,3,2,0:T(8,128)S(1)} fusion(f32[2,32,1,32,128]{4,3,1,0,2:T(8,128)} %bitcast.206, s32[]{:T(128)S(6)} %select_n.111, f32[2,64,1,32]{1,3,0,2:T(8,128)S(1)} %copy-done.6), kind=kOutput, calls=%fused_computation.27 | convolution fusion | flops 100663296 | bytes 2637828 | tf_op jit(solution)/shard_map/eyj,xrjl->rxeyl/dot_general | solution.py:181
  87.2 11.1 %collective-permute-done.6 = f32[32,1,32,128]{3,2,0,1:T(8,128)S(1)} collective-permute-done((f32[32,1,32,128]{3,2,0,1:T(8,128)S(1)}, f32[32,1,32,128]{3,2,0,1:T(8,128)S(1)}, u32[]{:S(2)}, u32[]{:S(2)}) %collective-permute-start.6) | collective-permute-done | bytes 524320 | tf_op jit(solution)/shard_map/ppermute | solution.py:74
  98.3 2.4 %add_bitcast_fusion.in_ref = f32[32,2,64,128]{3,2,1,0:T(8,128)} fusion(f32[32,128,2,64]{1,3,2,0:T(8,128)S(1)} %fusion.16, f32[32,1,32,128]{3,2,0,1:T(8,128)S(1)} %collective-permute-done.6, f32[2,64,1,32]{1,3,0,2:T(8,128)S(1)} %copy-done.4), kind=kOutput, calls=%fused_computation.16 | convolution fusion | flops 101187584 | bytes 4734976 | tf_op jit(solution)/shard_map/eyj,xrjl->rxeyl/dot_general | solution.py:181
  100.7 3.0 %shard_map.74 = f32[1,32,64,128]{3,2,1,0:T(8,128)} custom-call(f32[32,2,64,128]{3,2,1,0:T(8,128)} %add_bitcast_fusion.in_ref), custom_call_target="tpu_custom_call" | custom-call | flops 786432 | bytes 3145728 | tf_op jit(solution)/shard_map/pallas_call | solution.py:42
  103.7 1.9 %convolution_multiply_fusion = f32[32,64,64]{2,1,0:T(8,128)S(1)} fusion(f32[1,32,64,128]{3,2,1,0:T(8,128)} %shard_map.74, f32[64,64]{0,1:T(8,128)S(1)} %get-tuple-element.12, f32[64,64]{0,1:T(8,128)S(1)} %get-tuple-element.13), kind=kOutput, calls=%fused_computation.17 | convolution fusion | flops 100802560 | bytes 1605632 | tf_op jit(solution)/shard_map/rxyl,lz->rxyz/dot_general | solution.py:192
  106.7 1.6 %gather_fusion = f32[8,512]{1,0:T(8,128)S(1)} fusion(f32[256,512]{1,0:T(8,128)} %reshape.303, s32[1024]{0:T(1024)S(1)} %pad_clamp_fusion), kind=kCustom, calls=%fused_computation | custom fusion | bytes 32800 | tf_op jit(solution)/shard_map/gather | solution.py:199
  108.3 1.6 %fusion.76 = f32[8,512]{1,0:T(8,128)S(1)} fusion(f32[8,512]{1,0:T(8,128)S(1)} %gather_fusion, f32[512,512]{1,0:T(8,128)} %param.9), kind=kOutput, calls=%fused_computation.130 | convolution fusion | flops 12582912 | bytes 1081344 | tf_op jit(solution)/shard_map/dot_general | solution.py:208
  110.1 9.6 %all_to_all.5 = f32[8,2,512]{2,1,0:T(2,128)S(1)} all-to-all(f32[8,2,512]{2,1,0:T(2,128)S(1)} %reshape.305), channel_id=1, replica_groups=mesh['grp'=2,'rot'=4,'sub'=2,'ref'=2] {'rot','ref'}, dimensions={0} | all-to-all | bytes 65536 | tf_op jit(solution)/shard_map/all_to_all | solution.py:210
  (56 shorter events, 14.7 us)
Async XLA Ops:
  0.6 1.6 %copy-start = (f32[2,4,16,32,64]{4,3,2,1,0:T(8,128)S(1)}, f32[2,4,16,32,64]{4,3,2,1,0:T(8,128)}, u32[]{:S(2)}) copy-start(f32[2,4,16,32,64]{4,3,2,1,0:T(8,128)} %param.6) | copy-start | bytes 3145732
  3.3 39.9 %collective-permute-start.2 = (bf16[4,16,16,128]{3,1,2,0:T(8,128)(2,1)}, bf16[4,16,16,128]{3,1,2,0:T(8,128)(2,1)S(1)}, u32[]{:S(2)}, u32[]{:S(2)}) collective-permute-start(bf16[4,16,16,128]{3,1,2,0:T(8,128)(2,1)} %fusion.75), channel_id=1, source_target_pairs={{0,12},{4,0},{8,4},{12,8},{1,13},{5,1},{9,5},{13,9},{2,14},{6,2},{... | collective-permute-start | bytes 786440 | tf_op jit(solution)/shard_map/ppermute | solution.py:62
  8.3 34.9 %collective-permute-start.3 = (bf16[4,16,16,128]{3,1,2,0:T(8,128)(2,1)}, bf16[4,16,16,128]{3,1,2,0:T(8,128)(2,1)S(1)}, u32[]{:S(2)}, u32[]{:S(2)}) collective-permute-start(bf16[4,16,16,128]{3,1,2,0:T(8,128)(2,1)} %fusion.75), channel_id=1, source_target_pairs={{0,8},{4,12},{8,0},{12,4},{1,9},{5,13},{9,1},{13,5},{2,10},{6,14},... | collective-permute-start | bytes 786440 | tf_op jit(solution)/shard_map/ppermute | solution.py:62
  8.3 34.9 %collective-permute-start.4 = (bf16[4,16,16,128]{3,1,2,0:T(8,128)(2,1)}, bf16[4,16,16,128]{3,1,2,0:T(8,128)(2,1)S(1)}, u32[]{:S(2)}, u32[]{:S(2)}) collective-permute-start(bf16[4,16,16,128]{3,1,2,0:T(8,128)(2,1)} %fusion.75), channel_id=1, source_target_pairs={{0,4},{4,8},{8,12},{12,0},{1,5},{5,9},{9,13},{13,1},{2,6},{6,10},{... | collective-permute-start | bytes 786440 | tf_op jit(solution)/shard_map/ppermute | solution.py:62
  21.0 27.1 %collective-permute-start = (bf16[1,2,32,32,128]{4,2,3,1,0:T(8,128)(2,1)}, bf16[1,2,32,32,128]{4,2,3,1,0:T(8,128)(2,1)S(1)}, u32[]{:S(2)}, u32[]{:S(2)}) collective-permute-start(bf16[1,2,32,32,128]{4,2,3,1,0:T(8,128)(2,1)} %bitcast.192), channel_id=1, source_target_pairs={{0,2},{2,0},{1,3},{3,1},{4,6},{6,4},{5,7},{7,5},{8,10},{10,8},{9,1... | collective-permute-start | bytes 1572872 | tf_op jit(solution)/shard_map/ppermute | solution.py:74
  33.9 23.0 %collective-permute-start.1 = (bf16[1,2,32,32,128]{4,2,3,1,0:T(8,128)(2,1)}, bf16[1,2,32,32,128]{4,2,3,1,0:T(8,128)(2,1)S(1)}, u32[]{:S(2)}, u32[]{:S(2)}) collective-permute-start(bf16[1,2,32,32,128]{4,2,3,1,0:T(8,128)(2,1)} %bitcast.191), channel_id=1, source_target_pairs={{0,2},{2,0},{1,3},{3,1},{4,6},{6,4},{5,7},{7,5},{8,10},{10,8},{9,1... | collective-permute-start | bytes 1572872 | tf_op jit(solution)/shard_map/ppermute | solution.py:74
  36.6 3.3 %copy-start.5 = (f32[2,64,1,32]{1,3,0,2:T(8,128)}, f32[2,64,1,32]{1,3,0,2:T(8,128)S(1)}, u32[]{:S(2)}) copy-start(f32[2,64,1,32]{1,3,0,2:T(8,128)S(1)} %get-tuple-element.9) | copy-start | bytes 49156
  39.9 3.2 %copy-start.7 = (s32[1,1,1,8]{3,2,1,0:T(1,128)S(1)}, s32[1,1,1,8]{3,2,1,0:T(1,128)}, u32[]{:S(2)}) copy-start(s32[1,1,1,8]{3,2,1,0:T(1,128)} %param.7) | copy-start | bytes 100
  43.5 2.9 %copy-start.8 = (s32[1,1,1,8,1]{3,4,2,1,0:T(1,128)S(1)}, s32[1,1,1,8,1]{3,4,2,1,0:T(1,128)}, u32[]{:S(2)}) copy-start(s32[1,1,1,8,1]{3,4,2,1,0:T(1,128)} %param.8) | copy-start | bytes 100
  43.8 1.4 %copy-start.3 = (bf16[8,4,16,16,128]{4,2,3,1,0:T(8,128)(2,1)}, bf16[8,4,16,16,128]{4,2,3,1,0:T(8,128)(2,1)S(1)}, u32[]{:S(2)}) copy-start(bf16[8,4,16,16,128]{4,2,3,1,0:T(8,128)(2,1)S(1)} %bitcast_dynamic-update-slice_fusion.1) | copy-start | bytes 6291460
  45.2 2.8 %copy-start.4 = (f32[2,64,1,32]{1,3,0,2:T(8,128)S(1)}, f32[2,64,1,32]{1,3,0,2:T(8,128)}, u32[]{:S(2)}) copy-start(f32[2,64,1,32]{1,3,0,2:T(8,128)} %get-tuple-element.8) | copy-start | bytes 49156
  46.4 19.3 %collective-permute-start.5 = (bf16[4,4,16,16,128]{4,2,3,1,0:T(8,128)(2,1)}, bf16[4,4,16,16,128]{4,2,3,1,0:T(8,128)(2,1)}, u32[]{:S(2)}, u32[]{:S(2)}) collective-permute-start(bf16[4,4,16,16,128]{4,2,3,1,0:T(8,128)(2,1)} %constant_dynamic-slice_fusion), channel_id=1, source_target_pairs={{0,1},{1,0},{2,3},{3,2},{4,5},{5,4},{6,7},{7,6},{8,9},{9,8},{10,11... | collective-permute-start | bytes 3145736 | tf_op jit(solution)/shard_map/ppermute | solution.py:62
  79.9 5.2 %copy-start.6 = (f32[2,64,1,32]{1,3,0,2:T(8,128)S(1)}, f32[2,64,1,32]{1,3,0,2:T(8,128)}, u32[]{:S(2)}) copy-start(f32[2,64,1,32]{1,3,0,2:T(8,128)} %copy-done.5) | copy-start | bytes 49156
  83.5 14.8 %collective-permute-start.6 = (f32[32,1,32,128]{3,2,0,1:T(8,128)S(1)}, f32[32,1,32,128]{3,2,0,1:T(8,128)S(1)}, u32[]{:S(2)}, u32[]{:S(2)}) collective-permute-start(f32[32,1,32,128]{3,2,0,1:T(8,128)S(1)} %dynamic-slice_bitcast_fusion), channel_id=1, source_target_pairs={{0,2},{2,0},{1,3},{3,1},{4,6},{6,4},{5,7},{7,5},{8,10},{10,8},{9,1... | collective-permute-start | bytes 1572872 | tf_op jit(solution)/shard_map/ppermute | solution.py:74
  100.7 19.7 %copy-start.1 = (f32[2,4,16,32,64]{4,3,2,1,0:T(8,128)S(1)}, f32[2,4,16,32,64]{4,3,2,1,0:T(8,128)}, u32[]{:S(2)}) copy-start(f32[2,4,16,32,64]{4,3,2,1,0:T(8,128)} %param.6) | copy-start | bytes 3145732
  105.6 14.7 %copy-start.2 = (f32[32,64,64]{2,1,0:T(8,128)}, f32[32,64,64]{2,1,0:T(8,128)S(1)}, u32[]{:S(2)}) copy-start(f32[32,64,64]{2,1,0:T(8,128)S(1)} %convolution_multiply_fusion) | copy-start | bytes 1572868

commit v4 on v3

--- a/solution.py
+++ b/solution.py
@@ -207,7 +207,11 @@
     )
     done = jnp.dot(chosen, refine_weight, precision=highest)
     packed = jnp.dot(placing, done, precision=highest).reshape(owner_count, CAP, tile_cells)
-    refined = lax.all_to_all(packed, ("rot", "ref"), split_axis=0, concat_axis=0, tiled=True)
+    owner_axes = ("rot", "ref")
+    arrived = [piece for _, piece in exchange(packed, owner_axes)]
+    me = lax.axis_index(owner_axes)
+    doubled = jnp.stack(arrived[::-1] * 2)
+    refined = lax.dynamic_slice_in_dim(doubled, (owner_count - 1 - me) % owner_count, owner_count)
     return (scores, refined.reshape(1, 1, owner_count, CAP, tile_cells))
 
 

time: 121 us -> 124 us (1.025)
  blocking collectives: 9.63 us -> 0 us
  starting transfers between devices: 9.65 us -> 17.6 us
  waiting for transfers between devices: 11.1 us -> 15.9 us
    all_to_all x1 -> x0, blocking collectives: 9.63 us -> none  [local(): lax.all_to_all(packed, ('rot', 'ref'), split_axis=0, concat_axis=0, tiled...]
    ppermute x3 -> x10, starting transfers between devices: 3.58 us -> 11.5 us  [exchange(): pieces.append(((me - shift) % count, lax.ppermute(piece, axis, pairs)))]
    ppermute x3 -> x10, waiting for transfers between devices: 11.1 us -> 15.8 us  [exchange(): pieces.append(((me - shift) % count, lax.ppermute(piece, axis, pairs)))]
    unnamed x25 -> x41, local copies, waits for them, and re-layouts: 3.82 us -> 3.3 us
  transfers between devices with their start and end apart: 7 -> 14, of which waited for: 1 -> 5; matrix products, arithmetic and copies ran while one was open for 34% -> 33% of each run, Pallas kernels for 11% -> 11%
where the time goes in v4:
time: 124 us; the launch traced here: 123 us
  matrix products  39.2 us (32%)
  Pallas kernels  23.8 us (19%)
  local copies, waits for them, and re-layouts  19.6 us (16%)
  starting transfers between devices  17.6 us (14%)
  waiting for transfers between devices  15.9 us (13%)
  other arithmetic  6.03 us (5%)
    pallas_call x6, Pallas kernels, combine_call(): pl.pallas_call(functools.partial(combine_kernel, first=first, second=seco...  18.9 us
    dot_general x4, matrix products, local(): jnp.einsum('ekx,rtxjl->rtjekl', lax.dynamic_index_in_dim(pair_x, source,...  17.5 us
    ppermute x10, waiting for transfers between devices, exchange(): pieces.append(((me - shift) % count, lax.ppermute(piece, axis, pairs)))  15.8 us
    ppermute x10, starting transfers between devices, exchange(): pieces.append(((me - shift) % count, lax.ppermute(piece, axis, pairs)))  11.5 us
    dot_general x2, matrix products, local(): along_y = jnp.einsum('ejy,rtxyl->rtxejl', pair, along_z, precision=highest)  7.48 us
    ppermute x4, starting transfers between devices, gather_by_shifts(): pieces.append(lax.ppermute(piece, axis, pairs))  6.06 us
    pallas_call x1, Pallas kernels, correlate(): pl.pallas_call(product_kernel, grid=(rots, rows // block), in_specs=[pl.B...  4.94 us
    dynamic_slice x4, local copies, waits for them, and re-layouts, exchange(): lax.dynamic_index_in_dim(sending, (me + shift) % count, axis=0, keepdims=...  4.62 us
  transfers between devices with their start and end apart: 14, of which 5 were waited for; matrix products, arithmetic and copies ran while one was open for 33% of the time, Pallas kernels for 11%

profile of v4, /device:TPU:0, one launch (start us, length us, event | category | flops | bytes accessed | tf_op | source)
XLA Modules:
  0.0 123.2 jit_solution(15559342411584354738)
XLA Ops:
  0.7 1.6 %copy-done = f32[2,4,16,32,64]{4,3,2,1,0:T(8,128)S(1)} copy-done((f32[2,4,16,32,64]{4,3,2,1,0:T(8,128)S(1)}, f32[2,4,16,32,64]{4,3,2,1,0:T(8,128)}, u32[]{:S(2)}) %copy-start) | copy-done | bytes 1048600
  3.3 5.0 %collective-permute-start.2 = (bf16[4,16,16,128]{3,1,2,0:T(8,128)(2,1)}, bf16[4,16,16,128]{3,1,2,0:T(8,128)(2,1)S(1)}, u32[]{:S(2)}, u32[]{:S(2)}) collective-permute-start(bf16[4,16,16,128]{3,1,2,0:T(8,128)(2,1)} %fusion.82), channel_id=1, source_target_pairs={{0,12},{4,0},{8,4},{12,8},{1,13},{5,1},{9,5},{13,9},{2,14},{6,2},{... | collective-permute-start | bytes 786440 | tf_op jit(solution)/shard_map/ppermute | solution.py:62
  9.7 1.9 %fusion.11 = f32[128,2,32,64]{0,3,2,1:T(8,128)S(1)} fusion(bf16[1,4,32,64,64]{4,3,2,1,0:T(8,128)(2,1)} %param.5, f32[64,64]{0,1:T(8,128)S(1)} %get-tuple-element.19, f32[64,64]{0,1:T(8,128)S(1)} %get-tuple-element.20), kind=kOutput, calls=%fused_computation.21 | convolution fusion | flops 201334784 | bytes 3178496 | tf_op jit(solution)/shard_map/rtxyz,zl->rtxyl/dot_general | solution.py:154
  11.6 3.7 %fusion.6 = f32[2,32,128,2,64]{2,4,3,1,0:T(8,128)} fusion(f32[128,2,32,64]{0,3,2,1:T(8,128)S(1)} %fusion.11, f32[1,64,64]{2,1,0:T(8,128)S(1)} %get-tuple-element.21, f32[1,64,64]{2,1,0:T(8,128)S(1)} %get-tuple-element.22), kind=kOutput, calls=%fused_computation.13 | convolution fusion | flops 402661376 | bytes 6324224 | tf_op jit(solution)/shard_map/ejy,rtxyl->rtxejl/dot_general | solution.py:155
  15.4 3.4 %shard_map.68 = bf16[2,64,32,128]{3,2,1,0:T(8,128)(2,1)} custom-call(f32[64,2,64,128]{3,2,1,0:T(8,128)} %bitcast.231), custom_call_target="tpu_custom_call" | custom-call | flops 1572864 | bytes 5242880 | tf_op jit(solution)/shard_map/pallas_call | solution.py:42
  22.5 1.9 %fusion.9 = f32[128,2,32,64]{0,3,2,1:T(8,128)S(1)} fusion(bf16[1,4,32,64,64]{4,3,2,1,0:T(8,128)(2,1)} %param.5, f32[64,64]{0,1:T(8,128)S(1)} %get-tuple-element.19, f32[64,64]{0,1:T(8,128)S(1)} %get-tuple-element.20), kind=kOutput, calls=%fused_computation.19 | convolution fusion | flops 201334784 | bytes 3178496 | tf_op jit(solution)/shard_map/rtxyz,zl->rtxyl/dot_general | solution.py:154
  24.5 3.7 %fusion.4 = f32[2,32,128,2,64]{2,4,3,1,0:T(8,128)} fusion(f32[128,2,32,64]{0,3,2,1:T(8,128)S(1)} %fusion.9, f32[1,64,64]{2,1,0:T(8,128)S(1)} %get-tuple-element.21, f32[1,64,64]{2,1,0:T(8,128)S(1)} %get-tuple-element.22), kind=kOutput, calls=%fused_computation.11 | convolution fusion | flops 402661376 | bytes 6324224 | tf_op jit(solution)/shard_map/ejy,rtxyl->rtxejl/dot_general | solution.py:155
  28.2 3.4 %shard_map.70 = bf16[2,64,32,128]{3,2,1,0:T(8,128)(2,1)} custom-call(f32[64,2,64,128]{3,2,1,0:T(8,128)} %bitcast.232), custom_call_target="tpu_custom_call" | custom-call | flops 1572864 | bytes 5242880 | tf_op jit(solution)/shard_map/pallas_call | solution.py:42
  36.1 3.3 %fusion.22 = f32[2,32,128,2,64]{2,4,3,1,0:T(8,128)} fusion(bf16[1,1,2,32,32,128]{5,4,3,2,0,1:T(8,128)(2,1)S(1)} %get-tuple-element.5, f32[2,64,1,32]{1,3,0,2:T(8,128)S(1)} %get-tuple-element.9), kind=kOutput, calls=%fused_computation.33 | convolution fusion | flops 201326592 | bytes 4734976 | tf_op jit(solution)/shard_map/ekx,rtxjl->rtjekl/dot_general | solution.py:160
  39.4 3.3 %fusion.19 = f32[2,32,128,2,64]{2,4,3,1,0:T(8,128)} fusion(bf16[1,1,2,32,32,128]{5,4,3,2,0,1:T(8,128)(2,1)S(1)} %get-tuple-element.3, f32[2,64,1,32]{1,3,0,2:T(8,128)S(1)} %get-tuple-element.9), kind=kOutput, calls=%fused_computation.30 | convolution fusion | flops 201326592 | bytes 4734976 | tf_op jit(solution)/shard_map/ekx,rtxjl->rtjekl/dot_general | solution.py:160
  47.5 5.5 %convolution_add_fusion.1 = f32[2,32,128,2,64]{2,4,3,1,0:T(8,128)} fusion(f32[2,32,128,2,64]{2,4,3,1,0:T(8,128)} %fusion.22, bf16[1,2,32,32,128]{4,2,3,1,0:T(8,128)(2,1)S(1)} %collective-permute-done, f32[2,64,1,32]{1,3,0,2:T(8,128)S(1)} %get-tuple-element.8), kind=kOutput, calls=%fused_computation.6 | convolution fusion | flops 202375168 | bytes 8929280 | tf_op jit(solution)/shard_map/ekx,rtxjl->rtjekl/dot_general | solution.py:160
  53.0 3.4 %shard_map.69 = bf16[1,64,64,128]{3,2,1,0:T(8,128)(2,1)} custom-call(f32[64,2,64,128]{3,2,1,0:T(8,128)} %bitcast.229), custom_call_target="tpu_custom_call" | custom-call | flops 1572864 | bytes 5242880 | tf_op jit(solution)/shard_map/pallas_call | solution.py:42
  56.4 5.4 %convolution_add_fusion = f32[2,32,128,2,64]{2,4,3,1,0:T(8,128)} fusion(f32[2,32,128,2,64]{2,4,3,1,0:T(8,128)} %fusion.19, bf16[1,2,32,32,128]{4,2,3,1,0:T(8,128)(2,1)S(1)} %collective-permute-done.1, f32[2,64,1,32]{1,3,0,2:T(8,128)S(1)} %get-tuple-element.8), kind=kOutput, calls=%fused_computation.5 | convolution fusion | flops 202375168 | bytes 8929280 | tf_op jit(solution)/shard_map/ekx,rtxjl->rtjekl/dot_general | solution.py:160
  61.8 3.4 %shard_map.71 = bf16[1,64,64,128]{3,2,1,0:T(8,128)(2,1)} custom-call(f32[64,2,64,128]{3,2,1,0:T(8,128)} %bitcast.230), custom_call_target="tpu_custom_call" | custom-call | flops 1572864 | bytes 5242880 | tf_op jit(solution)/shard_map/pallas_call | solution.py:42
  65.2 2.7 %fusion.3 = bf16[4,2,16,4,16,128]{5,2,4,0,3,1:T(8,128)(2,1)S(1)} fusion(s32[]{:T(128)S(6)} %select_n.181, bf16[1,4,4,16,16,128]{5,3,4,2,1,0:T(8,128)(2,1)} %bitcast.61, bf16[1,4,4,16,16,128]{5,3,4,2,1,0:T(8,128)(2,1)S(1)} %fusion.88), kind=kLoop, calls=%fused_computation.10 | loop fusion | flops 3145728 | bytes 4194308 | tf_op jit(solution)/shard_map/transpose | solution.py:88
  67.9 1.9 %copy.17 = bf16[4,2,16,4,16,128]{5,4,3,2,1,0:T(8,128)(2,1)} copy(bf16[4,2,16,4,16,128]{5,2,4,0,3,1:T(8,128)(2,1)S(1)} %fusion.3) | data formatting | bytes 4194304 | tf_op jit(solution)/shard_map/transpose | solution.py:88
  69.8 4.9 %shard_map.72 = f32[1,2048,128]{2,1,0:T(8,128)} custom-call(bf16[1,2,2048,128]{3,2,1,0:T(8,128)(2,1)} %bitcast.235, bf16[1,2,2048,128]{3,2,1,0:T(8,128)(2,1)} %bitcast.236, bf16[4,2048,128]{2,1,0:T(8,128)(2,1)} %bitcast.233), custom_call_target="tpu_custom_call" | custom-call | flops 8388608 | bytes 5242880 | tf_op jit(solution)/shard_map/pallas_call | solution.py:119
  74.7 2.2 %fusion.27 = f32[32,128,2,64]{1,3,2,0:T(8,128)S(1)} fusion(f32[32,64,128,1]{2,1,3,0:T(8,128)} %bitcast.237, f32[1,64,64]{2,1,0:T(8,128)S(1)} %copy-done.5, f32[1,64,64]{2,1,0:T(8,128)S(1)} %copy-done.7), kind=kOutput, calls=%fused_computation.58 | convolution fusion | flops 201334784 | bytes 3178496 | tf_op jit(solution)/shard_map/exk,rjkl->xrejl/dot_general | solution.py:176
  76.9 2.6 %copy.43 = f32[32,128,2,64]{1,0,2,3:T(8,128)} copy(f32[32,128,2,64]{1,3,2,0:T(8,128)S(1)} %fusion.27) | data formatting | bytes 4194304 | tf_op jit(solution)/shard_map/exk,rjkl->xrejl/dot_general | solution.py:176
  79.5 2.5 %shard_map.73 = f32[1,64,32,128]{3,2,1,0:T(8,128)} custom-call(f32[64,2,32,128]{3,2,1,0:T(8,128)} %bitcast.234), custom_call_target="tpu_custom_call" | custom-call | flops 786432 | bytes 3145728 | tf_op jit(solution)/shard_map/pallas_call | solution.py:42
  83.1 1.6 %collective-permute-start.6 = (f32[32,1,32,128]{3,2,0,1:T(8,128)S(1)}, f32[32,1,32,128]{3,2,0,1:T(8,128)S(1)}, u32[]{:S(2)}, u32[]{:S(2)}) collective-permute-start(f32[32,1,32,128]{3,2,0,1:T(8,128)S(1)} %dynamic-slice_bitcast_fusion), channel_id=1, source_target_pairs={{0,2},{2,0},{1,3},{3,1},{4,6},{6,4},{5,7},{7,5},{8,10},{10,8},{9,1... | collective-permute-start | bytes 1572872 | tf_op jit(solution)/shard_map/ppermute | solution.py:74
  84.7 2.1 %fusion.16 = f32[32,128,2,64]{1,3,2,0:T(8,128)S(1)} fusion(f32[2,32,1,32,128]{4,3,1,0,2:T(8,128)} %bitcast.241, s32[]{:T(128)S(6)} %select_n.171, f32[2,64,1,32]{1,3,0,2:T(8,128)S(1)} %get-tuple-element.9), kind=kOutput, calls=%fused_computation.27 | convolution fusion | flops 100663296 | bytes 2637828 | tf_op jit(solution)/shard_map/eyj,xrjl->rxeyl/dot_general | solution.py:181
  86.7 11.1 %collective-permute-done.6 = f32[32,1,32,128]{3,2,0,1:T(8,128)S(1)} collective-permute-done((f32[32,1,32,128]{3,2,0,1:T(8,128)S(1)}, f32[32,1,32,128]{3,2,0,1:T(8,128)S(1)}, u32[]{:S(2)}, u32[]{:S(2)}) %collective-permute-start.6) | collective-permute-done | bytes 524320 | tf_op jit(solution)/shard_map/ppermute | solution.py:74
  97.8 2.4 %add_bitcast_fusion.in_ref = f32[32,2,64,128]{3,2,1,0:T(8,128)} fusion(f32[32,128,2,64]{1,3,2,0:T(8,128)S(1)} %fusion.16, f32[32,1,32,128]{3,2,0,1:T(8,128)S(1)} %collective-permute-done.6, f32[2,64,1,32]{1,3,0,2:T(8,128)S(1)} %get-tuple-element.8), kind=kOutput, calls=%fused_computation.16 | convolution fusion | flops 101187584 | bytes 4734976 | tf_op jit(solution)/shard_map/eyj,xrjl->rxeyl/dot_general | solution.py:181
  100.2 2.9 %shard_map.74 = f32[1,32,64,128]{3,2,1,0:T(8,128)} custom-call(f32[32,2,64,128]{3,2,1,0:T(8,128)} %add_bitcast_fusion.in_ref), custom_call_target="tpu_custom_call" | custom-call | flops 786432 | bytes 3145728 | tf_op jit(solution)/shard_map/pallas_call | solution.py:42
  103.1 2.0 %convolution_multiply_fusion = f32[32,64,64]{2,1,0:T(8,128)S(1)} fusion(f32[1,32,64,128]{3,2,1,0:T(8,128)} %shard_map.74, f32[64,64]{0,1:T(8,128)S(1)} %get-tuple-element.19, f32[64,64]{0,1:T(8,128)S(1)} %get-tuple-element.20), kind=kOutput, calls=%fused_computation.17 | convolution fusion | flops 100802560 | bytes 1605632 | tf_op jit(solution)/shard_map/rxyl,lz->rxyz/dot_general | solution.py:192
  106.3 1.6 %gather_fusion = f32[8,512]{1,0:T(8,128)S(1)} fusion(f32[256,512]{1,0:T(8,128)} %reshape.303, s32[1024]{0:T(1024)S(1)} %pad_clamp_fusion), kind=kCustom, calls=%fused_computation | custom fusion | bytes 32800 | tf_op jit(solution)/shard_map/gather | solution.py:199
  107.9 1.6 %fusion.83 = f32[8,512]{1,0:T(8,128)S(1)} fusion(f32[8,512]{1,0:T(8,128)S(1)} %gather_fusion, f32[512,512]{1,0:T(8,128)} %param.9), kind=kOutput, calls=%fused_computation.162 | convolution fusion | flops 12582912 | bytes 1081344 | tf_op jit(solution)/shard_map/dot_general | solution.py:208
  109.6 2.4 %collective-permute-start.7 = (f32[2,512]{1,0:T(2,128)S(1)}, f32[2,512]{1,0:T(2,128)S(1)}, u32[]{:S(2)}, u32[]{:S(2)}) collective-permute-start(f32[2,512]{1,0:T(2,128)S(1)} %get-tuple-element.16), channel_id=1, source_target_pairs={{0,13},{1,0},{4,1},{5,4},{8,5},{9,8},{12,9},{13,12},{2,15},{3,2},{... | collective-permute-start | bytes 12296 | tf_op jit(solution)/shard_map/ppermute | solution.py:74
  113.5 1.8 %collective-permute-start.10 = (f32[2,512]{1,0:T(2,128)S(1)}, f32[2,512]{1,0:T(2,128)S(1)}, u32[]{:S(2)}, u32[]{:S(2)}) collective-permute-start(f32[2,512]{1,0:T(2,128)S(1)} %get-tuple-element.13), channel_id=1, source_target_pairs={{0,8},{1,9},{4,12},{5,13},{8,0},{9,1},{12,4},{13,5},{2,10},{3,11},... | collective-permute-start | bytes 12296 | tf_op jit(solution)/shard_map/ppermute | solution.py:74
  115.3 2.3 %collective-permute-start.12 = (f32[2,512]{1,0:T(2,128)S(1)}, f32[2,512]{1,0:T(2,128)S(1)}, u32[]{:S(2)}, u32[]{:S(2)}) collective-permute-start(f32[2,512]{1,0:T(2,128)S(1)} %get-tuple-element.11), channel_id=1, source_target_pairs={{0,4},{1,5},{4,8},{5,9},{8,12},{9,13},{12,0},{13,1},{2,6},{3,7},{6... | collective-permute-start | bytes 12296 | tf_op jit(solution)/shard_map/ppermute | solution.py:74
  120.7 1.7 %collective-permute-done.13 = f32[2,512]{1,0:T(2,128)S(1)} collective-permute-done((f32[2,512]{1,0:T(2,128)S(1)}, f32[2,512]{1,0:T(2,128)S(1)}, u32[]{:S(2)}, u32[]{:S(2)}) %collective-permute-start.13) | collective-permute-done | bytes 4128 | tf_op jit(solution)/shard_map/ppermute | solution.py:74
  (88 shorter events, 23.0 us)
Async XLA Ops:
  0.6 1.6 %copy-start = (f32[2,4,16,32,64]{4,3,2,1,0:T(8,128)S(1)}, f32[2,4,16,32,64]{4,3,2,1,0:T(8,128)}, u32[]{:S(2)}) copy-start(f32[2,4,16,32,64]{4,3,2,1,0:T(8,128)} %param.6) | copy-start | bytes 3145732
  3.3 39.4 %collective-permute-start.2 = (bf16[4,16,16,128]{3,1,2,0:T(8,128)(2,1)}, bf16[4,16,16,128]{3,1,2,0:T(8,128)(2,1)S(1)}, u32[]{:S(2)}, u32[]{:S(2)}) collective-permute-start(bf16[4,16,16,128]{3,1,2,0:T(8,128)(2,1)} %fusion.82), channel_id=1, source_target_pairs={{0,12},{4,0},{8,4},{12,8},{1,13},{5,1},{9,5},{13,9},{2,14},{6,2},{... | collective-permute-start | bytes 786440 | tf_op jit(solution)/shard_map/ppermute | solution.py:62
  8.3 34.4 %collective-permute-start.3 = (bf16[4,16,16,128]{3,1,2,0:T(8,128)(2,1)}, bf16[4,16,16,128]{3,1,2,0:T(8,128)(2,1)S(1)}, u32[]{:S(2)}, u32[]{:S(2)}) collective-permute-start(bf16[4,16,16,128]{3,1,2,0:T(8,128)(2,1)} %fusion.82), channel_id=1, source_target_pairs={{0,8},{4,12},{8,0},{12,4},{1,9},{5,13},{9,1},{13,5},{2,10},{6,14},... | collective-permute-start | bytes 786440 | tf_op jit(solution)/shard_map/ppermute | solution.py:62
  8.3 34.4 %collective-permute-start.4 = (bf16[4,16,16,128]{3,1,2,0:T(8,128)(2,1)}, bf16[4,16,16,128]{3,1,2,0:T(8,128)(2,1)S(1)}, u32[]{:S(2)}, u32[]{:S(2)}) collective-permute-start(bf16[4,16,16,128]{3,1,2,0:T(8,128)(2,1)} %fusion.82), channel_id=1, source_target_pairs={{0,4},{4,8},{8,12},{12,0},{1,5},{5,9},{9,13},{13,1},{2,6},{6,10},{... | collective-permute-start | bytes 786440 | tf_op jit(solution)/shard_map/ppermute | solution.py:62
  9.6 14.8 %copy-start.4 = (f32[1,64,64]{2,1,0:T(8,128)}, f32[1,64,64]{2,1,0:T(8,128)S(1)}, u32[]{:S(2)}) copy-start(f32[1,64,64]{2,1,0:T(8,128)S(1)} %get-tuple-element.21) | copy-start | bytes 49156
  9.6 14.8 %copy-start.6 = (f32[1,64,64]{2,1,0:T(8,128)}, f32[1,64,64]{2,1,0:T(8,128)S(1)}, u32[]{:S(2)}) copy-start(f32[1,64,64]{2,1,0:T(8,128)S(1)} %get-tuple-element.22) | copy-start | bytes 49156
  21.0 26.5 %collective-permute-start = (bf16[1,2,32,32,128]{4,2,3,1,0:T(8,128)(2,1)}, bf16[1,2,32,32,128]{4,2,3,1,0:T(8,128)(2,1)S(1)}, u32[]{:S(2)}, u32[]{:S(2)}) collective-permute-start(bf16[1,2,32,32,128]{4,2,3,1,0:T(8,128)(2,1)} %bitcast.228), channel_id=1, source_target_pairs={{0,2},{2,0},{1,3},{3,1},{4,6},{6,4},{5,7},{7,5},{8,10},{10,8},{9,1... | collective-permute-start | bytes 1572872 | tf_op jit(solution)/shard_map/ppermute | solution.py:74
  33.9 22.5 %collective-permute-start.1 = (bf16[1,2,32,32,128]{4,2,3,1,0:T(8,128)(2,1)}, bf16[1,2,32,32,128]{4,2,3,1,0:T(8,128)(2,1)S(1)}, u32[]{:S(2)}, u32[]{:S(2)}) collective-permute-start(bf16[1,2,32,32,128]{4,2,3,1,0:T(8,128)(2,1)} %bitcast.227), channel_id=1, source_target_pairs={{0,2},{2,0},{1,3},{3,1},{4,6},{6,4},{5,7},{7,5},{8,10},{10,8},{9,1... | collective-permute-start | bytes 1572872 | tf_op jit(solution)/shard_map/ppermute | solution.py:74
  39.4 3.3 %copy-start.8 = (s32[1,1,1,8]{3,2,1,0:T(1,128)S(1)}, s32[1,1,1,8]{3,2,1,0:T(1,128)}, u32[]{:S(2)}) copy-start(s32[1,1,1,8]{3,2,1,0:T(1,128)} %param.7) | copy-start | bytes 100
  43.0 2.8 %copy-start.9 = (s32[1,1,1,8,1]{3,4,2,1,0:T(1,128)S(1)}, s32[1,1,1,8,1]{3,4,2,1,0:T(1,128)}, u32[]{:S(2)}) copy-start(s32[1,1,1,8,1]{3,4,2,1,0:T(1,128)} %param.8) | copy-start | bytes 100
  43.3 1.4 %copy-start.3 = (bf16[8,4,16,16,128]{4,2,3,1,0:T(8,128)(2,1)}, bf16[8,4,16,16,128]{4,2,3,1,0:T(8,128)(2,1)S(1)}, u32[]{:S(2)}) copy-start(bf16[8,4,16,16,128]{4,2,3,1,0:T(8,128)(2,1)S(1)} %bitcast_dynamic-update-slice_fusion.1) | copy-start | bytes 6291460
  45.9 19.4 %collective-permute-start.5 = (bf16[4,4,16,16,128]{4,2,3,1,0:T(8,128)(2,1)}, bf16[4,4,16,16,128]{4,2,3,1,0:T(8,128)(2,1)}, u32[]{:S(2)}, u32[]{:S(2)}) collective-permute-start(bf16[4,4,16,16,128]{4,2,3,1,0:T(8,128)(2,1)} %constant_dynamic-slice_fusion.8), channel_id=1, source_target_pairs={{0,1},{1,0},{2,3},{3,2},{4,5},{5,4},{6,7},{7,6},{8,9},{9,8},{10,11... | collective-permute-start | bytes 3145736 | tf_op jit(solution)/shard_map/ppermute | solution.py:62
  69.8 4.9 %copy-start.5 = (f32[1,64,64]{2,1,0:T(8,128)S(1)}, f32[1,64,64]{2,1,0:T(8,128)}, u32[]{:S(2)}) copy-start(f32[1,64,64]{2,1,0:T(8,128)} %copy-done.4) | copy-start | bytes 49156
  69.8 4.9 %copy-start.7 = (f32[1,64,64]{2,1,0:T(8,128)S(1)}, f32[1,64,64]{2,1,0:T(8,128)}, u32[]{:S(2)}) copy-start(f32[1,64,64]{2,1,0:T(8,128)} %copy-done.6) | copy-start | bytes 49156
  83.1 14.7 %collective-permute-start.6 = (f32[32,1,32,128]{3,2,0,1:T(8,128)S(1)}, f32[32,1,32,128]{3,2,0,1:T(8,128)S(1)}, u32[]{:S(2)}, u32[]{:S(2)}) collective-permute-start(f32[32,1,32,128]{3,2,0,1:T(8,128)S(1)} %dynamic-slice_bitcast_fusion), channel_id=1, source_target_pairs={{0,2},{2,0},{1,3},{3,1},{4,6},{6,4},{5,7},{7,5},{8,10},{10,8},{9,1... | collective-permute-start | bytes 1572872 | tf_op jit(solution)/shard_map/ppermute | solution.py:74
  103.1 20.1 %copy-start.1 = (f32[2,4,16,32,64]{4,3,2,1,0:T(8,128)S(1)}, f32[2,4,16,32,64]{4,3,2,1,0:T(8,128)}, u32[]{:S(2)}) copy-start(f32[2,4,16,32,64]{4,3,2,1,0:T(8,128)} %param.6) | copy-start | bytes 3145732
  105.1 18.1 %copy-start.2 = (f32[32,64,64]{2,1,0:T(8,128)}, f32[32,64,64]{2,1,0:T(8,128)S(1)}, u32[]{:S(2)}) copy-start(f32[32,64,64]{2,1,0:T(8,128)S(1)} %convolution_multiply_fusion) | copy-start | bytes 1572868
  109.6 5.6 %collective-permute-start.7 = (f32[2,512]{1,0:T(2,128)S(1)}, f32[2,512]{1,0:T(2,128)S(1)}, u32[]{:S(2)}, u32[]{:S(2)}) collective-permute-start(f32[2,512]{1,0:T(2,128)S(1)} %get-tuple-element.16), channel_id=1, source_target_pairs={{0,13},{1,0},{4,1},{5,4},{8,5},{9,8},{12,9},{13,12},{2,15},{3,2},{... | collective-permute-start | bytes 12296 | tf_op jit(solution)/shard_map/ppermute | solution.py:74
  112.1 5.5 %collective-permute-start.8 = (f32[2,512]{1,0:T(2,128)S(1)}, f32[2,512]{1,0:T(2,128)S(1)}, u32[]{:S(2)}, u32[]{:S(2)}) collective-permute-start(f32[2,512]{1,0:T(2,128)S(1)} %get-tuple-element.15), channel_id=1, source_target_pairs={{0,12},{1,13},{4,0},{5,1},{8,4},{9,5},{12,8},{13,9},{2,14},{3,15},... | collective-permute-start | bytes 12296 | tf_op jit(solution)/shard_map/ppermute | solution.py:74
  112.7 5.0 %collective-permute-start.9 = (f32[2,512]{1,0:T(2,128)S(1)}, f32[2,512]{1,0:T(2,128)S(1)}, u32[]{:S(2)}, u32[]{:S(2)}) collective-permute-start(f32[2,512]{1,0:T(2,128)S(1)} %get-tuple-element.14), channel_id=1, source_target_pairs={{0,9},{1,12},{4,13},{5,0},{8,1},{9,4},{12,5},{13,8},{2,11},{3,14},... | collective-permute-start | bytes 12296 | tf_op jit(solution)/shard_map/ppermute | solution.py:74
  113.5 4.5 %collective-permute-start.10 = (f32[2,512]{1,0:T(2,128)S(1)}, f32[2,512]{1,0:T(2,128)S(1)}, u32[]{:S(2)}, u32[]{:S(2)}) collective-permute-start(f32[2,512]{1,0:T(2,128)S(1)} %get-tuple-element.13), channel_id=1, source_target_pairs={{0,8},{1,9},{4,12},{5,13},{8,0},{9,1},{12,4},{13,5},{2,10},{3,11},... | collective-permute-start | bytes 12296 | tf_op jit(solution)/shard_map/ppermute | solution.py:74
  115.3 3.9 %collective-permute-start.11 = (f32[2,512]{1,0:T(2,128)S(1)}, f32[2,512]{1,0:T(2,128)S(1)}, u32[]{:S(2)}, u32[]{:S(2)}) collective-permute-start(f32[2,512]{1,0:T(2,128)S(1)} %get-tuple-element.12), channel_id=1, source_target_pairs={{0,5},{1,8},{4,9},{5,12},{8,13},{9,0},{12,1},{13,4},{2,7},{3,10},{... | collective-permute-start | bytes 12296 | tf_op jit(solution)/shard_map/ppermute | solution.py:74
  115.3 5.4 %collective-permute-start.12 = (f32[2,512]{1,0:T(2,128)S(1)}, f32[2,512]{1,0:T(2,128)S(1)}, u32[]{:S(2)}, u32[]{:S(2)}) collective-permute-start(f32[2,512]{1,0:T(2,128)S(1)} %get-tuple-element.11), channel_id=1, source_target_pairs={{0,4},{1,5},{4,8},{5,9},{8,12},{9,13},{12,0},{13,1},{2,6},{3,7},{6... | collective-permute-start | bytes 12296 | tf_op jit(solution)/shard_map/ppermute | solution.py:74
  117.6 4.8 %collective-permute-start.13 = (f32[2,512]{1,0:T(2,128)S(1)}, f32[2,512]{1,0:T(2,128)S(1)}, u32[]{:S(2)}, u32[]{:S(2)}) collective-permute-start(f32[2,512]{1,0:T(2,128)S(1)} %get-tuple-element.10), channel_id=1, source_target_pairs={{0,1},{1,4},{4,5},{5,8},{8,9},{9,12},{12,13},{13,0},{2,3},{3,6},{6... | collective-permute-start | bytes 12296 | tf_op jit(solution)/shard_map/ppermute | solution.py:74

commit v5 on v3

--- a/solution.py
+++ b/solution.py
@@ -173,19 +173,26 @@
     whole_receptor = gather_receptor(receptor)
     product = correlate(spectra, whole_receptor)
 
-    back_x = jnp.einsum("exk,rjkl->xrejl", pair, product, precision=highest)
-    back_x = combine_call(back_x.reshape(-1, 2, y_local, 2 * length), -1.0, 1.0, 1, jnp.float32)
-    back_x = back_x.reshape(n_sub, x_local, rots, y_local, 2 * length)
+    halves = 2 if y_local % 16 == 0 else 1
+    rows_half = y_local // halves
     pair_y = pair.reshape(2, length, n_sub, y_local)
-    back_y = sum(
-        jnp.einsum(
-            "eyj,xrjl->rxeyl",
-            lax.dynamic_index_in_dim(pair_y, source, axis=2, keepdims=False),
-            piece,
-            precision=highest,
-        )
-        for source, piece in exchange(back_x, "sub")
-    )
+    back_y = 0.0
+    for h in range(halves):
+        rows = slice(h * rows_half, (h + 1) * rows_half)
+        back_x = jnp.einsum("exk,rjkl->xrejl", pair, product[:, rows], precision=highest)
+        back_x = combine_call(
+            back_x.reshape(-1, 2, rows_half, 2 * length), -1.0, 1.0, 1, jnp.float32
+        )
+        back_x = back_x.reshape(n_sub, x_local, rots, rows_half, 2 * length)
+        back_y = back_y + sum(
+            jnp.einsum(
+                "eyj,xrjl->rxeyl",
+                lax.dynamic_index_in_dim(pair_y[..., rows], source, axis=2, keepdims=False),
+                piece,
+                precision=highest,
+            )
+            for source, piece in exchange(back_x, "sub")
+        )
     back_y = combine_call(back_y.reshape(-1, 2, ny, 2 * length), -1.0, 1.0, 1, jnp.float32)
     back_y = back_y.reshape(rots, x_local, ny, 2 * length)
     last_table = jnp.concatenate([cos_table, -sin_table], axis=0)

time: 121 us -> 123 us (1.017)
  matrix products: 38.9 us -> 41.5 us
  waiting for transfers between devices: 11.1 us -> 9.44 us
  Pallas kernels: 23.9 us -> 25.5 us
  other arithmetic: 6.64 us -> 5.24 us
    dot_general x3 -> x6, matrix products: 6.61 us -> 9.07 us  [the longest x4 5.87 us: local(): jnp.einsum('eyj,xrjl->rxeyl', lax.dynamic_index_in_dim(pair_y[..., rows],...]
    ppermute x3 -> x4, waiting for transfers between devices: 11.1 us -> 9.43 us  [exchange(): pieces.append(((me - shift) % count, lax.ppermute(piece, axis, pairs)))]
    pallas_call x6 -> x7, Pallas kernels: 19 us -> 20.6 us  [combine_call(): pl.pallas_call(functools.partial(combine_kernel, first=first, second=seco...]
    dot_general x1 -> x2, local copies, waits for them, and re-layouts: 2.56 us -> 3.16 us  [local(): jnp.einsum('exk,rjkl->xrejl', pair, product[:, rows], precision=highest)]
    ppermute x3 -> x4, starting transfers between devices: 3.58 us -> 4.18 us  [exchange(): pieces.append(((me - shift) % count, lax.ppermute(piece, axis, pairs)))]
    unnamed x25 -> x33, local copies, waits for them, and re-layouts: 3.82 us -> 3.83 us
  transfers between devices with their start and end apart: 7 -> 8, of which waited for: 1 -> 2; matrix products, arithmetic and copies ran while one was open for 34% -> 33% of each run, Pallas kernels for 11% -> 11%
where the time goes in v5:
time: 123 us
  matrix products  41.5 us (34%)
  Pallas kernels  25.5 us (21%)
  local copies, waits for them, and re-layouts  20.1 us (16%)
  starting transfers between devices  10.2 us (8%)
  blocking collectives  9.63 us (8%)
  waiting for transfers between devices  9.44 us (8%)
  other arithmetic  5.24 us (4%)
    pallas_call x7, Pallas kernels, combine_call(): pl.pallas_call(functools.partial(combine_kernel, first=first, second=seco...  20.6 us
    dot_general x4, matrix products, local(): jnp.einsum('ekx,rtxjl->rtjekl', lax.dynamic_index_in_dim(pair_x, source,...  17.5 us
    all_to_all x1, blocking collectives, local(): lax.all_to_all(packed, ('rot', 'ref'), split_axis=0, concat_axis=0, tiled...  9.63 us
    ppermute x4, waiting for transfers between devices, exchange(): pieces.append(((me - shift) % count, lax.ppermute(piece, axis, pairs)))  9.43 us
    dot_general x2, matrix products, local(): along_y = jnp.einsum('ejy,rtxyl->rtxejl', pair, along_z, precision=highest)  7.46 us
    ppermute x4, starting transfers between devices, gather_by_shifts(): pieces.append(lax.ppermute(piece, axis, pairs))  6.06 us
    dot_general x4, matrix products, local(): jnp.einsum('eyj,xrjl->rxeyl', lax.dynamic_index_in_dim(pair_y[..., rows],...  5.87 us
    pallas_call x1, Pallas kernels, correlate(): pl.pallas_call(product_kernel, grid=(rots, rows // block), in_specs=[pl.B...  4.93 us
  transfers between devices with their start and end apart: 8, of which 2 were waited for; matrix products, arithmetic and copies ran while one was open for 33% of the time, Pallas kernels for 11%

profile of v5, /device:TPU:0, one launch (start us, length us, event | category | flops | bytes accessed | tf_op | source)
XLA Modules:
  0.0 122.6 jit_solution(17163036966138253313)
XLA Ops:
  0.7 1.6 %copy-done = f32[2,4,16,32,64]{4,3,2,1,0:T(8,128)S(1)} copy-done((f32[2,4,16,32,64]{4,3,2,1,0:T(8,128)S(1)}, f32[2,4,16,32,64]{4,3,2,1,0:T(8,128)}, u32[]{:S(2)}) %copy-start) | copy-done | bytes 1048600
  3.3 5.0 %collective-permute-start.2 = (bf16[4,16,16,128]{3,1,2,0:T(8,128)(2,1)}, bf16[4,16,16,128]{3,1,2,0:T(8,128)(2,1)S(1)}, u32[]{:S(2)}, u32[]{:S(2)}) collective-permute-start(bf16[4,16,16,128]{3,1,2,0:T(8,128)(2,1)} %fusion.107), channel_id=1, source_target_pairs={{0,12},{4,0},{8,4},{12,8},{1,13},{5,1},{9,5},{13,9},{2,14},{6,2},{... | collective-permute-start | bytes 786440 | tf_op jit(solution)/shard_map/ppermute | solution.py:62
  9.7 1.9 %fusion.11 = f32[128,2,32,64]{0,3,2,1:T(8,128)S(1)} fusion(bf16[1,4,32,64,64]{4,3,2,1,0:T(8,128)(2,1)} %param.5, f32[64,64]{0,1:T(8,128)S(1)} %get-tuple-element.10, f32[64,64]{0,1:T(8,128)S(1)} %get-tuple-element.11), kind=kOutput, calls=%fused_computation.20 | convolution fusion | flops 201334784 | bytes 3178496 | tf_op jit(solution)/shard_map/rtxyz,zl->rtxyl/dot_general | solution.py:154
  11.6 3.7 %fusion.6 = f32[2,32,128,2,64]{2,4,3,1,0:T(8,128)} fusion(f32[128,2,32,64]{0,3,2,1:T(8,128)S(1)} %fusion.11, f32[1,64,64]{2,1,0:T(8,128)S(1)} %get-tuple-element.12, f32[1,64,64]{2,1,0:T(8,128)S(1)} %get-tuple-element.13), kind=kOutput, calls=%fused_computation.13 | convolution fusion | flops 402661376 | bytes 6324224 | tf_op jit(solution)/shard_map/ejy,rtxyl->rtxejl/dot_general | solution.py:155
  15.3 3.4 %shard_map.68 = bf16[2,64,32,128]{3,2,1,0:T(8,128)(2,1)} custom-call(f32[64,2,64,128]{3,2,1,0:T(8,128)} %bitcast.235), custom_call_target="tpu_custom_call" | custom-call | flops 1572864 | bytes 5242880 | tf_op jit(solution)/shard_map/pallas_call | solution.py:42
  22.5 1.9 %fusion.9 = f32[128,2,32,64]{0,3,2,1:T(8,128)S(1)} fusion(bf16[1,4,32,64,64]{4,3,2,1,0:T(8,128)(2,1)} %param.5, f32[64,64]{0,1:T(8,128)S(1)} %get-tuple-element.10, f32[64,64]{0,1:T(8,128)S(1)} %get-tuple-element.11), kind=kOutput, calls=%fused_computation.18 | convolution fusion | flops 201334784 | bytes 3178496 | tf_op jit(solution)/shard_map/rtxyz,zl->rtxyl/dot_general | solution.py:154
  24.4 3.7 %fusion.4 = f32[2,32,128,2,64]{2,4,3,1,0:T(8,128)} fusion(f32[128,2,32,64]{0,3,2,1:T(8,128)S(1)} %fusion.9, f32[1,64,64]{2,1,0:T(8,128)S(1)} %get-tuple-element.12, f32[1,64,64]{2,1,0:T(8,128)S(1)} %get-tuple-element.13), kind=kOutput, calls=%fused_computation.11 | convolution fusion | flops 402661376 | bytes 6324224 | tf_op jit(solution)/shard_map/ejy,rtxyl->rtxejl/dot_general | solution.py:155
  28.1 3.4 %shard_map.70 = bf16[2,64,32,128]{3,2,1,0:T(8,128)(2,1)} custom-call(f32[64,2,64,128]{3,2,1,0:T(8,128)} %bitcast.236), custom_call_target="tpu_custom_call" | custom-call | flops 1572864 | bytes 5242880 | tf_op jit(solution)/shard_map/pallas_call | solution.py:42
  34.6 3.3 %fusion.21 = f32[2,32,128,2,64]{2,4,3,1,0:T(8,128)} fusion(bf16[1,1,2,32,32,128]{5,4,3,2,0,1:T(8,128)(2,1)S(1)} %get-tuple-element.5, s32[]{:T(128)S(6)} %select_n.120, f32[1,64,2,32]{1,3,0,2:T(8,128)S(1)} %get-tuple-element.9, f32[1,64,2,32]{1,3,0,2:T(8,128)S(1)} %get-tuple-element.8), kind=kOutput, calls=%fused_computation.35 | convolution fusion | flops 201330688 | bytes 4751364 | tf_op jit(solution)/shard_map/ekx,rtxjl->rtjekl/dot_general | solution.py:160
  37.9 3.2 %fusion.18 = f32[2,32,128,2,64]{2,4,3,1,0:T(8,128)} fusion(bf16[1,1,2,32,32,128]{5,4,3,2,0,1:T(8,128)(2,1)S(1)} %get-tuple-element.3, s32[]{:T(128)S(6)} %select_n.120, f32[1,64,2,32]{1,3,0,2:T(8,128)S(1)} %get-tuple-element.9, f32[1,64,2,32]{1,3,0,2:T(8,128)S(1)} %get-tuple-element.8), kind=kOutput, calls=%fused_computation.32 | convolution fusion | flops 201330688 | bytes 4751364 | tf_op jit(solution)/shard_map/ekx,rtxjl->rtjekl/dot_general | solution.py:160
  46.7 5.5 %convolution_add_fusion.1 = f32[2,32,128,2,64]{2,4,3,1,0:T(8,128)} fusion(f32[2,32,128,2,64]{2,4,3,1,0:T(8,128)} %fusion.21, bf16[1,2,32,32,128]{4,2,3,1,0:T(8,128)(2,1)S(1)} %collective-permute-done, s32[]{:T(128)S(6)} %select_n.125, f32[1,64,2,32]{1,3,0,2:T(8,128)S(1)} %get-tuple-element.9, f32[1,64,2,32]{1,3,0,2:T(8,128)S(1)} %get-tuple-element.8), kind=kOutput, calls=%fused_computation.6 | convolution fusion | flops 202379264 | bytes 8945668 | tf_op jit(solution)/shard_map/ekx,rtxjl->rtjekl/dot_general | solution.py:160
  52.2 3.4 %shard_map.69 = bf16[1,64,64,128]{3,2,1,0:T(8,128)(2,1)} custom-call(f32[64,2,64,128]{3,2,1,0:T(8,128)} %bitcast.233), custom_call_target="tpu_custom_call" | custom-call | flops 1572864 | bytes 5242880 | tf_op jit(solution)/shard_map/pallas_call | solution.py:42
  55.6 5.4 %convolution_add_fusion = f32[2,32,128,2,64]{2,4,3,1,0:T(8,128)} fusion(f32[2,32,128,2,64]{2,4,3,1,0:T(8,128)} %fusion.18, bf16[1,2,32,32,128]{4,2,3,1,0:T(8,128)(2,1)S(1)} %collective-permute-done.1, s32[]{:T(128)S(6)} %select_n.125, f32[1,64,2,32]{1,3,0,2:T(8,128)S(1)} %get-tuple-element.9, f32[1,64,2,32]{1,3,0,2:T(8,128)S(1)} %get-tuple-element.8), kind=kOutput, calls=%fused_computation.5 | convolution fusion | flops 202379264 | bytes 8945668 | tf_op jit(solution)/shard_map/ekx,rtxjl->rtjekl/dot_general | solution.py:160
  61.0 3.4 %shard_map.71 = bf16[1,64,64,128]{3,2,1,0:T(8,128)(2,1)} custom-call(f32[64,2,64,128]{3,2,1,0:T(8,128)} %bitcast.234), custom_call_target="tpu_custom_call" | custom-call | flops 1572864 | bytes 5242880 | tf_op jit(solution)/shard_map/pallas_call | solution.py:42
  64.4 2.7 %fusion.3 = bf16[4,2,16,4,16,128]{5,2,4,0,3,1:T(8,128)(2,1)S(1)} fusion(s32[]{:T(128)S(6)} %select_n.130, bf16[1,4,4,16,16,128]{5,3,4,2,1,0:T(8,128)(2,1)} %bitcast.61, bf16[1,4,4,16,16,128]{5,3,4,2,1,0:T(8,128)(2,1)S(1)} %fusion.112), kind=kLoop, calls=%fused_computation.10 | loop fusion | flops 3145728 | bytes 4194308 | tf_op jit(solution)/shard_map/transpose | solution.py:88
  67.1 1.9 %copy.18 = bf16[4,2,16,4,16,128]{5,4,3,2,1,0:T(8,128)(2,1)} copy(bf16[4,2,16,4,16,128]{5,2,4,0,3,1:T(8,128)(2,1)S(1)} %fusion.3) | data formatting | bytes 4194304 | tf_op jit(solution)/shard_map/transpose | solution.py:88
  68.9 4.9 %shard_map.72 = f32[1,2048,128]{2,1,0:T(8,128)} custom-call(bf16[1,2,2048,128]{3,2,1,0:T(8,128)(2,1)} %bitcast.238, bf16[1,2,2048,128]{3,2,1,0:T(8,128)(2,1)} %bitcast.239, bf16[4,2048,128]{2,1,0:T(8,128)(2,1)} %bitcast.237), custom_call_target="tpu_custom_call" | custom-call | flops 8388608 | bytes 5242880 | tf_op jit(solution)/shard_map/pallas_call | solution.py:119
  73.9 1.6 %fusion.15 = f32[16,128,2,64]{1,3,2,0:T(8,128)S(1)} fusion(f32[1,32,64,128]{3,2,1,0:T(8,128)} %bitcast.240, f32[1,64,64]{2,1,0:T(8,128)S(1)} %get-tuple-element.12, f32[1,64,64]{2,1,0:T(8,128)S(1)} %get-tuple-element.13), kind=kOutput, calls=%fused_computation.28 | convolution fusion | flops 100671488 | bytes 1605632 | tf_op jit(solution)/shard_map/exk,rjkl->xrejl/dot_general | solution.py:182
  75.5 1.6 %fusion.16 = f32[16,128,2,64]{1,3,2,0:T(8,128)S(1)} fusion(f32[1,32,64,128]{3,2,1,0:T(8,128)} %bitcast.241, f32[1,64,64]{2,1,0:T(8,128)S(1)} %get-tuple-element.12, f32[1,64,64]{2,1,0:T(8,128)S(1)} %get-tuple-element.13), kind=kOutput, calls=%fused_computation.30 | convolution fusion | flops 100671488 | bytes 1605632 | tf_op jit(solution)/shard_map/exk,rjkl->xrejl/dot_general | solution.py:182
  77.1 1.6 %copy.49 = f32[16,128,2,64]{1,0,2,3:T(8,128)} copy(f32[16,128,2,64]{1,3,2,0:T(8,128)S(1)} %fusion.15) | data formatting | bytes 2097152 | tf_op jit(solution)/shard_map/exk,rjkl->xrejl/dot_general | solution.py:182
  78.7 2.0 %shard_map.74 = f32[1,64,16,128]{3,2,1,0:T(8,128)} custom-call(f32[64,2,16,128]{3,2,1,0:T(8,128)} %bitcast.245), custom_call_target="tpu_custom_call" | custom-call | flops 393216 | bytes 1572864 | tf_op jit(solution)/shard_map/pallas_call | solution.py:42
  80.7 1.6 %copy.50 = f32[16,128,2,64]{1,0,2,3:T(8,128)} copy(f32[16,128,2,64]{1,3,2,0:T(8,128)S(1)} %fusion.16) | data formatting | bytes 2097152 | tf_op jit(solution)/shard_map/exk,rjkl->xrejl/dot_general | solution.py:182
  82.3 2.0 %shard_map.73 = f32[1,64,16,128]{3,2,1,0:T(8,128)} custom-call(f32[64,2,16,128]{3,2,1,0:T(8,128)} %bitcast.246), custom_call_target="tpu_custom_call" | custom-call | flops 393216 | bytes 1572864 | tf_op jit(solution)/shard_map/pallas_call | solution.py:42
  85.4 1.6 %collective-permute-start.6 = (f32[32,1,16,128]{3,2,0,1:T(8,128)S(1)}, f32[32,1,16,128]{3,2,0,1:T(8,128)S(1)}, u32[]{:S(2)}, u32[]{:S(2)}) collective-permute-start(f32[32,1,16,128]{3,2,0,1:T(8,128)S(1)} %dynamic-slice_bitcast_fusion.1), channel_id=1, source_target_pairs={{0,2},{2,0},{1,3},{3,1},{4,6},{6,4},{5,7},{7,5},{8,10},{10,8},{9,1... | collective-permute-start | bytes 786440 | tf_op jit(solution)/shard_map/ppermute | solution.py:74
  89.7 5.0 %collective-permute-done.6 = f32[32,1,16,128]{3,2,0,1:T(8,128)S(1)} collective-permute-done((f32[32,1,16,128]{3,2,0,1:T(8,128)S(1)}, f32[32,1,16,128]{3,2,0,1:T(8,128)S(1)}, u32[]{:S(2)}, u32[]{:S(2)}) %collective-permute-start.6) | collective-permute-done | bytes 262176 | tf_op jit(solution)/shard_map/ppermute | solution.py:74
  95.7 4.4 %collective-permute-done.7 = f32[32,1,16,128]{3,2,0,1:T(8,128)S(1)} collective-permute-done((f32[32,1,16,128]{3,2,0,1:T(8,128)S(1)}, f32[32,1,16,128]{3,2,0,1:T(8,128)S(1)}, u32[]{:S(2)}, u32[]{:S(2)}) %collective-permute-start.7) | collective-permute-done | bytes 262176 | tf_op jit(solution)/shard_map/ppermute | solution.py:74
  100.1 2.8 %add_bitcast_fusion.in_ref = f32[32,2,64,128]{3,2,1,0:T(8,128)} fusion(f32[32,128,2,64]{1,3,2,0:T(8,128)S(1)} %fusion.26, f32[32,128,2,64]{1,3,2,0:T(8,128)S(1)} %fusion.30, f32[32,128,2,64]{1,3,2,0:T(8,128)S(1)} %fusion.28, f32[32,1,16,128]{3,2,0,1:T(8,128)S(1)} %collective-permute-done.7, s32[]{:T(128)S(6)} %select_n.125, ...), kind=kOutput, calls=%fused_computation.15 | convolution fusion | flops 51906560 | bytes 8683524 | tf_op jit(solution)/shard_map/eyj,xrjl->rxeyl/dot_general | solution.py:188
  102.9 3.0 %shard_map.75 = f32[1,32,64,128]{3,2,1,0:T(8,128)} custom-call(f32[32,2,64,128]{3,2,1,0:T(8,128)} %add_bitcast_fusion.in_ref), custom_call_target="tpu_custom_call" | custom-call | flops 786432 | bytes 3145728 | tf_op jit(solution)/shard_map/pallas_call | solution.py:42
  106.0 1.9 %convolution_multiply_fusion = f32[32,64,64]{2,1,0:T(8,128)S(1)} fusion(f32[1,32,64,128]{3,2,1,0:T(8,128)} %shard_map.75, f32[64,64]{0,1:T(8,128)S(1)} %copy-done.7, f32[64,64]{0,1:T(8,128)S(1)} %copy-done.9), kind=kOutput, calls=%fused_computation.16 | convolution fusion | flops 100802560 | bytes 1605632 | tf_op jit(solution)/shard_map/rxyl,lz->rxyz/dot_general | solution.py:199
  109.0 1.6 %gather_fusion = f32[8,512]{1,0:T(8,128)S(1)} fusion(f32[256,512]{1,0:T(8,128)} %reshape.331, s32[1024]{0:T(1024)S(1)} %pad_clamp_fusion), kind=kCustom, calls=%fused_computation | custom fusion | bytes 32800 | tf_op jit(solution)/shard_map/gather | solution.py:206
  110.6 1.6 %fusion.108 = f32[8,512]{1,0:T(8,128)S(1)} fusion(f32[8,512]{1,0:T(8,128)S(1)} %gather_fusion, f32[512,512]{1,0:T(8,128)} %param.9), kind=kOutput, calls=%fused_computation.166 | convolution fusion | flops 12582912 | bytes 1081344 | tf_op jit(solution)/shard_map/dot_general | solution.py:215
  112.4 9.6 %all_to_all.5 = f32[8,2,512]{2,1,0:T(2,128)S(1)} all-to-all(f32[8,2,512]{2,1,0:T(2,128)S(1)} %reshape.333), channel_id=1, replica_groups=mesh['grp'=2,'rot'=4,'sub'=2,'ref'=2] {'rot','ref'}, dimensions={0} | all-to-all | bytes 65536 | tf_op jit(solution)/shard_map/all_to_all | solution.py:217
  (72 shorter events, 21.3 us)
Async XLA Ops:
  0.6 1.6 %copy-start = (f32[2,4,16,32,64]{4,3,2,1,0:T(8,128)S(1)}, f32[2,4,16,32,64]{4,3,2,1,0:T(8,128)}, u32[]{:S(2)}) copy-start(f32[2,4,16,32,64]{4,3,2,1,0:T(8,128)} %param.6) | copy-start | bytes 3145732
  3.3 38.7 %collective-permute-start.2 = (bf16[4,16,16,128]{3,1,2,0:T(8,128)(2,1)}, bf16[4,16,16,128]{3,1,2,0:T(8,128)(2,1)S(1)}, u32[]{:S(2)}, u32[]{:S(2)}) collective-permute-start(bf16[4,16,16,128]{3,1,2,0:T(8,128)(2,1)} %fusion.107), channel_id=1, source_target_pairs={{0,12},{4,0},{8,4},{12,8},{1,13},{5,1},{9,5},{13,9},{2,14},{6,2},{... | collective-permute-start | bytes 786440 | tf_op jit(solution)/shard_map/ppermute | solution.py:62
  8.3 33.7 %collective-permute-start.3 = (bf16[4,16,16,128]{3,1,2,0:T(8,128)(2,1)}, bf16[4,16,16,128]{3,1,2,0:T(8,128)(2,1)S(1)}, u32[]{:S(2)}, u32[]{:S(2)}) collective-permute-start(bf16[4,16,16,128]{3,1,2,0:T(8,128)(2,1)} %fusion.107), channel_id=1, source_target_pairs={{0,8},{4,12},{8,0},{12,4},{1,9},{5,13},{9,1},{13,5},{2,10},{6,14},... | collective-permute-start | bytes 786440 | tf_op jit(solution)/shard_map/ppermute | solution.py:62
  8.3 33.8 %collective-permute-start.4 = (bf16[4,16,16,128]{3,1,2,0:T(8,128)(2,1)}, bf16[4,16,16,128]{3,1,2,0:T(8,128)(2,1)S(1)}, u32[]{:S(2)}, u32[]{:S(2)}) collective-permute-start(bf16[4,16,16,128]{3,1,2,0:T(8,128)(2,1)} %fusion.107), channel_id=1, source_target_pairs={{0,4},{4,8},{8,12},{12,0},{1,5},{5,9},{9,13},{13,1},{2,6},{6,10},{... | collective-permute-start | bytes 786440 | tf_op jit(solution)/shard_map/ppermute | solution.py:62
  9.5 13.0 %copy-start.6 = (f32[64,64]{0,1:T(8,128)}, f32[64,64]{0,1:T(8,128)S(1)}, u32[]{:S(2)}) copy-start(f32[64,64]{0,1:T(8,128)S(1)} %get-tuple-element.10) | copy-start | bytes 49156
  9.5 13.0 %copy-start.8 = (f32[64,64]{0,1:T(8,128)}, f32[64,64]{0,1:T(8,128)S(1)}, u32[]{:S(2)}) copy-start(f32[64,64]{0,1:T(8,128)S(1)} %get-tuple-element.11) | copy-start | bytes 49156
  21.0 25.7 %collective-permute-start = (bf16[1,2,32,32,128]{4,2,3,1,0:T(8,128)(2,1)}, bf16[1,2,32,32,128]{4,2,3,1,0:T(8,128)(2,1)S(1)}, u32[]{:S(2)}, u32[]{:S(2)}) collective-permute-start(bf16[1,2,32,32,128]{4,2,3,1,0:T(8,128)(2,1)} %bitcast.232), channel_id=1, source_target_pairs={{0,2},{2,0},{1,3},{3,1},{4,6},{6,4},{5,7},{7,5},{8,10},{10,8},{9,1... | collective-permute-start | bytes 1572872 | tf_op jit(solution)/shard_map/ppermute | solution.py:74
  33.8 21.7 %collective-permute-start.1 = (bf16[1,2,32,32,128]{4,2,3,1,0:T(8,128)(2,1)}, bf16[1,2,32,32,128]{4,2,3,1,0:T(8,128)(2,1)S(1)}, u32[]{:S(2)}, u32[]{:S(2)}) collective-permute-start(bf16[1,2,32,32,128]{4,2,3,1,0:T(8,128)(2,1)} %bitcast.231), channel_id=1, source_target_pairs={{0,2},{2,0},{1,3},{3,1},{4,6},{6,4},{5,7},{7,5},{8,10},{10,8},{9,1... | collective-permute-start | bytes 1572872 | tf_op jit(solution)/shard_map/ppermute | solution.py:74
  37.9 3.3 %copy-start.11 = (s32[1,1,1,8,1]{3,4,2,1,0:T(1,128)S(1)}, s32[1,1,1,8,1]{3,4,2,1,0:T(1,128)}, u32[]{:S(2)}) copy-start(s32[1,1,1,8,1]{3,4,2,1,0:T(1,128)} %param.8) | copy-start | bytes 100
  37.9 3.4 %copy-start.12 = (s32[1,1,1,8]{3,2,1,0:T(1,128)S(1)}, s32[1,1,1,8]{3,2,1,0:T(1,128)}, u32[]{:S(2)}) copy-start(s32[1,1,1,8]{3,2,1,0:T(1,128)} %param.7) | copy-start | bytes 100
  42.6 1.4 %copy-start.3 = (bf16[8,4,16,16,128]{4,2,3,1,0:T(8,128)(2,1)}, bf16[8,4,16,16,128]{4,2,3,1,0:T(8,128)(2,1)S(1)}, u32[]{:S(2)}) copy-start(bf16[8,4,16,16,128]{4,2,3,1,0:T(8,128)(2,1)S(1)} %bitcast_dynamic-update-slice_fusion.1) | copy-start | bytes 6291460
  45.2 19.2 %collective-permute-start.5 = (bf16[4,4,16,16,128]{4,2,3,1,0:T(8,128)(2,1)}, bf16[4,4,16,16,128]{4,2,3,1,0:T(8,128)(2,1)}, u32[]{:S(2)}, u32[]{:S(2)}) collective-permute-start(bf16[4,4,16,16,128]{4,2,3,1,0:T(8,128)(2,1)} %constant_dynamic-slice_fusion), channel_id=1, source_target_pairs={{0,1},{1,0},{2,3},{3,2},{4,5},{5,4},{6,7},{7,6},{8,9},{9,8},{10,11... | collective-permute-start | bytes 3145736 | tf_op jit(solution)/shard_map/ppermute | solution.py:62
  80.7 6.2 %copy-start.4 = (f32[1,64,16,128]{3,2,1,0:T(8,128)S(1)}, f32[1,64,16,128]{3,2,1,0:T(8,128)}, u32[]{:S(2)}) copy-start(f32[1,64,16,128]{3,2,1,0:T(8,128)} %shard_map.74) | copy-start | bytes 1572868
  84.3 4.3 %copy-start.5 = (f32[1,64,16,128]{3,2,1,0:T(8,128)S(1)}, f32[1,64,16,128]{3,2,1,0:T(8,128)}, u32[]{:S(2)}) copy-start(f32[1,64,16,128]{3,2,1,0:T(8,128)} %shard_map.73) | copy-start | bytes 1572868
  84.3 4.3 %copy-start.10 = (f32[2,64,2,16]{1,3,0,2:T(8,128)S(1)}, f32[2,64,2,16]{1,3,0,2:T(8,128)}, u32[]{:S(2)}) copy-start(f32[2,64,2,16]{1,3,0,2:T(8,128)} %fusion.47) | copy-start | bytes 49156
  85.4 9.2 %collective-permute-start.6 = (f32[32,1,16,128]{3,2,0,1:T(8,128)S(1)}, f32[32,1,16,128]{3,2,0,1:T(8,128)S(1)}, u32[]{:S(2)}, u32[]{:S(2)}) collective-permute-start(f32[32,1,16,128]{3,2,0,1:T(8,128)S(1)} %dynamic-slice_bitcast_fusion.1), channel_id=1, source_target_pairs={{0,2},{2,0},{1,3},{3,1},{4,6},{6,4},{5,7},{7,5},{8,10},{10,8},{9,1... | collective-permute-start | bytes 786440 | tf_op jit(solution)/shard_map/ppermute | solution.py:74
  87.0 13.1 %collective-permute-start.7 = (f32[32,1,16,128]{3,2,0,1:T(8,128)S(1)}, f32[32,1,16,128]{3,2,0,1:T(8,128)S(1)}, u32[]{:S(2)}, u32[]{:S(2)}) collective-permute-start(f32[32,1,16,128]{3,2,0,1:T(8,128)S(1)} %dynamic-slice_bitcast_fusion), channel_id=1, source_target_pairs={{0,2},{2,0},{1,3},{3,1},{4,6},{6,4},{5,7},{7,5},{8,10},{10,8},{9,1... | collective-permute-start | bytes 786440 | tf_op jit(solution)/shard_map/ppermute | solution.py:74
  102.9 3.1 %copy-start.7 = (f32[64,64]{0,1:T(8,128)S(1)}, f32[64,64]{0,1:T(8,128)}, u32[]{:S(2)}) copy-start(f32[64,64]{0,1:T(8,128)} %copy-done.6) | copy-start | bytes 49156
  102.9 3.1 %copy-start.9 = (f32[64,64]{0,1:T(8,128)S(1)}, f32[64,64]{0,1:T(8,128)}, u32[]{:S(2)}) copy-start(f32[64,64]{0,1:T(8,128)} %copy-done.8) | copy-start | bytes 49156
  102.9 19.7 %copy-start.1 = (f32[2,4,16,32,64]{4,3,2,1,0:T(8,128)S(1)}, f32[2,4,16,32,64]{4,3,2,1,0:T(8,128)}, u32[]{:S(2)}) copy-start(f32[2,4,16,32,64]{4,3,2,1,0:T(8,128)} %param.6) | copy-start | bytes 3145732
  107.9 14.8 %copy-start.2 = (f32[32,64,64]{2,1,0:T(8,128)}, f32[32,64,64]{2,1,0:T(8,128)S(1)}, u32[]{:S(2)}) copy-start(f32[32,64,64]{2,1,0:T(8,128)S(1)} %convolution_multiply_fusion) | copy-start | bytes 1572868

commit v6 on v3

--- a/solution.py
+++ b/solution.py
@@ -73,6 +73,13 @@
         pairs = [(k, (k + shift) % count) for k in range(count)]
         pieces.append(((me - shift) % count, lax.ppermute(piece, axis, pairs)))
     return pieces
+
+
+def table_for(tables, source):
+    chosen = tables[:, :, 0]
+    for index in range(1, tables.shape[2]):
+        chosen = jnp.where(source == index, tables[:, :, index], chosen)
+    return chosen
 
 
 def gather_receptor(receptor):
@@ -159,7 +166,7 @@
         along_x = sum(
             jnp.einsum(
                 "ekx,rtxjl->rtjekl",
-                lax.dynamic_index_in_dim(pair_x, source, axis=2, keepdims=False),
+                table_for(pair_x, source),
                 piece.astype(jnp.float32),
                 precision=highest,
             )
@@ -180,7 +187,7 @@
     back_y = sum(
         jnp.einsum(
             "eyj,xrjl->rxeyl",
-            lax.dynamic_index_in_dim(pair_y, source, axis=2, keepdims=False),
+            table_for(pair_y, source),
             piece,
             precision=highest,
         )

time: 121 us -> 120 us (level)
  other arithmetic: 6.64 us -> 5.24 us
    another operation x1 -> x0, other arithmetic: 1.39 us -> none  [local(): pair = jnp.stack([cos_table, sin_table])]
where the time goes in v6:
time: 120 us; the launch traced here: 119 us
  matrix products  38.9 us (32%)
  Pallas kernels  23.9 us (20%)
  local copies, waits for them, and re-layouts  19.5 us (16%)
  waiting for transfers between devices  11.1 us (9%)
  starting transfers between devices  9.64 us (8%)
  blocking collectives  9.63 us (8%)
  other arithmetic  5.24 us (4%)
    pallas_call x6, Pallas kernels, combine_call(): pl.pallas_call(functools.partial(combine_kernel, first=first, second=seco...  19 us
    dot_general x4, matrix products, local(): jnp.einsum('ekx,rtxjl->rtjekl', table_for(pair_x, source), piece.astype(j...  17.4 us
    ppermute x3, waiting for transfers between devices, exchange(): pieces.append(((me - shift) % count, lax.ppermute(piece, axis, pairs)))  11.1 us
    all_to_all x1, blocking collectives, local(): lax.all_to_all(packed, ('rot', 'ref'), split_axis=0, concat_axis=0, tiled...  9.63 us
    dot_general x2, matrix products, local(): along_y = jnp.einsum('ejy,rtxyl->rtxejl', pair, along_z, precision=highest)  7.46 us
    ppermute x4, starting transfers between devices, gather_by_shifts(): pieces.append(lax.ppermute(piece, axis, pairs))  6.06 us
    pallas_call x1, Pallas kernels, correlate(): pl.pallas_call(product_kernel, grid=(rots, rows // block), in_specs=[pl.B...  4.92 us
    dynamic_slice x4, local copies, waits for them, and re-layouts, exchange(): lax.dynamic_index_in_dim(sending, (me + shift) % count, axis=0, keepdims=...  4.64 us
  transfers between devices with their start and end apart: 7, of which 1 were waited for; matrix products, arithmetic and copies ran while one was open for 34% of the time, Pallas kernels for 11%

profile of v6, /device:TPU:0, one launch (start us, length us, event | category | flops | bytes accessed | tf_op | source)
XLA Modules:
  0.0 118.9 jit_solution(8496443713747239166)
XLA Ops:
  0.7 1.6 %copy-done = f32[2,4,16,32,64]{4,3,2,1,0:T(8,128)S(1)} copy-done((f32[2,4,16,32,64]{4,3,2,1,0:T(8,128)S(1)}, f32[2,4,16,32,64]{4,3,2,1,0:T(8,128)}, u32[]{:S(2)}) %copy-start) | copy-done | bytes 1048600
  3.3 5.0 %collective-permute-start.2 = (bf16[4,16,16,128]{3,1,2,0:T(8,128)(2,1)}, bf16[4,16,16,128]{3,1,2,0:T(8,128)(2,1)S(1)}, u32[]{:S(2)}, u32[]{:S(2)}) collective-permute-start(bf16[4,16,16,128]{3,1,2,0:T(8,128)(2,1)} %fusion.74), channel_id=1, source_target_pairs={{0,12},{4,0},{8,4},{12,8},{1,13},{5,1},{9,5},{13,9},{2,14},{6,2},{... | collective-permute-start | bytes 786440 | tf_op jit(solution)/shard_map/ppermute | solution.py:62
  9.6 1.9 %fusion.11 = f32[128,2,32,64]{0,3,2,1:T(8,128)S(1)} fusion(bf16[1,4,32,64,64]{4,3,2,1,0:T(8,128)(2,1)} %param.5, f32[64,64]{0,1:T(8,128)S(1)} %get-tuple-element.12, f32[64,64]{0,1:T(8,128)S(1)} %get-tuple-element.13), kind=kOutput, calls=%fused_computation.21 | convolution fusion | flops 201334784 | bytes 3178496 | tf_op jit(solution)/shard_map/rtxyz,zl->rtxyl/dot_general | solution.py:161
  11.6 3.7 %fusion.6 = f32[2,32,128,2,64]{2,4,3,1,0:T(8,128)} fusion(f32[128,2,32,64]{0,3,2,1:T(8,128)S(1)} %fusion.11, f32[1,64,64]{2,1,0:T(8,128)S(1)} %get-tuple-element.14, f32[1,64,64]{2,1,0:T(8,128)S(1)} %get-tuple-element.15), kind=kOutput, calls=%fused_computation.13 | convolution fusion | flops 402661376 | bytes 6324224 | tf_op jit(solution)/shard_map/ejy,rtxyl->rtxejl/dot_general | solution.py:162
  15.3 3.4 %shard_map.68 = bf16[2,64,32,128]{3,2,1,0:T(8,128)(2,1)} custom-call(f32[64,2,64,128]{3,2,1,0:T(8,128)} %bitcast.195), custom_call_target="tpu_custom_call" | custom-call | flops 1572864 | bytes 5242880 | tf_op jit(solution)/shard_map/pallas_call | solution.py:42
  21.0 1.5 %collective-permute-start = (bf16[1,2,32,32,128]{4,2,3,1,0:T(8,128)(2,1)}, bf16[1,2,32,32,128]{4,2,3,1,0:T(8,128)(2,1)S(1)}, u32[]{:S(2)}, u32[]{:S(2)}) collective-permute-start(bf16[1,2,32,32,128]{4,2,3,1,0:T(8,128)(2,1)} %bitcast.192), channel_id=1, source_target_pairs={{0,2},{2,0},{1,3},{3,1},{4,6},{6,4},{5,7},{7,5},{8,10},{10,8},{9,1... | collective-permute-start | bytes 1572872 | tf_op jit(solution)/shard_map/ppermute | solution.py:74
  22.5 1.9 %fusion.9 = f32[128,2,32,64]{0,3,2,1:T(8,128)S(1)} fusion(bf16[1,4,32,64,64]{4,3,2,1,0:T(8,128)(2,1)} %param.5, f32[64,64]{0,1:T(8,128)S(1)} %get-tuple-element.12, f32[64,64]{0,1:T(8,128)S(1)} %get-tuple-element.13), kind=kOutput, calls=%fused_computation.19 | convolution fusion | flops 201334784 | bytes 3178496 | tf_op jit(solution)/shard_map/rtxyz,zl->rtxyl/dot_general | solution.py:161
  24.4 3.7 %fusion.4 = f32[2,32,128,2,64]{2,4,3,1,0:T(8,128)} fusion(f32[128,2,32,64]{0,3,2,1:T(8,128)S(1)} %fusion.9, f32[1,64,64]{2,1,0:T(8,128)S(1)} %get-tuple-element.14, f32[1,64,64]{2,1,0:T(8,128)S(1)} %get-tuple-element.15), kind=kOutput, calls=%fused_computation.11 | convolution fusion | flops 402661376 | bytes 6324224 | tf_op jit(solution)/shard_map/ejy,rtxyl->rtxejl/dot_general | solution.py:162
  28.2 3.4 %shard_map.70 = bf16[2,64,32,128]{3,2,1,0:T(8,128)(2,1)} custom-call(f32[64,2,64,128]{3,2,1,0:T(8,128)} %bitcast.196), custom_call_target="tpu_custom_call" | custom-call | flops 1572864 | bytes 5242880 | tf_op jit(solution)/shard_map/pallas_call | solution.py:42
  35.2 3.3 %fusion.22 = f32[2,32,128,2,64]{2,4,3,1,0:T(8,128)} fusion(bf16[1,1,2,32,32,128]{5,4,3,2,0,1:T(8,128)(2,1)S(1)} %get-tuple-element.5, f32[2,64,1,32]{1,3,0,2:T(8,128)S(1)} %get-tuple-element.9), kind=kOutput, calls=%fused_computation.33 | convolution fusion | flops 201326592 | bytes 4734976 | tf_op jit(solution)/shard_map/ekx,rtxjl->rtjekl/dot_general | solution.py:167
  38.5 3.2 %fusion.19 = f32[2,32,128,2,64]{2,4,3,1,0:T(8,128)} fusion(bf16[1,1,2,32,32,128]{5,4,3,2,0,1:T(8,128)(2,1)S(1)} %get-tuple-element.3, f32[2,64,1,32]{1,3,0,2:T(8,128)S(1)} %get-tuple-element.9), kind=kOutput, calls=%fused_computation.30 | convolution fusion | flops 201326592 | bytes 4734976 | tf_op jit(solution)/shard_map/ekx,rtxjl->rtjekl/dot_general | solution.py:167
  42.5 1.4 %copy-done.3 = bf16[8,4,16,16,128]{4,2,3,1,0:T(8,128)(2,1)} copy-done((bf16[8,4,16,16,128]{4,2,3,1,0:T(8,128)(2,1)}, bf16[8,4,16,16,128]{4,2,3,1,0:T(8,128)(2,1)S(1)}, u32[]{:S(2)}) %copy-start.3) | copy-done | bytes 2097176
  45.2 1.5 %fusion.80 = bf16[1,4,4,16,16,128]{5,3,4,2,1,0:T(8,128)(2,1)S(1)} fusion(bf16[8,4,16,16,128]{4,2,3,1,0:T(8,128)(2,1)} %copy-done.3, s32[]{:T(128)S(6)} %select_n.147), kind=kLoop, calls=%fused_computation.131 | loop fusion | bytes 2097156 | tf_op jit(solution)/shard_map/stack | solution.py:63
  46.7 5.5 %convolution_add_fusion.1 = f32[2,32,128,2,64]{2,4,3,1,0:T(8,128)} fusion(f32[2,32,128,2,64]{2,4,3,1,0:T(8,128)} %fusion.22, bf16[1,2,32,32,128]{4,2,3,1,0:T(8,128)(2,1)S(1)} %collective-permute-done, f32[2,64,1,32]{1,3,0,2:T(8,128)S(1)} %copy-done.4), kind=kOutput, calls=%fused_computation.6 | convolution fusion | flops 202375168 | bytes 8929280 | tf_op jit(solution)/shard_map/ekx,rtxjl->rtjekl/dot_general | solution.py:167
  52.1 3.4 %shard_map.69 = bf16[1,64,64,128]{3,2,1,0:T(8,128)(2,1)} custom-call(f32[64,2,64,128]{3,2,1,0:T(8,128)} %bitcast.193), custom_call_target="tpu_custom_call" | custom-call | flops 1572864 | bytes 5242880 | tf_op jit(solution)/shard_map/pallas_call | solution.py:42
  55.5 5.4 %convolution_add_fusion = f32[2,32,128,2,64]{2,4,3,1,0:T(8,128)} fusion(f32[2,32,128,2,64]{2,4,3,1,0:T(8,128)} %fusion.19, bf16[1,2,32,32,128]{4,2,3,1,0:T(8,128)(2,1)S(1)} %collective-permute-done.1, f32[2,64,1,32]{1,3,0,2:T(8,128)S(1)} %copy-done.4), kind=kOutput, calls=%fused_computation.5 | convolution fusion | flops 202375168 | bytes 8929280 | tf_op jit(solution)/shard_map/ekx,rtxjl->rtjekl/dot_general | solution.py:167
  60.9 3.4 %shard_map.71 = bf16[1,64,64,128]{3,2,1,0:T(8,128)(2,1)} custom-call(f32[64,2,64,128]{3,2,1,0:T(8,128)} %bitcast.194), custom_call_target="tpu_custom_call" | custom-call | flops 1572864 | bytes 5242880 | tf_op jit(solution)/shard_map/pallas_call | solution.py:42
  64.3 2.7 %fusion.3 = bf16[4,2,16,4,16,128]{5,2,4,0,3,1:T(8,128)(2,1)S(1)} fusion(s32[]{:T(128)S(6)} %select_n.149, bf16[1,4,4,16,16,128]{5,3,4,2,1,0:T(8,128)(2,1)} %bitcast.61, bf16[1,4,4,16,16,128]{5,3,4,2,1,0:T(8,128)(2,1)S(1)} %fusion.80), kind=kLoop, calls=%fused_computation.10 | loop fusion | flops 3145728 | bytes 4194308 | tf_op jit(solution)/shard_map/transpose | solution.py:95
  67.0 1.9 %copy.17 = bf16[4,2,16,4,16,128]{5,4,3,2,1,0:T(8,128)(2,1)} copy(bf16[4,2,16,4,16,128]{5,2,4,0,3,1:T(8,128)(2,1)S(1)} %fusion.3) | data formatting | bytes 4194304 | tf_op jit(solution)/shard_map/transpose | solution.py:95
  68.9 4.9 %shard_map.72 = f32[1,2048,128]{2,1,0:T(8,128)} custom-call(bf16[1,2,2048,128]{3,2,1,0:T(8,128)(2,1)} %bitcast.199, bf16[1,2,2048,128]{3,2,1,0:T(8,128)(2,1)} %bitcast.200, bf16[4,2048,128]{2,1,0:T(8,128)(2,1)} %bitcast.197), custom_call_target="tpu_custom_call" | custom-call | flops 8388608 | bytes 5242880 | tf_op jit(solution)/shard_map/pallas_call | solution.py:126
  73.8 2.2 %fusion.27 = f32[32,128,2,64]{1,3,2,0:T(8,128)S(1)} fusion(f32[32,64,128,1]{2,1,3,0:T(8,128)} %bitcast.201, f32[1,64,64]{2,1,0:T(8,128)S(1)} %get-tuple-element.14, f32[1,64,64]{2,1,0:T(8,128)S(1)} %get-tuple-element.15), kind=kOutput, calls=%fused_computation.56 | convolution fusion | flops 201334784 | bytes 3178496 | tf_op jit(solution)/shard_map/exk,rjkl->xrejl/dot_general | solution.py:183
  76.0 2.6 %copy.43 = f32[32,128,2,64]{1,0,2,3:T(8,128)} copy(f32[32,128,2,64]{1,3,2,0:T(8,128)S(1)} %fusion.27) | data formatting | bytes 4194304 | tf_op jit(solution)/shard_map/exk,rjkl->xrejl/dot_general | solution.py:183
  78.5 2.5 %shard_map.73 = f32[1,64,32,128]{3,2,1,0:T(8,128)} custom-call(f32[64,2,32,128]{3,2,1,0:T(8,128)} %bitcast.198), custom_call_target="tpu_custom_call" | custom-call | flops 786432 | bytes 3145728 | tf_op jit(solution)/shard_map/pallas_call | solution.py:42
  82.2 1.5 %collective-permute-start.6 = (f32[32,1,32,128]{3,2,0,1:T(8,128)S(1)}, f32[32,1,32,128]{3,2,0,1:T(8,128)S(1)}, u32[]{:S(2)}, u32[]{:S(2)}) collective-permute-start(f32[32,1,32,128]{3,2,0,1:T(8,128)S(1)} %dynamic-slice_bitcast_fusion), channel_id=1, source_target_pairs={{0,2},{2,0},{1,3},{3,1},{4,6},{6,4},{5,7},{7,5},{8,10},{10,8},{9,1... | collective-permute-start | bytes 1572872 | tf_op jit(solution)/shard_map/ppermute | solution.py:74
  83.7 2.1 %fusion.16 = f32[32,128,2,64]{1,3,2,0:T(8,128)S(1)} fusion(f32[2,32,1,32,128]{4,3,1,0,2:T(8,128)} %bitcast.206, s32[]{:T(128)S(6)} %select_n.134, f32[2,64,1,32]{1,3,0,2:T(8,128)S(1)} %copy-done.6), kind=kOutput, calls=%fused_computation.27 | convolution fusion | flops 100663296 | bytes 2637828 | tf_op jit(solution)/shard_map/eyj,xrjl->rxeyl/dot_general | solution.py:188
  85.8 11.1 %collective-permute-done.6 = f32[32,1,32,128]{3,2,0,1:T(8,128)S(1)} collective-permute-done((f32[32,1,32,128]{3,2,0,1:T(8,128)S(1)}, f32[32,1,32,128]{3,2,0,1:T(8,128)S(1)}, u32[]{:S(2)}, u32[]{:S(2)}) %collective-permute-start.6) | collective-permute-done | bytes 524320 | tf_op jit(solution)/shard_map/ppermute | solution.py:74
  96.9 2.4 %add_bitcast_fusion.in_ref = f32[32,2,64,128]{3,2,1,0:T(8,128)} fusion(f32[32,128,2,64]{1,3,2,0:T(8,128)S(1)} %fusion.16, f32[32,1,32,128]{3,2,0,1:T(8,128)S(1)} %collective-permute-done.6, f32[2,64,1,32]{1,3,0,2:T(8,128)S(1)} %copy-done.4), kind=kOutput, calls=%fused_computation.16 | convolution fusion | flops 101187584 | bytes 4734976 | tf_op jit(solution)/shard_map/eyj,xrjl->rxeyl/dot_general | solution.py:188
  99.3 3.0 %shard_map.74 = f32[1,32,64,128]{3,2,1,0:T(8,128)} custom-call(f32[32,2,64,128]{3,2,1,0:T(8,128)} %add_bitcast_fusion.in_ref), custom_call_target="tpu_custom_call" | custom-call | flops 786432 | bytes 3145728 | tf_op jit(solution)/shard_map/pallas_call | solution.py:42
  102.3 1.9 %convolution_multiply_fusion = f32[32,64,64]{2,1,0:T(8,128)S(1)} fusion(f32[1,32,64,128]{3,2,1,0:T(8,128)} %shard_map.74, f32[64,64]{0,1:T(8,128)S(1)} %get-tuple-element.12, f32[64,64]{0,1:T(8,128)S(1)} %get-tuple-element.13), kind=kOutput, calls=%fused_computation.17 | convolution fusion | flops 100802560 | bytes 1605632 | tf_op jit(solution)/shard_map/rxyl,lz->rxyz/dot_general | solution.py:199
  105.3 1.6 %gather_fusion = f32[8,512]{1,0:T(8,128)S(1)} fusion(f32[256,512]{1,0:T(8,128)} %reshape.309, s32[1024]{0:T(1024)S(1)} %pad_clamp_fusion), kind=kCustom, calls=%fused_computation | custom fusion | bytes 32800 | tf_op jit(solution)/shard_map/gather | solution.py:206
  106.9 1.6 %fusion.75 = f32[8,512]{1,0:T(8,128)S(1)} fusion(f32[8,512]{1,0:T(8,128)S(1)} %gather_fusion, f32[512,512]{1,0:T(8,128)} %param.9), kind=kOutput, calls=%fused_computation.130 | convolution fusion | flops 12582912 | bytes 1081344 | tf_op jit(solution)/shard_map/dot_general | solution.py:215
  108.7 9.6 %all_to_all.5 = f32[8,2,512]{2,1,0:T(2,128)S(1)} all-to-all(f32[8,2,512]{2,1,0:T(2,128)S(1)} %reshape.311), channel_id=1, replica_groups=mesh['grp'=2,'rot'=4,'sub'=2,'ref'=2] {'rot','ref'}, dimensions={0} | all-to-all | bytes 65536 | tf_op jit(solution)/shard_map/all_to_all | solution.py:217
  (56 shorter events, 13.3 us)
Async XLA Ops:
  0.6 1.6 %copy-start = (f32[2,4,16,32,64]{4,3,2,1,0:T(8,128)S(1)}, f32[2,4,16,32,64]{4,3,2,1,0:T(8,128)}, u32[]{:S(2)}) copy-start(f32[2,4,16,32,64]{4,3,2,1,0:T(8,128)} %param.6) | copy-start | bytes 3145732
  3.3 38.5 %collective-permute-start.2 = (bf16[4,16,16,128]{3,1,2,0:T(8,128)(2,1)}, bf16[4,16,16,128]{3,1,2,0:T(8,128)(2,1)S(1)}, u32[]{:S(2)}, u32[]{:S(2)}) collective-permute-start(bf16[4,16,16,128]{3,1,2,0:T(8,128)(2,1)} %fusion.74), channel_id=1, source_target_pairs={{0,12},{4,0},{8,4},{12,8},{1,13},{5,1},{9,5},{13,9},{2,14},{6,2},{... | collective-permute-start | bytes 786440 | tf_op jit(solution)/shard_map/ppermute | solution.py:62
  8.3 33.5 %collective-permute-start.3 = (bf16[4,16,16,128]{3,1,2,0:T(8,128)(2,1)}, bf16[4,16,16,128]{3,1,2,0:T(8,128)(2,1)S(1)}, u32[]{:S(2)}, u32[]{:S(2)}) collective-permute-start(bf16[4,16,16,128]{3,1,2,0:T(8,128)(2,1)} %fusion.74), channel_id=1, source_target_pairs={{0,8},{4,12},{8,0},{12,4},{1,9},{5,13},{9,1},{13,5},{2,10},{6,14},... | collective-permute-start | bytes 786440 | tf_op jit(solution)/shard_map/ppermute | solution.py:62
  8.3 33.5 %collective-permute-start.4 = (bf16[4,16,16,128]{3,1,2,0:T(8,128)(2,1)}, bf16[4,16,16,128]{3,1,2,0:T(8,128)(2,1)S(1)}, u32[]{:S(2)}, u32[]{:S(2)}) collective-permute-start(bf16[4,16,16,128]{3,1,2,0:T(8,128)(2,1)} %fusion.74), channel_id=1, source_target_pairs={{0,4},{4,8},{8,12},{12,0},{1,5},{5,9},{9,13},{13,1},{2,6},{6,10},{... | collective-permute-start | bytes 786440 | tf_op jit(solution)/shard_map/ppermute | solution.py:62
  21.0 25.7 %collective-permute-start = (bf16[1,2,32,32,128]{4,2,3,1,0:T(8,128)(2,1)}, bf16[1,2,32,32,128]{4,2,3,1,0:T(8,128)(2,1)S(1)}, u32[]{:S(2)}, u32[]{:S(2)}) collective-permute-start(bf16[1,2,32,32,128]{4,2,3,1,0:T(8,128)(2,1)} %bitcast.192), channel_id=1, source_target_pairs={{0,2},{2,0},{1,3},{3,1},{4,6},{6,4},{5,7},{7,5},{8,10},{10,8},{9,1... | collective-permute-start | bytes 1572872 | tf_op jit(solution)/shard_map/ppermute | solution.py:74
  33.9 21.6 %collective-permute-start.1 = (bf16[1,2,32,32,128]{4,2,3,1,0:T(8,128)(2,1)}, bf16[1,2,32,32,128]{4,2,3,1,0:T(8,128)(2,1)S(1)}, u32[]{:S(2)}, u32[]{:S(2)}) collective-permute-start(bf16[1,2,32,32,128]{4,2,3,1,0:T(8,128)(2,1)} %bitcast.191), channel_id=1, source_target_pairs={{0,2},{2,0},{1,3},{3,1},{4,6},{6,4},{5,7},{7,5},{8,10},{10,8},{9,1... | collective-permute-start | bytes 1572872 | tf_op jit(solution)/shard_map/ppermute | solution.py:74
  35.2 3.3 %copy-start.5 = (f32[2,64,1,32]{1,3,0,2:T(8,128)}, f32[2,64,1,32]{1,3,0,2:T(8,128)S(1)}, u32[]{:S(2)}) copy-start(f32[2,64,1,32]{1,3,0,2:T(8,128)S(1)} %get-tuple-element.9) | copy-start | bytes 49156
  38.5 3.2 %copy-start.7 = (s32[1,1,1,8]{3,2,1,0:T(1,128)S(1)}, s32[1,1,1,8]{3,2,1,0:T(1,128)}, u32[]{:S(2)}) copy-start(s32[1,1,1,8]{3,2,1,0:T(1,128)} %param.7) | copy-start | bytes 100
  42.1 2.9 %copy-start.8 = (s32[1,1,1,8,1]{3,4,2,1,0:T(1,128)S(1)}, s32[1,1,1,8,1]{3,4,2,1,0:T(1,128)}, u32[]{:S(2)}) copy-start(s32[1,1,1,8,1]{3,4,2,1,0:T(1,128)} %param.8) | copy-start | bytes 100
  42.4 1.4 %copy-start.3 = (bf16[8,4,16,16,128]{4,2,3,1,0:T(8,128)(2,1)}, bf16[8,4,16,16,128]{4,2,3,1,0:T(8,128)(2,1)S(1)}, u32[]{:S(2)}) copy-start(bf16[8,4,16,16,128]{4,2,3,1,0:T(8,128)(2,1)S(1)} %bitcast_dynamic-update-slice_fusion.1) | copy-start | bytes 6291460
  43.8 2.8 %copy-start.4 = (f32[2,64,1,32]{1,3,0,2:T(8,128)S(1)}, f32[2,64,1,32]{1,3,0,2:T(8,128)}, u32[]{:S(2)}) copy-start(f32[2,64,1,32]{1,3,0,2:T(8,128)} %get-tuple-element.8) | copy-start | bytes 49156
  45.0 19.3 %collective-permute-start.5 = (bf16[4,4,16,16,128]{4,2,3,1,0:T(8,128)(2,1)}, bf16[4,4,16,16,128]{4,2,3,1,0:T(8,128)(2,1)}, u32[]{:S(2)}, u32[]{:S(2)}) collective-permute-start(bf16[4,4,16,16,128]{4,2,3,1,0:T(8,128)(2,1)} %constant_dynamic-slice_fusion), channel_id=1, source_target_pairs={{0,1},{1,0},{2,3},{3,2},{4,5},{5,4},{6,7},{7,6},{8,9},{9,8},{10,11... | collective-permute-start | bytes 3145736 | tf_op jit(solution)/shard_map/ppermute | solution.py:62
  78.5 5.2 %copy-start.6 = (f32[2,64,1,32]{1,3,0,2:T(8,128)S(1)}, f32[2,64,1,32]{1,3,0,2:T(8,128)}, u32[]{:S(2)}) copy-start(f32[2,64,1,32]{1,3,0,2:T(8,128)} %copy-done.5) | copy-start | bytes 49156
  82.2 14.8 %collective-permute-start.6 = (f32[32,1,32,128]{3,2,0,1:T(8,128)S(1)}, f32[32,1,32,128]{3,2,0,1:T(8,128)S(1)}, u32[]{:S(2)}, u32[]{:S(2)}) collective-permute-start(f32[32,1,32,128]{3,2,0,1:T(8,128)S(1)} %dynamic-slice_bitcast_fusion), channel_id=1, source_target_pairs={{0,2},{2,0},{1,3},{3,1},{4,6},{6,4},{5,7},{7,5},{8,10},{10,8},{9,1... | collective-permute-start | bytes 1572872 | tf_op jit(solution)/shard_map/ppermute | solution.py:74
  99.3 19.7 %copy-start.1 = (f32[2,4,16,32,64]{4,3,2,1,0:T(8,128)S(1)}, f32[2,4,16,32,64]{4,3,2,1,0:T(8,128)}, u32[]{:S(2)}) copy-start(f32[2,4,16,32,64]{4,3,2,1,0:T(8,128)} %param.6) | copy-start | bytes 3145732
  104.2 14.7 %copy-start.2 = (f32[32,64,64]{2,1,0:T(8,128)}, f32[32,64,64]{2,1,0:T(8,128)S(1)}, u32[]{:S(2)}) copy-start(f32[32,64,64]{2,1,0:T(8,128)S(1)} %convolution_multiply_fusion) | copy-start | bytes 1572868

commit v7 on v6

--- a/solution.py
+++ b/solution.py
@@ -21,36 +21,41 @@
     return (jnp.cos(angles), jnp.sin(angles))
 
 
-def combine_kernel(in_ref, out_ref, *, first, second):
+def combine_kernel(me_ref, in_ref, out_ref, *, first, second):
     batch, _, rows, lanes = in_ref.shape
     split = out_ref.shape[0]
     part = rows // split
     half = lanes // 2
-    cos_part = in_ref[:, 0].reshape(batch * rows, lanes)
-    sin_part = in_ref[:, 1].reshape(batch * rows, lanes)
     low = lax.broadcasted_iota(jnp.int32, (1, lanes), 1) < half
     signs = jnp.where(low, first, second).astype(jnp.float32)
-    result = (cos_part + pltpu.roll(sin_part, half, 1) * signs).reshape(batch, rows, lanes)
+    me = me_ref[0]
     for piece in range(split):
-        out_ref[piece] = result[:, piece * part:(piece + 1) * part].astype(out_ref.dtype)
-
-
-def combine_call(stacked, first, second, split, dtype):
+        start = pl.multiple_of(((me + piece) % split) * part, 8)
+        cos_part = in_ref[:, 0, pl.ds(start, part), :].reshape(batch * part, lanes)
+        sin_part = in_ref[:, 1, pl.ds(start, part), :].reshape(batch * part, lanes)
+        result = cos_part + pltpu.roll(sin_part, half, 1) * signs
+        out_ref[piece] = result.reshape(batch, part, lanes).astype(out_ref.dtype)
+
+
+def combine_call(stacked, first, second, split, dtype, me=0):
     batch, _, rows, lanes = stacked.shape
     block = max(b for b in range(1, 33) if batch % b == 0)
     part = rows // split
     return pl.pallas_call(
         functools.partial(combine_kernel, first=first, second=second),
-        grid=(batch // block,),
-        in_specs=[pl.BlockSpec((block, 2, rows, lanes), lambda i: (i, 0, 0, 0))],
-        out_specs=pl.BlockSpec((split, block, part, lanes), lambda i: (0, i, 0, 0)),
+        grid_spec=pltpu.PrefetchScalarGridSpec(
+            num_scalar_prefetch=1,
+            grid=(batch // block,),
+            in_specs=[pl.BlockSpec((block, 2, rows, lanes), lambda i, me: (i, 0, 0, 0))],
+            out_specs=pl.BlockSpec((split, block, part, lanes), lambda i, me: (0, i, 0, 0)),
+        ),
         out_shape=jax.ShapeDtypeStruct((split, batch, part, lanes), dtype),
         cost_estimate=pl.CostEstimate(
             flops=3 * batch * rows * lanes,
             bytes_accessed=(8 + jnp.dtype(dtype).itemsize) * batch * rows * lanes,
             transcendentals=0,
         ),
-    )(stacked)
+    )(jnp.reshape(jnp.asarray(me, jnp.int32), (1,)), stacked)
 
 
 def gather_by_shifts(piece, axis):
@@ -64,14 +69,19 @@
     return lax.dynamic_slice_in_dim(doubled, (count - 1 - me) % count, count, axis=0)
 
 
-def exchange(sending, axis):
+def exchange(sending, axis, rotated=False):
     count = lax.axis_size(axis)
     me = lax.axis_index(axis)
-    pieces = [(me, lax.dynamic_index_in_dim(sending, me, axis=0, keepdims=False))]
+
+    def entry(shift):
+        if rotated:
+            return sending[shift]
+        return lax.dynamic_index_in_dim(sending, (me + shift) % count, axis=0, keepdims=False)
+
+    pieces = [(me, entry(0))]
     for shift in range(1, count):
-        piece = lax.dynamic_index_in_dim(sending, (me + shift) % count, axis=0, keepdims=False)
         pairs = [(k, (k + shift) % count) for k in range(count)]
-        pieces.append(((me - shift) % count, lax.ppermute(piece, axis, pairs)))
+        pieces.append(((me - shift) % count, lax.ppermute(entry(shift), axis, pairs)))
     return pieces
 
 
@@ -161,7 +171,8 @@
         along_z = jnp.einsum("rtxyz,zl->rtxyl", part, z_table, precision=highest)
         along_y = jnp.einsum("ejy,rtxyl->rtxejl", pair, along_z, precision=highest)
         sending = combine_call(
-            along_y.reshape(-1, 2, ny, 2 * length), 1.0, -1.0, n_sub, jnp.bfloat16
+            along_y.reshape(-1, 2, ny, 2 * length), 1.0, -1.0, n_sub, jnp.bfloat16,
+            lax.axis_index("sub"),
         ).reshape(n_sub, rots, part_terms, x_local, y_local, 2 * length)
         along_x = sum(
             jnp.einsum(
@@ -170,7 +181,7 @@
                 piece.astype(jnp.float32),
                 precision=highest,
             )
-            for source, piece in exchange(sending, "sub")
+            for source, piece in exchange(sending, "sub", rotated=True)
         )
         spectrum = combine_call(
             along_x.reshape(-1, 2, length, 2 * length), 1.0, -1.0, 1, jnp.bfloat16

time: 120 us -> 120 us (level)
    dynamic_slice x4 -> x0, local copies, waits for them, and re-layouts: 4.64 us -> none  [exchange(): lax.dynamic_index_in_dim(sending, (me + shift) % count, axis=0, keepdims=...]
    squeeze x1 -> x3, local copies, waits for them, and re-layouts: 1.08 us -> 3.94 us  [the longest x2 2.06 us: entry(): return sending[shift]]
    slice x0 -> x2, local copies, waits for them, and re-layouts: none -> 2.69 us  [entry(): return sending[shift]]
    dot_general x2, matrix products: 3.87 us -> 2.65 us  [local(): along_z = jnp.einsum('rtxyz,zl->rtxyl', part, z_table, precision=highest)]
    unnamed x25 -> x27, local copies, waits for them, and re-layouts: 3.82 us -> 3.83 us
  transfers between devices with their start and end apart: 7 -> 7, of which waited for: 1 -> 1; matrix products, arithmetic and copies ran while one was open for 34% -> 33% of each run, Pallas kernels for 11% -> 11%
where the time goes in v7:
time: 120 us; the launch traced here: 119 us
  matrix products  37.7 us (31%)
  Pallas kernels  23.9 us (20%)
  local copies, waits for them, and re-layouts  20.4 us (17%)
  waiting for transfers between devices  11.3 us (9%)
  blocking collectives  9.63 us (8%)
  starting transfers between devices  9.59 us (8%)
  other arithmetic  5.23 us (4%)
    pallas_call x6, Pallas kernels, combine_call(): pl.pallas_call(functools.partial(combine_kernel, first=first, second=seco...  19 us
    dot_general x4, matrix products, local(): jnp.einsum('ekx,rtxjl->rtjekl', table_for(pair_x, source), piece.astype(j...  17.4 us
    ppermute x3, waiting for transfers between devices, exchange(): lax.ppermute(entry(shift), axis, pairs)  11.3 us
    all_to_all x1, blocking collectives, local(): lax.all_to_all(packed, ('rot', 'ref'), split_axis=0, concat_axis=0, tiled...  9.63 us
    dot_general x2, matrix products, local(): along_y = jnp.einsum('ejy,rtxyl->rtxejl', pair, along_z, precision=highest)  7.45 us
    ppermute x4, starting transfers between devices, gather_by_shifts(): pieces.append(lax.ppermute(piece, axis, pairs))  6.06 us
    pallas_call x1, Pallas kernels, correlate(): pl.pallas_call(product_kernel, grid=(rots, rows // block), in_specs=[pl.B...  4.92 us
    dot_general x2, matrix products, local(): jnp.einsum('eyj,xrjl->rxeyl', table_for(pair_y, source), piece, precision...  4.42 us
  transfers between devices with their start and end apart: 7, of which 1 were waited for; matrix products, arithmetic and copies ran while one was open for 33% of the time, Pallas kernels for 11%

profile of v7, /device:TPU:0, one launch (start us, length us, event | category | flops | bytes accessed | tf_op | source)
XLA Modules:
  0.0 118.7 jit_solution(18336031149536757856)
XLA Ops:
  0.7 1.6 %copy-done = f32[2,4,16,32,64]{4,3,2,1,0:T(8,128)S(1)} copy-done((f32[2,4,16,32,64]{4,3,2,1,0:T(8,128)S(1)}, f32[2,4,16,32,64]{4,3,2,1,0:T(8,128)}, u32[]{:S(2)}) %copy-start) | copy-done | bytes 1048600
  3.3 5.0 %collective-permute-start.2 = (bf16[4,16,16,128]{3,1,2,0:T(8,128)(2,1)}, bf16[4,16,16,128]{3,1,2,0:T(8,128)(2,1)S(1)}, u32[]{:S(2)}, u32[]{:S(2)}) collective-permute-start(bf16[4,16,16,128]{3,1,2,0:T(8,128)(2,1)} %fusion.72), channel_id=1, source_target_pairs={{0,12},{4,0},{8,4},{12,8},{1,13},{5,1},{9,5},{13,9},{2,14},{6,2},{... | collective-permute-start | bytes 786440 | tf_op jit(solution)/shard_map/ppermute | solution.py:67
  9.6 1.9 %fusion.11 = f32[128,2,32,64]{0,3,2,1:T(8,128)S(1)} fusion(bf16[1,4,32,64,64]{4,3,2,1,0:T(8,128)(2,1)} %param.5, f32[64,64]{0,1:T(8,128)S(1)} %get-tuple-element.12, f32[64,64]{0,1:T(8,128)S(1)} %get-tuple-element.13), kind=kOutput, calls=%fused_computation.21 | convolution fusion | flops 201334784 | bytes 3178496 | tf_op jit(solution)/shard_map/rtxyz,zl->rtxyl/dot_general | solution.py:171
  11.6 3.7 %fusion.6 = f32[2,32,128,2,64]{2,4,3,1,0:T(8,128)} fusion(f32[128,2,32,64]{0,3,2,1:T(8,128)S(1)} %fusion.11, f32[1,64,64]{2,1,0:T(8,128)S(1)} %get-tuple-element.14, f32[1,64,64]{2,1,0:T(8,128)S(1)} %get-tuple-element.15), kind=kOutput, calls=%fused_computation.13 | convolution fusion | flops 402661376 | bytes 6324224 | tf_op jit(solution)/shard_map/ejy,rtxyl->rtxejl/dot_general | solution.py:172
  15.3 3.4 %shard_map.68 = bf16[2,64,32,128]{3,2,1,0:T(8,128)(2,1)} custom-call(s32[1]{0:T(128)} %bitcast.me_ref, f32[64,2,64,128]{3,2,1,0:T(8,128)} %bitcast.182), custom_call_target="tpu_custom_call" | custom-call | flops 1572864 | bytes 5242880 | tf_op jit(solution)/shard_map/pallas_call | solution.py:44
  18.7 1.4 %fusion.74 = (bf16[1,64,32,128]{3,2,1,0:T(8,128)(2,1)S(1)}, bf16[1,64,32,128]{3,2,1,0:T(8,128)(2,1)S(1)}) fusion(bf16[2,64,32,128]{3,2,1,0:T(8,128)(2,1)} %shard_map.68), kind=kLoop, calls=%fused_computation.123 | loop fusion | bytes 2097152 | tf_op jit(solution)/shard_map/slice | solution.py:78
  21.1 1.5 %collective-permute-start = (bf16[1,2,32,32,128]{4,2,3,1,0:T(8,128)(2,1)}, bf16[1,2,32,32,128]{4,2,3,1,0:T(8,128)(2,1)S(1)}, u32[]{:S(2)}, u32[]{:S(2)}) collective-permute-start(bf16[1,2,32,32,128]{4,2,3,1,0:T(8,128)(2,1)} %copy.14), channel_id=1, source_target_pairs={{0,2},{2,0},{1,3},{3,1},{4,6},{6,4},{5,7},{7,5},{8,10},{10,8},{9,1... | collective-permute-start | bytes 1572872 | tf_op jit(solution)/shard_map/ppermute | solution.py:84
  23.3 3.7 %fusion.4 = f32[2,32,128,2,64]{2,4,3,1,0:T(8,128)} fusion(f32[128,2,32,64]{0,3,2,1:T(8,128)S(1)} %fusion.9, f32[1,64,64]{2,1,0:T(8,128)S(1)} %get-tuple-element.14, f32[1,64,64]{2,1,0:T(8,128)S(1)} %get-tuple-element.15), kind=kOutput, calls=%fused_computation.11 | convolution fusion | flops 402661376 | bytes 6324224 | tf_op jit(solution)/shard_map/ejy,rtxyl->rtxejl/dot_general | solution.py:172
  27.0 3.4 %shard_map.70 = bf16[2,64,32,128]{3,2,1,0:T(8,128)(2,1)} custom-call(s32[1]{0:T(128)} %bitcast.me_ref, f32[64,2,64,128]{3,2,1,0:T(8,128)} %bitcast.183), custom_call_target="tpu_custom_call" | custom-call | flops 1572864 | bytes 5242880 | tf_op jit(solution)/shard_map/pallas_call | solution.py:44
  34.1 3.3 %fusion.22 = f32[2,32,128,2,64]{2,4,3,1,0:T(8,128)} fusion(bf16[2,32,32,128,1]{3,2,1,0,4:T(8,128)(2,1)S(1)} %bitcast.186, f32[2,64,1,32]{1,3,0,2:T(8,128)S(1)} %get-tuple-element.9), kind=kOutput, calls=%fused_computation.33 | convolution fusion | flops 201326592 | bytes 4734976 | tf_op jit(solution)/shard_map/ekx,rtxjl->rtjekl/dot_general | solution.py:178
  37.4 3.2 %fusion.20 = f32[2,32,128,2,64]{2,4,3,1,0:T(8,128)} fusion(bf16[2,32,32,128,1]{3,2,1,0,4:T(8,128)(2,1)S(1)} %bitcast.187, f32[2,64,1,32]{1,3,0,2:T(8,128)S(1)} %get-tuple-element.9), kind=kOutput, calls=%fused_computation.31 | convolution fusion | flops 201326592 | bytes 4734976 | tf_op jit(solution)/shard_map/ekx,rtxjl->rtjekl/dot_general | solution.py:178
  44.1 1.5 %fusion.80 = bf16[1,4,4,16,16,128]{5,3,4,2,1,0:T(8,128)(2,1)S(1)} fusion(bf16[8,4,16,16,128]{4,2,3,1,0:T(8,128)(2,1)} %copy-done.3, s32[]{:T(128)S(6)} %select_n.139), kind=kLoop, calls=%fused_computation.125 | loop fusion | bytes 2097156 | tf_op jit(solution)/shard_map/stack | solution.py:68
  45.6 5.5 %convolution_add_fusion.1 = f32[2,32,128,2,64]{2,4,3,1,0:T(8,128)} fusion(f32[2,32,128,2,64]{2,4,3,1,0:T(8,128)} %fusion.22, bf16[1,2,32,32,128]{4,2,3,1,0:T(8,128)(2,1)S(1)} %collective-permute-done, f32[2,64,1,32]{1,3,0,2:T(8,128)S(1)} %copy-done.5), kind=kOutput, calls=%fused_computation.6 | convolution fusion | flops 202375168 | bytes 8929280 | tf_op jit(solution)/shard_map/ekx,rtxjl->rtjekl/dot_general | solution.py:178
  51.0 3.4 %shard_map.69 = bf16[1,64,64,128]{3,2,1,0:T(8,128)(2,1)} custom-call(s32[1]{0:T(128)} %constant.80.clone.1.me_ref, f32[64,2,64,128]{3,2,1,0:T(8,128)} %bitcast.180), custom_call_target="tpu_custom_call" | custom-call | flops 1572864 | bytes 5242880 | tf_op jit(solution)/shard_map/pallas_call | solution.py:44
  54.4 5.4 %convolution_add_fusion = f32[2,32,128,2,64]{2,4,3,1,0:T(8,128)} fusion(f32[2,32,128,2,64]{2,4,3,1,0:T(8,128)} %fusion.20, bf16[1,2,32,32,128]{4,2,3,1,0:T(8,128)(2,1)S(1)} %collective-permute-done.1, f32[2,64,1,32]{1,3,0,2:T(8,128)S(1)} %copy-done.5), kind=kOutput, calls=%fused_computation.5 | convolution fusion | flops 202375168 | bytes 8929280 | tf_op jit(solution)/shard_map/ekx,rtxjl->rtjekl/dot_general | solution.py:178
  59.8 3.3 %shard_map.71 = bf16[1,64,64,128]{3,2,1,0:T(8,128)(2,1)} custom-call(s32[1]{0:T(128)} %constant.80.clone.1.me_ref, f32[64,2,64,128]{3,2,1,0:T(8,128)} %bitcast.181), custom_call_target="tpu_custom_call" | custom-call | flops 1572864 | bytes 5242880 | tf_op jit(solution)/shard_map/pallas_call | solution.py:44
  63.2 2.7 %fusion.3 = bf16[4,2,16,4,16,128]{5,2,4,0,3,1:T(8,128)(2,1)S(1)} fusion(s32[]{:T(128)S(6)} %select_n.141, bf16[1,4,4,16,16,128]{5,3,4,2,1,0:T(8,128)(2,1)} %bitcast.58, bf16[1,4,4,16,16,128]{5,3,4,2,1,0:T(8,128)(2,1)S(1)} %fusion.80), kind=kLoop, calls=%fused_computation.10 | loop fusion | flops 3145728 | bytes 4194308 | tf_op jit(solution)/shard_map/transpose | solution.py:105
  65.9 1.9 %copy.17 = bf16[4,2,16,4,16,128]{5,4,3,2,1,0:T(8,128)(2,1)} copy(bf16[4,2,16,4,16,128]{5,2,4,0,3,1:T(8,128)(2,1)S(1)} %fusion.3) | data formatting | bytes 4194304 | tf_op jit(solution)/shard_map/transpose | solution.py:105
  67.7 4.9 %shard_map.72 = f32[1,2048,128]{2,1,0:T(8,128)} custom-call(bf16[1,2,2048,128]{3,2,1,0:T(8,128)(2,1)} %bitcast.190, bf16[1,2,2048,128]{3,2,1,0:T(8,128)(2,1)} %bitcast.191, bf16[4,2048,128]{2,1,0:T(8,128)(2,1)} %bitcast.184), custom_call_target="tpu_custom_call" | custom-call | flops 8388608 | bytes 5242880 | tf_op jit(solution)/shard_map/pallas_call | solution.py:136
  72.7 2.2 %fusion.25 = f32[32,128,2,64]{1,3,2,0:T(8,128)S(1)} fusion(f32[32,64,128,1]{2,1,3,0:T(8,128)} %bitcast.188, f32[1,64,64]{2,1,0:T(8,128)S(1)} %get-tuple-element.14, f32[1,64,64]{2,1,0:T(8,128)S(1)} %get-tuple-element.15), kind=kOutput, calls=%fused_computation.52 | convolution fusion | flops 201334784 | bytes 3178496 | tf_op jit(solution)/shard_map/exk,rjkl->xrejl/dot_general | solution.py:194
  74.8 2.5 %copy.41 = f32[32,128,2,64]{1,0,2,3:T(8,128)} copy(f32[32,128,2,64]{1,3,2,0:T(8,128)S(1)} %fusion.25) | data formatting | bytes 4194304 | tf_op jit(solution)/shard_map/exk,rjkl->xrejl/dot_general | solution.py:194
  77.4 2.5 %shard_map.73 = f32[1,64,32,128]{3,2,1,0:T(8,128)} custom-call(s32[1]{0:T(128)} %constant.80.clone.1.me_ref, f32[64,2,32,128]{3,2,1,0:T(8,128)} %bitcast.185), custom_call_target="tpu_custom_call" | custom-call | flops 786432 | bytes 3145728 | tf_op jit(solution)/shard_map/pallas_call | solution.py:44
  79.9 1.9 %dynamic-slice_bitcast_fusion = f32[32,1,32,128]{3,2,0,1:T(8,128)} fusion(f32[2,32,1,32,128]{4,3,1,0,2:T(8,128)} %bitcast.192, s32[]{:T(128)S(6)} %select_n.145), kind=kLoop, calls=%fused_computation.35 | loop fusion | bytes 1048580 | tf_op jit(solution)/shard_map/jit(dynamic_index_in_dim)/squeeze | solution.py:79
  81.8 1.5 %collective-permute-start.6 = (f32[32,1,32,128]{3,2,0,1:T(8,128)}, f32[32,1,32,128]{3,2,0,1:T(8,128)S(1)}, u32[]{:S(2)}, u32[]{:S(2)}) collective-permute-start(f32[32,1,32,128]{3,2,0,1:T(8,128)} %dynamic-slice_bitcast_fusion), channel_id=1, source_target_pairs={{0,2},{2,0},{1,3},{3,1},{4,6},{6,4},{5,7},{7,5},{8,10},{10,8},{9,1... | collective-permute-start | bytes 1572872 | tf_op jit(solution)/shard_map/ppermute | solution.py:84
  83.3 2.1 %fusion.16 = f32[32,128,2,64]{1,3,2,0:T(8,128)S(1)} fusion(f32[2,32,1,32,128]{4,3,1,0,2:T(8,128)} %bitcast.193, s32[]{:T(128)S(6)} %select_n.143, f32[2,64,1,32]{1,3,0,2:T(8,128)S(1)} %copy-done.7), kind=kOutput, calls=%fused_computation.27 | convolution fusion | flops 100663296 | bytes 2637828 | tf_op jit(solution)/shard_map/eyj,xrjl->rxeyl/dot_general | solution.py:199
  85.4 11.3 %collective-permute-done.6 = f32[32,1,32,128]{3,2,0,1:T(8,128)S(1)} collective-permute-done((f32[32,1,32,128]{3,2,0,1:T(8,128)}, f32[32,1,32,128]{3,2,0,1:T(8,128)S(1)}, u32[]{:S(2)}, u32[]{:S(2)}) %collective-permute-start.6) | collective-permute-done | bytes 524320 | tf_op jit(solution)/shard_map/ppermute | solution.py:84
  96.7 2.4 %add_bitcast_fusion.in_ref = f32[32,2,64,128]{3,2,1,0:T(8,128)} fusion(f32[32,128,2,64]{1,3,2,0:T(8,128)S(1)} %fusion.16, f32[32,1,32,128]{3,2,0,1:T(8,128)S(1)} %collective-permute-done.6, f32[2,64,1,32]{1,3,0,2:T(8,128)S(1)} %copy-done.5), kind=kOutput, calls=%fused_computation.16 | convolution fusion | flops 101187584 | bytes 4734976 | tf_op jit(solution)/shard_map/eyj,xrjl->rxeyl/dot_general | solution.py:199
  99.0 3.0 %shard_map.74 = f32[1,32,64,128]{3,2,1,0:T(8,128)} custom-call(s32[1]{0:T(128)} %constant.80.clone.1.me_ref, f32[32,2,64,128]{3,2,1,0:T(8,128)} %add_bitcast_fusion.in_ref), custom_call_target="tpu_custom_call" | custom-call | flops 786432 | bytes 3145728 | tf_op jit(solution)/shard_map/pallas_call | solution.py:44
  102.1 1.9 %convolution_multiply_fusion = f32[32,64,64]{2,1,0:T(8,128)S(1)} fusion(f32[1,32,64,128]{3,2,1,0:T(8,128)} %shard_map.74, f32[64,64]{0,1:T(8,128)S(1)} %get-tuple-element.12, f32[64,64]{0,1:T(8,128)S(1)} %get-tuple-element.13), kind=kOutput, calls=%fused_computation.17 | convolution fusion | flops 100802560 | bytes 1605632 | tf_op jit(solution)/shard_map/rxyl,lz->rxyz/dot_general | solution.py:210
  105.1 1.6 %gather_fusion = f32[8,512]{1,0:T(8,128)S(1)} fusion(f32[256,512]{1,0:T(8,128)} %reshape.316, s32[1024]{0:T(1024)S(1)} %pad_clamp_fusion), kind=kCustom, calls=%fused_computation | custom fusion | bytes 32800 | tf_op jit(solution)/shard_map/gather | solution.py:217
  106.7 1.6 %fusion.75 = f32[8,512]{1,0:T(8,128)S(1)} fusion(f32[8,512]{1,0:T(8,128)S(1)} %gather_fusion, f32[512,512]{1,0:T(8,128)} %param.9), kind=kOutput, calls=%fused_computation.124 | convolution fusion | flops 12582912 | bytes 1081344 | tf_op jit(solution)/shard_map/dot_general | solution.py:226
  108.5 9.6 %all_to_all.5 = f32[8,2,512]{2,1,0:T(2,128)S(1)} all-to-all(f32[8,2,512]{2,1,0:T(2,128)S(1)} %reshape.318), channel_id=1, replica_groups=mesh['grp'=2,'rot'=4,'sub'=2,'ref'=2] {'rot','ref'}, dimensions={0} | all-to-all | bytes 65536 | tf_op jit(solution)/shard_map/all_to_all | solution.py:228
  (58 shorter events, 13.0 us)
Async XLA Ops:
  0.6 1.6 %copy-start = (f32[2,4,16,32,64]{4,3,2,1,0:T(8,128)S(1)}, f32[2,4,16,32,64]{4,3,2,1,0:T(8,128)}, u32[]{:S(2)}) copy-start(f32[2,4,16,32,64]{4,3,2,1,0:T(8,128)} %param.6) | copy-start | bytes 3145732
  3.3 37.4 %collective-permute-start.2 = (bf16[4,16,16,128]{3,1,2,0:T(8,128)(2,1)}, bf16[4,16,16,128]{3,1,2,0:T(8,128)(2,1)S(1)}, u32[]{:S(2)}, u32[]{:S(2)}) collective-permute-start(bf16[4,16,16,128]{3,1,2,0:T(8,128)(2,1)} %fusion.72), channel_id=1, source_target_pairs={{0,12},{4,0},{8,4},{12,8},{1,13},{5,1},{9,5},{13,9},{2,14},{6,2},{... | collective-permute-start | bytes 786440 | tf_op jit(solution)/shard_map/ppermute | solution.py:67
  8.3 32.4 %collective-permute-start.3 = (bf16[4,16,16,128]{3,1,2,0:T(8,128)(2,1)}, bf16[4,16,16,128]{3,1,2,0:T(8,128)(2,1)S(1)}, u32[]{:S(2)}, u32[]{:S(2)}) collective-permute-start(bf16[4,16,16,128]{3,1,2,0:T(8,128)(2,1)} %fusion.72), channel_id=1, source_target_pairs={{0,8},{4,12},{8,0},{12,4},{1,9},{5,13},{9,1},{13,5},{2,10},{6,14},... | collective-permute-start | bytes 786440 | tf_op jit(solution)/shard_map/ppermute | solution.py:67
  8.3 32.4 %collective-permute-start.4 = (bf16[4,16,16,128]{3,1,2,0:T(8,128)(2,1)}, bf16[4,16,16,128]{3,1,2,0:T(8,128)(2,1)S(1)}, u32[]{:S(2)}, u32[]{:S(2)}) collective-permute-start(bf16[4,16,16,128]{3,1,2,0:T(8,128)(2,1)} %fusion.72), channel_id=1, source_target_pairs={{0,4},{4,8},{8,12},{12,0},{1,5},{5,9},{9,13},{13,1},{2,6},{6,10},{... | collective-permute-start | bytes 786440 | tf_op jit(solution)/shard_map/ppermute | solution.py:67
  18.7 3.9 %copy-start.4 = (bf16[1,4,32,64,64]{4,3,2,1,0:T(8,128)(2,1)S(1)}, bf16[1,4,32,64,64]{4,3,2,1,0:T(8,128)(2,1)}, u32[]{:S(2)}) copy-start(bf16[1,4,32,64,64]{4,3,2,1,0:T(8,128)(2,1)} %param.5) | copy-start | bytes 3145732
  21.1 24.5 %collective-permute-start = (bf16[1,2,32,32,128]{4,2,3,1,0:T(8,128)(2,1)}, bf16[1,2,32,32,128]{4,2,3,1,0:T(8,128)(2,1)S(1)}, u32[]{:S(2)}, u32[]{:S(2)}) collective-permute-start(bf16[1,2,32,32,128]{4,2,3,1,0:T(8,128)(2,1)} %copy.14), channel_id=1, source_target_pairs={{0,2},{2,0},{1,3},{3,1},{4,6},{6,4},{5,7},{7,5},{8,10},{10,8},{9,1... | collective-permute-start | bytes 1572872 | tf_op jit(solution)/shard_map/ppermute | solution.py:84
  32.7 21.7 %collective-permute-start.1 = (bf16[1,2,32,32,128]{4,2,3,1,0:T(8,128)(2,1)}, bf16[1,2,32,32,128]{4,2,3,1,0:T(8,128)(2,1)S(1)}, u32[]{:S(2)}, u32[]{:S(2)}) collective-permute-start(bf16[1,2,32,32,128]{4,2,3,1,0:T(8,128)(2,1)} %copy.16), channel_id=1, source_target_pairs={{0,2},{2,0},{1,3},{3,1},{4,6},{6,4},{5,7},{7,5},{8,10},{10,8},{9,1... | collective-permute-start | bytes 1572872 | tf_op jit(solution)/shard_map/ppermute | solution.py:84
  34.1 3.3 %copy-start.6 = (f32[2,64,1,32]{1,3,0,2:T(8,128)}, f32[2,64,1,32]{1,3,0,2:T(8,128)S(1)}, u32[]{:S(2)}) copy-start(f32[2,64,1,32]{1,3,0,2:T(8,128)S(1)} %get-tuple-element.9) | copy-start | bytes 49156
  37.4 3.2 %copy-start.8 = (s32[1,1,1,8]{3,2,1,0:T(1,128)S(1)}, s32[1,1,1,8]{3,2,1,0:T(1,128)}, u32[]{:S(2)}) copy-start(s32[1,1,1,8]{3,2,1,0:T(1,128)} %param.7) | copy-start | bytes 100
  41.0 2.9 %copy-start.9 = (s32[1,1,1,8,1]{3,4,2,1,0:T(1,128)S(1)}, s32[1,1,1,8,1]{3,4,2,1,0:T(1,128)}, u32[]{:S(2)}) copy-start(s32[1,1,1,8,1]{3,4,2,1,0:T(1,128)} %param.8) | copy-start | bytes 100
  41.3 1.4 %copy-start.3 = (bf16[8,4,16,16,128]{4,2,3,1,0:T(8,128)(2,1)}, bf16[8,4,16,16,128]{4,2,3,1,0:T(8,128)(2,1)S(1)}, u32[]{:S(2)}) copy-start(bf16[8,4,16,16,128]{4,2,3,1,0:T(8,128)(2,1)S(1)} %bitcast_dynamic-update-slice_fusion.1) | copy-start | bytes 6291460
  42.7 2.8 %copy-start.5 = (f32[2,64,1,32]{1,3,0,2:T(8,128)S(1)}, f32[2,64,1,32]{1,3,0,2:T(8,128)}, u32[]{:S(2)}) copy-start(f32[2,64,1,32]{1,3,0,2:T(8,128)} %get-tuple-element.8) | copy-start | bytes 49156
  43.9 19.3 %collective-permute-start.5 = (bf16[4,4,16,16,128]{4,2,3,1,0:T(8,128)(2,1)}, bf16[4,4,16,16,128]{4,2,3,1,0:T(8,128)(2,1)}, u32[]{:S(2)}, u32[]{:S(2)}) collective-permute-start(bf16[4,4,16,16,128]{4,2,3,1,0:T(8,128)(2,1)} %constant_dynamic-slice_fusion), channel_id=1, source_target_pairs={{0,1},{1,0},{2,3},{3,2},{4,5},{5,4},{6,7},{7,6},{8,9},{9,8},{10,11... | collective-permute-start | bytes 3145736 | tf_op jit(solution)/shard_map/ppermute | solution.py:67
  77.4 5.9 %copy-start.7 = (f32[2,64,1,32]{1,3,0,2:T(8,128)S(1)}, f32[2,64,1,32]{1,3,0,2:T(8,128)}, u32[]{:S(2)}) copy-start(f32[2,64,1,32]{1,3,0,2:T(8,128)} %copy-done.6) | copy-start | bytes 49156
  81.8 14.9 %collective-permute-start.6 = (f32[32,1,32,128]{3,2,0,1:T(8,128)}, f32[32,1,32,128]{3,2,0,1:T(8,128)S(1)}, u32[]{:S(2)}, u32[]{:S(2)}) collective-permute-start(f32[32,1,32,128]{3,2,0,1:T(8,128)} %dynamic-slice_bitcast_fusion), channel_id=1, source_target_pairs={{0,2},{2,0},{1,3},{3,1},{4,6},{6,4},{5,7},{7,5},{8,10},{10,8},{9,1... | collective-permute-start | bytes 1572872 | tf_op jit(solution)/shard_map/ppermute | solution.py:84
  99.0 19.7 %copy-start.1 = (f32[2,4,16,32,64]{4,3,2,1,0:T(8,128)S(1)}, f32[2,4,16,32,64]{4,3,2,1,0:T(8,128)}, u32[]{:S(2)}) copy-start(f32[2,4,16,32,64]{4,3,2,1,0:T(8,128)} %param.6) | copy-start | bytes 3145732
  104.0 14.8 %copy-start.2 = (f32[32,64,64]{2,1,0:T(8,128)}, f32[32,64,64]{2,1,0:T(8,128)S(1)}, u32[]{:S(2)}) copy-start(f32[32,64,64]{2,1,0:T(8,128)S(1)} %convolution_multiply_fusion) | copy-start | bytes 1572868

commit v8 on v7

--- a/solution.py
+++ b/solution.py
@@ -85,11 +85,14 @@
     return pieces
 
 
-def table_for(tables, source):
-    chosen = tables[:, :, 0]
-    for index in range(1, tables.shape[2]):
-        chosen = jnp.where(source == index, tables[:, :, index], chosen)
-    return chosen
+def by_source(pieces):
+    ordered = []
+    for source in range(len(pieces)):
+        chosen = pieces[0][1]
+        for index, piece in pieces[1:]:
+            chosen = jnp.where(index == source, piece, chosen)
+        ordered.append(chosen)
+    return ordered
 
 
 def gather_receptor(receptor):
@@ -176,12 +179,10 @@
         ).reshape(n_sub, rots, part_terms, x_local, y_local, 2 * length)
         along_x = sum(
             jnp.einsum(
-                "ekx,rtxjl->rtjekl",
-                table_for(pair_x, source),
-                piece.astype(jnp.float32),
+                "ekx,rtxjl->rtjekl", pair_x[:, :, source], piece.astype(jnp.float32),
                 precision=highest,
             )
-            for source, piece in exchange(sending, "sub", rotated=True)
+            for source, piece in enumerate(by_source(exchange(sending, "sub", rotated=True)))
         )
         spectrum = combine_call(
             along_x.reshape(-1, 2, length, 2 * length), 1.0, -1.0, 1, jnp.bfloat16
@@ -196,13 +197,8 @@
     back_x = back_x.reshape(n_sub, x_local, rots, y_local, 2 * length)
     pair_y = pair.reshape(2, length, n_sub, y_local)
     back_y = sum(
-        jnp.einsum(
-            "eyj,xrjl->rxeyl",
-            table_for(pair_y, source),
-            piece,
-            precision=highest,
-        )
-        for source, piece in exchange(back_x, "sub")
+        jnp.einsum("eyj,xrjl->rxeyl", pair_y[:, :, source], piece, precision=highest)
+        for source, piece in enumerate(by_source(exchange(back_x, "sub")))
     )
     back_y = combine_call(back_y.reshape(-1, 2, ny, 2 * length), -1.0, 1.0, 1, jnp.float32)
     back_y = back_y.reshape(rots, x_local, ny, 2 * length)

time: 120 us -> 110 us (0.917)
  matrix products: 37.7 us -> 30.1 us
  local copies, waits for them, and re-layouts: 20.4 us -> 17.1 us
  waiting for transfers between devices: 11.3 us -> 13.1 us
    dot_general x6, matrix products: 21.9 us -> 14.2 us  [the longest x4 9.81 us: local(): jnp.einsum('ekx,rtxjl->rtjekl', pair_x[:, :, source], piece.astype(jnp.fl...]
    ppermute x3, waiting for transfers between devices: 11.3 us -> 13.1 us  [exchange(): lax.ppermute(entry(shift), axis, pairs)]
    unnamed x27 -> x29, local copies, waits for them, and re-layouts: 3.83 us -> 2.45 us
    another operation x1, local copies, waits for them, and re-layouts: 1.45 us -> 0.23 us  [gather_by_shifts(): doubled = jnp.stack(pieces[::-1] * 2)]
  transfers between devices with their start and end apart: 7 -> 7, of which waited for: 1 -> 2; matrix products, arithmetic and copies ran while one was open for 33% -> 25% of each run, Pallas kernels for 11% -> 12%
where the time goes in v8:
time: 110 us; the launch traced here: 109 us
  matrix products  30.1 us (27%)
  Pallas kernels  24 us (22%)
  local copies, waits for them, and re-layouts  17.1 us (16%)
  waiting for transfers between devices  13.1 us (12%)
  blocking collectives  9.63 us (9%)
  starting transfers between devices  9.57 us (9%)
  other arithmetic  4.63 us (4%)
    pallas_call x6, Pallas kernels, combine_call(): pl.pallas_call(functools.partial(combine_kernel, first=first, second=seco...  19 us
    ppermute x3, waiting for transfers between devices, exchange(): lax.ppermute(entry(shift), axis, pairs)  13.1 us
    dot_general x4, matrix products, local(): jnp.einsum('ekx,rtxjl->rtjekl', pair_x[:, :, source], piece.astype(jnp.fl...  9.81 us
    all_to_all x1, blocking collectives, local(): lax.all_to_all(packed, ('rot', 'ref'), split_axis=0, concat_axis=0, tiled...  9.63 us
    dot_general x2, matrix products, local(): along_y = jnp.einsum('ejy,rtxyl->rtxejl', pair, along_z, precision=highest)  7.45 us
    ppermute x4, starting transfers between devices, gather_by_shifts(): pieces.append(lax.ppermute(piece, axis, pairs))  6.06 us
    pallas_call x1, Pallas kernels, correlate(): pl.pallas_call(product_kernel, grid=(rots, rows // block), in_specs=[pl.B...  4.94 us
    dot_general x2, matrix products, local(): jnp.einsum('eyj,xrjl->rxeyl', pair_y[:, :, source], piece, precision=high...  4.42 us
  transfers between devices with their start and end apart: 7, of which 2 were waited for; matrix products, arithmetic and copies ran while one was open for 25% of the time, Pallas kernels for 12%

profile of v8, /device:TPU:0, one launch (start us, length us, event | category | flops | bytes accessed | tf_op | source)
XLA Modules:
  0.0 109.1 jit_solution(10142079045263271986)
XLA Ops:
  0.7 1.6 %copy-done = f32[2,4,16,32,64]{4,3,2,1,0:T(8,128)S(1)} copy-done((f32[2,4,16,32,64]{4,3,2,1,0:T(8,128)S(1)}, f32[2,4,16,32,64]{4,3,2,1,0:T(8,128)}, u32[]{:S(2)}) %copy-start) | copy-done | bytes 1048600
  3.3 5.0 %collective-permute-start.2 = (bf16[4,16,16,128]{3,1,2,0:T(8,128)(2,1)}, bf16[4,16,16,128]{3,1,2,0:T(8,128)(2,1)S(1)}, u32[]{:S(2)}, u32[]{:S(2)}) collective-permute-start(bf16[4,16,16,128]{3,1,2,0:T(8,128)(2,1)} %fusion.91), channel_id=1, source_target_pairs={{0,12},{4,0},{8,4},{12,8},{1,13},{5,1},{9,5},{13,9},{2,14},{6,2},{... | collective-permute-start | bytes 786440 | tf_op jit(solution)/shard_map/ppermute | solution.py:67
  9.7 2.0 %fusion.11 = f32[128,2,32,64]{0,3,2,1:T(8,128)S(1)} fusion(bf16[1,4,32,64,64]{4,3,2,1,0:T(8,128)(2,1)} %param.5, f32[64,64]{0,1:T(8,128)S(1)} %get-tuple-element.10, f32[64,64]{0,1:T(8,128)S(1)} %get-tuple-element.11), kind=kOutput, calls=%fused_computation.21 | convolution fusion | flops 201334784 | bytes 3178496 | tf_op jit(solution)/shard_map/rtxyz,zl->rtxyl/dot_general | solution.py:174
  11.6 3.7 %fusion.6 = f32[2,32,128,2,64]{2,4,3,1,0:T(8,128)} fusion(f32[128,2,32,64]{0,3,2,1:T(8,128)S(1)} %fusion.11, f32[1,64,64]{2,1,0:T(8,128)S(1)} %get-tuple-element.12, f32[1,64,64]{2,1,0:T(8,128)S(1)} %get-tuple-element.13), kind=kOutput, calls=%fused_computation.13 | convolution fusion | flops 402661376 | bytes 6324224 | tf_op jit(solution)/shard_map/ejy,rtxyl->rtxejl/dot_general | solution.py:175
  15.3 3.4 %shard_map.68 = bf16[2,64,32,128]{3,2,1,0:T(8,128)(2,1)} custom-call(s32[1]{0:T(128)} %bitcast.me_ref, f32[64,2,64,128]{3,2,1,0:T(8,128)} %bitcast.198), custom_call_target="tpu_custom_call" | custom-call | flops 1572864 | bytes 5242880 | tf_op jit(solution)/shard_map/pallas_call | solution.py:44
  18.7 1.4 %fusion.93 = (bf16[1,64,32,128]{3,2,1,0:T(8,128)(2,1)S(1)}, bf16[1,64,32,128]{3,2,1,0:T(8,128)(2,1)S(1)}) fusion(bf16[2,64,32,128]{3,2,1,0:T(8,128)(2,1)} %shard_map.68), kind=kLoop, calls=%fused_computation.139 | loop fusion | bytes 2097152 | tf_op jit(solution)/shard_map/slice | solution.py:78
  21.1 1.5 %collective-permute-start = (bf16[1,2,32,32,128]{4,2,3,1,0:T(8,128)(2,1)}, bf16[1,2,32,32,128]{4,2,3,1,0:T(8,128)(2,1)S(1)}, u32[]{:S(2)}, u32[]{:S(2)}) collective-permute-start(bf16[1,2,32,32,128]{4,2,3,1,0:T(8,128)(2,1)} %copy.15), channel_id=1, source_target_pairs={{0,2},{2,0},{1,3},{3,1},{4,6},{6,4},{5,7},{7,5},{8,10},{10,8},{9,1... | collective-permute-start | bytes 1572872 | tf_op jit(solution)/shard_map/ppermute | solution.py:84
  23.4 3.7 %fusion.4 = f32[2,32,128,2,64]{2,4,3,1,0:T(8,128)} fusion(f32[128,2,32,64]{0,3,2,1:T(8,128)S(1)} %fusion.9, f32[1,64,64]{2,1,0:T(8,128)S(1)} %get-tuple-element.12, f32[1,64,64]{2,1,0:T(8,128)S(1)} %get-tuple-element.13), kind=kOutput, calls=%fused_computation.11 | convolution fusion | flops 402661376 | bytes 6324224 | tf_op jit(solution)/shard_map/ejy,rtxyl->rtxejl/dot_general | solution.py:175
  27.1 3.4 %shard_map.70 = bf16[2,64,32,128]{3,2,1,0:T(8,128)(2,1)} custom-call(s32[1]{0:T(128)} %bitcast.me_ref, f32[64,2,64,128]{3,2,1,0:T(8,128)} %bitcast.199), custom_call_target="tpu_custom_call" | custom-call | flops 1572864 | bytes 5242880 | tf_op jit(solution)/shard_map/pallas_call | solution.py:44
  30.4 1.3 %fusion.92 = (bf16[1,64,32,128]{3,2,1,0:T(8,128)(2,1)S(1)}, bf16[1,64,32,128]{3,2,1,0:T(8,128)(2,1)S(1)}) fusion(bf16[2,64,32,128]{3,2,1,0:T(8,128)(2,1)} %shard_map.70), kind=kLoop, calls=%fused_computation.138 | loop fusion | bytes 2097152 | tf_op jit(solution)/shard_map/slice | solution.py:78
  35.6 1.3 %fusion.21 = f32[2,32,128,2,64]{2,4,3,1,0:T(8,128)S(1)} fusion(bf16[1,2,32,32,128]{4,2,3,1,0:T(8,128)(2,1)S(1)} %collective-permute-done, pred[]{:T(512)S(6)} %eq.47, bf16[1,2,32,32,128]{4,3,2,1,0:T(8,128)(2,1)S(1)} %bitcast.200, f32[1,64,2,32]{1,3,0,2:T(8,128)S(1)} %get-tuple-element.9, f32[1,64,2,32]{1,3,0,2:T(8,128)S(1)} %get-tuple-element.8), kind=kOutput, calls=%fused_computation.32 | convolution fusion | flops 201592832 | bytes 5275649 | tf_op jit(solution)/shard_map/ekx,rtxjl->rtjekl/dot_general | solution.py:181
  36.9 3.6 %convolution_add_fusion.1 = f32[2,32,128,2,64]{2,4,3,1,0:T(8,128)} fusion(f32[2,32,128,2,64]{2,4,3,1,0:T(8,128)S(1)} %fusion.21, bf16[1,2,32,32,128]{4,2,3,1,0:T(8,128)(2,1)S(1)} %collective-permute-done, pred[]{:T(512)S(6)} %eq.46, bf16[1,2,32,32,128]{4,3,2,1,0:T(8,128)(2,1)S(1)} %bitcast.201, f32[1,64,2,32]{1,3,0,2:T(8,128)S(1)} %get-tuple-element.8, ...), kind=kOutput, calls=%fused_computation.6 | convolution fusion | flops 202641408 | bytes 9469953 | tf_op jit(solution)/shard_map/ekx,rtxjl->rtjekl/dot_general | solution.py:181
  40.5 3.4 %shard_map.69 = bf16[1,64,64,128]{3,2,1,0:T(8,128)(2,1)} custom-call(s32[1]{0:T(128)} %constant.80.clone.1.me_ref, f32[64,2,64,128]{3,2,1,0:T(8,128)} %bitcast.196), custom_call_target="tpu_custom_call" | custom-call | flops 1572864 | bytes 5242880 | tf_op jit(solution)/shard_map/pallas_call | solution.py:44
  43.9 1.6 %collective-permute-done.1 = bf16[1,2,32,32,128]{4,2,3,1,0:T(8,128)(2,1)S(1)} collective-permute-done((bf16[1,2,32,32,128]{4,2,3,1,0:T(8,128)(2,1)}, bf16[1,2,32,32,128]{4,2,3,1,0:T(8,128)(2,1)S(1)}, u32[]{:S(2)}, u32[]{:S(2)}) %collective-permute-start.1) | collective-permute-done | bytes 524320 | tf_op jit(solution)/shard_map/ppermute | solution.py:84
  45.5 1.3 %fusion.18 = f32[2,32,128,2,64]{2,4,3,1,0:T(8,128)S(1)} fusion(bf16[1,2,32,32,128]{4,2,3,1,0:T(8,128)(2,1)S(1)} %collective-permute-done.1, pred[]{:T(512)S(6)} %eq.47, bf16[1,2,32,32,128]{4,3,2,1,0:T(8,128)(2,1)S(1)} %bitcast.202, f32[1,64,2,32]{1,3,0,2:T(8,128)S(1)} %get-tuple-element.9, f32[1,64,2,32]{1,3,0,2:T(8,128)S(1)} %get-tuple-element.8), kind=kOutput, calls=%fused_computation.29 | convolution fusion | flops 201592832 | bytes 5275649 | tf_op jit(solution)/shard_map/ekx,rtxjl->rtjekl/dot_general | solution.py:181
  46.8 3.6 %convolution_add_fusion = f32[2,32,128,2,64]{2,4,3,1,0:T(8,128)} fusion(f32[2,32,128,2,64]{2,4,3,1,0:T(8,128)S(1)} %fusion.18, bf16[1,2,32,32,128]{4,2,3,1,0:T(8,128)(2,1)S(1)} %collective-permute-done.1, pred[]{:T(512)S(6)} %eq.46, bf16[1,2,32,32,128]{4,3,2,1,0:T(8,128)(2,1)S(1)} %bitcast.203, f32[1,64,2,32]{1,3,0,2:T(8,128)S(1)} %get-tuple-element.8, ...), kind=kOutput, calls=%fused_computation.5 | convolution fusion | flops 202641408 | bytes 9469953 | tf_op jit(solution)/shard_map/ekx,rtxjl->rtjekl/dot_general | solution.py:181
  50.4 3.4 %shard_map.71 = bf16[1,64,64,128]{3,2,1,0:T(8,128)(2,1)} custom-call(s32[1]{0:T(128)} %constant.80.clone.1.me_ref, f32[64,2,64,128]{3,2,1,0:T(8,128)} %bitcast.197), custom_call_target="tpu_custom_call" | custom-call | flops 1572864 | bytes 5242880 | tf_op jit(solution)/shard_map/pallas_call | solution.py:44
  53.8 2.7 %fusion.3 = bf16[4,2,16,4,16,128]{5,2,4,0,3,1:T(8,128)(2,1)S(1)} fusion(s32[]{:T(128)S(6)} %select_n.146, bf16[1,4,4,16,16,128]{5,3,4,2,1,0:T(8,128)(2,1)} %bitcast.62, bf16[1,4,4,16,16,128]{5,3,4,2,1,0:T(8,128)(2,1)S(1)} %fusion.99), kind=kLoop, calls=%fused_computation.10 | loop fusion | flops 3145728 | bytes 4194308 | tf_op jit(solution)/shard_map/transpose | solution.py:108
  56.4 1.9 %copy.21 = bf16[4,2,16,4,16,128]{5,4,3,2,1,0:T(8,128)(2,1)} copy(bf16[4,2,16,4,16,128]{5,2,4,0,3,1:T(8,128)(2,1)S(1)} %fusion.3) | data formatting | bytes 4194304 | tf_op jit(solution)/shard_map/transpose | solution.py:108
  58.3 4.9 %shard_map.72 = f32[1,2048,128]{2,1,0:T(8,128)} custom-call(bf16[1,2,2048,128]{3,2,1,0:T(8,128)(2,1)} %bitcast.210, bf16[1,2,2048,128]{3,2,1,0:T(8,128)(2,1)} %bitcast.212, bf16[4,2048,128]{2,1,0:T(8,128)(2,1)} %bitcast.204), custom_call_target="tpu_custom_call" | custom-call | flops 8388608 | bytes 5242880 | tf_op jit(solution)/shard_map/pallas_call | solution.py:139
  63.3 2.2 %fusion.40 = f32[32,128,2,64]{1,3,2,0:T(8,128)S(1)} fusion(f32[32,64,128,1]{2,1,3,0:T(8,128)} %bitcast.209, f32[1,64,64]{2,1,0:T(8,128)S(1)} %copy-done.6, f32[1,64,64]{2,1,0:T(8,128)S(1)} %copy-done.8), kind=kOutput, calls=%fused_computation.69 | convolution fusion | flops 201334784 | bytes 3178496 | tf_op jit(solution)/shard_map/exk,rjkl->xrejl/dot_general | solution.py:195
  65.5 2.5 %copy.53 = f32[32,128,2,64]{1,0,2,3:T(8,128)} copy(f32[32,128,2,64]{1,3,2,0:T(8,128)S(1)} %fusion.40) | data formatting | bytes 4194304 | tf_op jit(solution)/shard_map/exk,rjkl->xrejl/dot_general | solution.py:195
  68.0 2.6 %shard_map.73 = f32[1,64,32,128]{3,2,1,0:T(8,128)} custom-call(s32[1]{0:T(128)} %constant.80.clone.1.me_ref, f32[64,2,32,128]{3,2,1,0:T(8,128)} %bitcast.205), custom_call_target="tpu_custom_call" | custom-call | flops 786432 | bytes 3145728 | tf_op jit(solution)/shard_map/pallas_call | solution.py:44
  71.7 1.5 %collective-permute-start.6 = (f32[32,1,32,128]{3,2,0,1:T(8,128)S(1)}, f32[32,1,32,128]{3,2,0,1:T(8,128)S(1)}, u32[]{:S(2)}, u32[]{:S(2)}) collective-permute-start(f32[32,1,32,128]{3,2,0,1:T(8,128)S(1)} %dynamic-slice_bitcast_fusion), channel_id=1, source_target_pairs={{0,2},{2,0},{1,3},{3,1},{4,6},{6,4},{5,7},{7,5},{8,10},{10,8},{9,1... | collective-permute-start | bytes 1572872 | tf_op jit(solution)/shard_map/ppermute | solution.py:84
  73.4 11.5 %collective-permute-done.6 = f32[32,1,32,128]{3,2,0,1:T(8,128)S(1)} collective-permute-done((f32[32,1,32,128]{3,2,0,1:T(8,128)S(1)}, f32[32,1,32,128]{3,2,0,1:T(8,128)S(1)}, u32[]{:S(2)}, u32[]{:S(2)}) %collective-permute-start.6) | collective-permute-done | bytes 524320 | tf_op jit(solution)/shard_map/ppermute | solution.py:84
  84.9 2.1 %fusion.15 = f32[32,128,2,64]{1,3,2,0:T(8,128)S(1)} fusion(f32[32,1,32,128]{3,2,0,1:T(8,128)S(1)} %collective-permute-done.6, f32[2,32,1,32,128]{4,3,1,0,2:T(8,128)} %bitcast.207, s32[]{:T(128)S(6)} %select_n.150, pred[]{:T(512)S(6)} %eq.47, f32[1,64,2,32]{1,3,0,2:T(8,128)S(1)} %get-tuple-element.9, f32[1,64,2,32]{1,3,0,2:T(8,128)S(1)} %get-tuple-element.8), kind=kOutput, calls=%fused_computation.26 | convolution fusion | flops 100798464 | bytes 3178501 | tf_op jit(solution)/shard_map/eyj,xrjl->rxeyl/dot_general | solution.py:200
  87.0 2.4 %add_bitcast_fusion.in_ref = f32[32,2,64,128]{3,2,1,0:T(8,128)} fusion(f32[32,128,2,64]{1,3,2,0:T(8,128)S(1)} %fusion.15, f32[32,1,32,128]{3,2,0,1:T(8,128)S(1)} %collective-permute-done.6, f32[2,32,1,32,128]{4,3,1,0,2:T(8,128)S(1)} %bitcast.208, s32[]{:T(128)S(6)} %select_n.150, pred[]{:T(512)S(6)} %eq.46, f32[1,64,2,32]{1,3,0,2:T(8,128)S(1)} %get-tuple-element.8, ...), kind=kOutput, calls=%fused_computation.16 | convolution fusion | flops 101322752 | bytes 5308421 | tf_op jit(solution)/shard_map/eyj,xrjl->rxeyl/dot_general | solution.py:200
  89.4 3.0 %shard_map.74 = f32[1,32,64,128]{3,2,1,0:T(8,128)} custom-call(s32[1]{0:T(128)} %constant.80.clone.1.me_ref, f32[32,2,64,128]{3,2,1,0:T(8,128)} %add_bitcast_fusion.in_ref), custom_call_target="tpu_custom_call" | custom-call | flops 786432 | bytes 3145728 | tf_op jit(solution)/shard_map/pallas_call | solution.py:44
  92.4 1.9 %convolution_multiply_fusion = f32[32,64,64]{2,1,0:T(8,128)S(1)} fusion(f32[1,32,64,128]{3,2,1,0:T(8,128)} %shard_map.74, f32[64,64]{0,1:T(8,128)S(1)} %get-tuple-element.10, f32[64,64]{0,1:T(8,128)S(1)} %get-tuple-element.11), kind=kOutput, calls=%fused_computation.17 | convolution fusion | flops 100802560 | bytes 1605632 | tf_op jit(solution)/shard_map/rxyl,lz->rxyz/dot_general | solution.py:206
  95.5 1.6 %gather_fusion = f32[8,512]{1,0:T(8,128)S(1)} fusion(f32[256,512]{1,0:T(8,128)} %reshape.307, s32[1024]{0:T(1024)S(1)} %pad_clamp_fusion), kind=kCustom, calls=%fused_computation | custom fusion | bytes 32800 | tf_op jit(solution)/shard_map/gather | solution.py:213
  97.1 1.6 %fusion.94 = f32[8,512]{1,0:T(8,128)S(1)} fusion(f32[8,512]{1,0:T(8,128)S(1)} %gather_fusion, f32[512,512]{1,0:T(8,128)} %param.9), kind=kOutput, calls=%fused_computation.140 | convolution fusion | flops 12582912 | bytes 1081344 | tf_op jit(solution)/shard_map/dot_general | solution.py:222
  98.8 9.6 %all_to_all.5 = f32[8,2,512]{2,1,0:T(2,128)S(1)} all-to-all(f32[8,2,512]{2,1,0:T(2,128)S(1)} %reshape.309), channel_id=1, replica_groups=mesh['grp'=2,'rot'=4,'sub'=2,'ref'=2] {'rot','ref'}, dimensions={0} | all-to-all | bytes 65536 | tf_op jit(solution)/shard_map/all_to_all | solution.py:224
  (59 shorter events, 11.1 us)
Async XLA Ops:
  0.6 1.6 %copy-start = (f32[2,4,16,32,64]{4,3,2,1,0:T(8,128)S(1)}, f32[2,4,16,32,64]{4,3,2,1,0:T(8,128)}, u32[]{:S(2)}) copy-start(f32[2,4,16,32,64]{4,3,2,1,0:T(8,128)} %param.6) | copy-start | bytes 3145732
  3.3 30.3 %collective-permute-start.2 = (bf16[4,16,16,128]{3,1,2,0:T(8,128)(2,1)}, bf16[4,16,16,128]{3,1,2,0:T(8,128)(2,1)S(1)}, u32[]{:S(2)}, u32[]{:S(2)}) collective-permute-start(bf16[4,16,16,128]{3,1,2,0:T(8,128)(2,1)} %fusion.91), channel_id=1, source_target_pairs={{0,12},{4,0},{8,4},{12,8},{1,13},{5,1},{9,5},{13,9},{2,14},{6,2},{... | collective-permute-start | bytes 786440 | tf_op jit(solution)/shard_map/ppermute | solution.py:67
  8.3 25.3 %collective-permute-start.3 = (bf16[4,16,16,128]{3,1,2,0:T(8,128)(2,1)}, bf16[4,16,16,128]{3,1,2,0:T(8,128)(2,1)S(1)}, u32[]{:S(2)}, u32[]{:S(2)}) collective-permute-start(bf16[4,16,16,128]{3,1,2,0:T(8,128)(2,1)} %fusion.91), channel_id=1, source_target_pairs={{0,8},{4,12},{8,0},{12,4},{1,9},{5,13},{9,1},{13,5},{2,10},{6,14},... | collective-permute-start | bytes 786440 | tf_op jit(solution)/shard_map/ppermute | solution.py:67
  8.3 25.3 %collective-permute-start.4 = (bf16[4,16,16,128]{3,1,2,0:T(8,128)(2,1)}, bf16[4,16,16,128]{3,1,2,0:T(8,128)(2,1)S(1)}, u32[]{:S(2)}, u32[]{:S(2)}) collective-permute-start(bf16[4,16,16,128]{3,1,2,0:T(8,128)(2,1)} %fusion.91), channel_id=1, source_target_pairs={{0,4},{4,8},{8,12},{12,0},{1,5},{5,9},{9,13},{13,1},{2,6},{6,10},{... | collective-permute-start | bytes 786440 | tf_op jit(solution)/shard_map/ppermute | solution.py:67
  9.6 13.7 %copy-start.5 = (f32[1,64,64]{2,1,0:T(8,128)}, f32[1,64,64]{2,1,0:T(8,128)S(1)}, u32[]{:S(2)}) copy-start(f32[1,64,64]{2,1,0:T(8,128)S(1)} %get-tuple-element.12) | copy-start | bytes 49156
  9.6 13.7 %copy-start.7 = (f32[1,64,64]{2,1,0:T(8,128)}, f32[1,64,64]{2,1,0:T(8,128)S(1)}, u32[]{:S(2)}) copy-start(f32[1,64,64]{2,1,0:T(8,128)S(1)} %get-tuple-element.13) | copy-start | bytes 49156
  18.7 3.9 %copy-start.4 = (bf16[1,4,32,64,64]{4,3,2,1,0:T(8,128)(2,1)S(1)}, bf16[1,4,32,64,64]{4,3,2,1,0:T(8,128)(2,1)}, u32[]{:S(2)}) copy-start(bf16[1,4,32,64,64]{4,3,2,1,0:T(8,128)(2,1)} %param.5) | copy-start | bytes 3145732
  21.1 14.5 %collective-permute-start = (bf16[1,2,32,32,128]{4,2,3,1,0:T(8,128)(2,1)}, bf16[1,2,32,32,128]{4,2,3,1,0:T(8,128)(2,1)S(1)}, u32[]{:S(2)}, u32[]{:S(2)}) collective-permute-start(bf16[1,2,32,32,128]{4,2,3,1,0:T(8,128)(2,1)} %copy.15), channel_id=1, source_target_pairs={{0,2},{2,0},{1,3},{3,1},{4,6},{6,4},{5,7},{7,5},{8,10},{10,8},{9,1... | collective-permute-start | bytes 1572872 | tf_op jit(solution)/shard_map/ppermute | solution.py:84
  32.7 12.8 %collective-permute-start.1 = (bf16[1,2,32,32,128]{4,2,3,1,0:T(8,128)(2,1)}, bf16[1,2,32,32,128]{4,2,3,1,0:T(8,128)(2,1)S(1)}, u32[]{:S(2)}, u32[]{:S(2)}) collective-permute-start(bf16[1,2,32,32,128]{4,2,3,1,0:T(8,128)(2,1)} %copy.18), channel_id=1, source_target_pairs={{0,2},{2,0},{1,3},{3,1},{4,6},{6,4},{5,7},{7,5},{8,10},{10,8},{9,1... | collective-permute-start | bytes 1572872 | tf_op jit(solution)/shard_map/ppermute | solution.py:84
  35.4 18.4 %collective-permute-start.5 = (bf16[4,4,16,16,128]{4,2,3,1,0:T(8,128)(2,1)}, bf16[4,4,16,16,128]{4,2,3,1,0:T(8,128)(2,1)}, u32[]{:S(2)}, u32[]{:S(2)}) collective-permute-start(bf16[4,4,16,16,128]{4,2,3,1,0:T(8,128)(2,1)} %constant_dynamic-slice_fusion), channel_id=1, source_target_pairs={{0,1},{1,0},{2,3},{3,2},{4,5},{5,4},{6,7},{7,6},{8,9},{9,8},{10,11... | collective-permute-start | bytes 3145736 | tf_op jit(solution)/shard_map/ppermute | solution.py:67
  58.3 4.9 %copy-start.6 = (f32[1,64,64]{2,1,0:T(8,128)S(1)}, f32[1,64,64]{2,1,0:T(8,128)}, u32[]{:S(2)}) copy-start(f32[1,64,64]{2,1,0:T(8,128)} %copy-done.5) | copy-start | bytes 49156
  58.3 4.9 %copy-start.8 = (f32[1,64,64]{2,1,0:T(8,128)S(1)}, f32[1,64,64]{2,1,0:T(8,128)}, u32[]{:S(2)}) copy-start(f32[1,64,64]{2,1,0:T(8,128)} %copy-done.7) | copy-start | bytes 49156
  68.0 5.2 %copy-start.9 = (s32[1,1,1,8]{3,2,1,0:T(1,128)S(1)}, s32[1,1,1,8]{3,2,1,0:T(1,128)}, u32[]{:S(2)}) copy-start(s32[1,1,1,8]{3,2,1,0:T(1,128)} %param.7) | copy-start | bytes 100
  68.0 5.2 %copy-start.10 = (s32[1,1,1,8,1]{3,4,2,1,0:T(1,128)S(1)}, s32[1,1,1,8,1]{3,4,2,1,0:T(1,128)}, u32[]{:S(2)}) copy-start(s32[1,1,1,8,1]{3,4,2,1,0:T(1,128)} %param.8) | copy-start | bytes 100
  70.6 16.4 %copy-start.2 = (f32[1,64,32,128]{3,2,1,0:T(8,128)S(1)}, f32[1,64,32,128]{3,2,1,0:T(8,128)}, u32[]{:S(2)}) copy-start(f32[1,64,32,128]{3,2,1,0:T(8,128)} %shard_map.73) | copy-start | bytes 3145732
  71.7 13.2 %collective-permute-start.6 = (f32[32,1,32,128]{3,2,0,1:T(8,128)S(1)}, f32[32,1,32,128]{3,2,0,1:T(8,128)S(1)}, u32[]{:S(2)}, u32[]{:S(2)}) collective-permute-start(f32[32,1,32,128]{3,2,0,1:T(8,128)S(1)} %dynamic-slice_bitcast_fusion), channel_id=1, source_target_pairs={{0,2},{2,0},{1,3},{3,1},{4,6},{6,4},{5,7},{7,5},{8,10},{10,8},{9,1... | collective-permute-start | bytes 1572872 | tf_op jit(solution)/shard_map/ppermute | solution.py:84
  89.4 19.7 %copy-start.1 = (f32[2,4,16,32,64]{4,3,2,1,0:T(8,128)S(1)}, f32[2,4,16,32,64]{4,3,2,1,0:T(8,128)}, u32[]{:S(2)}) copy-start(f32[2,4,16,32,64]{4,3,2,1,0:T(8,128)} %param.6) | copy-start | bytes 3145732
  94.3 14.8 %copy-start.3 = (f32[32,64,64]{2,1,0:T(8,128)}, f32[32,64,64]{2,1,0:T(8,128)S(1)}, u32[]{:S(2)}) copy-start(f32[32,64,64]{2,1,0:T(8,128)S(1)} %convolution_multiply_fusion) | copy-start | bytes 1572868

commit v9 on v8

--- a/solution.py
+++ b/solution.py
@@ -192,18 +192,21 @@
     whole_receptor = gather_receptor(receptor)
     product = correlate(spectra, whole_receptor)
 
-    back_x = jnp.einsum("exk,rjkl->xrejl", pair, product, precision=highest)
-    back_x = combine_call(back_x.reshape(-1, 2, y_local, 2 * length), -1.0, 1.0, 1, jnp.float32)
-    back_x = back_x.reshape(n_sub, x_local, rots, y_local, 2 * length)
+    back_x = jnp.einsum("exk,rjkl->rjexl", pair, product, precision=highest)
+    back_x = combine_call(
+        back_x.reshape(-1, 2, length, 2 * length), -1.0, 1.0, n_sub, jnp.float32,
+        lax.axis_index("sub"),
+    ).reshape(n_sub, rots, y_local, x_local, 2 * length)
     pair_y = pair.reshape(2, length, n_sub, y_local)
     back_y = sum(
-        jnp.einsum("eyj,xrjl->rxeyl", pair_y[:, :, source], piece, precision=highest)
-        for source, piece in enumerate(by_source(exchange(back_x, "sub")))
-    )
-    back_y = combine_call(back_y.reshape(-1, 2, ny, 2 * length), -1.0, 1.0, 1, jnp.float32)
-    back_y = back_y.reshape(rots, x_local, ny, 2 * length)
+        jnp.einsum("eyj,rjxl->reyxl", pair_y[:, :, source], piece, precision=highest)
+        for source, piece in enumerate(by_source(exchange(back_x, "sub", rotated=True)))
+    )
+    back_y = combine_call(
+        back_y.reshape(rots, 2, ny * x_local, 2 * length), -1.0, 1.0, 1, jnp.float32
+    ).reshape(rots, ny, x_local, 2 * length)
     last_table = jnp.concatenate([cos_table, -sin_table], axis=0)
-    scores = jnp.einsum("rxyl,lz->rxyz", back_y, last_table, precision=highest) / float(length**3)
+    scores = jnp.einsum("ryxl,lz->rxyz", back_y, last_table, precision=highest) / float(length**3)
 
     tile_cells = 8 * length
     tile_rows = scores.reshape(-1, tile_cells)

time: 110 us -> 114 us (1.036)
  matrix products: 30.1 us -> 31.6 us
  local copies, waits for them, and re-layouts: 17.1 us -> 18.5 us
    add x0 -> x1, local copies, waits for them, and re-layouts: none -> 2.55 us  [local(): sum((jnp.einsum('eyj,rjxl->reyxl', pair_y[:, :, source], piece, precision...]
    dot_general x1 -> x0, local copies, waits for them, and re-layouts: 2.55 us -> none  [local(): back_x = jnp.einsum('exk,rjkl->xrejl', pair, product, precision=highest)]
    unnamed x29 -> x28, local copies, waits for them, and re-layouts: 2.45 us -> 4 us
    dot_general x4, matrix products: 8.48 us -> 9.89 us  [the longest x1 4.23 us: local(): jnp.einsum('ryxl,lz->rxyz', back_y, last_table, precision=highest)]
    squeeze x1 -> x0, local copies, waits for them, and re-layouts: 1.16 us -> none  [entry(): lax.dynamic_index_in_dim(sending, (me + shift) % count, axis=0, keepdims=...]
    slice x2 -> x3, local copies, waits for them, and re-layouts: 2.69 us -> 3.76 us  [entry(): return sending[shift]]
  transfers between devices with their start and end apart: 7 -> 7, of which waited for: 2 -> 2; matrix products, arithmetic and copies ran while one was open for 25% -> 24% of each run, Pallas kernels for 12% -> 12%
where the time goes in v9:
time: 114 us; the launch traced here: 113 us
  matrix products  31.6 us (28%)
  Pallas kernels  24.2 us (21%)
  local copies, waits for them, and re-layouts  18.5 us (16%)
  waiting for transfers between devices  13.1 us (11%)
  blocking collectives  9.63 us (8%)
  starting transfers between devices  9.53 us (8%)
  other arithmetic  5.76 us (5%)
    pallas_call x6, Pallas kernels, combine_call(): pl.pallas_call(functools.partial(combine_kernel, first=first, second=seco...  19.3 us
    ppermute x3, waiting for transfers between devices, exchange(): lax.ppermute(entry(shift), axis, pairs)  13.1 us
    dot_general x4, matrix products, local(): jnp.einsum('ekx,rtxjl->rtjekl', pair_x[:, :, source], piece.astype(jnp.fl...  9.8 us
    all_to_all x1, blocking collectives, local(): lax.all_to_all(packed, ('rot', 'ref'), split_axis=0, concat_axis=0, tiled...  9.63 us
    dot_general x2, matrix products, local(): along_y = jnp.einsum('ejy,rtxyl->rtxejl', pair, along_z, precision=highest)  7.46 us
    ppermute x4, starting transfers between devices, gather_by_shifts(): pieces.append(lax.ppermute(piece, axis, pairs))  6.06 us
    pallas_call x1, Pallas kernels, correlate(): pl.pallas_call(product_kernel, grid=(rots, rows // block), in_specs=[pl.B...  4.94 us
    dot_general x1, matrix products, local(): jnp.einsum('ryxl,lz->rxyz', back_y, last_table, precision=highest)  4.23 us
  transfers between devices with their start and end apart: 7, of which 2 were waited for; matrix products, arithmetic and copies ran while one was open for 24% of the time, Pallas kernels for 12%

profile of v9, /device:TPU:0, one launch (start us, length us, event | category | flops | bytes accessed | tf_op | source)
XLA Modules:
  0.0 113.4 jit_solution(17777169167159712957)
XLA Ops:
  0.7 1.6 %copy-done = f32[2,4,16,32,64]{4,3,2,1,0:T(8,128)S(1)} copy-done((f32[2,4,16,32,64]{4,3,2,1,0:T(8,128)S(1)}, f32[2,4,16,32,64]{4,3,2,1,0:T(8,128)}, u32[]{:S(2)}) %copy-start) | copy-done | bytes 1048600
  3.3 5.0 %collective-permute-start.2 = (bf16[4,16,16,128]{3,1,2,0:T(8,128)(2,1)}, bf16[4,16,16,128]{3,1,2,0:T(8,128)(2,1)S(1)}, u32[]{:S(2)}, u32[]{:S(2)}) collective-permute-start(bf16[4,16,16,128]{3,1,2,0:T(8,128)(2,1)} %fusion.85), channel_id=1, source_target_pairs={{0,12},{4,0},{8,4},{12,8},{1,13},{5,1},{9,5},{13,9},{2,14},{6,2},{... | collective-permute-start | bytes 786440 | tf_op jit(solution)/shard_map/ppermute | solution.py:67
  9.7 2.0 %fusion.11 = f32[128,2,32,64]{0,3,2,1:T(8,128)S(1)} fusion(bf16[1,4,32,64,64]{4,3,2,1,0:T(8,128)(2,1)} %param.5, f32[64,64]{1,0:T(8,128)S(1)} %get-tuple-element.18, f32[64,64]{1,0:T(8,128)S(1)} %get-tuple-element.19), kind=kOutput, calls=%fused_computation.21 | convolution fusion | flops 201334784 | bytes 3178496 | tf_op jit(solution)/shard_map/rtxyz,zl->rtxyl/dot_general | solution.py:174
  11.7 3.7 %fusion.6 = f32[2,32,128,2,64]{2,4,3,1,0:T(8,128)} fusion(f32[128,2,32,64]{0,3,2,1:T(8,128)S(1)} %fusion.11, f32[1,64,64]{2,1,0:T(8,128)S(1)} %get-tuple-element.20, f32[1,64,64]{2,1,0:T(8,128)S(1)} %get-tuple-element.21), kind=kOutput, calls=%fused_computation.13 | convolution fusion | flops 402661376 | bytes 6324224 | tf_op jit(solution)/shard_map/ejy,rtxyl->rtxejl/dot_general | solution.py:175
  15.4 3.4 %shard_map.68 = bf16[2,64,32,128]{3,2,1,0:T(8,128)(2,1)} custom-call(s32[1]{0:T(128)} %bitcast.1.me_ref, f32[64,2,64,128]{3,2,1,0:T(8,128)} %bitcast.183), custom_call_target="tpu_custom_call" | custom-call | flops 1572864 | bytes 5242880 | tf_op jit(solution)/shard_map/pallas_call | solution.py:44
  18.8 1.4 %fusion.87 = (bf16[1,64,32,128]{3,2,1,0:T(8,128)(2,1)S(1)}, bf16[1,64,32,128]{3,2,1,0:T(8,128)(2,1)S(1)}) fusion(bf16[2,64,32,128]{3,2,1,0:T(8,128)(2,1)} %shard_map.68), kind=kLoop, calls=%fused_computation.132 | loop fusion | bytes 2097152 | tf_op jit(solution)/shard_map/slice | solution.py:78
  21.2 1.5 %collective-permute-start = (bf16[1,2,32,32,128]{4,2,3,1,0:T(8,128)(2,1)}, bf16[1,2,32,32,128]{4,2,3,1,0:T(8,128)(2,1)S(1)}, u32[]{:S(2)}, u32[]{:S(2)}) collective-permute-start(bf16[1,2,32,32,128]{4,2,3,1,0:T(8,128)(2,1)} %copy.32), channel_id=1, source_target_pairs={{0,2},{2,0},{1,3},{3,1},{4,6},{6,4},{5,7},{7,5},{8,10},{10,8},{9,1... | collective-permute-start | bytes 1572872 | tf_op jit(solution)/shard_map/ppermute | solution.py:84
  23.5 3.7 %fusion.4 = f32[2,32,128,2,64]{2,4,3,1,0:T(8,128)} fusion(f32[128,2,32,64]{0,3,2,1:T(8,128)S(1)} %fusion.9, f32[1,64,64]{2,1,0:T(8,128)S(1)} %get-tuple-element.20, f32[1,64,64]{2,1,0:T(8,128)S(1)} %get-tuple-element.21), kind=kOutput, calls=%fused_computation.11 | convolution fusion | flops 402661376 | bytes 6324224 | tf_op jit(solution)/shard_map/ejy,rtxyl->rtxejl/dot_general | solution.py:175
  27.2 3.4 %shard_map.70 = bf16[2,64,32,128]{3,2,1,0:T(8,128)(2,1)} custom-call(s32[1]{0:T(128)} %bitcast.1.me_ref, f32[64,2,64,128]{3,2,1,0:T(8,128)} %bitcast.184), custom_call_target="tpu_custom_call" | custom-call | flops 1572864 | bytes 5242880 | tf_op jit(solution)/shard_map/pallas_call | solution.py:44
  30.5 1.3 %fusion.86 = (bf16[1,64,32,128]{3,2,1,0:T(8,128)(2,1)S(1)}, bf16[1,64,32,128]{3,2,1,0:T(8,128)(2,1)S(1)}) fusion(bf16[2,64,32,128]{3,2,1,0:T(8,128)(2,1)} %shard_map.70), kind=kLoop, calls=%fused_computation.131 | loop fusion | bytes 2097152 | tf_op jit(solution)/shard_map/slice | solution.py:78
  34.3 1.2 %constant_dynamic-slice_fusion = bf16[4,4,16,16,128]{4,2,3,1,0:T(8,128)(2,1)} fusion(bf16[8,4,16,16,128]{4,2,3,1,0:T(8,128)(2,1)S(1)} %bitcast_dynamic-update-slice_fusion.1, s32[]{:T(128)S(6)} %select_n.129), kind=kLoop, calls=%fused_computation.120 | loop fusion | bytes 2097156 | tf_op jit(solution)/shard_map/dynamic_slice | solution.py:69
  35.7 1.3 %fusion.19 = f32[2,32,128,2,64]{2,4,3,1,0:T(8,128)S(1)} fusion(bf16[1,2,32,32,128]{4,2,3,1,0:T(8,128)(2,1)S(1)} %collective-permute-done, pred[]{:T(512)S(6)} %eq.45, bf16[1,2,32,32,128]{4,3,2,1,0:T(8,128)(2,1)S(1)} %bitcast.185, f32[1,64,2,32]{1,3,0,2:T(8,128)S(1)} %get-tuple-element.17, f32[1,64,2,32]{1,3,0,2:T(8,128)S(1)} %get-tuple-element.16), kind=kOutput, calls=%fused_computation.30 | convolution fusion | flops 201592832 | bytes 5275649 | tf_op jit(solution)/shard_map/ekx,rtxjl->rtjekl/dot_general | solution.py:181
  37.0 3.6 %convolution_add_fusion.1 = f32[2,32,128,2,64]{2,4,3,1,0:T(8,128)} fusion(f32[2,32,128,2,64]{2,4,3,1,0:T(8,128)S(1)} %fusion.19, bf16[1,2,32,32,128]{4,2,3,1,0:T(8,128)(2,1)S(1)} %collective-permute-done, pred[]{:T(512)S(6)} %eq.44, bf16[1,2,32,32,128]{4,3,2,1,0:T(8,128)(2,1)S(1)} %bitcast.186, f32[1,64,2,32]{1,3,0,2:T(8,128)S(1)} %get-tuple-element.16, ...), kind=kOutput, calls=%fused_computation.6 | convolution fusion | flops 202641408 | bytes 9469953 | tf_op jit(solution)/shard_map/ekx,rtxjl->rtjekl/dot_general | solution.py:181
  40.6 3.4 %shard_map.69 = bf16[1,64,64,128]{3,2,1,0:T(8,128)(2,1)} custom-call(s32[1]{0:T(128)} %constant.70.clone.1.me_ref, f32[64,2,64,128]{3,2,1,0:T(8,128)} %bitcast.181), custom_call_target="tpu_custom_call" | custom-call | flops 1572864 | bytes 5242880 | tf_op jit(solution)/shard_map/pallas_call | solution.py:44
  44.0 1.6 %collective-permute-done.1 = bf16[1,2,32,32,128]{4,2,3,1,0:T(8,128)(2,1)S(1)} collective-permute-done((bf16[1,2,32,32,128]{4,2,3,1,0:T(8,128)(2,1)}, bf16[1,2,32,32,128]{4,2,3,1,0:T(8,128)(2,1)S(1)}, u32[]{:S(2)}, u32[]{:S(2)}) %collective-permute-start.1) | collective-permute-done | bytes 524320 | tf_op jit(solution)/shard_map/ppermute | solution.py:84
  45.6 1.3 %fusion.16 = f32[2,32,128,2,64]{2,4,3,1,0:T(8,128)S(1)} fusion(bf16[1,2,32,32,128]{4,2,3,1,0:T(8,128)(2,1)S(1)} %collective-permute-done.1, pred[]{:T(512)S(6)} %eq.45, bf16[1,2,32,32,128]{4,3,2,1,0:T(8,128)(2,1)S(1)} %bitcast.187, f32[1,64,2,32]{1,3,0,2:T(8,128)S(1)} %get-tuple-element.17, f32[1,64,2,32]{1,3,0,2:T(8,128)S(1)} %get-tuple-element.16), kind=kOutput, calls=%fused_computation.27 | convolution fusion | flops 201592832 | bytes 5275649 | tf_op jit(solution)/shard_map/ekx,rtxjl->rtjekl/dot_general | solution.py:181
  46.9 3.6 %convolution_add_fusion = f32[2,32,128,2,64]{2,4,3,1,0:T(8,128)} fusion(f32[2,32,128,2,64]{2,4,3,1,0:T(8,128)S(1)} %fusion.16, bf16[1,2,32,32,128]{4,2,3,1,0:T(8,128)(2,1)S(1)} %collective-permute-done.1, pred[]{:T(512)S(6)} %eq.44, bf16[1,2,32,32,128]{4,3,2,1,0:T(8,128)(2,1)S(1)} %bitcast.188, f32[1,64,2,32]{1,3,0,2:T(8,128)S(1)} %get-tuple-element.16, ...), kind=kOutput, calls=%fused_computation.5 | convolution fusion | flops 202641408 | bytes 9469953 | tf_op jit(solution)/shard_map/ekx,rtxjl->rtjekl/dot_general | solution.py:181
  50.5 3.4 %shard_map.71 = bf16[1,64,64,128]{3,2,1,0:T(8,128)(2,1)} custom-call(s32[1]{0:T(128)} %constant.70.clone.1.me_ref, f32[64,2,64,128]{3,2,1,0:T(8,128)} %bitcast.182), custom_call_target="tpu_custom_call" | custom-call | flops 1572864 | bytes 5242880 | tf_op jit(solution)/shard_map/pallas_call | solution.py:44
  53.8 2.7 %fusion.3 = bf16[4,2,16,4,16,128]{5,2,4,0,3,1:T(8,128)(2,1)S(1)} fusion(s32[]{:T(128)S(6)} %select_n.131, bf16[1,4,4,16,16,128]{5,3,4,2,1,0:T(8,128)(2,1)} %bitcast.63, bf16[1,4,4,16,16,128]{5,3,4,2,1,0:T(8,128)(2,1)S(1)} %fusion.93), kind=kLoop, calls=%fused_computation.10 | loop fusion | flops 3145728 | bytes 4194308 | tf_op jit(solution)/shard_map/transpose | solution.py:108
  56.5 1.9 %copy.38 = bf16[4,2,16,4,16,128]{5,4,3,2,1,0:T(8,128)(2,1)} copy(bf16[4,2,16,4,16,128]{5,2,4,0,3,1:T(8,128)(2,1)S(1)} %fusion.3) | data formatting | bytes 4194304 | tf_op jit(solution)/shard_map/transpose | solution.py:108
  58.4 4.9 %shard_map.72 = f32[1,2048,128]{2,1,0:T(8,128)} custom-call(bf16[1,2,2048,128]{3,2,1,0:T(8,128)(2,1)} %bitcast.192, bf16[1,2,2048,128]{3,2,1,0:T(8,128)(2,1)} %bitcast.193, bf16[4,2048,128]{2,1,0:T(8,128)(2,1)} %bitcast.189), custom_call_target="tpu_custom_call" | custom-call | flops 8388608 | bytes 5242880 | tf_op jit(solution)/shard_map/pallas_call | solution.py:139
  63.4 3.5 %convolution_bitcast_fusion.in_ref = f32[32,2,64,128]{3,2,1,0:T(8,128)} fusion(f32[32,64,128,1]{2,1,3,0:T(8,128)} %bitcast.191, f32[1,64,64]{2,1,0:T(8,128)S(1)} %copy-done.5, f32[1,64,64]{2,1,0:T(8,128)S(1)} %copy-done.7), kind=kOutput, calls=%fused_computation.16 | convolution fusion | flops 201334784 | bytes 3178496 | tf_op jit(solution)/shard_map/exk,rjkl->rjexl/dot_general | solution.py:195
  66.9 2.9 %shard_map.73 = f32[2,32,32,128]{3,2,1,0:T(8,128)} custom-call(s32[1]{0:T(128)} %bitcast.1.me_ref, f32[32,2,64,128]{3,2,1,0:T(8,128)} %convolution_bitcast_fusion.in_ref), custom_call_target="tpu_custom_call" | custom-call | flops 786432 | bytes 3145728 | tf_op jit(solution)/shard_map/pallas_call | solution.py:44
  70.9 1.4 %collective-permute-start.6 = (f32[1,32,32,128]{3,2,1,0:T(8,128)S(1)}, f32[1,32,32,128]{3,2,1,0:T(8,128)S(1)}, u32[]{:S(2)}, u32[]{:S(2)}) collective-permute-start(f32[1,32,32,128]{3,2,1,0:T(8,128)S(1)} %slice.70), channel_id=1, source_target_pairs={{0,2},{2,0},{1,3},{3,1},{4,6},{6,4},{5,7},{7,5},{8,10},{10,8},{9,1... | collective-permute-start | bytes 1572872 | tf_op jit(solution)/shard_map/ppermute | solution.py:84
  72.5 11.5 %collective-permute-done.6 = f32[1,32,32,128]{3,2,1,0:T(8,128)S(1)} collective-permute-done((f32[1,32,32,128]{3,2,1,0:T(8,128)S(1)}, f32[1,32,32,128]{3,2,1,0:T(8,128)S(1)}, u32[]{:S(2)}, u32[]{:S(2)}) %collective-permute-start.6) | collective-permute-done | bytes 524320 | tf_op jit(solution)/shard_map/ppermute | solution.py:84
  87.4 2.5 %copy.41 = f32[1,2,64,32,128]{4,3,2,1,0:T(8,128)} copy(f32[1,2,64,32,128]{4,2,1,3,0:T(8,128)S(1)} %add_bitcast_fusion) | data formatting | bytes 4194304 | tf_op jit(solution)/shard_map/add | solution.py:201
  89.9 2.9 %shard_map.74 = f32[1,1,2048,128]{3,2,1,0:T(8,128)} custom-call(s32[1]{0:T(128)} %constant.70.clone.1.me_ref, f32[1,2,2048,128]{3,2,1,0:T(8,128)} %bitcast.190), custom_call_target="tpu_custom_call" | custom-call | flops 786432 | bytes 3145728 | tf_op jit(solution)/shard_map/pallas_call | solution.py:44
  92.8 4.2 %fusion.8 = f32[1,32,64,64]{2,3,1,0:T(8,128)} fusion(f32[64,32,128]{2,1,0:T(8,128)} %bitcast.194, f32[64,64]{1,0:T(8,128)S(1)} %get-tuple-element.18, f32[64,64]{1,0:T(8,128)S(1)} %get-tuple-element.19), kind=kOutput, calls=%fused_computation.18 | convolution fusion | flops 100802560 | bytes 1605632 | tf_op jit(solution)/shard_map/ryxl,lz->rxyz/dot_general | solution.py:209
  97.1 1.6 %copy.45 = f32[1,32,64,64]{3,2,1,0:T(8,128)S(1)} copy(f32[1,32,64,64]{2,3,1,0:T(8,128)} %fusion.8) | data formatting | bytes 1048576
  99.8 1.6 %gather_fusion = f32[8,512]{1,0:T(8,128)S(1)} fusion(f32[256,512]{1,0:T(8,128)} %reshape.311, s32[1024]{0:T(1024)S(1)} %pad_clamp_fusion), kind=kCustom, calls=%fused_computation | custom fusion | bytes 32800 | tf_op jit(solution)/shard_map/gather | solution.py:216
  101.4 1.6 %fusion.88 = f32[8,512]{1,0:T(8,128)S(1)} fusion(f32[8,512]{1,0:T(8,128)S(1)} %gather_fusion, f32[512,512]{1,0:T(8,128)} %param.9), kind=kOutput, calls=%fused_computation.133 | convolution fusion | flops 12582912 | bytes 1081344 | tf_op jit(solution)/shard_map/dot_general | solution.py:225
  103.1 9.6 %all_to_all.5 = f32[8,2,512]{2,1,0:T(2,128)S(1)} all-to-all(f32[8,2,512]{2,1,0:T(2,128)S(1)} %reshape.313), channel_id=1, replica_groups=mesh['grp'=2,'rot'=4,'sub'=2,'ref'=2] {'rot','ref'}, dimensions={0} | all-to-all | bytes 65536 | tf_op jit(solution)/shard_map/all_to_all | solution.py:227
  (59 shorter events, 13.2 us)
Async XLA Ops:
  0.6 1.6 %copy-start = (f32[2,4,16,32,64]{4,3,2,1,0:T(8,128)S(1)}, f32[2,4,16,32,64]{4,3,2,1,0:T(8,128)}, u32[]{:S(2)}) copy-start(f32[2,4,16,32,64]{4,3,2,1,0:T(8,128)} %param.6) | copy-start | bytes 3145732
  3.3 30.4 %collective-permute-start.2 = (bf16[4,16,16,128]{3,1,2,0:T(8,128)(2,1)}, bf16[4,16,16,128]{3,1,2,0:T(8,128)(2,1)S(1)}, u32[]{:S(2)}, u32[]{:S(2)}) collective-permute-start(bf16[4,16,16,128]{3,1,2,0:T(8,128)(2,1)} %fusion.85), channel_id=1, source_target_pairs={{0,12},{4,0},{8,4},{12,8},{1,13},{5,1},{9,5},{13,9},{2,14},{6,2},{... | collective-permute-start | bytes 786440 | tf_op jit(solution)/shard_map/ppermute | solution.py:67
  8.3 25.4 %collective-permute-start.3 = (bf16[4,16,16,128]{3,1,2,0:T(8,128)(2,1)}, bf16[4,16,16,128]{3,1,2,0:T(8,128)(2,1)S(1)}, u32[]{:S(2)}, u32[]{:S(2)}) collective-permute-start(bf16[4,16,16,128]{3,1,2,0:T(8,128)(2,1)} %fusion.85), channel_id=1, source_target_pairs={{0,8},{4,12},{8,0},{12,4},{1,9},{5,13},{9,1},{13,5},{2,10},{6,14},... | collective-permute-start | bytes 786440 | tf_op jit(solution)/shard_map/ppermute | solution.py:67
  8.3 25.4 %collective-permute-start.4 = (bf16[4,16,16,128]{3,1,2,0:T(8,128)(2,1)}, bf16[4,16,16,128]{3,1,2,0:T(8,128)(2,1)S(1)}, u32[]{:S(2)}, u32[]{:S(2)}) collective-permute-start(bf16[4,16,16,128]{3,1,2,0:T(8,128)(2,1)} %fusion.85), channel_id=1, source_target_pairs={{0,4},{4,8},{8,12},{12,0},{1,5},{5,9},{9,13},{13,1},{2,6},{6,10},{... | collective-permute-start | bytes 786440 | tf_op jit(solution)/shard_map/ppermute | solution.py:67
  9.6 13.8 %copy-start.4 = (f32[1,64,64]{2,1,0:T(8,128)}, f32[1,64,64]{2,1,0:T(8,128)S(1)}, u32[]{:S(2)}) copy-start(f32[1,64,64]{2,1,0:T(8,128)S(1)} %get-tuple-element.20) | copy-start | bytes 49156
  9.6 13.8 %copy-start.6 = (f32[1,64,64]{2,1,0:T(8,128)}, f32[1,64,64]{2,1,0:T(8,128)S(1)}, u32[]{:S(2)}) copy-start(f32[1,64,64]{2,1,0:T(8,128)S(1)} %get-tuple-element.21) | copy-start | bytes 49156
  18.8 3.9 %copy-start.3 = (bf16[1,4,32,64,64]{4,3,2,1,0:T(8,128)(2,1)S(1)}, bf16[1,4,32,64,64]{4,3,2,1,0:T(8,128)(2,1)}, u32[]{:S(2)}) copy-start(bf16[1,4,32,64,64]{4,3,2,1,0:T(8,128)(2,1)} %param.5) | copy-start | bytes 3145732
  21.2 14.5 %collective-permute-start = (bf16[1,2,32,32,128]{4,2,3,1,0:T(8,128)(2,1)}, bf16[1,2,32,32,128]{4,2,3,1,0:T(8,128)(2,1)S(1)}, u32[]{:S(2)}, u32[]{:S(2)}) collective-permute-start(bf16[1,2,32,32,128]{4,2,3,1,0:T(8,128)(2,1)} %copy.32), channel_id=1, source_target_pairs={{0,2},{2,0},{1,3},{3,1},{4,6},{6,4},{5,7},{7,5},{8,10},{10,8},{9,1... | collective-permute-start | bytes 1572872 | tf_op jit(solution)/shard_map/ppermute | solution.py:84
  32.8 12.8 %collective-permute-start.1 = (bf16[1,2,32,32,128]{4,2,3,1,0:T(8,128)(2,1)}, bf16[1,2,32,32,128]{4,2,3,1,0:T(8,128)(2,1)S(1)}, u32[]{:S(2)}, u32[]{:S(2)}) collective-permute-start(bf16[1,2,32,32,128]{4,2,3,1,0:T(8,128)(2,1)} %copy.35), channel_id=1, source_target_pairs={{0,2},{2,0},{1,3},{3,1},{4,6},{6,4},{5,7},{7,5},{8,10},{10,8},{9,1... | collective-permute-start | bytes 1572872 | tf_op jit(solution)/shard_map/ppermute | solution.py:84
  35.5 18.4 %collective-permute-start.5 = (bf16[4,4,16,16,128]{4,2,3,1,0:T(8,128)(2,1)}, bf16[4,4,16,16,128]{4,2,3,1,0:T(8,128)(2,1)}, u32[]{:S(2)}, u32[]{:S(2)}) collective-permute-start(bf16[4,4,16,16,128]{4,2,3,1,0:T(8,128)(2,1)} %constant_dynamic-slice_fusion), channel_id=1, source_target_pairs={{0,1},{1,0},{2,3},{3,2},{4,5},{5,4},{6,7},{7,6},{8,9},{9,8},{10,11... | collective-permute-start | bytes 3145736 | tf_op jit(solution)/shard_map/ppermute | solution.py:67
  58.4 4.9 %copy-start.5 = (f32[1,64,64]{2,1,0:T(8,128)S(1)}, f32[1,64,64]{2,1,0:T(8,128)}, u32[]{:S(2)}) copy-start(f32[1,64,64]{2,1,0:T(8,128)} %copy-done.4) | copy-start | bytes 49156
  58.4 4.9 %copy-start.7 = (f32[1,64,64]{2,1,0:T(8,128)S(1)}, f32[1,64,64]{2,1,0:T(8,128)}, u32[]{:S(2)}) copy-start(f32[1,64,64]{2,1,0:T(8,128)} %copy-done.6) | copy-start | bytes 49156
  66.9 5.4 %copy-start.8 = (s32[1,1,1,8]{3,2,1,0:T(1,128)S(1)}, s32[1,1,1,8]{3,2,1,0:T(1,128)}, u32[]{:S(2)}) copy-start(s32[1,1,1,8]{3,2,1,0:T(1,128)} %param.7) | copy-start | bytes 100
  66.9 5.5 %copy-start.9 = (s32[1,1,1,8,1]{3,4,2,1,0:T(1,128)S(1)}, s32[1,1,1,8,1]{3,4,2,1,0:T(1,128)}, u32[]{:S(2)}) copy-start(s32[1,1,1,8,1]{3,4,2,1,0:T(1,128)} %param.8) | copy-start | bytes 100
  70.9 13.2 %collective-permute-start.6 = (f32[1,32,32,128]{3,2,1,0:T(8,128)S(1)}, f32[1,32,32,128]{3,2,1,0:T(8,128)S(1)}, u32[]{:S(2)}, u32[]{:S(2)}) collective-permute-start(f32[1,32,32,128]{3,2,1,0:T(8,128)S(1)} %slice.70), channel_id=1, source_target_pairs={{0,2},{2,0},{1,3},{3,1},{4,6},{6,4},{5,7},{7,5},{8,10},{10,8},{9,1... | collective-permute-start | bytes 1572872 | tf_op jit(solution)/shard_map/ppermute | solution.py:84
  92.8 20.6 %copy-start.1 = (f32[2,4,16,32,64]{4,3,2,1,0:T(8,128)S(1)}, f32[2,4,16,32,64]{4,3,2,1,0:T(8,128)}, u32[]{:S(2)}) copy-start(f32[2,4,16,32,64]{4,3,2,1,0:T(8,128)} %param.6) | copy-start | bytes 3145732
  98.6 14.8 %copy-start.2 = (f32[1,32,64,64]{3,2,1,0:T(8,128)}, f32[1,32,64,64]{3,2,1,0:T(8,128)S(1)}, u32[]{:S(2)}) copy-start(f32[1,32,64,64]{3,2,1,0:T(8,128)S(1)} %copy.45) | copy-start | bytes 1572868

commit v10 on v8

--- a/solution.py
+++ b/solution.py
@@ -58,17 +58,6 @@
     )(jnp.reshape(jnp.asarray(me, jnp.int32), (1,)), stacked)
 
 
-def gather_by_shifts(piece, axis):
-    count = lax.axis_size(axis)
-    me = lax.axis_index(axis)
-    pieces = [piece]
-    for shift in range(1, count):
-        pairs = [(k, (k + shift) % count) for k in range(count)]
-        pieces.append(lax.ppermute(piece, axis, pairs))
-    doubled = jnp.stack(pieces[::-1] * 2)
-    return lax.dynamic_slice_in_dim(doubled, (count - 1 - me) % count, count, axis=0)
-
-
 def exchange(sending, axis, rotated=False):
     count = lax.axis_size(axis)
     me = lax.axis_index(axis)
@@ -103,8 +92,8 @@
     block = lax.dynamic_slice_in_dim(receptor, lax.axis_index("ref") * rows, rows, axis=3)
     mine = jnp.concatenate([block[0], block[1]], axis=-1).astype(jnp.bfloat16)
     mine = jnp.swapaxes(mine, 1, 2)
-    along_rot = gather_by_shifts(mine, "rot")
-    both = gather_by_shifts(along_rot, "ref")
+    along_rot = jnp.stack(by_source(exchange(jnp.stack([mine] * n_rot), "rot", rotated=True)))
+    both = jnp.stack(by_source(exchange(jnp.stack([along_rot] * n_ref), "ref", rotated=True)))
     both = jnp.transpose(both, (2, 0, 3, 1, 4, 5))
     return both.reshape(terms, ky_local, n_rot * kx_local, 2 * kz)
 

time: 110 us -> 109 us (level)
    ppermute x3 -> x7, starting transfers between devices: 3.5 us -> 9.7 us  [exchange(): lax.ppermute(entry(shift), axis, pairs)]
    ppermute x4 -> x0, starting transfers between devices: 6.06 us -> none  [gather_by_shifts(): pieces.append(lax.ppermute(piece, axis, pairs))]
    another operation x1 -> x3, other arithmetic: 0.19 us -> 3.79 us  [the longest x2 2.37 us: gather_receptor(): jnp.stack(by_source(exchange(jnp.stack([mine] * n_rot), 'rot', rotated=Tr...]
    transpose x1, other arithmetic: 2.68 us -> 0.19 us  [gather_receptor(): both = jnp.transpose(both, (2, 0, 3, 1, 4, 5))]
    unnamed x29 -> x27, local copies, waits for them, and re-layouts: 2.45 us -> 3.64 us
    dynamic_slice x1 -> x0, local copies, waits for them, and re-layouts: 1.17 us -> none  [gather_by_shifts(): lax.dynamic_slice_in_dim(doubled, (count - 1 - me) % count, count, axis=0)]
    ppermute x3 -> x7, waiting for transfers between devices: 13.1 us -> 12.7 us  [exchange(): lax.ppermute(entry(shift), axis, pairs)]
  transfers between devices with their start and end apart: 7 -> 7, of which waited for: 2 -> 1; matrix products, arithmetic and copies ran while one was open for 25% -> 25% of each run, Pallas kernels for 12% -> 12%
where the time goes in v10:
time: 109 us
  matrix products  30.1 us (28%)
  Pallas kernels  24 us (22%)
  local copies, waits for them, and re-layouts  16.9 us (16%)
  waiting for transfers between devices  12.7 us (12%)
  starting transfers between devices  9.7 us (9%)
  blocking collectives  9.63 us (9%)
  other arithmetic  4.84 us (4%)
    pallas_call x6, Pallas kernels, combine_call(): pl.pallas_call(functools.partial(combine_kernel, first=first, second=seco...  19 us
    ppermute x7, waiting for transfers between devices, exchange(): lax.ppermute(entry(shift), axis, pairs)  12.7 us
    dot_general x4, matrix products, local(): jnp.einsum('ekx,rtxjl->rtjekl', pair_x[:, :, source], piece.astype(jnp.fl...  9.8 us
    ppermute x7, starting transfers between devices, exchange(): lax.ppermute(entry(shift), axis, pairs)  9.7 us
    all_to_all x1, blocking collectives, local(): lax.all_to_all(packed, ('rot', 'ref'), split_axis=0, concat_axis=0, tiled...  9.63 us
    dot_general x2, matrix products, local(): along_y = jnp.einsum('ejy,rtxyl->rtxejl', pair, along_z, precision=highest)  7.45 us
    pallas_call x1, Pallas kernels, correlate(): pl.pallas_call(product_kernel, grid=(rots, rows // block), in_specs=[pl.B...  4.95 us
    dot_general x2, matrix products, local(): jnp.einsum('eyj,xrjl->rxeyl', pair_y[:, :, source], piece, precision=high...  4.43 us
  transfers between devices with their start and end apart: 7, of which 1 were waited for; matrix products, arithmetic and copies ran while one was open for 25% of the time, Pallas kernels for 12%

profile of v10, /device:TPU:0, one launch (start us, length us, event | category | flops | bytes accessed | tf_op | source)
XLA Modules:
  0.0 108.8 jit_solution(17817070107281136963)
XLA Ops:
  0.7 1.6 %copy-done = f32[2,4,16,32,64]{4,3,2,1,0:T(8,128)S(1)} copy-done((f32[2,4,16,32,64]{4,3,2,1,0:T(8,128)S(1)}, f32[2,4,16,32,64]{4,3,2,1,0:T(8,128)}, u32[]{:S(2)}) %copy-start) | copy-done | bytes 1048600
  2.6 5.1 %collective-permute-start.2 = (bf16[4,16,16,128]{3,1,2,0:T(8,128)(2,1)S(1)}, bf16[4,16,16,128]{3,1,2,0:T(8,128)(2,1)S(1)}, u32[]{:S(2)}, u32[]{:S(2)}) collective-permute-start(bf16[4,16,16,128]{3,1,2,0:T(8,128)(2,1)S(1)} %maximum_bitcast_fusion.1), channel_id=1, source_target_pairs={{0,12},{4,0},{8,4},{12,8},{1,13},{5,1},{9,5},{13,9},{2,14},{6,2},{... | collective-permute-start | bytes 786440 | tf_op jit(solution)/shard_map/ppermute | solution.py:73
  9.0 2.0 %fusion.7 = f32[128,2,32,64]{0,3,2,1:T(8,128)S(1)} fusion(bf16[1,4,32,64,64]{4,3,2,1,0:T(8,128)(2,1)} %param.5, f32[64,64]{0,1:T(8,128)S(1)} %get-tuple-element.16, f32[64,64]{0,1:T(8,128)S(1)} %get-tuple-element.17), kind=kOutput, calls=%fused_computation.15 | convolution fusion | flops 201334784 | bytes 3178496 | tf_op jit(solution)/shard_map/rtxyz,zl->rtxyl/dot_general | solution.py:163
  11.0 3.7 %fusion.2 = f32[2,32,128,2,64]{2,4,3,1,0:T(8,128)} fusion(f32[128,2,32,64]{0,3,2,1:T(8,128)S(1)} %fusion.7, f32[1,64,64]{2,1,0:T(8,128)S(1)} %get-tuple-element.18, f32[1,64,64]{2,1,0:T(8,128)S(1)} %get-tuple-element.19), kind=kOutput, calls=%fused_computation.6 | convolution fusion | flops 402661376 | bytes 6324224 | tf_op jit(solution)/shard_map/ejy,rtxyl->rtxejl/dot_general | solution.py:164
  14.7 3.4 %shard_map.68 = bf16[2,64,32,128]{3,2,1,0:T(8,128)(2,1)} custom-call(s32[1]{0:T(128)} %bitcast.me_ref, f32[64,2,64,128]{3,2,1,0:T(8,128)} %bitcast.194), custom_call_target="tpu_custom_call" | custom-call | flops 1572864 | bytes 5242880 | tf_op jit(solution)/shard_map/pallas_call | solution.py:44
  18.0 1.4 %fusion.88 = (bf16[1,64,32,128]{3,2,1,0:T(8,128)(2,1)S(1)}, bf16[1,64,32,128]{3,2,1,0:T(8,128)(2,1)S(1)}) fusion(bf16[2,64,32,128]{3,2,1,0:T(8,128)(2,1)} %shard_map.68), kind=kLoop, calls=%fused_computation.129 | loop fusion | bytes 2097152 | tf_op jit(solution)/shard_map/slice | solution.py:67
  20.5 1.5 %collective-permute-start = (bf16[1,2,32,32,128]{4,2,3,1,0:T(8,128)(2,1)}, bf16[1,2,32,32,128]{4,2,3,1,0:T(8,128)(2,1)S(1)}, u32[]{:S(2)}, u32[]{:S(2)}) collective-permute-start(bf16[1,2,32,32,128]{4,2,3,1,0:T(8,128)(2,1)} %copy.15), channel_id=1, source_target_pairs={{0,2},{2,0},{1,3},{3,1},{4,6},{6,4},{5,7},{7,5},{8,10},{10,8},{9,1... | collective-permute-start | bytes 1572872 | tf_op jit(solution)/shard_map/ppermute | solution.py:73
  22.7 3.7 %fusion = f32[2,32,128,2,64]{2,4,3,1,0:T(8,128)} fusion(f32[128,2,32,64]{0,3,2,1:T(8,128)S(1)} %fusion.5, f32[1,64,64]{2,1,0:T(8,128)S(1)} %get-tuple-element.18, f32[1,64,64]{2,1,0:T(8,128)S(1)} %get-tuple-element.19), kind=kOutput, calls=%fused_computation.4 | convolution fusion | flops 402661376 | bytes 6324224 | tf_op jit(solution)/shard_map/ejy,rtxyl->rtxejl/dot_general | solution.py:164
  26.4 3.4 %shard_map.70 = bf16[2,64,32,128]{3,2,1,0:T(8,128)(2,1)} custom-call(s32[1]{0:T(128)} %bitcast.me_ref, f32[64,2,64,128]{3,2,1,0:T(8,128)} %bitcast.195), custom_call_target="tpu_custom_call" | custom-call | flops 1572864 | bytes 5242880 | tf_op jit(solution)/shard_map/pallas_call | solution.py:44
  29.8 1.3 %fusion.87 = (bf16[1,64,32,128]{3,2,1,0:T(8,128)(2,1)S(1)}, bf16[1,64,32,128]{3,2,1,0:T(8,128)(2,1)S(1)}) fusion(bf16[2,64,32,128]{3,2,1,0:T(8,128)(2,1)} %shard_map.70), kind=kLoop, calls=%fused_computation.128 | loop fusion | bytes 2097152 | tf_op jit(solution)/shard_map/slice | solution.py:67
  34.4 1.2 %select_bitcast_fusion.5 = (bf16[1,4,16,16,128]{4,2,3,1,0:T(8,128)(2,1)S(1)}, bf16[1,4,16,16,128]{4,2,3,1,0:T(8,128)(2,1)S(1)}, bf16[1,4,16,16,128]{4,2,3,1,0:T(8,128)(2,1)S(1)}, bf16[1,4,16,16,128]{4,2,3,1,0:T(8,128)(2,1)S(1)}) fusion(bf16[4,16,16,128]{3,1,2,0:T(8,128)(2,1)} %copy-done.9, bf16[4,16,16,128]{3,1,2,0:T(8,128)(2,1)} %copy-done.10, ...), kind=kLoop, calls=%fused_computation.54 | loop fusion | flops 1572864 | bytes 2097164 | tf_op jit(solution)/shard_map/stack | solution.py:95
  36.8 1.3 %fusion.17 = f32[2,32,128,2,64]{2,4,3,1,0:T(8,128)S(1)} fusion(bf16[1,2,32,32,128]{4,2,3,1,0:T(8,128)(2,1)S(1)} %collective-permute-done, pred[]{:T(512)S(6)} %eq.91, bf16[1,2,32,32,128]{4,3,2,1,0:T(8,128)(2,1)S(1)} %bitcast.196, f32[1,64,2,32]{1,3,0,2:T(8,128)S(1)} %get-tuple-element.15, f32[1,64,2,32]{1,3,0,2:T(8,128)S(1)} %get-tuple-element.14), kind=kOutput, calls=%fused_computation.28 | convolution fusion | flops 201592832 | bytes 5275649 | tf_op jit(solution)/shard_map/ekx,rtxjl->rtjekl/dot_general | solution.py:170
  38.1 3.6 %convolution_add_fusion.1 = f32[2,32,128,2,64]{2,4,3,1,0:T(8,128)} fusion(f32[2,32,128,2,64]{2,4,3,1,0:T(8,128)S(1)} %fusion.17, bf16[1,2,32,32,128]{4,2,3,1,0:T(8,128)(2,1)S(1)} %collective-permute-done, pred[]{:T(512)S(6)} %eq.90, bf16[1,2,32,32,128]{4,3,2,1,0:T(8,128)(2,1)S(1)} %bitcast.197, f32[1,64,2,32]{1,3,0,2:T(8,128)S(1)} %get-tuple-element.14, ...), kind=kOutput, calls=%fused_computation.2 | convolution fusion | flops 202641408 | bytes 9469953 | tf_op jit(solution)/shard_map/ekx,rtxjl->rtjekl/dot_general | solution.py:170
  41.7 3.4 %shard_map.69 = bf16[1,64,64,128]{3,2,1,0:T(8,128)(2,1)} custom-call(s32[1]{0:T(128)} %constant.91.clone.1.me_ref, f32[64,2,64,128]{3,2,1,0:T(8,128)} %bitcast.192), custom_call_target="tpu_custom_call" | custom-call | flops 1572864 | bytes 5242880 | tf_op jit(solution)/shard_map/pallas_call | solution.py:44
  45.0 1.3 %fusion.14 = f32[2,32,128,2,64]{2,4,3,1,0:T(8,128)S(1)} fusion(bf16[1,2,32,32,128]{4,2,3,1,0:T(8,128)(2,1)S(1)} %collective-permute-done.1, pred[]{:T(512)S(6)} %eq.91, bf16[1,2,32,32,128]{4,3,2,1,0:T(8,128)(2,1)S(1)} %bitcast.198, f32[1,64,2,32]{1,3,0,2:T(8,128)S(1)} %get-tuple-element.15, f32[1,64,2,32]{1,3,0,2:T(8,128)S(1)} %get-tuple-element.14), kind=kOutput, calls=%fused_computation.25 | convolution fusion | flops 201592832 | bytes 5275649 | tf_op jit(solution)/shard_map/ekx,rtxjl->rtjekl/dot_general | solution.py:170
  46.3 3.6 %convolution_add_fusion = f32[2,32,128,2,64]{2,4,3,1,0:T(8,128)} fusion(f32[2,32,128,2,64]{2,4,3,1,0:T(8,128)S(1)} %fusion.14, bf16[1,2,32,32,128]{4,2,3,1,0:T(8,128)(2,1)S(1)} %collective-permute-done.1, pred[]{:T(512)S(6)} %eq.90, bf16[1,2,32,32,128]{4,3,2,1,0:T(8,128)(2,1)S(1)} %bitcast.199, f32[1,64,2,32]{1,3,0,2:T(8,128)S(1)} %get-tuple-element.14, ...), kind=kOutput, calls=%fused_computation.1 | convolution fusion | flops 202641408 | bytes 9469953 | tf_op jit(solution)/shard_map/ekx,rtxjl->rtjekl/dot_general | solution.py:170
  49.9 3.4 %shard_map.71 = bf16[1,64,64,128]{3,2,1,0:T(8,128)(2,1)} custom-call(s32[1]{0:T(128)} %constant.91.clone.1.me_ref, f32[64,2,64,128]{3,2,1,0:T(8,128)} %bitcast.193), custom_call_target="tpu_custom_call" | custom-call | flops 1572864 | bytes 5242880 | tf_op jit(solution)/shard_map/pallas_call | solution.py:44
  53.3 1.4 %select_bitcast_fusion.1 = (bf16[1,4,4,16,16,128]{5,3,4,2,1,0:T(8,128)(2,1)S(1)}, bf16[1,4,4,16,16,128]{5,3,4,2,1,0:T(8,128)(2,1)S(1)}) fusion(bf16[4,4,16,16,128]{4,2,3,1,0:T(8,128)(2,1)} %collective-permute-done.5, pred[]{:T(512)S(6)} %eq.92, bf16[1,4,16,16,128]{4,2,3,1,0:T(8,128)(2,1)S(1)} %get-tuple-element.5, ...), kind=kLoop, calls=%fused_computation.18 | loop fusion | flops 2621440 | bytes 4194306 | tf_op jit(solution)/shard_map/stack | solution.py:96
  54.9 1.9 %copy.21 = bf16[4,2,16,4,16,128]{5,4,3,2,1,0:T(8,128)(2,1)} copy(bf16[4,2,16,4,16,128]{5,2,4,0,3,1:T(8,128)(2,1)S(1)} %maximum_bitcast_fusion) | data formatting | bytes 4194304 | tf_op jit(solution)/shard_map/transpose | solution.py:97
  56.8 4.9 %shard_map.72 = f32[1,2048,128]{2,1,0:T(8,128)} custom-call(bf16[1,2,2048,128]{3,2,1,0:T(8,128)(2,1)} %bitcast.206, bf16[1,2,2048,128]{3,2,1,0:T(8,128)(2,1)} %bitcast.208, bf16[4,2048,128]{2,1,0:T(8,128)(2,1)} %bitcast.200), custom_call_target="tpu_custom_call" | custom-call | flops 8388608 | bytes 5242880 | tf_op jit(solution)/shard_map/pallas_call | solution.py:128
  61.8 2.2 %fusion.36 = f32[32,128,2,64]{1,3,2,0:T(8,128)S(1)} fusion(f32[32,64,128,1]{2,1,3,0:T(8,128)} %bitcast.205, f32[1,64,64]{2,1,0:T(8,128)S(1)} %copy-done.6, f32[1,64,64]{2,1,0:T(8,128)S(1)} %copy-done.8), kind=kOutput, calls=%fused_computation.61 | convolution fusion | flops 201334784 | bytes 3178496 | tf_op jit(solution)/shard_map/exk,rjkl->xrejl/dot_general | solution.py:184
  64.0 2.6 %copy.53 = f32[32,128,2,64]{1,0,2,3:T(8,128)} copy(f32[32,128,2,64]{1,3,2,0:T(8,128)S(1)} %fusion.36) | data formatting | bytes 4194304 | tf_op jit(solution)/shard_map/exk,rjkl->xrejl/dot_general | solution.py:184
  66.5 2.6 %shard_map.73 = f32[1,64,32,128]{3,2,1,0:T(8,128)} custom-call(s32[1]{0:T(128)} %constant.91.clone.1.me_ref, f32[64,2,32,128]{3,2,1,0:T(8,128)} %bitcast.201), custom_call_target="tpu_custom_call" | custom-call | flops 786432 | bytes 3145728 | tf_op jit(solution)/shard_map/pallas_call | solution.py:44
  70.2 1.6 %collective-permute-start.6 = (f32[32,1,32,128]{3,2,0,1:T(8,128)S(1)}, f32[32,1,32,128]{3,2,0,1:T(8,128)S(1)}, u32[]{:S(2)}, u32[]{:S(2)}) collective-permute-start(f32[32,1,32,128]{3,2,0,1:T(8,128)S(1)} %dynamic-slice_bitcast_fusion), channel_id=1, source_target_pairs={{0,2},{2,0},{1,3},{3,1},{4,6},{6,4},{5,7},{7,5},{8,10},{10,8},{9,1... | collective-permute-start | bytes 1572872 | tf_op jit(solution)/shard_map/ppermute | solution.py:73
  72.0 12.6 %collective-permute-done.6 = f32[32,1,32,128]{3,2,0,1:T(8,128)S(1)} collective-permute-done((f32[32,1,32,128]{3,2,0,1:T(8,128)S(1)}, f32[32,1,32,128]{3,2,0,1:T(8,128)S(1)}, u32[]{:S(2)}, u32[]{:S(2)}) %collective-permute-start.6) | collective-permute-done | bytes 524320 | tf_op jit(solution)/shard_map/ppermute | solution.py:73
  84.7 2.1 %fusion.11 = f32[32,128,2,64]{1,3,2,0:T(8,128)S(1)} fusion(f32[32,1,32,128]{3,2,0,1:T(8,128)S(1)} %collective-permute-done.6, f32[2,32,1,32,128]{4,3,1,0,2:T(8,128)} %bitcast.203, s32[]{:T(128)S(6)} %select_n.268, pred[]{:T(512)S(6)} %eq.91, f32[1,64,2,32]{1,3,0,2:T(8,128)S(1)} %get-tuple-element.15, f32[1,64,2,32]{1,3,0,2:T(8,128)S(1)} %get-tuple-element.14), kind=kOutput, calls=%fused_computation.22 | convolution fusion | flops 100798464 | bytes 3178501 | tf_op jit(solution)/shard_map/eyj,xrjl->rxeyl/dot_general | solution.py:189
  86.7 2.4 %add_bitcast_fusion.in_ref = f32[32,2,64,128]{3,2,1,0:T(8,128)} fusion(f32[32,128,2,64]{1,3,2,0:T(8,128)S(1)} %fusion.11, f32[32,1,32,128]{3,2,0,1:T(8,128)S(1)} %collective-permute-done.6, f32[2,32,1,32,128]{4,3,1,0,2:T(8,128)S(1)} %bitcast.204, s32[]{:T(128)S(6)} %select_n.268, pred[]{:T(512)S(6)} %eq.90, f32[1,64,2,32]{1,3,0,2:T(8,128)S(1)} %get-tuple-element.14, ...), kind=kOutput, calls=%fused_computation.9 | convolution fusion | flops 101322752 | bytes 5308421 | tf_op jit(solution)/shard_map/eyj,xrjl->rxeyl/dot_general | solution.py:189
  89.1 3.0 %shard_map.74 = f32[1,32,64,128]{3,2,1,0:T(8,128)} custom-call(s32[1]{0:T(128)} %constant.91.clone.1.me_ref, f32[32,2,64,128]{3,2,1,0:T(8,128)} %add_bitcast_fusion.in_ref), custom_call_target="tpu_custom_call" | custom-call | flops 786432 | bytes 3145728 | tf_op jit(solution)/shard_map/pallas_call | solution.py:44
  92.1 1.9 %convolution_multiply_fusion = f32[32,64,64]{2,1,0:T(8,128)S(1)} fusion(f32[1,32,64,128]{3,2,1,0:T(8,128)} %shard_map.74, f32[64,64]{0,1:T(8,128)S(1)} %get-tuple-element.16, f32[64,64]{0,1:T(8,128)S(1)} %get-tuple-element.17), kind=kOutput, calls=%fused_computation.10 | convolution fusion | flops 100802560 | bytes 1605632 | tf_op jit(solution)/shard_map/rxyl,lz->rxyz/dot_general | solution.py:195
  95.2 1.6 %gather_fusion = f32[8,512]{1,0:T(8,128)S(1)} fusion(f32[256,512]{1,0:T(8,128)} %reshape.307, s32[1024]{0:T(1024)S(1)} %pad_clamp_fusion), kind=kCustom, calls=%fused_computation | custom fusion | bytes 32800 | tf_op jit(solution)/shard_map/gather | solution.py:202
  96.8 1.6 %fusion.89 = f32[8,512]{1,0:T(8,128)S(1)} fusion(f32[8,512]{1,0:T(8,128)S(1)} %gather_fusion, f32[512,512]{1,0:T(8,128)} %param.9), kind=kOutput, calls=%fused_computation.130 | convolution fusion | flops 12582912 | bytes 1081344 | tf_op jit(solution)/shard_map/dot_general | solution.py:211
  98.5 9.6 %all_to_all.5 = f32[8,2,512]{2,1,0:T(2,128)S(1)} all-to-all(f32[8,2,512]{2,1,0:T(2,128)S(1)} %reshape.309), channel_id=1, replica_groups=mesh['grp'=2,'rot'=4,'sub'=2,'ref'=2] {'rot','ref'}, dimensions={0} | all-to-all | bytes 65536 | tf_op jit(solution)/shard_map/all_to_all | solution.py:213
  (56 shorter events, 11.2 us)
Async XLA Ops:
  0.6 1.6 %copy-start = (f32[2,4,16,32,64]{4,3,2,1,0:T(8,128)S(1)}, f32[2,4,16,32,64]{4,3,2,1,0:T(8,128)}, u32[]{:S(2)}) copy-start(f32[2,4,16,32,64]{4,3,2,1,0:T(8,128)} %param.6) | copy-start | bytes 3145732
  2.6 30.4 %collective-permute-start.2 = (bf16[4,16,16,128]{3,1,2,0:T(8,128)(2,1)S(1)}, bf16[4,16,16,128]{3,1,2,0:T(8,128)(2,1)S(1)}, u32[]{:S(2)}, u32[]{:S(2)}) collective-permute-start(bf16[4,16,16,128]{3,1,2,0:T(8,128)(2,1)S(1)} %maximum_bitcast_fusion.1), channel_id=1, source_target_pairs={{0,12},{4,0},{8,4},{12,8},{1,13},{5,1},{9,5},{13,9},{2,14},{6,2},{... | collective-permute-start | bytes 786440 | tf_op jit(solution)/shard_map/ppermute | solution.py:73
  7.7 25.3 %collective-permute-start.3 = (bf16[4,16,16,128]{3,1,2,0:T(8,128)(2,1)S(1)}, bf16[4,16,16,128]{3,1,2,0:T(8,128)(2,1)S(1)}, u32[]{:S(2)}, u32[]{:S(2)}) collective-permute-start(bf16[4,16,16,128]{3,1,2,0:T(8,128)(2,1)S(1)} %maximum_bitcast_fusion.1), channel_id=1, source_target_pairs={{0,8},{4,12},{8,0},{12,4},{1,9},{5,13},{9,1},{13,5},{2,10},{6,14},... | collective-permute-start | bytes 786440 | tf_op jit(solution)/shard_map/ppermute | solution.py:73
  7.7 26.7 %collective-permute-start.4 = (bf16[4,16,16,128]{3,1,2,0:T(8,128)(2,1)S(1)}, bf16[4,16,16,128]{3,1,2,0:T(8,128)(2,1)}, u32[]{:S(2)}, u32[]{:S(2)}) collective-permute-start(bf16[4,16,16,128]{3,1,2,0:T(8,128)(2,1)S(1)} %maximum_bitcast_fusion.1), channel_id=1, source_target_pairs={{0,4},{4,8},{8,12},{12,0},{1,5},{5,9},{9,13},{13,1},{2,6},{6,10},{... | collective-permute-start | bytes 786440 | tf_op jit(solution)/shard_map/ppermute | solution.py:73
  9.0 13.7 %copy-start.5 = (f32[1,64,64]{2,1,0:T(8,128)}, f32[1,64,64]{2,1,0:T(8,128)S(1)}, u32[]{:S(2)}) copy-start(f32[1,64,64]{2,1,0:T(8,128)S(1)} %get-tuple-element.18) | copy-start | bytes 49156
  9.0 13.7 %copy-start.7 = (f32[1,64,64]{2,1,0:T(8,128)}, f32[1,64,64]{2,1,0:T(8,128)S(1)}, u32[]{:S(2)}) copy-start(f32[1,64,64]{2,1,0:T(8,128)S(1)} %get-tuple-element.19) | copy-start | bytes 49156
  18.0 3.9 %copy-start.4 = (bf16[1,4,32,64,64]{4,3,2,1,0:T(8,128)(2,1)S(1)}, bf16[1,4,32,64,64]{4,3,2,1,0:T(8,128)(2,1)}, u32[]{:S(2)}) copy-start(bf16[1,4,32,64,64]{4,3,2,1,0:T(8,128)(2,1)} %param.5) | copy-start | bytes 3145732
  20.5 16.3 %collective-permute-start = (bf16[1,2,32,32,128]{4,2,3,1,0:T(8,128)(2,1)}, bf16[1,2,32,32,128]{4,2,3,1,0:T(8,128)(2,1)S(1)}, u32[]{:S(2)}, u32[]{:S(2)}) collective-permute-start(bf16[1,2,32,32,128]{4,2,3,1,0:T(8,128)(2,1)} %copy.15), channel_id=1, source_target_pairs={{0,2},{2,0},{1,3},{3,1},{4,6},{6,4},{5,7},{7,5},{8,10},{10,8},{9,1... | collective-permute-start | bytes 1572872 | tf_op jit(solution)/shard_map/ppermute | solution.py:73
  32.1 13.0 %collective-permute-start.1 = (bf16[1,2,32,32,128]{4,2,3,1,0:T(8,128)(2,1)}, bf16[1,2,32,32,128]{4,2,3,1,0:T(8,128)(2,1)S(1)}, u32[]{:S(2)}, u32[]{:S(2)}) collective-permute-start(bf16[1,2,32,32,128]{4,2,3,1,0:T(8,128)(2,1)} %copy.18), channel_id=1, source_target_pairs={{0,2},{2,0},{1,3},{3,1},{4,6},{6,4},{5,7},{7,5},{8,10},{10,8},{9,1... | collective-permute-start | bytes 1572872 | tf_op jit(solution)/shard_map/ppermute | solution.py:73
  33.0 0.7 copy-start.9
  33.7 0.7 copy-start.10
  36.8 16.5 %collective-permute-start.5 = (bf16[4,4,16,16,128]{4,2,3,1,0:T(8,128)(2,1)}, bf16[4,4,16,16,128]{4,2,3,1,0:T(8,128)(2,1)}, u32[]{:S(2)}, u32[]{:S(2)}) collective-permute-start(bf16[4,4,16,16,128]{4,2,3,1,0:T(8,128)(2,1)} %pad_maximum_fusion), channel_id=1, source_target_pairs={{0,1},{1,0},{2,3},{3,2},{4,5},{5,4},{6,7},{7,6},{8,9},{9,8},{10,11... | collective-permute-start | bytes 3145736 | tf_op jit(solution)/shard_map/ppermute | solution.py:73
  56.8 5.0 %copy-start.6 = (f32[1,64,64]{2,1,0:T(8,128)S(1)}, f32[1,64,64]{2,1,0:T(8,128)}, u32[]{:S(2)}) copy-start(f32[1,64,64]{2,1,0:T(8,128)} %copy-done.5) | copy-start | bytes 49156
  56.8 5.0 %copy-start.8 = (f32[1,64,64]{2,1,0:T(8,128)S(1)}, f32[1,64,64]{2,1,0:T(8,128)}, u32[]{:S(2)}) copy-start(f32[1,64,64]{2,1,0:T(8,128)} %copy-done.7) | copy-start | bytes 49156
  66.5 5.3 %copy-start.11 = (s32[1,1,1,8]{3,2,1,0:T(1,128)S(1)}, s32[1,1,1,8]{3,2,1,0:T(1,128)}, u32[]{:S(2)}) copy-start(s32[1,1,1,8]{3,2,1,0:T(1,128)} %param.7) | copy-start | bytes 100
  66.5 5.3 %copy-start.12 = (s32[1,1,1,8,1]{3,4,2,1,0:T(1,128)S(1)}, s32[1,1,1,8,1]{3,4,2,1,0:T(1,128)}, u32[]{:S(2)}) copy-start(s32[1,1,1,8,1]{3,4,2,1,0:T(1,128)} %param.8) | copy-start | bytes 100
  69.1 17.6 %copy-start.2 = (f32[1,64,32,128]{3,2,1,0:T(8,128)S(1)}, f32[1,64,32,128]{3,2,1,0:T(8,128)}, u32[]{:S(2)}) copy-start(f32[1,64,32,128]{3,2,1,0:T(8,128)} %shard_map.73) | copy-start | bytes 3145732
  70.2 14.4 %collective-permute-start.6 = (f32[32,1,32,128]{3,2,0,1:T(8,128)S(1)}, f32[32,1,32,128]{3,2,0,1:T(8,128)S(1)}, u32[]{:S(2)}, u32[]{:S(2)}) collective-permute-start(f32[32,1,32,128]{3,2,0,1:T(8,128)S(1)} %dynamic-slice_bitcast_fusion), channel_id=1, source_target_pairs={{0,2},{2,0},{1,3},{3,1},{4,6},{6,4},{5,7},{7,5},{8,10},{10,8},{9,1... | collective-permute-start | bytes 1572872 | tf_op jit(solution)/shard_map/ppermute | solution.py:73
  89.1 19.7 %copy-start.1 = (f32[2,4,16,32,64]{4,3,2,1,0:T(8,128)S(1)}, f32[2,4,16,32,64]{4,3,2,1,0:T(8,128)}, u32[]{:S(2)}) copy-start(f32[2,4,16,32,64]{4,3,2,1,0:T(8,128)} %param.6) | copy-start | bytes 3145732
  94.0 14.8 %copy-start.3 = (f32[32,64,64]{2,1,0:T(8,128)}, f32[32,64,64]{2,1,0:T(8,128)S(1)}, u32[]{:S(2)}) copy-start(f32[32,64,64]{2,1,0:T(8,128)S(1)} %convolution_multiply_fusion) | copy-start | bytes 1572868

commit v11 on v8

--- a/solution.py
+++ b/solution.py
@@ -111,48 +111,51 @@
 
 def product_kernel(*refs):
     *spec_refs, rec_ref, out_ref = refs
-    lanes = out_ref.shape[-1]
+    rows, kx, lanes = out_ref.shape
     half = lanes // 2
+    low = lax.broadcasted_iota(jnp.int32, (1, lanes), 1) < half
+    signs = jnp.where(low, 1.0, -1.0).astype(jnp.float32)
     total = None
     term = 0
     for spec_ref in spec_refs:
         for inner in range(spec_ref.shape[0]):
-            spec = spec_ref[inner].astype(jnp.float32)
-            rec = rec_ref[term].astype(jnp.float32)
+            cos_part = spec_ref[inner, :, 0].reshape(rows * kx, lanes)
+            sin_part = spec_ref[inner, :, 1].reshape(rows * kx, lanes)
+            spec = cos_part + pltpu.roll(sin_part, half, 1) * signs
+            spec = spec.astype(jnp.bfloat16).astype(jnp.float32)
+            rec = rec_ref[term].reshape(rows * kx, lanes).astype(jnp.float32)
             term += 1
-            low = lax.broadcasted_iota(jnp.int32, (1, lanes), 1) < half
             rec_turned = pltpu.roll(rec, half, 1)
             rec_real = jnp.where(low, rec, rec_turned)
             rec_imag = jnp.where(low, rec_turned, -rec)
             part = rec_real * spec + rec_imag * pltpu.roll(spec, half, 1)
             total = part if total is None else total + part
-    out_ref[...] = total
-
-
-def correlate(spectra, receptor):
-    rots, _, kx, ky, lanes = spectra[0].shape
+    out_ref[...] = total.reshape(rows, kx, lanes)
+
+
+def correlate(parts, receptor):
+    rots, _, ky, _, kx, lanes = parts[0].shape
     terms = receptor.shape[0]
-    rows = kx * ky
-    block = min(rows, 512)
-    specs = [part.reshape(rots, part.shape[1], rows, lanes) for part in spectra]
-    rec = receptor.reshape(terms, rows, lanes)
+    block = 8 if ky % 8 == 0 else ky
     out = pl.pallas_call(
         product_kernel,
-        grid=(rots, rows // block),
+        grid=(rots, ky // block),
         in_specs=[
-            pl.BlockSpec((None, part.shape[1], block, lanes), lambda r, i: (r, 0, i, 0))
-            for part in specs
+            pl.BlockSpec(
+                (None, part.shape[1], block, 2, kx, lanes), lambda r, i: (r, 0, i, 0, 0, 0)
+            )
+            for part in parts
         ]
-        + [pl.BlockSpec((terms, block, lanes), lambda r, i: (0, i, 0))],
-        out_specs=pl.BlockSpec((None, block, lanes), lambda r, i: (r, i, 0)),
-        out_shape=jax.ShapeDtypeStruct((rots, rows, lanes), jnp.float32),
+        + [pl.BlockSpec((terms, block, kx, lanes), lambda r, i: (0, i, 0, 0))],
+        out_specs=pl.BlockSpec((None, block, kx, lanes), lambda r, i: (r, i, 0, 0)),
+        out_shape=jax.ShapeDtypeStruct((rots, ky, kx, lanes), jnp.float32),
         cost_estimate=pl.CostEstimate(
-            flops=8 * rots * terms * rows * lanes,
-            bytes_accessed=2 * (rots + 1) * terms * rows * lanes + 4 * rots * rows * lanes,
+            flops=11 * rots * terms * ky * kx * lanes,
+            bytes_accessed=(8 * rots + 2) * terms * ky * kx * lanes + 4 * rots * ky * kx * lanes,
             transcendentals=0,
         ),
-    )(*specs, rec)
-    return out.reshape(rots, kx, ky, lanes)
+    )(*parts, receptor)
+    return out
 
 
 def local(ligand, receptor, tile_list, tile_owner, refine_weight):
@@ -184,10 +187,7 @@
             )
             for source, piece in enumerate(by_source(exchange(sending, "sub", rotated=True)))
         )
-        spectrum = combine_call(
-            along_x.reshape(-1, 2, length, 2 * length), 1.0, -1.0, 1, jnp.bfloat16
-        )
-        spectra.append(spectrum.reshape(rots, part_terms, y_local, length, 2 * length))
+        spectra.append(along_x)
 
     whole_receptor = gather_receptor(receptor)
     product = correlate(spectra, whole_receptor)

time: 110 us -> 114 us (1.036)
  local copies, waits for them, and re-layouts: 17.1 us -> 22.7 us
  Pallas kernels: 24 us -> 18.9 us
  matrix products: 30.1 us -> 32.3 us
  waiting for transfers between devices: 13.1 us -> 15 us
  blocking collectives: 9.63 us -> 8.12 us
    pallas_call x6 -> x4, Pallas kernels: 19 us -> 12.2 us  [combine_call(): pl.pallas_call(functools.partial(combine_kernel, first=first, second=seco...]
    unnamed x29 -> x31, local copies, waits for them, and re-layouts: 2.45 us -> 8.19 us
    dot_general x4, matrix products: 9.81 us -> 11.9 us  [local(): jnp.einsum('ekx,rtxjl->rtjekl', pair_x[:, :, source], piece.astype(jnp.fl...]
    ppermute x3, waiting for transfers between devices: 13.1 us -> 15 us  [exchange(): lax.ppermute(entry(shift), axis, pairs)]
    pallas_call x1, Pallas kernels: 4.94 us -> 6.68 us  [correlate(): pl.pallas_call(product_kernel, grid=(rots, ky // block), in_specs=[pl.Blo...]
    all_to_all x1, blocking collectives: 9.63 us -> 8.12 us  [local(): lax.all_to_all(packed, ('rot', 'ref'), split_axis=0, concat_axis=0, tiled...]
    transpose x1, other arithmetic: 2.68 us -> 1.44 us  [gather_receptor(): both = jnp.transpose(both, (2, 0, 3, 1, 4, 5))]
  transfers between devices with their start and end apart: 7 -> 7, of which waited for: 2 -> 2; matrix products, arithmetic and copies ran while one was open for 25% -> 31% of each run, Pallas kernels for 12% -> 6%
where the time goes in v11:
time: 114 us; the launch traced here: 113 us
  matrix products  32.3 us (28%)
  local copies, waits for them, and re-layouts  22.7 us (20%)
  Pallas kernels  18.9 us (17%)
  waiting for transfers between devices  15 us (13%)
  starting transfers between devices  10.5 us (9%)
  blocking collectives  8.12 us (7%)
  other arithmetic  4.32 us (4%)
    ppermute x3, waiting for transfers between devices, exchange(): lax.ppermute(entry(shift), axis, pairs)  15 us
    pallas_call x4, Pallas kernels, combine_call(): pl.pallas_call(functools.partial(combine_kernel, first=first, second=seco...  12.2 us
    dot_general x4, matrix products, local(): jnp.einsum('ekx,rtxjl->rtjekl', pair_x[:, :, source], piece.astype(jnp.fl...  11.9 us
    unnamed x31, local copies, waits for them, and re-layouts  8.19 us
    all_to_all x1, blocking collectives, local(): lax.all_to_all(packed, ('rot', 'ref'), split_axis=0, concat_axis=0, tiled...  8.12 us
    dot_general x2, matrix products, local(): along_y = jnp.einsum('ejy,rtxyl->rtxejl', pair, along_z, precision=highest)  7.44 us
    ppermute x4, starting transfers between devices, gather_by_shifts(): pieces.append(lax.ppermute(piece, axis, pairs))  7.03 us
    pallas_call x1, Pallas kernels, correlate(): pl.pallas_call(product_kernel, grid=(rots, ky // block), in_specs=[pl.Blo...  6.68 us
  transfers between devices with their start and end apart: 7, of which 2 were waited for; matrix products, arithmetic and copies ran while one was open for 31% of the time, Pallas kernels for 6%

profile of v11, /device:TPU:0, one launch (start us, length us, event | category | flops | bytes accessed | tf_op | source)
XLA Modules:
  0.0 112.9 jit_solution(12142565581136141300)
XLA Ops:
  0.6 1.6 %copy-done = f32[2,4,16,32,64]{4,3,2,1,0:T(8,128)S(1)} copy-done((f32[2,4,16,32,64]{4,3,2,1,0:T(8,128)S(1)}, f32[2,4,16,32,64]{4,3,2,1,0:T(8,128)}, u32[]{:S(2)}) %copy-start) | copy-done | bytes 1048600
  3.2 3.0 %collective-permute-start.4 = (bf16[4,16,16,128]{3,1,2,0:T(8,128)(2,1)}, bf16[4,16,16,128]{3,1,2,0:T(8,128)(2,1)}, u32[]{:S(2)}, u32[]{:S(2)}) collective-permute-start(bf16[4,16,16,128]{3,1,2,0:T(8,128)(2,1)} %fusion.92), channel_id=1, source_target_pairs={{0,4},{4,8},{8,12},{12,0},{1,5},{5,9},{9,13},{13,1},{2,6},{6,10},{... | collective-permute-start | bytes 786440 | tf_op jit(solution)/shard_map/ppermute | solution.py:67
  6.3 2.6 %collective-permute-start.3 = (bf16[4,16,16,128]{3,1,2,0:T(8,128)(2,1)}, bf16[4,16,16,128]{3,1,2,0:T(8,128)(2,1)}, u32[]{:S(2)}, u32[]{:S(2)}) collective-permute-start(bf16[4,16,16,128]{3,1,2,0:T(8,128)(2,1)} %fusion.92), channel_id=1, source_target_pairs={{0,8},{4,12},{8,0},{12,4},{1,9},{5,13},{9,1},{13,5},{2,10},{6,14},... | collective-permute-start | bytes 786440 | tf_op jit(solution)/shard_map/ppermute | solution.py:67
  8.9 1.3 %collective-permute-start.2 = (bf16[4,16,16,128]{3,1,2,0:T(8,128)(2,1)}, bf16[4,16,16,128]{3,1,2,0:T(8,128)(2,1)}, u32[]{:S(2)}, u32[]{:S(2)}) collective-permute-start(bf16[4,16,16,128]{3,1,2,0:T(8,128)(2,1)} %fusion.92), channel_id=1, source_target_pairs={{0,12},{4,0},{8,4},{12,8},{1,13},{5,1},{9,5},{13,9},{2,14},{6,2},{... | collective-permute-start | bytes 786440 | tf_op jit(solution)/shard_map/ppermute | solution.py:67
  10.5 1.9 %fusion.11 = f32[128,2,32,64]{0,3,2,1:T(8,128)S(1)} fusion(bf16[1,4,32,64,64]{4,3,2,1,0:T(8,128)(2,1)} %param.5, f32[64,64]{0,1:T(8,128)S(1)} %get-tuple-element.10, f32[64,64]{0,1:T(8,128)S(1)} %get-tuple-element.11), kind=kOutput, calls=%fused_computation.21 | convolution fusion | flops 201334784 | bytes 3178496 | tf_op jit(solution)/shard_map/rtxyz,zl->rtxyl/dot_general | solution.py:177
  12.5 3.7 %fusion.4 = f32[2,32,128,2,64]{2,4,3,1,0:T(8,128)} fusion(f32[128,2,32,64]{0,3,2,1:T(8,128)S(1)} %fusion.11, f32[1,64,64]{2,1,0:T(8,128)S(1)} %get-tuple-element.12, f32[1,64,64]{2,1,0:T(8,128)S(1)} %get-tuple-element.13), kind=kOutput, calls=%fused_computation.11 | convolution fusion | flops 402661376 | bytes 6324224 | tf_op jit(solution)/shard_map/ejy,rtxyl->rtxejl/dot_general | solution.py:178
  16.2 3.4 %shard_map.69 = bf16[2,64,32,128]{3,2,1,0:T(8,128)(2,1)} custom-call(s32[1]{0:T(128)} %bitcast.me_ref, f32[64,2,64,128]{3,2,1,0:T(8,128)} %bitcast.192), custom_call_target="tpu_custom_call" | custom-call | flops 1572864 | bytes 5242880 | tf_op jit(solution)/shard_map/pallas_call | solution.py:44
  19.6 1.4 %fusion.93 = (bf16[1,64,32,128]{3,2,1,0:T(8,128)(2,1)S(1)}, bf16[1,64,32,128]{3,2,1,0:T(8,128)(2,1)S(1)}) fusion(bf16[2,64,32,128]{3,2,1,0:T(8,128)(2,1)} %shard_map.69), kind=kLoop, calls=%fused_computation.139 | loop fusion | bytes 2097152 | tf_op jit(solution)/shard_map/slice | solution.py:78
  22.0 1.5 %collective-permute-start.1 = (bf16[1,2,32,32,128]{4,2,3,1,0:T(8,128)(2,1)}, bf16[1,2,32,32,128]{4,2,3,1,0:T(8,128)(2,1)}, u32[]{:S(2)}, u32[]{:S(2)}) collective-permute-start(bf16[1,2,32,32,128]{4,2,3,1,0:T(8,128)(2,1)} %copy.18), channel_id=1, source_target_pairs={{0,2},{2,0},{1,3},{3,1},{4,6},{6,4},{5,7},{7,5},{8,10},{10,8},{9,1... | collective-permute-start | bytes 1572872 | tf_op jit(solution)/shard_map/ppermute | solution.py:84
  24.2 3.7 %fusion.6 = f32[2,32,128,2,64]{2,4,3,1,0:T(8,128)} fusion(f32[128,2,32,64]{0,3,2,1:T(8,128)S(1)} %fusion.13, f32[1,64,64]{2,1,0:T(8,128)S(1)} %get-tuple-element.12, f32[1,64,64]{2,1,0:T(8,128)S(1)} %get-tuple-element.13), kind=kOutput, calls=%fused_computation.13 | convolution fusion | flops 402661376 | bytes 6324224 | tf_op jit(solution)/shard_map/ejy,rtxyl->rtxejl/dot_general | solution.py:178
  28.0 3.4 %shard_map.68 = bf16[2,64,32,128]{3,2,1,0:T(8,128)(2,1)} custom-call(s32[1]{0:T(128)} %bitcast.me_ref, f32[64,2,64,128]{3,2,1,0:T(8,128)} %bitcast.193), custom_call_target="tpu_custom_call" | custom-call | flops 1572864 | bytes 5242880 | tf_op jit(solution)/shard_map/pallas_call | solution.py:44
  42.3 4.2 %collective-permute-done = bf16[1,2,32,32,128]{4,2,3,1,0:T(8,128)(2,1)} collective-permute-done((bf16[1,2,32,32,128]{4,2,3,1,0:T(8,128)(2,1)}, bf16[1,2,32,32,128]{4,2,3,1,0:T(8,128)(2,1)}, u32[]{:S(2)}, u32[]{:S(2)}) %collective-permute-start) | collective-permute-done | bytes 524320 | tf_op jit(solution)/shard_map/ppermute | solution.py:84
  46.4 2.3 %fusion.23 = f32[2,32,128,2,64]{2,4,3,1,0:T(8,128)S(1)} fusion(bf16[1,2,32,32,128]{4,2,3,1,0:T(8,128)(2,1)} %collective-permute-done, pred[]{:T(512)S(6)} %eq.47, bf16[1,2,32,32,128]{4,3,2,1,0:T(8,128)(2,1)S(1)} %bitcast.196, f32[1,64,2,32]{1,3,0,2:T(8,128)S(1)} %get-tuple-element.9, f32[1,64,2,32]{1,3,0,2:T(8,128)S(1)} %get-tuple-element.8), kind=kOutput, calls=%fused_computation.34 | convolution fusion | flops 201592832 | bytes 5275649 | tf_op jit(solution)/shard_map/ekx,rtxjl->rtjekl/dot_general | solution.py:184
  48.8 3.6 %add_bitcast_fusion.1.refs_0_ = f32[1,2,32,2,64,128]{5,4,3,2,1,0:T(8,128)} fusion(f32[2,32,128,2,64]{2,4,3,1,0:T(8,128)S(1)} %fusion.23, bf16[1,2,32,32,128]{4,2,3,1,0:T(8,128)(2,1)} %collective-permute-done, pred[]{:T(512)S(6)} %eq.46, bf16[1,2,32,32,128]{4,3,2,1,0:T(8,128)(2,1)S(1)} %bitcast.197, f32[1,64,2,32]{1,3,0,2:T(8,128)S(1)} %get-tuple-element.8, ...), kind=kOutput, calls=%fused_computation.6 | convolution fusion | flops 202641408 | bytes 9469953 | tf_op jit(solution)/shard_map/ekx,rtxjl->rtjekl/dot_general | solution.py:184
  52.4 2.3 %fusion.20 = f32[2,32,128,2,64]{2,4,3,1,0:T(8,128)S(1)} fusion(bf16[1,2,32,32,128]{4,2,3,1,0:T(8,128)(2,1)} %collective-permute-done.1, pred[]{:T(512)S(6)} %eq.47, bf16[1,2,32,32,128]{4,3,2,1,0:T(8,128)(2,1)S(1)} %bitcast.194, f32[1,64,2,32]{1,3,0,2:T(8,128)S(1)} %get-tuple-element.9, f32[1,64,2,32]{1,3,0,2:T(8,128)S(1)} %get-tuple-element.8), kind=kOutput, calls=%fused_computation.31 | convolution fusion | flops 201592832 | bytes 5275649 | tf_op jit(solution)/shard_map/ekx,rtxjl->rtjekl/dot_general | solution.py:184
  54.7 3.6 %add_bitcast_fusion.refs_1_ = f32[1,2,32,2,64,128]{5,4,3,2,1,0:T(8,128)} fusion(f32[2,32,128,2,64]{2,4,3,1,0:T(8,128)S(1)} %fusion.20, bf16[1,2,32,32,128]{4,2,3,1,0:T(8,128)(2,1)} %collective-permute-done.1, pred[]{:T(512)S(6)} %eq.46, bf16[1,2,32,32,128]{4,3,2,1,0:T(8,128)(2,1)S(1)} %bitcast.195, f32[1,64,2,32]{1,3,0,2:T(8,128)S(1)} %get-tuple-element.8, ...), kind=kOutput, calls=%fused_computation.5 | convolution fusion | flops 202641408 | bytes 9469953 | tf_op jit(solution)/shard_map/ekx,rtxjl->rtjekl/dot_general | solution.py:184
  58.4 1.4 %fusion.3 = bf16[4,2,16,4,16,128]{5,2,4,0,3,1:T(8,128)(2,1)S(1)} fusion(s32[]{:T(128)S(6)} %select_n.146, bf16[1,4,4,16,16,128]{5,3,4,2,1,0:T(8,128)(2,1)S(1)} %bitcast.206, bf16[1,4,4,16,16,128]{5,3,4,2,1,0:T(8,128)(2,1)S(1)} %fusion.99), kind=kLoop, calls=%fused_computation.10 | loop fusion | flops 3145728 | bytes 4194308 | tf_op jit(solution)/shard_map/transpose | solution.py:108
  59.8 1.9 %copy.21 = bf16[4,2,16,4,16,128]{5,4,3,2,1,0:T(8,128)(2,1)} copy(bf16[4,2,16,4,16,128]{5,2,4,0,3,1:T(8,128)(2,1)S(1)} %fusion.3) | data formatting | bytes 4194304 | tf_op jit(solution)/shard_map/transpose | solution.py:108
  61.7 6.7 %shard_map.70 = f32[1,32,64,128]{3,2,1,0:T(8,128)} custom-call(f32[1,2,32,2,64,128]{5,4,3,2,1,0:T(8,128)} %add_bitcast_fusion.1.refs_0_, f32[1,2,32,2,64,128]{5,4,3,2,1,0:T(8,128)} %add_bitcast_fusion.refs_1_, bf16[4,32,64,128]{3,2,1,0:T(8,128)(2,1)} %bitcast.199), custom_call_target="tpu_custom_call" | custom-call | flops 11534336 | bytes 11534336 | tf_op jit(solution)/shard_map/pallas_call | solution.py:140
  68.4 2.2 %fusion.8 = f32[32,128,2,64]{1,3,2,0:T(8,128)S(1)} fusion(f32[1,32,64,128]{3,2,1,0:T(8,128)} %shard_map.70, f32[1,64,64]{2,1,0:T(8,128)S(1)} %copy-done.7, f32[1,64,64]{2,1,0:T(8,128)S(1)} %copy-done.9), kind=kOutput, calls=%fused_computation.18 | convolution fusion | flops 201334784 | bytes 3178496 | tf_op jit(solution)/shard_map/exk,rjkl->xrejl/dot_general | solution.py:195
  70.6 2.5 %copy.53 = f32[32,128,2,64]{1,0,2,3:T(8,128)} copy(f32[32,128,2,64]{1,3,2,0:T(8,128)S(1)} %fusion.8) | data formatting | bytes 4194304 | tf_op jit(solution)/shard_map/exk,rjkl->xrejl/dot_general | solution.py:195
  73.2 2.6 %shard_map.71 = f32[1,64,32,128]{3,2,1,0:T(8,128)} custom-call(s32[1]{0:T(128)} %constant.80.clone.1.me_ref, f32[64,2,32,128]{3,2,1,0:T(8,128)} %bitcast.198), custom_call_target="tpu_custom_call" | custom-call | flops 786432 | bytes 3145728 | tf_op jit(solution)/shard_map/pallas_call | solution.py:44
  75.8 2.0 %dynamic-slice_bitcast_fusion = f32[32,1,32,128]{3,2,0,1:T(8,128)} fusion(f32[2,32,1,32,128]{4,3,1,0,2:T(8,128)} %bitcast.200, s32[]{:T(128)S(6)} %select_n.148), kind=kLoop, calls=%fused_computation.39 | loop fusion | bytes 1048580 | tf_op jit(solution)/shard_map/jit(dynamic_index_in_dim)/squeeze | solution.py:79
  77.7 1.4 %collective-permute-start.6 = (f32[32,1,32,128]{3,2,0,1:T(8,128)}, f32[32,1,32,128]{3,2,0,1:T(8,128)}, u32[]{:S(2)}, u32[]{:S(2)}) collective-permute-start(f32[32,1,32,128]{3,2,0,1:T(8,128)} %dynamic-slice_bitcast_fusion), channel_id=1, source_target_pairs={{0,2},{2,0},{1,3},{3,1},{4,6},{6,4},{5,7},{7,5},{8,10},{10,8},{9,1... | collective-permute-start | bytes 1572872 | tf_op jit(solution)/shard_map/ppermute | solution.py:84
  79.4 10.9 %collective-permute-done.6 = f32[32,1,32,128]{3,2,0,1:T(8,128)} collective-permute-done((f32[32,1,32,128]{3,2,0,1:T(8,128)}, f32[32,1,32,128]{3,2,0,1:T(8,128)}, u32[]{:S(2)}, u32[]{:S(2)}) %collective-permute-start.6) | collective-permute-done | bytes 524320 | tf_op jit(solution)/shard_map/ppermute | solution.py:84
  90.2 2.2 %fusion.17 = f32[32,128,2,64]{1,3,2,0:T(8,128)S(1)} fusion(f32[32,1,32,128]{3,2,0,1:T(8,128)} %collective-permute-done.6, f32[2,32,1,32,128]{4,3,1,0,2:T(8,128)} %bitcast.201, s32[]{:T(128)S(6)} %select_n.150, pred[]{:T(512)S(6)} %eq.47, f32[1,64,2,32]{1,3,0,2:T(8,128)S(1)} %get-tuple-element.9, f32[1,64,2,32]{1,3,0,2:T(8,128)S(1)} %get-tuple-element.8), kind=kOutput, calls=%fused_computation.28 | convolution fusion | flops 100798464 | bytes 3178501 | tf_op jit(solution)/shard_map/eyj,xrjl->rxeyl/dot_general | solution.py:200
  92.5 2.4 %add_bitcast_fusion.2.in_ref = f32[32,2,64,128]{3,2,1,0:T(8,128)} fusion(f32[32,128,2,64]{1,3,2,0:T(8,128)S(1)} %fusion.17, f32[32,1,32,128]{3,2,0,1:T(8,128)} %collective-permute-done.6, f32[2,32,1,32,128]{4,3,1,0,2:T(8,128)S(1)} %bitcast.202, s32[]{:T(128)S(6)} %select_n.150, pred[]{:T(512)S(6)} %eq.46, f32[1,64,2,32]{1,3,0,2:T(8,128)S(1)} %get-tuple-element.8, ...), kind=kOutput, calls=%fused_computation.16 | convolution fusion | flops 101322752 | bytes 5308421 | tf_op jit(solution)/shard_map/eyj,xrjl->rxeyl/dot_general | solution.py:200
  94.8 2.9 %shard_map.72 = f32[1,32,64,128]{3,2,1,0:T(8,128)} custom-call(s32[1]{0:T(128)} %constant.80.clone.1.me_ref, f32[32,2,64,128]{3,2,1,0:T(8,128)} %add_bitcast_fusion.2.in_ref), custom_call_target="tpu_custom_call" | custom-call | flops 786432 | bytes 3145728 | tf_op jit(solution)/shard_map/pallas_call | solution.py:44
  97.7 1.9 %convolution_multiply_fusion = f32[32,64,64]{2,1,0:T(8,128)S(1)} fusion(f32[1,32,64,128]{3,2,1,0:T(8,128)} %shard_map.72, f32[64,64]{0,1:T(8,128)S(1)} %get-tuple-element.10, f32[64,64]{0,1:T(8,128)S(1)} %get-tuple-element.11), kind=kOutput, calls=%fused_computation.17 | convolution fusion | flops 100802560 | bytes 1605632 | tf_op jit(solution)/shard_map/rxyl,lz->rxyz/dot_general | solution.py:206
  100.8 1.6 %gather_fusion = f32[8,512]{1,0:T(8,128)S(1)} fusion(f32[256,512]{1,0:T(8,128)} %reshape.301, s32[1024]{0:T(1024)S(1)} %pad_clamp_fusion), kind=kCustom, calls=%fused_computation | custom fusion | bytes 32800 | tf_op jit(solution)/shard_map/gather | solution.py:213
  102.4 1.6 %fusion.95 = f32[8,512]{1,0:T(8,128)S(1)} fusion(f32[8,512]{1,0:T(8,128)S(1)} %gather_fusion, f32[512,512]{1,0:T(8,128)} %param.9), kind=kOutput, calls=%fused_computation.141 | convolution fusion | flops 12582912 | bytes 1081344 | tf_op jit(solution)/shard_map/dot_general | solution.py:222
  104.1 8.1 %all_to_all.5 = f32[8,2,512]{2,1,0:T(2,128)S(1)} all-to-all(f32[8,2,512]{2,1,0:T(2,128)S(1)} %reshape.303), channel_id=1, replica_groups=mesh['grp'=2,'rot'=4,'sub'=2,'ref'=2] {'rot','ref'}, dimensions={0} | all-to-all | bytes 65536 | tf_op jit(solution)/shard_map/all_to_all | solution.py:224
  (59 shorter events, 16.0 us)
Async XLA Ops:
  0.6 1.6 %copy-start = (f32[2,4,16,32,64]{4,3,2,1,0:T(8,128)S(1)}, f32[2,4,16,32,64]{4,3,2,1,0:T(8,128)}, u32[]{:S(2)}) copy-start(f32[2,4,16,32,64]{4,3,2,1,0:T(8,128)} %param.6) | copy-start | bytes 3145732
  2.4 13.8 %copy-start.2 = (bf16[4,16,16,64]{3,2,1,0:T(8,128)(2,1)}, bf16[4,16,16,64]{3,2,1,0:T(8,128)(2,1)S(1)}, u32[]{:S(2)}) copy-start(bf16[4,16,16,64]{3,2,1,0:T(8,128)(2,1)S(1)} %get-tuple-element.7) | copy-start | bytes 393220
  3.2 33.2 %collective-permute-start.4 = (bf16[4,16,16,128]{3,1,2,0:T(8,128)(2,1)}, bf16[4,16,16,128]{3,1,2,0:T(8,128)(2,1)}, u32[]{:S(2)}, u32[]{:S(2)}) collective-permute-start(bf16[4,16,16,128]{3,1,2,0:T(8,128)(2,1)} %fusion.92), channel_id=1, source_target_pairs={{0,4},{4,8},{8,12},{12,0},{1,5},{5,9},{9,13},{13,1},{2,6},{6,10},{... | collective-permute-start | bytes 786440 | tf_op jit(solution)/shard_map/ppermute | solution.py:67
  6.3 29.2 %collective-permute-start.3 = (bf16[4,16,16,128]{3,1,2,0:T(8,128)(2,1)}, bf16[4,16,16,128]{3,1,2,0:T(8,128)(2,1)}, u32[]{:S(2)}, u32[]{:S(2)}) collective-permute-start(bf16[4,16,16,128]{3,1,2,0:T(8,128)(2,1)} %fusion.92), channel_id=1, source_target_pairs={{0,8},{4,12},{8,0},{12,4},{1,9},{5,13},{9,1},{13,5},{2,10},{6,14},... | collective-permute-start | bytes 786440 | tf_op jit(solution)/shard_map/ppermute | solution.py:67
  8.9 25.6 %collective-permute-start.2 = (bf16[4,16,16,128]{3,1,2,0:T(8,128)(2,1)}, bf16[4,16,16,128]{3,1,2,0:T(8,128)(2,1)}, u32[]{:S(2)}, u32[]{:S(2)}) collective-permute-start(bf16[4,16,16,128]{3,1,2,0:T(8,128)(2,1)} %fusion.92), channel_id=1, source_target_pairs={{0,12},{4,0},{8,4},{12,8},{1,13},{5,1},{9,5},{13,9},{2,14},{6,2},{... | collective-permute-start | bytes 786440 | tf_op jit(solution)/shard_map/ppermute | solution.py:67
  10.4 13.9 %copy-start.6 = (f32[1,64,64]{2,1,0:T(8,128)}, f32[1,64,64]{2,1,0:T(8,128)S(1)}, u32[]{:S(2)}) copy-start(f32[1,64,64]{2,1,0:T(8,128)S(1)} %get-tuple-element.12) | copy-start | bytes 49156
  10.4 13.9 %copy-start.8 = (f32[1,64,64]{2,1,0:T(8,128)}, f32[1,64,64]{2,1,0:T(8,128)S(1)}, u32[]{:S(2)}) copy-start(f32[1,64,64]{2,1,0:T(8,128)S(1)} %get-tuple-element.13) | copy-start | bytes 49156
  19.6 3.9 %copy-start.5 = (bf16[1,4,32,64,64]{4,3,2,1,0:T(8,128)(2,1)S(1)}, bf16[1,4,32,64,64]{4,3,2,1,0:T(8,128)(2,1)}, u32[]{:S(2)}) copy-start(bf16[1,4,32,64,64]{4,3,2,1,0:T(8,128)(2,1)} %param.5) | copy-start | bytes 3145732
  22.0 30.4 %collective-permute-start.1 = (bf16[1,2,32,32,128]{4,2,3,1,0:T(8,128)(2,1)}, bf16[1,2,32,32,128]{4,2,3,1,0:T(8,128)(2,1)}, u32[]{:S(2)}, u32[]{:S(2)}) collective-permute-start(bf16[1,2,32,32,128]{4,2,3,1,0:T(8,128)(2,1)} %copy.18), channel_id=1, source_target_pairs={{0,2},{2,0},{1,3},{3,1},{4,6},{6,4},{5,7},{7,5},{8,10},{10,8},{9,1... | collective-permute-start | bytes 1572872 | tf_op jit(solution)/shard_map/ppermute | solution.py:84
  33.6 12.9 %collective-permute-start = (bf16[1,2,32,32,128]{4,2,3,1,0:T(8,128)(2,1)}, bf16[1,2,32,32,128]{4,2,3,1,0:T(8,128)(2,1)}, u32[]{:S(2)}, u32[]{:S(2)}) collective-permute-start(bf16[1,2,32,32,128]{4,2,3,1,0:T(8,128)(2,1)} %copy.15), channel_id=1, source_target_pairs={{0,2},{2,0},{1,3},{3,1},{4,6},{6,4},{5,7},{7,5},{8,10},{10,8},{9,1... | collective-permute-start | bytes 1572872 | tf_op jit(solution)/shard_map/ppermute | solution.py:84
  34.4 7.2 %copy-start.3 = (bf16[4,16,16,64]{3,2,1,0:T(8,128)(2,1)S(1)}, bf16[4,16,16,64]{3,2,1,0:T(8,128)(2,1)}, u32[]{:S(2)}) copy-start(bf16[4,16,16,64]{3,2,1,0:T(8,128)(2,1)} %copy-done.2) | copy-start | bytes 393220
  42.0 16.4 %collective-permute-start.5 = (bf16[4,4,16,16,128]{4,2,3,1,0:T(8,128)(2,1)S(1)}, bf16[4,4,16,16,128]{4,2,3,1,0:T(8,128)(2,1)S(1)}, u32[]{:S(2)}, u32[]{:S(2)}) collective-permute-start(bf16[4,4,16,16,128]{4,2,3,1,0:T(8,128)(2,1)S(1)} %constant_dynamic-slice_fusion), channel_id=1, source_target_pairs={{0,1},{1,0},{2,3},{3,2},{4,5},{5,4},{6,7},{7,6},{8,9},{9,8},{10,11... | collective-permute-start | bytes 3145736 | tf_op jit(solution)/shard_map/ppermute | solution.py:67
  61.7 6.7 %copy-start.7 = (f32[1,64,64]{2,1,0:T(8,128)S(1)}, f32[1,64,64]{2,1,0:T(8,128)}, u32[]{:S(2)}) copy-start(f32[1,64,64]{2,1,0:T(8,128)} %copy-done.6) | copy-start | bytes 49156
  61.7 6.7 %copy-start.9 = (f32[1,64,64]{2,1,0:T(8,128)S(1)}, f32[1,64,64]{2,1,0:T(8,128)}, u32[]{:S(2)}) copy-start(f32[1,64,64]{2,1,0:T(8,128)} %copy-done.8) | copy-start | bytes 49156
  73.2 6.0 %copy-start.10 = (s32[1,1,1,8]{3,2,1,0:T(1,128)S(1)}, s32[1,1,1,8]{3,2,1,0:T(1,128)}, u32[]{:S(2)}) copy-start(s32[1,1,1,8]{3,2,1,0:T(1,128)} %param.7) | copy-start | bytes 100
  73.2 6.0 %copy-start.11 = (s32[1,1,1,8,1]{3,4,2,1,0:T(1,128)S(1)}, s32[1,1,1,8,1]{3,4,2,1,0:T(1,128)}, u32[]{:S(2)}) copy-start(s32[1,1,1,8,1]{3,4,2,1,0:T(1,128)} %param.8) | copy-start | bytes 100
  75.7 16.7 %copy-start.1 = (f32[1,64,32,128]{3,2,1,0:T(8,128)S(1)}, f32[1,64,32,128]{3,2,1,0:T(8,128)}, u32[]{:S(2)}) copy-start(f32[1,64,32,128]{3,2,1,0:T(8,128)} %shard_map.71) | copy-start | bytes 3145732
  77.7 12.5 %collective-permute-start.6 = (f32[32,1,32,128]{3,2,0,1:T(8,128)}, f32[32,1,32,128]{3,2,0,1:T(8,128)}, u32[]{:S(2)}, u32[]{:S(2)}) collective-permute-start(f32[32,1,32,128]{3,2,0,1:T(8,128)} %dynamic-slice_bitcast_fusion), channel_id=1, source_target_pairs={{0,2},{2,0},{1,3},{3,1},{4,6},{6,4},{5,7},{7,5},{8,10},{10,8},{9,1... | collective-permute-start | bytes 1572872 | tf_op jit(solution)/shard_map/ppermute | solution.py:84
  99.6 13.2 %copy-start.4 = (f32[32,64,64]{2,1,0:T(8,128)}, f32[32,64,64]{2,1,0:T(8,128)S(1)}, u32[]{:S(2)}) copy-start(f32[32,64,64]{2,1,0:T(8,128)S(1)} %convolution_multiply_fusion) | copy-start | bytes 1572868

commit v12 on v8

--- a/solution.py
+++ b/solution.py
@@ -39,7 +39,7 @@
 
 def combine_call(stacked, first, second, split, dtype, me=0):
     batch, _, rows, lanes = stacked.shape
-    block = max(b for b in range(1, 33) if batch % b == 0)
+    block = max(b for b in range(1, 9) if batch % b == 0)
     part = rows // split
     return pl.pallas_call(
         functools.partial(combine_kernel, first=first, second=second),

time: 110 us -> 126 us (1.15)
  Pallas kernels: 24 us -> 39.7 us
    pallas_call x6, Pallas kernels: 19 us -> 34.8 us  [combine_call(): pl.pallas_call(functools.partial(combine_kernel, first=first, second=seco...]
  transfers between devices with their start and end apart: 7 -> 7, of which waited for: 2 -> 1; matrix products, arithmetic and copies ran while one was open for 25% -> 22% of each run, Pallas kernels for 12% -> 20%
where the time goes in v12:
time: 126 us; the launch traced here: 125 us
  Pallas kernels  39.7 us (32%)
  matrix products  30.1 us (24%)
  local copies, waits for them, and re-layouts  17.1 us (14%)
  waiting for transfers between devices  13 us (10%)
  starting transfers between devices  9.65 us (8%)
  blocking collectives  9.63 us (8%)
  other arithmetic  4.63 us (4%)
    pallas_call x6, Pallas kernels, combine_call(): pl.pallas_call(functools.partial(combine_kernel, first=first, second=seco...  34.8 us
    ppermute x3, waiting for transfers between devices, exchange(): lax.ppermute(entry(shift), axis, pairs)  13 us
    dot_general x4, matrix products, local(): jnp.einsum('ekx,rtxjl->rtjekl', pair_x[:, :, source], piece.astype(jnp.fl...  9.8 us
    all_to_all x1, blocking collectives, local(): lax.all_to_all(packed, ('rot', 'ref'), split_axis=0, concat_axis=0, tiled...  9.63 us
    dot_general x2, matrix products, local(): along_y = jnp.einsum('ejy,rtxyl->rtxejl', pair, along_z, precision=highest)  7.45 us
    ppermute x4, starting transfers between devices, gather_by_shifts(): pieces.append(lax.ppermute(piece, axis, pairs))  6.06 us
    pallas_call x1, Pallas kernels, correlate(): pl.pallas_call(product_kernel, grid=(rots, rows // block), in_specs=[pl.B...  4.94 us
    dot_general x2, matrix products, local(): jnp.einsum('eyj,xrjl->rxeyl', pair_y[:, :, source], piece, precision=high...  4.42 us
  transfers between devices with their start and end apart: 7, of which 1 were waited for; matrix products, arithmetic and copies ran while one was open for 22% of the time, Pallas kernels for 20%

profile of v12, /device:TPU:0, one launch (start us, length us, event | category | flops | bytes accessed | tf_op | source)
XLA Modules:
  0.0 124.8 jit_solution(10141853331315373469)
XLA Ops:
  0.7 1.6 %copy-done = f32[2,4,16,32,64]{4,3,2,1,0:T(8,128)S(1)} copy-done((f32[2,4,16,32,64]{4,3,2,1,0:T(8,128)S(1)}, f32[2,4,16,32,64]{4,3,2,1,0:T(8,128)}, u32[]{:S(2)}) %copy-start) | copy-done | bytes 1048600
  3.3 5.0 %collective-permute-start.2 = (bf16[4,16,16,128]{3,1,2,0:T(8,128)(2,1)}, bf16[4,16,16,128]{3,1,2,0:T(8,128)(2,1)S(1)}, u32[]{:S(2)}, u32[]{:S(2)}) collective-permute-start(bf16[4,16,16,128]{3,1,2,0:T(8,128)(2,1)} %fusion.91), channel_id=1, source_target_pairs={{0,12},{4,0},{8,4},{12,8},{1,13},{5,1},{9,5},{13,9},{2,14},{6,2},{... | collective-permute-start | bytes 786440 | tf_op jit(solution)/shard_map/ppermute | solution.py:67
  9.7 2.0 %fusion.11 = f32[128,2,32,64]{0,3,2,1:T(8,128)S(1)} fusion(bf16[1,4,32,64,64]{4,3,2,1,0:T(8,128)(2,1)} %param.5, f32[64,64]{0,1:T(8,128)S(1)} %get-tuple-element.10, f32[64,64]{0,1:T(8,128)S(1)} %get-tuple-element.11), kind=kOutput, calls=%fused_computation.21 | convolution fusion | flops 201334784 | bytes 3178496 | tf_op jit(solution)/shard_map/rtxyz,zl->rtxyl/dot_general | solution.py:174
  11.6 3.7 %fusion.6 = f32[2,32,128,2,64]{2,4,3,1,0:T(8,128)} fusion(f32[128,2,32,64]{0,3,2,1:T(8,128)S(1)} %fusion.11, f32[1,64,64]{2,1,0:T(8,128)S(1)} %get-tuple-element.12, f32[1,64,64]{2,1,0:T(8,128)S(1)} %get-tuple-element.13), kind=kOutput, calls=%fused_computation.13 | convolution fusion | flops 402661376 | bytes 6324224 | tf_op jit(solution)/shard_map/ejy,rtxyl->rtxejl/dot_general | solution.py:175
  15.3 6.3 %shard_map.68 = bf16[2,64,32,128]{3,2,1,0:T(8,128)(2,1)} custom-call(s32[1]{0:T(128)} %bitcast.me_ref, f32[64,2,64,128]{3,2,1,0:T(8,128)} %bitcast.198), custom_call_target="tpu_custom_call" | custom-call | flops 1572864 | bytes 5242880 | tf_op jit(solution)/shard_map/pallas_call | solution.py:44
  21.6 1.4 %fusion.93 = (bf16[1,64,32,128]{3,2,1,0:T(8,128)(2,1)S(1)}, bf16[1,64,32,128]{3,2,1,0:T(8,128)(2,1)S(1)}) fusion(bf16[2,64,32,128]{3,2,1,0:T(8,128)(2,1)} %shard_map.68), kind=kLoop, calls=%fused_computation.139 | loop fusion | bytes 2097152 | tf_op jit(solution)/shard_map/slice | solution.py:78
  24.0 1.5 %collective-permute-start = (bf16[1,2,32,32,128]{4,2,3,1,0:T(8,128)(2,1)}, bf16[1,2,32,32,128]{4,2,3,1,0:T(8,128)(2,1)S(1)}, u32[]{:S(2)}, u32[]{:S(2)}) collective-permute-start(bf16[1,2,32,32,128]{4,2,3,1,0:T(8,128)(2,1)} %copy.15), channel_id=1, source_target_pairs={{0,2},{2,0},{1,3},{3,1},{4,6},{6,4},{5,7},{7,5},{8,10},{10,8},{9,1... | collective-permute-start | bytes 1572872 | tf_op jit(solution)/shard_map/ppermute | solution.py:84
  26.3 3.7 %fusion.4 = f32[2,32,128,2,64]{2,4,3,1,0:T(8,128)} fusion(f32[128,2,32,64]{0,3,2,1:T(8,128)S(1)} %fusion.9, f32[1,64,64]{2,1,0:T(8,128)S(1)} %get-tuple-element.12, f32[1,64,64]{2,1,0:T(8,128)S(1)} %get-tuple-element.13), kind=kOutput, calls=%fused_computation.11 | convolution fusion | flops 402661376 | bytes 6324224 | tf_op jit(solution)/shard_map/ejy,rtxyl->rtxejl/dot_general | solution.py:175
  30.0 6.3 %shard_map.70 = bf16[2,64,32,128]{3,2,1,0:T(8,128)(2,1)} custom-call(s32[1]{0:T(128)} %bitcast.me_ref, f32[64,2,64,128]{3,2,1,0:T(8,128)} %bitcast.199), custom_call_target="tpu_custom_call" | custom-call | flops 1572864 | bytes 5242880 | tf_op jit(solution)/shard_map/pallas_call | solution.py:44
  36.3 1.3 %fusion.92 = (bf16[1,64,32,128]{3,2,1,0:T(8,128)(2,1)S(1)}, bf16[1,64,32,128]{3,2,1,0:T(8,128)(2,1)S(1)}) fusion(bf16[2,64,32,128]{3,2,1,0:T(8,128)(2,1)} %shard_map.70), kind=kLoop, calls=%fused_computation.138 | loop fusion | bytes 2097152 | tf_op jit(solution)/shard_map/slice | solution.py:78
  40.1 1.2 constant_dynamic-slice_fusion
  41.5 1.3 %fusion.21 = f32[2,32,128,2,64]{2,4,3,1,0:T(8,128)S(1)} fusion(bf16[1,2,32,32,128]{4,2,3,1,0:T(8,128)(2,1)S(1)} %collective-permute-done, pred[]{:T(512)S(6)} %eq.47, bf16[1,2,32,32,128]{4,3,2,1,0:T(8,128)(2,1)S(1)} %bitcast.200, f32[1,64,2,32]{1,3,0,2:T(8,128)S(1)} %get-tuple-element.9, f32[1,64,2,32]{1,3,0,2:T(8,128)S(1)} %get-tuple-element.8), kind=kOutput, calls=%fused_computation.32 | convolution fusion | flops 201592832 | bytes 5275649 | tf_op jit(solution)/shard_map/ekx,rtxjl->rtjekl/dot_general | solution.py:181
  42.8 3.6 %convolution_add_fusion.1 = f32[2,32,128,2,64]{2,4,3,1,0:T(8,128)} fusion(f32[2,32,128,2,64]{2,4,3,1,0:T(8,128)S(1)} %fusion.21, bf16[1,2,32,32,128]{4,2,3,1,0:T(8,128)(2,1)S(1)} %collective-permute-done, pred[]{:T(512)S(6)} %eq.46, bf16[1,2,32,32,128]{4,3,2,1,0:T(8,128)(2,1)S(1)} %bitcast.201, f32[1,64,2,32]{1,3,0,2:T(8,128)S(1)} %get-tuple-element.8, ...), kind=kOutput, calls=%fused_computation.6 | convolution fusion | flops 202641408 | bytes 9469953 | tf_op jit(solution)/shard_map/ekx,rtxjl->rtjekl/dot_general | solution.py:181
  46.4 6.3 %shard_map.69 = bf16[1,64,64,128]{3,2,1,0:T(8,128)(2,1)} custom-call(s32[1]{0:T(128)} %constant.80.clone.1.me_ref, f32[64,2,64,128]{3,2,1,0:T(8,128)} %bitcast.196), custom_call_target="tpu_custom_call" | custom-call | flops 1572864 | bytes 5242880 | tf_op jit(solution)/shard_map/pallas_call | solution.py:44
  52.7 1.3 %fusion.18 = f32[2,32,128,2,64]{2,4,3,1,0:T(8,128)S(1)} fusion(bf16[1,2,32,32,128]{4,2,3,1,0:T(8,128)(2,1)S(1)} %collective-permute-done.1, pred[]{:T(512)S(6)} %eq.47, bf16[1,2,32,32,128]{4,3,2,1,0:T(8,128)(2,1)S(1)} %bitcast.202, f32[1,64,2,32]{1,3,0,2:T(8,128)S(1)} %get-tuple-element.9, f32[1,64,2,32]{1,3,0,2:T(8,128)S(1)} %get-tuple-element.8), kind=kOutput, calls=%fused_computation.29 | convolution fusion | flops 201592832 | bytes 5275649 | tf_op jit(solution)/shard_map/ekx,rtxjl->rtjekl/dot_general | solution.py:181
  54.0 3.6 %convolution_add_fusion = f32[2,32,128,2,64]{2,4,3,1,0:T(8,128)} fusion(f32[2,32,128,2,64]{2,4,3,1,0:T(8,128)S(1)} %fusion.18, bf16[1,2,32,32,128]{4,2,3,1,0:T(8,128)(2,1)S(1)} %collective-permute-done.1, pred[]{:T(512)S(6)} %eq.46, bf16[1,2,32,32,128]{4,3,2,1,0:T(8,128)(2,1)S(1)} %bitcast.203, f32[1,64,2,32]{1,3,0,2:T(8,128)S(1)} %get-tuple-element.8, ...), kind=kOutput, calls=%fused_computation.5 | convolution fusion | flops 202641408 | bytes 9469953 | tf_op jit(solution)/shard_map/ekx,rtxjl->rtjekl/dot_general | solution.py:181
  57.6 6.3 %shard_map.71 = bf16[1,64,64,128]{3,2,1,0:T(8,128)(2,1)} custom-call(s32[1]{0:T(128)} %constant.80.clone.1.me_ref, f32[64,2,64,128]{3,2,1,0:T(8,128)} %bitcast.197), custom_call_target="tpu_custom_call" | custom-call | flops 1572864 | bytes 5242880 | tf_op jit(solution)/shard_map/pallas_call | solution.py:44
  63.8 2.7 %fusion.3 = bf16[4,2,16,4,16,128]{5,2,4,0,3,1:T(8,128)(2,1)S(1)} fusion(s32[]{:T(128)S(6)} %select_n.146, bf16[1,4,4,16,16,128]{5,3,4,2,1,0:T(8,128)(2,1)} %bitcast.62, bf16[1,4,4,16,16,128]{5,3,4,2,1,0:T(8,128)(2,1)S(1)} %fusion.99), kind=kLoop, calls=%fused_computation.10 | loop fusion | flops 3145728 | bytes 4194308 | tf_op jit(solution)/shard_map/transpose | solution.py:108
  66.5 1.9 %copy.21 = bf16[4,2,16,4,16,128]{5,4,3,2,1,0:T(8,128)(2,1)} copy(bf16[4,2,16,4,16,128]{5,2,4,0,3,1:T(8,128)(2,1)S(1)} %fusion.3) | data formatting | bytes 4194304 | tf_op jit(solution)/shard_map/transpose | solution.py:108
  68.4 4.9 %shard_map.72 = f32[1,2048,128]{2,1,0:T(8,128)} custom-call(bf16[1,2,2048,128]{3,2,1,0:T(8,128)(2,1)} %bitcast.210, bf16[1,2,2048,128]{3,2,1,0:T(8,128)(2,1)} %bitcast.212, bf16[4,2048,128]{2,1,0:T(8,128)(2,1)} %bitcast.204), custom_call_target="tpu_custom_call" | custom-call | flops 8388608 | bytes 5242880 | tf_op jit(solution)/shard_map/pallas_call | solution.py:139
  73.4 2.2 %fusion.40 = f32[32,128,2,64]{1,3,2,0:T(8,128)S(1)} fusion(f32[32,64,128,1]{2,1,3,0:T(8,128)} %bitcast.209, f32[1,64,64]{2,1,0:T(8,128)S(1)} %copy-done.6, f32[1,64,64]{2,1,0:T(8,128)S(1)} %copy-done.8), kind=kOutput, calls=%fused_computation.69 | convolution fusion | flops 201334784 | bytes 3178496 | tf_op jit(solution)/shard_map/exk,rjkl->xrejl/dot_general | solution.py:195
  75.6 2.5 %copy.53 = f32[32,128,2,64]{1,0,2,3:T(8,128)} copy(f32[32,128,2,64]{1,3,2,0:T(8,128)S(1)} %fusion.40) | data formatting | bytes 4194304 | tf_op jit(solution)/shard_map/exk,rjkl->xrejl/dot_general | solution.py:195
  78.1 5.7 %shard_map.73 = f32[1,64,32,128]{3,2,1,0:T(8,128)} custom-call(s32[1]{0:T(128)} %constant.80.clone.1.me_ref, f32[64,2,32,128]{3,2,1,0:T(8,128)} %bitcast.205), custom_call_target="tpu_custom_call" | custom-call | flops 786432 | bytes 3145728 | tf_op jit(solution)/shard_map/pallas_call | solution.py:44
  85.0 1.6 %collective-permute-start.6 = (f32[32,1,32,128]{3,2,0,1:T(8,128)S(1)}, f32[32,1,32,128]{3,2,0,1:T(8,128)S(1)}, u32[]{:S(2)}, u32[]{:S(2)}) collective-permute-start(f32[32,1,32,128]{3,2,0,1:T(8,128)S(1)} %dynamic-slice_bitcast_fusion), channel_id=1, source_target_pairs={{0,2},{2,0},{1,3},{3,1},{4,6},{6,4},{5,7},{7,5},{8,10},{10,8},{9,1... | collective-permute-start | bytes 1572872 | tf_op jit(solution)/shard_map/ppermute | solution.py:84
  86.8 13.0 %collective-permute-done.6 = f32[32,1,32,128]{3,2,0,1:T(8,128)S(1)} collective-permute-done((f32[32,1,32,128]{3,2,0,1:T(8,128)S(1)}, f32[32,1,32,128]{3,2,0,1:T(8,128)S(1)}, u32[]{:S(2)}, u32[]{:S(2)}) %collective-permute-start.6) | collective-permute-done | bytes 524320 | tf_op jit(solution)/shard_map/ppermute | solution.py:84
  99.8 2.1 %fusion.15 = f32[32,128,2,64]{1,3,2,0:T(8,128)S(1)} fusion(f32[32,1,32,128]{3,2,0,1:T(8,128)S(1)} %collective-permute-done.6, f32[2,32,1,32,128]{4,3,1,0,2:T(8,128)} %bitcast.207, s32[]{:T(128)S(6)} %select_n.150, pred[]{:T(512)S(6)} %eq.47, f32[1,64,2,32]{1,3,0,2:T(8,128)S(1)} %get-tuple-element.9, f32[1,64,2,32]{1,3,0,2:T(8,128)S(1)} %get-tuple-element.8), kind=kOutput, calls=%fused_computation.26 | convolution fusion | flops 100798464 | bytes 3178501 | tf_op jit(solution)/shard_map/eyj,xrjl->rxeyl/dot_general | solution.py:200
  101.9 2.4 %add_bitcast_fusion.in_ref = f32[32,2,64,128]{3,2,1,0:T(8,128)} fusion(f32[32,128,2,64]{1,3,2,0:T(8,128)S(1)} %fusion.15, f32[32,1,32,128]{3,2,0,1:T(8,128)S(1)} %collective-permute-done.6, f32[2,32,1,32,128]{4,3,1,0,2:T(8,128)S(1)} %bitcast.208, s32[]{:T(128)S(6)} %select_n.150, pred[]{:T(512)S(6)} %eq.46, f32[1,64,2,32]{1,3,0,2:T(8,128)S(1)} %get-tuple-element.8, ...), kind=kOutput, calls=%fused_computation.16 | convolution fusion | flops 101322752 | bytes 5308421 | tf_op jit(solution)/shard_map/eyj,xrjl->rxeyl/dot_general | solution.py:200
  104.2 3.9 %shard_map.74 = f32[1,32,64,128]{3,2,1,0:T(8,128)} custom-call(s32[1]{0:T(128)} %constant.80.clone.1.me_ref, f32[32,2,64,128]{3,2,1,0:T(8,128)} %add_bitcast_fusion.in_ref), custom_call_target="tpu_custom_call" | custom-call | flops 786432 | bytes 3145728 | tf_op jit(solution)/shard_map/pallas_call | solution.py:44
  108.2 1.9 %convolution_multiply_fusion = f32[32,64,64]{2,1,0:T(8,128)S(1)} fusion(f32[1,32,64,128]{3,2,1,0:T(8,128)} %shard_map.74, f32[64,64]{0,1:T(8,128)S(1)} %get-tuple-element.10, f32[64,64]{0,1:T(8,128)S(1)} %get-tuple-element.11), kind=kOutput, calls=%fused_computation.17 | convolution fusion | flops 100802560 | bytes 1605632 | tf_op jit(solution)/shard_map/rxyl,lz->rxyz/dot_general | solution.py:206
  111.2 1.6 %gather_fusion = f32[8,512]{1,0:T(8,128)S(1)} fusion(f32[256,512]{1,0:T(8,128)} %reshape.307, s32[1024]{0:T(1024)S(1)} %pad_clamp_fusion), kind=kCustom, calls=%fused_computation | custom fusion | bytes 32800 | tf_op jit(solution)/shard_map/gather | solution.py:213
  112.8 1.6 %fusion.94 = f32[8,512]{1,0:T(8,128)S(1)} fusion(f32[8,512]{1,0:T(8,128)S(1)} %gather_fusion, f32[512,512]{1,0:T(8,128)} %param.9), kind=kOutput, calls=%fused_computation.140 | convolution fusion | flops 12582912 | bytes 1081344 | tf_op jit(solution)/shard_map/dot_general | solution.py:222
  114.6 9.6 %all_to_all.5 = f32[8,2,512]{2,1,0:T(2,128)S(1)} all-to-all(f32[8,2,512]{2,1,0:T(2,128)S(1)} %reshape.309), channel_id=1, replica_groups=mesh['grp'=2,'rot'=4,'sub'=2,'ref'=2] {'rot','ref'}, dimensions={0} | all-to-all | bytes 65536 | tf_op jit(solution)/shard_map/all_to_all | solution.py:224
  (59 shorter events, 10.0 us)
Async XLA Ops:
  0.6 1.6 %copy-start = (f32[2,4,16,32,64]{4,3,2,1,0:T(8,128)S(1)}, f32[2,4,16,32,64]{4,3,2,1,0:T(8,128)}, u32[]{:S(2)}) copy-start(f32[2,4,16,32,64]{4,3,2,1,0:T(8,128)} %param.6) | copy-start | bytes 3145732
  3.3 36.1 %collective-permute-start.2 = (bf16[4,16,16,128]{3,1,2,0:T(8,128)(2,1)}, bf16[4,16,16,128]{3,1,2,0:T(8,128)(2,1)S(1)}, u32[]{:S(2)}, u32[]{:S(2)}) collective-permute-start(bf16[4,16,16,128]{3,1,2,0:T(8,128)(2,1)} %fusion.91), channel_id=1, source_target_pairs={{0,12},{4,0},{8,4},{12,8},{1,13},{5,1},{9,5},{13,9},{2,14},{6,2},{... | collective-permute-start | bytes 786440 | tf_op jit(solution)/shard_map/ppermute | solution.py:67
  8.3 31.1 %collective-permute-start.3 = (bf16[4,16,16,128]{3,1,2,0:T(8,128)(2,1)}, bf16[4,16,16,128]{3,1,2,0:T(8,128)(2,1)S(1)}, u32[]{:S(2)}, u32[]{:S(2)}) collective-permute-start(bf16[4,16,16,128]{3,1,2,0:T(8,128)(2,1)} %fusion.91), channel_id=1, source_target_pairs={{0,8},{4,12},{8,0},{12,4},{1,9},{5,13},{9,1},{13,5},{2,10},{6,14},... | collective-permute-start | bytes 786440 | tf_op jit(solution)/shard_map/ppermute | solution.py:67
  8.3 31.2 %collective-permute-start.4 = (bf16[4,16,16,128]{3,1,2,0:T(8,128)(2,1)}, bf16[4,16,16,128]{3,1,2,0:T(8,128)(2,1)S(1)}, u32[]{:S(2)}, u32[]{:S(2)}) collective-permute-start(bf16[4,16,16,128]{3,1,2,0:T(8,128)(2,1)} %fusion.91), channel_id=1, source_target_pairs={{0,4},{4,8},{8,12},{12,0},{1,5},{5,9},{9,13},{13,1},{2,6},{6,10},{... | collective-permute-start | bytes 786440 | tf_op jit(solution)/shard_map/ppermute | solution.py:67
  9.6 16.6 %copy-start.5 = (f32[1,64,64]{2,1,0:T(8,128)}, f32[1,64,64]{2,1,0:T(8,128)S(1)}, u32[]{:S(2)}) copy-start(f32[1,64,64]{2,1,0:T(8,128)S(1)} %get-tuple-element.12) | copy-start | bytes 49156
  9.6 16.6 %copy-start.7 = (f32[1,64,64]{2,1,0:T(8,128)}, f32[1,64,64]{2,1,0:T(8,128)S(1)}, u32[]{:S(2)}) copy-start(f32[1,64,64]{2,1,0:T(8,128)S(1)} %get-tuple-element.13) | copy-start | bytes 49156
  21.6 3.9 %copy-start.4 = (bf16[1,4,32,64,64]{4,3,2,1,0:T(8,128)(2,1)S(1)}, bf16[1,4,32,64,64]{4,3,2,1,0:T(8,128)(2,1)}, u32[]{:S(2)}) copy-start(bf16[1,4,32,64,64]{4,3,2,1,0:T(8,128)(2,1)} %param.5) | copy-start | bytes 3145732
  24.0 17.4 %collective-permute-start = (bf16[1,2,32,32,128]{4,2,3,1,0:T(8,128)(2,1)}, bf16[1,2,32,32,128]{4,2,3,1,0:T(8,128)(2,1)S(1)}, u32[]{:S(2)}, u32[]{:S(2)}) collective-permute-start(bf16[1,2,32,32,128]{4,2,3,1,0:T(8,128)(2,1)} %copy.15), channel_id=1, source_target_pairs={{0,2},{2,0},{1,3},{3,1},{4,6},{6,4},{5,7},{7,5},{8,10},{10,8},{9,1... | collective-permute-start | bytes 1572872 | tf_op jit(solution)/shard_map/ppermute | solution.py:84
  38.6 14.1 %collective-permute-start.1 = (bf16[1,2,32,32,128]{4,2,3,1,0:T(8,128)(2,1)}, bf16[1,2,32,32,128]{4,2,3,1,0:T(8,128)(2,1)S(1)}, u32[]{:S(2)}, u32[]{:S(2)}) collective-permute-start(bf16[1,2,32,32,128]{4,2,3,1,0:T(8,128)(2,1)} %copy.18), channel_id=1, source_target_pairs={{0,2},{2,0},{1,3},{3,1},{4,6},{6,4},{5,7},{7,5},{8,10},{10,8},{9,1... | collective-permute-start | bytes 1572872 | tf_op jit(solution)/shard_map/ppermute | solution.py:84
  41.2 22.6 %collective-permute-start.5 = (bf16[4,4,16,16,128]{4,2,3,1,0:T(8,128)(2,1)}, bf16[4,4,16,16,128]{4,2,3,1,0:T(8,128)(2,1)}, u32[]{:S(2)}, u32[]{:S(2)}) collective-permute-start(bf16[4,4,16,16,128]{4,2,3,1,0:T(8,128)(2,1)} %constant_dynamic-slice_fusion), channel_id=1, source_target_pairs={{0,1},{1,0},{2,3},{3,2},{4,5},{5,4},{6,7},{7,6},{8,9},{9,8},{10,11... | collective-permute-start | bytes 3145736 | tf_op jit(solution)/shard_map/ppermute | solution.py:67
  68.4 4.9 %copy-start.6 = (f32[1,64,64]{2,1,0:T(8,128)S(1)}, f32[1,64,64]{2,1,0:T(8,128)}, u32[]{:S(2)}) copy-start(f32[1,64,64]{2,1,0:T(8,128)} %copy-done.5) | copy-start | bytes 49156
  68.4 4.9 %copy-start.8 = (f32[1,64,64]{2,1,0:T(8,128)S(1)}, f32[1,64,64]{2,1,0:T(8,128)}, u32[]{:S(2)}) copy-start(f32[1,64,64]{2,1,0:T(8,128)} %copy-done.7) | copy-start | bytes 49156
  78.1 8.5 %copy-start.9 = (s32[1,1,1,8]{3,2,1,0:T(1,128)S(1)}, s32[1,1,1,8]{3,2,1,0:T(1,128)}, u32[]{:S(2)}) copy-start(s32[1,1,1,8]{3,2,1,0:T(1,128)} %param.7) | copy-start | bytes 100
  78.1 8.5 %copy-start.10 = (s32[1,1,1,8,1]{3,4,2,1,0:T(1,128)S(1)}, s32[1,1,1,8,1]{3,4,2,1,0:T(1,128)}, u32[]{:S(2)}) copy-start(s32[1,1,1,8,1]{3,4,2,1,0:T(1,128)} %param.8) | copy-start | bytes 100
  83.8 18.0 %copy-start.2 = (f32[1,64,32,128]{3,2,1,0:T(8,128)S(1)}, f32[1,64,32,128]{3,2,1,0:T(8,128)}, u32[]{:S(2)}) copy-start(f32[1,64,32,128]{3,2,1,0:T(8,128)} %shard_map.73) | copy-start | bytes 3145732
  85.0 14.8 %collective-permute-start.6 = (f32[32,1,32,128]{3,2,0,1:T(8,128)S(1)}, f32[32,1,32,128]{3,2,0,1:T(8,128)S(1)}, u32[]{:S(2)}, u32[]{:S(2)}) collective-permute-start(f32[32,1,32,128]{3,2,0,1:T(8,128)S(1)} %dynamic-slice_bitcast_fusion), channel_id=1, source_target_pairs={{0,2},{2,0},{1,3},{3,1},{4,6},{6,4},{5,7},{7,5},{8,10},{10,8},{9,1... | collective-permute-start | bytes 1572872 | tf_op jit(solution)/shard_map/ppermute | solution.py:84
  104.2 20.6 %copy-start.1 = (f32[2,4,16,32,64]{4,3,2,1,0:T(8,128)S(1)}, f32[2,4,16,32,64]{4,3,2,1,0:T(8,128)}, u32[]{:S(2)}) copy-start(f32[2,4,16,32,64]{4,3,2,1,0:T(8,128)} %param.6) | copy-start | bytes 3145732
  110.0 14.8 %copy-start.3 = (f32[32,64,64]{2,1,0:T(8,128)}, f32[32,64,64]{2,1,0:T(8,128)S(1)}, u32[]{:S(2)}) copy-start(f32[32,64,64]{2,1,0:T(8,128)S(1)} %convolution_multiply_fusion) | copy-start | bytes 1572868

commit v13 on v12

--- a/solution.py
+++ b/solution.py
@@ -39,7 +39,7 @@
 
 def combine_call(stacked, first, second, split, dtype, me=0):
     batch, _, rows, lanes = stacked.shape
-    block = max(b for b in range(1, 9) if batch % b == 0)
+    block = max(b for b in range(1, 65) if batch % b == 0)
     part = rows // split
     return pl.pallas_call(
         functools.partial(combine_kernel, first=first, second=second),

time: 126 us -> 112 us (0.89)
  Pallas kernels: 39.7 us -> 26 us
    pallas_call x6, Pallas kernels: 34.8 us -> 21 us  [combine_call(): pl.pallas_call(functools.partial(combine_kernel, first=first, second=seco...]
  transfers between devices with their start and end apart: 7 -> 7, of which waited for: 1 -> 2; matrix products, arithmetic and copies ran while one was open for 22% -> 25% of each run, Pallas kernels for 20% -> 14%
where the time goes in v13:
time: 112 us; the launch traced here: 111 us
  matrix products  30.3 us (27%)
  Pallas kernels  26 us (23%)
  local copies, waits for them, and re-layouts  17.1 us (15%)
  waiting for transfers between devices  13.5 us (12%)
  blocking collectives  9.63 us (9%)
  starting transfers between devices  9.16 us (8%)
  other arithmetic  4.63 us (4%)
    pallas_call x6, Pallas kernels, combine_call(): pl.pallas_call(functools.partial(combine_kernel, first=first, second=seco...  21 us
    ppermute x3, waiting for transfers between devices, exchange(): lax.ppermute(entry(shift), axis, pairs)  13.5 us
    dot_general x4, matrix products, local(): jnp.einsum('ekx,rtxjl->rtjekl', pair_x[:, :, source], piece.astype(jnp.fl...  10 us
    all_to_all x1, blocking collectives, local(): lax.all_to_all(packed, ('rot', 'ref'), split_axis=0, concat_axis=0, tiled...  9.63 us
    dot_general x2, matrix products, local(): along_y = jnp.einsum('ejy,rtxyl->rtxejl', pair, along_z, precision=highest)  7.45 us
    ppermute x4, starting transfers between devices, gather_by_shifts(): pieces.append(lax.ppermute(piece, axis, pairs))  6.06 us
    pallas_call x1, Pallas kernels, correlate(): pl.pallas_call(product_kernel, grid=(rots, rows // block), in_specs=[pl.B...  4.94 us
    dot_general x2, matrix products, local(): jnp.einsum('eyj,xrjl->rxeyl', pair_y[:, :, source], piece, precision=high...  4.43 us
  transfers between devices with their start and end apart: 7, of which 2 were waited for; matrix products, arithmetic and copies ran while one was open for 25% of the time, Pallas kernels for 14%

profile of v13, /device:TPU:0, one launch (start us, length us, event | category | flops | bytes accessed | tf_op | source)
XLA Modules:
  0.0 111.3 jit_solution(13134861825136452413)
XLA Ops:
  0.7 1.6 %copy-done = f32[2,4,16,32,64]{4,3,2,1,0:T(8,128)S(1)} copy-done((f32[2,4,16,32,64]{4,3,2,1,0:T(8,128)S(1)}, f32[2,4,16,32,64]{4,3,2,1,0:T(8,128)}, u32[]{:S(2)}) %copy-start) | copy-done | bytes 1048600
  3.3 5.0 %collective-permute-start.2 = (bf16[4,16,16,128]{3,1,2,0:T(8,128)(2,1)}, bf16[4,16,16,128]{3,1,2,0:T(8,128)(2,1)S(1)}, u32[]{:S(2)}, u32[]{:S(2)}) collective-permute-start(bf16[4,16,16,128]{3,1,2,0:T(8,128)(2,1)} %fusion.91), channel_id=1, source_target_pairs={{0,12},{4,0},{8,4},{12,8},{1,13},{5,1},{9,5},{13,9},{2,14},{6,2},{... | collective-permute-start | bytes 786440 | tf_op jit(solution)/shard_map/ppermute | solution.py:67
  9.7 2.0 %fusion.11 = f32[128,2,32,64]{0,3,2,1:T(8,128)S(1)} fusion(bf16[1,4,32,64,64]{4,3,2,1,0:T(8,128)(2,1)} %param.5, f32[64,64]{0,1:T(8,128)S(1)} %get-tuple-element.10, f32[64,64]{0,1:T(8,128)S(1)} %get-tuple-element.11), kind=kOutput, calls=%fused_computation.21 | convolution fusion | flops 201334784 | bytes 3178496 | tf_op jit(solution)/shard_map/rtxyz,zl->rtxyl/dot_general | solution.py:174
  11.6 3.7 %fusion.6 = f32[2,32,128,2,64]{2,4,3,1,0:T(8,128)} fusion(f32[128,2,32,64]{0,3,2,1:T(8,128)S(1)} %fusion.11, f32[1,64,64]{2,1,0:T(8,128)S(1)} %get-tuple-element.12, f32[1,64,64]{2,1,0:T(8,128)S(1)} %get-tuple-element.13), kind=kOutput, calls=%fused_computation.13 | convolution fusion | flops 402661376 | bytes 6324224 | tf_op jit(solution)/shard_map/ejy,rtxyl->rtxejl/dot_general | solution.py:175
  15.3 3.8 %shard_map.68 = bf16[2,64,32,128]{3,2,1,0:T(8,128)(2,1)} custom-call(s32[1]{0:T(128)} %bitcast.me_ref, f32[64,2,64,128]{3,2,1,0:T(8,128)} %bitcast.198), custom_call_target="tpu_custom_call" | custom-call | flops 1572864 | bytes 5242880 | tf_op jit(solution)/shard_map/pallas_call | solution.py:44
  19.1 1.4 %fusion.93 = (bf16[1,64,32,128]{3,2,1,0:T(8,128)(2,1)S(1)}, bf16[1,64,32,128]{3,2,1,0:T(8,128)(2,1)S(1)}) fusion(bf16[2,64,32,128]{3,2,1,0:T(8,128)(2,1)} %shard_map.68), kind=kLoop, calls=%fused_computation.139 | loop fusion | bytes 2097152 | tf_op jit(solution)/shard_map/slice | solution.py:78
  21.5 1.5 %collective-permute-start = (bf16[1,2,32,32,128]{4,2,3,1,0:T(8,128)(2,1)}, bf16[1,2,32,32,128]{4,2,3,1,0:T(8,128)(2,1)S(1)}, u32[]{:S(2)}, u32[]{:S(2)}) collective-permute-start(bf16[1,2,32,32,128]{4,2,3,1,0:T(8,128)(2,1)} %copy.15), channel_id=1, source_target_pairs={{0,2},{2,0},{1,3},{3,1},{4,6},{6,4},{5,7},{7,5},{8,10},{10,8},{9,1... | collective-permute-start | bytes 1572872 | tf_op jit(solution)/shard_map/ppermute | solution.py:84
  23.8 3.7 %fusion.4 = f32[2,32,128,2,64]{2,4,3,1,0:T(8,128)} fusion(f32[128,2,32,64]{0,3,2,1:T(8,128)S(1)} %fusion.9, f32[1,64,64]{2,1,0:T(8,128)S(1)} %get-tuple-element.12, f32[1,64,64]{2,1,0:T(8,128)S(1)} %get-tuple-element.13), kind=kOutput, calls=%fused_computation.11 | convolution fusion | flops 402661376 | bytes 6324224 | tf_op jit(solution)/shard_map/ejy,rtxyl->rtxejl/dot_general | solution.py:175
  27.5 3.8 %shard_map.70 = bf16[2,64,32,128]{3,2,1,0:T(8,128)(2,1)} custom-call(s32[1]{0:T(128)} %bitcast.me_ref, f32[64,2,64,128]{3,2,1,0:T(8,128)} %bitcast.199), custom_call_target="tpu_custom_call" | custom-call | flops 1572864 | bytes 5242880 | tf_op jit(solution)/shard_map/pallas_call | solution.py:44
  31.3 1.3 %fusion.92 = (bf16[1,64,32,128]{3,2,1,0:T(8,128)(2,1)S(1)}, bf16[1,64,32,128]{3,2,1,0:T(8,128)(2,1)S(1)}) fusion(bf16[2,64,32,128]{3,2,1,0:T(8,128)(2,1)} %shard_map.70), kind=kLoop, calls=%fused_computation.138 | loop fusion | bytes 2097152 | tf_op jit(solution)/shard_map/slice | solution.py:78
  35.0 1.2 %constant_dynamic-slice_fusion = bf16[4,4,16,16,128]{4,2,3,1,0:T(8,128)(2,1)} fusion(bf16[8,4,16,16,128]{4,2,3,1,0:T(8,128)(2,1)S(1)} %bitcast_dynamic-update-slice_fusion.1, s32[]{:T(128)S(6)} %select_n.144), kind=kLoop, calls=%fused_computation.127 | loop fusion | bytes 2097156 | tf_op jit(solution)/shard_map/dynamic_slice | solution.py:69
  36.5 1.3 %fusion.21 = f32[2,32,128,2,64]{2,4,3,1,0:T(8,128)S(1)} fusion(bf16[1,2,32,32,128]{4,2,3,1,0:T(8,128)(2,1)S(1)} %collective-permute-done, pred[]{:T(512)S(6)} %eq.47, bf16[1,2,32,32,128]{4,3,2,1,0:T(8,128)(2,1)S(1)} %bitcast.200, f32[1,64,2,32]{1,3,0,2:T(8,128)S(1)} %get-tuple-element.9, f32[1,64,2,32]{1,3,0,2:T(8,128)S(1)} %get-tuple-element.8), kind=kOutput, calls=%fused_computation.32 | convolution fusion | flops 201592832 | bytes 5275649 | tf_op jit(solution)/shard_map/ekx,rtxjl->rtjekl/dot_general | solution.py:181
  37.8 3.6 %convolution_add_fusion.1 = f32[2,32,128,2,64]{2,4,3,1,0:T(8,128)} fusion(f32[2,32,128,2,64]{2,4,3,1,0:T(8,128)S(1)} %fusion.21, bf16[1,2,32,32,128]{4,2,3,1,0:T(8,128)(2,1)S(1)} %collective-permute-done, pred[]{:T(512)S(6)} %eq.46, bf16[1,2,32,32,128]{4,3,2,1,0:T(8,128)(2,1)S(1)} %bitcast.201, f32[1,64,2,32]{1,3,0,2:T(8,128)S(1)} %get-tuple-element.8, ...), kind=kOutput, calls=%fused_computation.6 | convolution fusion | flops 202641408 | bytes 9469953 | tf_op jit(solution)/shard_map/ekx,rtxjl->rtjekl/dot_general | solution.py:181
  41.4 3.8 %shard_map.69 = bf16[1,64,64,128]{3,2,1,0:T(8,128)(2,1)} custom-call(s32[1]{0:T(128)} %constant.80.clone.1.me_ref, f32[64,2,64,128]{3,2,1,0:T(8,128)} %bitcast.196), custom_call_target="tpu_custom_call" | custom-call | flops 1572864 | bytes 5242880 | tf_op jit(solution)/shard_map/pallas_call | solution.py:44
  46.3 1.5 %fusion.18 = f32[2,32,128,2,64]{2,4,3,1,0:T(8,128)S(1)} fusion(bf16[1,2,32,32,128]{4,2,3,1,0:T(8,128)(2,1)S(1)} %collective-permute-done.1, pred[]{:T(512)S(6)} %eq.47, bf16[1,2,32,32,128]{4,3,2,1,0:T(8,128)(2,1)S(1)} %bitcast.202, f32[1,64,2,32]{1,3,0,2:T(8,128)S(1)} %get-tuple-element.9, f32[1,64,2,32]{1,3,0,2:T(8,128)S(1)} %get-tuple-element.8), kind=kOutput, calls=%fused_computation.29 | convolution fusion | flops 201592832 | bytes 5275649 | tf_op jit(solution)/shard_map/ekx,rtxjl->rtjekl/dot_general | solution.py:181
  47.8 3.6 %convolution_add_fusion = f32[2,32,128,2,64]{2,4,3,1,0:T(8,128)} fusion(f32[2,32,128,2,64]{2,4,3,1,0:T(8,128)S(1)} %fusion.18, bf16[1,2,32,32,128]{4,2,3,1,0:T(8,128)(2,1)S(1)} %collective-permute-done.1, pred[]{:T(512)S(6)} %eq.46, bf16[1,2,32,32,128]{4,3,2,1,0:T(8,128)(2,1)S(1)} %bitcast.203, f32[1,64,2,32]{1,3,0,2:T(8,128)S(1)} %get-tuple-element.8, ...), kind=kOutput, calls=%fused_computation.5 | convolution fusion | flops 202641408 | bytes 9469953 | tf_op jit(solution)/shard_map/ekx,rtxjl->rtjekl/dot_general | solution.py:181
  51.4 3.8 %shard_map.71 = bf16[1,64,64,128]{3,2,1,0:T(8,128)(2,1)} custom-call(s32[1]{0:T(128)} %constant.80.clone.1.me_ref, f32[64,2,64,128]{3,2,1,0:T(8,128)} %bitcast.197), custom_call_target="tpu_custom_call" | custom-call | flops 1572864 | bytes 5242880 | tf_op jit(solution)/shard_map/pallas_call | solution.py:44
  55.2 2.7 %fusion.3 = bf16[4,2,16,4,16,128]{5,2,4,0,3,1:T(8,128)(2,1)S(1)} fusion(s32[]{:T(128)S(6)} %select_n.146, bf16[1,4,4,16,16,128]{5,3,4,2,1,0:T(8,128)(2,1)} %bitcast.62, bf16[1,4,4,16,16,128]{5,3,4,2,1,0:T(8,128)(2,1)S(1)} %fusion.99), kind=kLoop, calls=%fused_computation.10 | loop fusion | flops 3145728 | bytes 4194308 | tf_op jit(solution)/shard_map/transpose | solution.py:108
  57.9 1.9 %copy.21 = bf16[4,2,16,4,16,128]{5,4,3,2,1,0:T(8,128)(2,1)} copy(bf16[4,2,16,4,16,128]{5,2,4,0,3,1:T(8,128)(2,1)S(1)} %fusion.3) | data formatting | bytes 4194304 | tf_op jit(solution)/shard_map/transpose | solution.py:108
  59.8 4.9 %shard_map.72 = f32[1,2048,128]{2,1,0:T(8,128)} custom-call(bf16[1,2,2048,128]{3,2,1,0:T(8,128)(2,1)} %bitcast.210, bf16[1,2,2048,128]{3,2,1,0:T(8,128)(2,1)} %bitcast.212, bf16[4,2048,128]{2,1,0:T(8,128)(2,1)} %bitcast.204), custom_call_target="tpu_custom_call" | custom-call | flops 8388608 | bytes 5242880 | tf_op jit(solution)/shard_map/pallas_call | solution.py:139
  64.7 2.2 %fusion.40 = f32[32,128,2,64]{1,3,2,0:T(8,128)S(1)} fusion(f32[32,64,128,1]{2,1,3,0:T(8,128)} %bitcast.209, f32[1,64,64]{2,1,0:T(8,128)S(1)} %copy-done.6, f32[1,64,64]{2,1,0:T(8,128)S(1)} %copy-done.8), kind=kOutput, calls=%fused_computation.69 | convolution fusion | flops 201334784 | bytes 3178496 | tf_op jit(solution)/shard_map/exk,rjkl->xrejl/dot_general | solution.py:195
  66.9 2.5 %copy.53 = f32[32,128,2,64]{1,0,2,3:T(8,128)} copy(f32[32,128,2,64]{1,3,2,0:T(8,128)S(1)} %fusion.40) | data formatting | bytes 4194304 | tf_op jit(solution)/shard_map/exk,rjkl->xrejl/dot_general | solution.py:195
  69.5 2.9 %shard_map.73 = f32[1,64,32,128]{3,2,1,0:T(8,128)} custom-call(s32[1]{0:T(128)} %constant.80.clone.1.me_ref, f32[64,2,32,128]{3,2,1,0:T(8,128)} %bitcast.205), custom_call_target="tpu_custom_call" | custom-call | flops 786432 | bytes 3145728 | tf_op jit(solution)/shard_map/pallas_call | solution.py:44
  72.4 1.2 %dynamic-slice_bitcast_fusion = f32[32,1,32,128]{3,2,0,1:T(8,128)S(1)} fusion(f32[2,32,1,32,128]{4,3,1,0,2:T(8,128)} %bitcast.206, s32[]{:T(128)S(6)} %select_n.148), kind=kLoop, calls=%fused_computation.37 | loop fusion | bytes 1048580 | tf_op jit(solution)/shard_map/jit(dynamic_index_in_dim)/squeeze | solution.py:79
  74.8 12.3 %collective-permute-done.6 = f32[32,1,32,128]{3,2,0,1:T(8,128)S(1)} collective-permute-done((f32[32,1,32,128]{3,2,0,1:T(8,128)S(1)}, f32[32,1,32,128]{3,2,0,1:T(8,128)S(1)}, u32[]{:S(2)}, u32[]{:S(2)}) %collective-permute-start.6) | collective-permute-done | bytes 524320 | tf_op jit(solution)/shard_map/ppermute | solution.py:84
  87.2 2.1 %fusion.15 = f32[32,128,2,64]{1,3,2,0:T(8,128)S(1)} fusion(f32[32,1,32,128]{3,2,0,1:T(8,128)S(1)} %collective-permute-done.6, f32[2,32,1,32,128]{4,3,1,0,2:T(8,128)} %bitcast.207, s32[]{:T(128)S(6)} %select_n.150, pred[]{:T(512)S(6)} %eq.47, f32[1,64,2,32]{1,3,0,2:T(8,128)S(1)} %get-tuple-element.9, f32[1,64,2,32]{1,3,0,2:T(8,128)S(1)} %get-tuple-element.8), kind=kOutput, calls=%fused_computation.26 | convolution fusion | flops 100798464 | bytes 3178501 | tf_op jit(solution)/shard_map/eyj,xrjl->rxeyl/dot_general | solution.py:200
  89.2 2.4 %add_bitcast_fusion.in_ref = f32[32,2,64,128]{3,2,1,0:T(8,128)} fusion(f32[32,128,2,64]{1,3,2,0:T(8,128)S(1)} %fusion.15, f32[32,1,32,128]{3,2,0,1:T(8,128)S(1)} %collective-permute-done.6, f32[2,32,1,32,128]{4,3,1,0,2:T(8,128)S(1)} %bitcast.208, s32[]{:T(128)S(6)} %select_n.150, pred[]{:T(512)S(6)} %eq.46, f32[1,64,2,32]{1,3,0,2:T(8,128)S(1)} %get-tuple-element.8, ...), kind=kOutput, calls=%fused_computation.16 | convolution fusion | flops 101322752 | bytes 5308421 | tf_op jit(solution)/shard_map/eyj,xrjl->rxeyl/dot_general | solution.py:200
  91.6 3.0 %shard_map.74 = f32[1,32,64,128]{3,2,1,0:T(8,128)} custom-call(s32[1]{0:T(128)} %constant.80.clone.1.me_ref, f32[32,2,64,128]{3,2,1,0:T(8,128)} %add_bitcast_fusion.in_ref), custom_call_target="tpu_custom_call" | custom-call | flops 786432 | bytes 3145728 | tf_op jit(solution)/shard_map/pallas_call | solution.py:44
  94.7 1.9 %convolution_multiply_fusion = f32[32,64,64]{2,1,0:T(8,128)S(1)} fusion(f32[1,32,64,128]{3,2,1,0:T(8,128)} %shard_map.74, f32[64,64]{0,1:T(8,128)S(1)} %get-tuple-element.10, f32[64,64]{0,1:T(8,128)S(1)} %get-tuple-element.11), kind=kOutput, calls=%fused_computation.17 | convolution fusion | flops 100802560 | bytes 1605632 | tf_op jit(solution)/shard_map/rxyl,lz->rxyz/dot_general | solution.py:206
  97.7 1.6 %gather_fusion = f32[8,512]{1,0:T(8,128)S(1)} fusion(f32[256,512]{1,0:T(8,128)} %reshape.307, s32[1024]{0:T(1024)S(1)} %pad_clamp_fusion), kind=kCustom, calls=%fused_computation | custom fusion | bytes 32800 | tf_op jit(solution)/shard_map/gather | solution.py:213
  99.3 1.6 %fusion.94 = f32[8,512]{1,0:T(8,128)S(1)} fusion(f32[8,512]{1,0:T(8,128)S(1)} %gather_fusion, f32[512,512]{1,0:T(8,128)} %param.9), kind=kOutput, calls=%fused_computation.140 | convolution fusion | flops 12582912 | bytes 1081344 | tf_op jit(solution)/shard_map/dot_general | solution.py:222
  101.0 9.6 %all_to_all.5 = f32[8,2,512]{2,1,0:T(2,128)S(1)} all-to-all(f32[8,2,512]{2,1,0:T(2,128)S(1)} %reshape.309), channel_id=1, replica_groups=mesh['grp'=2,'rot'=4,'sub'=2,'ref'=2] {'rot','ref'}, dimensions={0} | all-to-all | bytes 65536 | tf_op jit(solution)/shard_map/all_to_all | solution.py:224
  (59 shorter events, 11.0 us)
Async XLA Ops:
  0.6 1.6 %copy-start = (f32[2,4,16,32,64]{4,3,2,1,0:T(8,128)S(1)}, f32[2,4,16,32,64]{4,3,2,1,0:T(8,128)}, u32[]{:S(2)}) copy-start(f32[2,4,16,32,64]{4,3,2,1,0:T(8,128)} %param.6) | copy-start | bytes 3145732
  3.3 31.1 %collective-permute-start.2 = (bf16[4,16,16,128]{3,1,2,0:T(8,128)(2,1)}, bf16[4,16,16,128]{3,1,2,0:T(8,128)(2,1)S(1)}, u32[]{:S(2)}, u32[]{:S(2)}) collective-permute-start(bf16[4,16,16,128]{3,1,2,0:T(8,128)(2,1)} %fusion.91), channel_id=1, source_target_pairs={{0,12},{4,0},{8,4},{12,8},{1,13},{5,1},{9,5},{13,9},{2,14},{6,2},{... | collective-permute-start | bytes 786440 | tf_op jit(solution)/shard_map/ppermute | solution.py:67
  8.3 26.1 %collective-permute-start.3 = (bf16[4,16,16,128]{3,1,2,0:T(8,128)(2,1)}, bf16[4,16,16,128]{3,1,2,0:T(8,128)(2,1)S(1)}, u32[]{:S(2)}, u32[]{:S(2)}) collective-permute-start(bf16[4,16,16,128]{3,1,2,0:T(8,128)(2,1)} %fusion.91), channel_id=1, source_target_pairs={{0,8},{4,12},{8,0},{12,4},{1,9},{5,13},{9,1},{13,5},{2,10},{6,14},... | collective-permute-start | bytes 786440 | tf_op jit(solution)/shard_map/ppermute | solution.py:67
  8.3 26.1 %collective-permute-start.4 = (bf16[4,16,16,128]{3,1,2,0:T(8,128)(2,1)}, bf16[4,16,16,128]{3,1,2,0:T(8,128)(2,1)S(1)}, u32[]{:S(2)}, u32[]{:S(2)}) collective-permute-start(bf16[4,16,16,128]{3,1,2,0:T(8,128)(2,1)} %fusion.91), channel_id=1, source_target_pairs={{0,4},{4,8},{8,12},{12,0},{1,5},{5,9},{9,13},{13,1},{2,6},{6,10},{... | collective-permute-start | bytes 786440 | tf_op jit(solution)/shard_map/ppermute | solution.py:67
  9.6 14.1 %copy-start.5 = (f32[1,64,64]{2,1,0:T(8,128)}, f32[1,64,64]{2,1,0:T(8,128)S(1)}, u32[]{:S(2)}) copy-start(f32[1,64,64]{2,1,0:T(8,128)S(1)} %get-tuple-element.12) | copy-start | bytes 49156
  9.6 14.1 %copy-start.7 = (f32[1,64,64]{2,1,0:T(8,128)}, f32[1,64,64]{2,1,0:T(8,128)S(1)}, u32[]{:S(2)}) copy-start(f32[1,64,64]{2,1,0:T(8,128)S(1)} %get-tuple-element.13) | copy-start | bytes 49156
  19.1 3.9 %copy-start.4 = (bf16[1,4,32,64,64]{4,3,2,1,0:T(8,128)(2,1)S(1)}, bf16[1,4,32,64,64]{4,3,2,1,0:T(8,128)(2,1)}, u32[]{:S(2)}) copy-start(bf16[1,4,32,64,64]{4,3,2,1,0:T(8,128)(2,1)} %param.5) | copy-start | bytes 3145732
  21.5 14.9 %collective-permute-start = (bf16[1,2,32,32,128]{4,2,3,1,0:T(8,128)(2,1)}, bf16[1,2,32,32,128]{4,2,3,1,0:T(8,128)(2,1)S(1)}, u32[]{:S(2)}, u32[]{:S(2)}) collective-permute-start(bf16[1,2,32,32,128]{4,2,3,1,0:T(8,128)(2,1)} %copy.15), channel_id=1, source_target_pairs={{0,2},{2,0},{1,3},{3,1},{4,6},{6,4},{5,7},{7,5},{8,10},{10,8},{9,1... | collective-permute-start | bytes 1572872 | tf_op jit(solution)/shard_map/ppermute | solution.py:84
  33.5 12.8 %collective-permute-start.1 = (bf16[1,2,32,32,128]{4,2,3,1,0:T(8,128)(2,1)}, bf16[1,2,32,32,128]{4,2,3,1,0:T(8,128)(2,1)S(1)}, u32[]{:S(2)}, u32[]{:S(2)}) collective-permute-start(bf16[1,2,32,32,128]{4,2,3,1,0:T(8,128)(2,1)} %copy.18), channel_id=1, source_target_pairs={{0,2},{2,0},{1,3},{3,1},{4,6},{6,4},{5,7},{7,5},{8,10},{10,8},{9,1... | collective-permute-start | bytes 1572872 | tf_op jit(solution)/shard_map/ppermute | solution.py:84
  36.2 19.0 %collective-permute-start.5 = (bf16[4,4,16,16,128]{4,2,3,1,0:T(8,128)(2,1)}, bf16[4,4,16,16,128]{4,2,3,1,0:T(8,128)(2,1)}, u32[]{:S(2)}, u32[]{:S(2)}) collective-permute-start(bf16[4,4,16,16,128]{4,2,3,1,0:T(8,128)(2,1)} %constant_dynamic-slice_fusion), channel_id=1, source_target_pairs={{0,1},{1,0},{2,3},{3,2},{4,5},{5,4},{6,7},{7,6},{8,9},{9,8},{10,11... | collective-permute-start | bytes 3145736 | tf_op jit(solution)/shard_map/ppermute | solution.py:67
  59.8 4.9 %copy-start.6 = (f32[1,64,64]{2,1,0:T(8,128)S(1)}, f32[1,64,64]{2,1,0:T(8,128)}, u32[]{:S(2)}) copy-start(f32[1,64,64]{2,1,0:T(8,128)} %copy-done.5) | copy-start | bytes 49156
  59.8 4.9 %copy-start.8 = (f32[1,64,64]{2,1,0:T(8,128)S(1)}, f32[1,64,64]{2,1,0:T(8,128)}, u32[]{:S(2)}) copy-start(f32[1,64,64]{2,1,0:T(8,128)} %copy-done.7) | copy-start | bytes 49156
  69.5 5.2 %copy-start.9 = (s32[1,1,1,8]{3,2,1,0:T(1,128)S(1)}, s32[1,1,1,8]{3,2,1,0:T(1,128)}, u32[]{:S(2)}) copy-start(s32[1,1,1,8]{3,2,1,0:T(1,128)} %param.7) | copy-start | bytes 100
  69.5 5.2 %copy-start.10 = (s32[1,1,1,8,1]{3,4,2,1,0:T(1,128)S(1)}, s32[1,1,1,8,1]{3,4,2,1,0:T(1,128)}, u32[]{:S(2)}) copy-start(s32[1,1,1,8,1]{3,4,2,1,0:T(1,128)} %param.8) | copy-start | bytes 100
  72.4 16.9 %copy-start.2 = (f32[1,64,32,128]{3,2,1,0:T(8,128)S(1)}, f32[1,64,32,128]{3,2,1,0:T(8,128)}, u32[]{:S(2)}) copy-start(f32[1,64,32,128]{3,2,1,0:T(8,128)} %shard_map.73) | copy-start | bytes 3145732
  73.6 13.6 %collective-permute-start.6 = (f32[32,1,32,128]{3,2,0,1:T(8,128)S(1)}, f32[32,1,32,128]{3,2,0,1:T(8,128)S(1)}, u32[]{:S(2)}, u32[]{:S(2)}) collective-permute-start(f32[32,1,32,128]{3,2,0,1:T(8,128)S(1)} %dynamic-slice_bitcast_fusion), channel_id=1, source_target_pairs={{0,2},{2,0},{1,3},{3,1},{4,6},{6,4},{5,7},{7,5},{8,10},{10,8},{9,1... | collective-permute-start | bytes 1572872 | tf_op jit(solution)/shard_map/ppermute | solution.py:84
  91.6 19.7 %copy-start.1 = (f32[2,4,16,32,64]{4,3,2,1,0:T(8,128)S(1)}, f32[2,4,16,32,64]{4,3,2,1,0:T(8,128)}, u32[]{:S(2)}) copy-start(f32[2,4,16,32,64]{4,3,2,1,0:T(8,128)} %param.6) | copy-start | bytes 3145732
  96.5 14.8 %copy-start.3 = (f32[32,64,64]{2,1,0:T(8,128)}, f32[32,64,64]{2,1,0:T(8,128)S(1)}, u32[]{:S(2)}) copy-start(f32[32,64,64]{2,1,0:T(8,128)S(1)} %convolution_multiply_fusion) | copy-start | bytes 1572868

commit v14 on v8

--- a/solution.py
+++ b/solution.py
@@ -133,7 +133,7 @@
     rots, _, kx, ky, lanes = spectra[0].shape
     terms = receptor.shape[0]
     rows = kx * ky
-    block = min(rows, 512)
+    block = min(rows, 1024)
     specs = [part.reshape(rots, part.shape[1], rows, lanes) for part in spectra]
     rec = receptor.reshape(terms, rows, lanes)
     out = pl.pallas_call(

time: 110 us -> 109 us (level)
  no operation moved by 1% of the time
where the time goes in v14:
time: 109 us; the launch traced here: 108 us
  matrix products  30.1 us (28%)
  Pallas kernels  23.4 us (21%)
  local copies, waits for them, and re-layouts  17.1 us (16%)
  waiting for transfers between devices  13.1 us (12%)
  blocking collectives  9.63 us (9%)
  starting transfers between devices  9.57 us (9%)
  other arithmetic  4.63 us (4%)
    pallas_call x6, Pallas kernels, combine_call(): pl.pallas_call(functools.partial(combine_kernel, first=first, second=seco...  19 us
    ppermute x3, waiting for transfers between devices, exchange(): lax.ppermute(entry(shift), axis, pairs)  13.1 us
    dot_general x4, matrix products, local(): jnp.einsum('ekx,rtxjl->rtjekl', pair_x[:, :, source], piece.astype(jnp.fl...  9.81 us
    all_to_all x1, blocking collectives, local(): lax.all_to_all(packed, ('rot', 'ref'), split_axis=0, concat_axis=0, tiled...  9.63 us
    dot_general x2, matrix products, local(): along_y = jnp.einsum('ejy,rtxyl->rtxejl', pair, along_z, precision=highest)  7.45 us
    ppermute x4, starting transfers between devices, gather_by_shifts(): pieces.append(lax.ppermute(piece, axis, pairs))  6.06 us
    dot_general x2, matrix products, local(): jnp.einsum('eyj,xrjl->rxeyl', pair_y[:, :, source], piece, precision=high...  4.42 us
    pallas_call x1, Pallas kernels, correlate(): pl.pallas_call(product_kernel, grid=(rots, rows // block), in_specs=[pl.B...  4.35 us
  transfers between devices with their start and end apart: 7, of which 2 were waited for; matrix products, arithmetic and copies ran while one was open for 25% of the time, Pallas kernels for 12%

profile of v14, /device:TPU:0, one launch (start us, length us, event | category | flops | bytes accessed | tf_op | source)
XLA Modules:
  0.0 108.5 jit_solution(16744045596795554604)
XLA Ops:
  0.7 1.6 %copy-done = f32[2,4,16,32,64]{4,3,2,1,0:T(8,128)S(1)} copy-done((f32[2,4,16,32,64]{4,3,2,1,0:T(8,128)S(1)}, f32[2,4,16,32,64]{4,3,2,1,0:T(8,128)}, u32[]{:S(2)}) %copy-start) | copy-done | bytes 1048600
  3.3 5.0 %collective-permute-start.2 = (bf16[4,16,16,128]{3,1,2,0:T(8,128)(2,1)}, bf16[4,16,16,128]{3,1,2,0:T(8,128)(2,1)S(1)}, u32[]{:S(2)}, u32[]{:S(2)}) collective-permute-start(bf16[4,16,16,128]{3,1,2,0:T(8,128)(2,1)} %fusion.91), channel_id=1, source_target_pairs={{0,12},{4,0},{8,4},{12,8},{1,13},{5,1},{9,5},{13,9},{2,14},{6,2},{... | collective-permute-start | bytes 786440 | tf_op jit(solution)/shard_map/ppermute | solution.py:67
  9.7 2.0 %fusion.11 = f32[128,2,32,64]{0,3,2,1:T(8,128)S(1)} fusion(bf16[1,4,32,64,64]{4,3,2,1,0:T(8,128)(2,1)} %param.5, f32[64,64]{0,1:T(8,128)S(1)} %get-tuple-element.10, f32[64,64]{0,1:T(8,128)S(1)} %get-tuple-element.11), kind=kOutput, calls=%fused_computation.21 | convolution fusion | flops 201334784 | bytes 3178496 | tf_op jit(solution)/shard_map/rtxyz,zl->rtxyl/dot_general | solution.py:174
  11.6 3.7 %fusion.6 = f32[2,32,128,2,64]{2,4,3,1,0:T(8,128)} fusion(f32[128,2,32,64]{0,3,2,1:T(8,128)S(1)} %fusion.11, f32[1,64,64]{2,1,0:T(8,128)S(1)} %get-tuple-element.12, f32[1,64,64]{2,1,0:T(8,128)S(1)} %get-tuple-element.13), kind=kOutput, calls=%fused_computation.13 | convolution fusion | flops 402661376 | bytes 6324224 | tf_op jit(solution)/shard_map/ejy,rtxyl->rtxejl/dot_general | solution.py:175
  15.3 3.4 %shard_map.68 = bf16[2,64,32,128]{3,2,1,0:T(8,128)(2,1)} custom-call(s32[1]{0:T(128)} %bitcast.me_ref, f32[64,2,64,128]{3,2,1,0:T(8,128)} %bitcast.198), custom_call_target="tpu_custom_call" | custom-call | flops 1572864 | bytes 5242880 | tf_op jit(solution)/shard_map/pallas_call | solution.py:44
  18.7 1.4 %fusion.93 = (bf16[1,64,32,128]{3,2,1,0:T(8,128)(2,1)S(1)}, bf16[1,64,32,128]{3,2,1,0:T(8,128)(2,1)S(1)}) fusion(bf16[2,64,32,128]{3,2,1,0:T(8,128)(2,1)} %shard_map.68), kind=kLoop, calls=%fused_computation.139 | loop fusion | bytes 2097152 | tf_op jit(solution)/shard_map/slice | solution.py:78
  21.1 1.5 %collective-permute-start = (bf16[1,2,32,32,128]{4,2,3,1,0:T(8,128)(2,1)}, bf16[1,2,32,32,128]{4,2,3,1,0:T(8,128)(2,1)S(1)}, u32[]{:S(2)}, u32[]{:S(2)}) collective-permute-start(bf16[1,2,32,32,128]{4,2,3,1,0:T(8,128)(2,1)} %copy.15), channel_id=1, source_target_pairs={{0,2},{2,0},{1,3},{3,1},{4,6},{6,4},{5,7},{7,5},{8,10},{10,8},{9,1... | collective-permute-start | bytes 1572872 | tf_op jit(solution)/shard_map/ppermute | solution.py:84
  23.4 3.7 %fusion.4 = f32[2,32,128,2,64]{2,4,3,1,0:T(8,128)} fusion(f32[128,2,32,64]{0,3,2,1:T(8,128)S(1)} %fusion.9, f32[1,64,64]{2,1,0:T(8,128)S(1)} %get-tuple-element.12, f32[1,64,64]{2,1,0:T(8,128)S(1)} %get-tuple-element.13), kind=kOutput, calls=%fused_computation.11 | convolution fusion | flops 402661376 | bytes 6324224 | tf_op jit(solution)/shard_map/ejy,rtxyl->rtxejl/dot_general | solution.py:175
  27.1 3.4 %shard_map.70 = bf16[2,64,32,128]{3,2,1,0:T(8,128)(2,1)} custom-call(s32[1]{0:T(128)} %bitcast.me_ref, f32[64,2,64,128]{3,2,1,0:T(8,128)} %bitcast.199), custom_call_target="tpu_custom_call" | custom-call | flops 1572864 | bytes 5242880 | tf_op jit(solution)/shard_map/pallas_call | solution.py:44
  30.4 1.3 %fusion.92 = (bf16[1,64,32,128]{3,2,1,0:T(8,128)(2,1)S(1)}, bf16[1,64,32,128]{3,2,1,0:T(8,128)(2,1)S(1)}) fusion(bf16[2,64,32,128]{3,2,1,0:T(8,128)(2,1)} %shard_map.70), kind=kLoop, calls=%fused_computation.138 | loop fusion | bytes 2097152 | tf_op jit(solution)/shard_map/slice | solution.py:78
  35.6 1.3 %fusion.21 = f32[2,32,128,2,64]{2,4,3,1,0:T(8,128)S(1)} fusion(bf16[1,2,32,32,128]{4,2,3,1,0:T(8,128)(2,1)S(1)} %collective-permute-done, pred[]{:T(512)S(6)} %eq.47, bf16[1,2,32,32,128]{4,3,2,1,0:T(8,128)(2,1)S(1)} %bitcast.200, f32[1,64,2,32]{1,3,0,2:T(8,128)S(1)} %get-tuple-element.9, f32[1,64,2,32]{1,3,0,2:T(8,128)S(1)} %get-tuple-element.8), kind=kOutput, calls=%fused_computation.32 | convolution fusion | flops 201592832 | bytes 5275649 | tf_op jit(solution)/shard_map/ekx,rtxjl->rtjekl/dot_general | solution.py:181
  36.9 3.6 %convolution_add_fusion.1 = f32[2,32,128,2,64]{2,4,3,1,0:T(8,128)} fusion(f32[2,32,128,2,64]{2,4,3,1,0:T(8,128)S(1)} %fusion.21, bf16[1,2,32,32,128]{4,2,3,1,0:T(8,128)(2,1)S(1)} %collective-permute-done, pred[]{:T(512)S(6)} %eq.46, bf16[1,2,32,32,128]{4,3,2,1,0:T(8,128)(2,1)S(1)} %bitcast.201, f32[1,64,2,32]{1,3,0,2:T(8,128)S(1)} %get-tuple-element.8, ...), kind=kOutput, calls=%fused_computation.6 | convolution fusion | flops 202641408 | bytes 9469953 | tf_op jit(solution)/shard_map/ekx,rtxjl->rtjekl/dot_general | solution.py:181
  40.5 3.4 %shard_map.69 = bf16[1,64,64,128]{3,2,1,0:T(8,128)(2,1)} custom-call(s32[1]{0:T(128)} %constant.80.clone.1.me_ref, f32[64,2,64,128]{3,2,1,0:T(8,128)} %bitcast.196), custom_call_target="tpu_custom_call" | custom-call | flops 1572864 | bytes 5242880 | tf_op jit(solution)/shard_map/pallas_call | solution.py:44
  43.9 1.6 %collective-permute-done.1 = bf16[1,2,32,32,128]{4,2,3,1,0:T(8,128)(2,1)S(1)} collective-permute-done((bf16[1,2,32,32,128]{4,2,3,1,0:T(8,128)(2,1)}, bf16[1,2,32,32,128]{4,2,3,1,0:T(8,128)(2,1)S(1)}, u32[]{:S(2)}, u32[]{:S(2)}) %collective-permute-start.1) | collective-permute-done | bytes 524320 | tf_op jit(solution)/shard_map/ppermute | solution.py:84
  45.5 1.3 %fusion.18 = f32[2,32,128,2,64]{2,4,3,1,0:T(8,128)S(1)} fusion(bf16[1,2,32,32,128]{4,2,3,1,0:T(8,128)(2,1)S(1)} %collective-permute-done.1, pred[]{:T(512)S(6)} %eq.47, bf16[1,2,32,32,128]{4,3,2,1,0:T(8,128)(2,1)S(1)} %bitcast.202, f32[1,64,2,32]{1,3,0,2:T(8,128)S(1)} %get-tuple-element.9, f32[1,64,2,32]{1,3,0,2:T(8,128)S(1)} %get-tuple-element.8), kind=kOutput, calls=%fused_computation.29 | convolution fusion | flops 201592832 | bytes 5275649 | tf_op jit(solution)/shard_map/ekx,rtxjl->rtjekl/dot_general | solution.py:181
  46.8 3.6 %convolution_add_fusion = f32[2,32,128,2,64]{2,4,3,1,0:T(8,128)} fusion(f32[2,32,128,2,64]{2,4,3,1,0:T(8,128)S(1)} %fusion.18, bf16[1,2,32,32,128]{4,2,3,1,0:T(8,128)(2,1)S(1)} %collective-permute-done.1, pred[]{:T(512)S(6)} %eq.46, bf16[1,2,32,32,128]{4,3,2,1,0:T(8,128)(2,1)S(1)} %bitcast.203, f32[1,64,2,32]{1,3,0,2:T(8,128)S(1)} %get-tuple-element.8, ...), kind=kOutput, calls=%fused_computation.5 | convolution fusion | flops 202641408 | bytes 9469953 | tf_op jit(solution)/shard_map/ekx,rtxjl->rtjekl/dot_general | solution.py:181
  50.4 3.4 %shard_map.71 = bf16[1,64,64,128]{3,2,1,0:T(8,128)(2,1)} custom-call(s32[1]{0:T(128)} %constant.80.clone.1.me_ref, f32[64,2,64,128]{3,2,1,0:T(8,128)} %bitcast.197), custom_call_target="tpu_custom_call" | custom-call | flops 1572864 | bytes 5242880 | tf_op jit(solution)/shard_map/pallas_call | solution.py:44
  53.8 2.7 %fusion.3 = bf16[4,2,16,4,16,128]{5,2,4,0,3,1:T(8,128)(2,1)S(1)} fusion(s32[]{:T(128)S(6)} %select_n.146, bf16[1,4,4,16,16,128]{5,3,4,2,1,0:T(8,128)(2,1)} %bitcast.62, bf16[1,4,4,16,16,128]{5,3,4,2,1,0:T(8,128)(2,1)S(1)} %fusion.99), kind=kLoop, calls=%fused_computation.10 | loop fusion | flops 3145728 | bytes 4194308 | tf_op jit(solution)/shard_map/transpose | solution.py:108
  56.4 1.9 %copy.21 = bf16[4,2,16,4,16,128]{5,4,3,2,1,0:T(8,128)(2,1)} copy(bf16[4,2,16,4,16,128]{5,2,4,0,3,1:T(8,128)(2,1)S(1)} %fusion.3) | data formatting | bytes 4194304 | tf_op jit(solution)/shard_map/transpose | solution.py:108
  58.3 4.3 %shard_map.72 = f32[1,2048,128]{2,1,0:T(8,128)} custom-call(bf16[1,2,2048,128]{3,2,1,0:T(8,128)(2,1)} %bitcast.210, bf16[1,2,2048,128]{3,2,1,0:T(8,128)(2,1)} %bitcast.212, bf16[4,2048,128]{2,1,0:T(8,128)(2,1)} %bitcast.204), custom_call_target="tpu_custom_call" | custom-call | flops 8388608 | bytes 5242880 | tf_op jit(solution)/shard_map/pallas_call | solution.py:139
  62.7 2.2 %fusion.40 = f32[32,128,2,64]{1,3,2,0:T(8,128)S(1)} fusion(f32[32,64,128,1]{2,1,3,0:T(8,128)} %bitcast.209, f32[1,64,64]{2,1,0:T(8,128)S(1)} %copy-done.6, f32[1,64,64]{2,1,0:T(8,128)S(1)} %copy-done.8), kind=kOutput, calls=%fused_computation.69 | convolution fusion | flops 201334784 | bytes 3178496 | tf_op jit(solution)/shard_map/exk,rjkl->xrejl/dot_general | solution.py:195
  64.9 2.5 %copy.53 = f32[32,128,2,64]{1,0,2,3:T(8,128)} copy(f32[32,128,2,64]{1,3,2,0:T(8,128)S(1)} %fusion.40) | data formatting | bytes 4194304 | tf_op jit(solution)/shard_map/exk,rjkl->xrejl/dot_general | solution.py:195
  67.4 2.6 %shard_map.73 = f32[1,64,32,128]{3,2,1,0:T(8,128)} custom-call(s32[1]{0:T(128)} %constant.80.clone.1.me_ref, f32[64,2,32,128]{3,2,1,0:T(8,128)} %bitcast.205), custom_call_target="tpu_custom_call" | custom-call | flops 786432 | bytes 3145728 | tf_op jit(solution)/shard_map/pallas_call | solution.py:44
  71.2 1.5 %collective-permute-start.6 = (f32[32,1,32,128]{3,2,0,1:T(8,128)S(1)}, f32[32,1,32,128]{3,2,0,1:T(8,128)S(1)}, u32[]{:S(2)}, u32[]{:S(2)}) collective-permute-start(f32[32,1,32,128]{3,2,0,1:T(8,128)S(1)} %dynamic-slice_bitcast_fusion), channel_id=1, source_target_pairs={{0,2},{2,0},{1,3},{3,1},{4,6},{6,4},{5,7},{7,5},{8,10},{10,8},{9,1... | collective-permute-start | bytes 1572872 | tf_op jit(solution)/shard_map/ppermute | solution.py:84
  72.8 11.5 %collective-permute-done.6 = f32[32,1,32,128]{3,2,0,1:T(8,128)S(1)} collective-permute-done((f32[32,1,32,128]{3,2,0,1:T(8,128)S(1)}, f32[32,1,32,128]{3,2,0,1:T(8,128)S(1)}, u32[]{:S(2)}, u32[]{:S(2)}) %collective-permute-start.6) | collective-permute-done | bytes 524320 | tf_op jit(solution)/shard_map/ppermute | solution.py:84
  84.4 2.1 %fusion.15 = f32[32,128,2,64]{1,3,2,0:T(8,128)S(1)} fusion(f32[32,1,32,128]{3,2,0,1:T(8,128)S(1)} %collective-permute-done.6, f32[2,32,1,32,128]{4,3,1,0,2:T(8,128)} %bitcast.207, s32[]{:T(128)S(6)} %select_n.150, pred[]{:T(512)S(6)} %eq.47, f32[1,64,2,32]{1,3,0,2:T(8,128)S(1)} %get-tuple-element.9, f32[1,64,2,32]{1,3,0,2:T(8,128)S(1)} %get-tuple-element.8), kind=kOutput, calls=%fused_computation.26 | convolution fusion | flops 100798464 | bytes 3178501 | tf_op jit(solution)/shard_map/eyj,xrjl->rxeyl/dot_general | solution.py:200
  86.4 2.4 %add_bitcast_fusion.in_ref = f32[32,2,64,128]{3,2,1,0:T(8,128)} fusion(f32[32,128,2,64]{1,3,2,0:T(8,128)S(1)} %fusion.15, f32[32,1,32,128]{3,2,0,1:T(8,128)S(1)} %collective-permute-done.6, f32[2,32,1,32,128]{4,3,1,0,2:T(8,128)S(1)} %bitcast.208, s32[]{:T(128)S(6)} %select_n.150, pred[]{:T(512)S(6)} %eq.46, f32[1,64,2,32]{1,3,0,2:T(8,128)S(1)} %get-tuple-element.8, ...), kind=kOutput, calls=%fused_computation.16 | convolution fusion | flops 101322752 | bytes 5308421 | tf_op jit(solution)/shard_map/eyj,xrjl->rxeyl/dot_general | solution.py:200
  88.8 3.0 %shard_map.74 = f32[1,32,64,128]{3,2,1,0:T(8,128)} custom-call(s32[1]{0:T(128)} %constant.80.clone.1.me_ref, f32[32,2,64,128]{3,2,1,0:T(8,128)} %add_bitcast_fusion.in_ref), custom_call_target="tpu_custom_call" | custom-call | flops 786432 | bytes 3145728 | tf_op jit(solution)/shard_map/pallas_call | solution.py:44
  91.8 1.9 %convolution_multiply_fusion = f32[32,64,64]{2,1,0:T(8,128)S(1)} fusion(f32[1,32,64,128]{3,2,1,0:T(8,128)} %shard_map.74, f32[64,64]{0,1:T(8,128)S(1)} %get-tuple-element.10, f32[64,64]{0,1:T(8,128)S(1)} %get-tuple-element.11), kind=kOutput, calls=%fused_computation.17 | convolution fusion | flops 100802560 | bytes 1605632 | tf_op jit(solution)/shard_map/rxyl,lz->rxyz/dot_general | solution.py:206
  94.9 1.6 %gather_fusion = f32[8,512]{1,0:T(8,128)S(1)} fusion(f32[256,512]{1,0:T(8,128)} %reshape.307, s32[1024]{0:T(1024)S(1)} %pad_clamp_fusion), kind=kCustom, calls=%fused_computation | custom fusion | bytes 32800 | tf_op jit(solution)/shard_map/gather | solution.py:213
  96.5 1.6 %fusion.94 = f32[8,512]{1,0:T(8,128)S(1)} fusion(f32[8,512]{1,0:T(8,128)S(1)} %gather_fusion, f32[512,512]{1,0:T(8,128)} %param.9), kind=kOutput, calls=%fused_computation.140 | convolution fusion | flops 12582912 | bytes 1081344 | tf_op jit(solution)/shard_map/dot_general | solution.py:222
  98.2 9.6 %all_to_all.5 = f32[8,2,512]{2,1,0:T(2,128)S(1)} all-to-all(f32[8,2,512]{2,1,0:T(2,128)S(1)} %reshape.309), channel_id=1, replica_groups=mesh['grp'=2,'rot'=4,'sub'=2,'ref'=2] {'rot','ref'}, dimensions={0} | all-to-all | bytes 65536 | tf_op jit(solution)/shard_map/all_to_all | solution.py:224
  (59 shorter events, 11.1 us)
Async XLA Ops:
  0.6 1.6 %copy-start = (f32[2,4,16,32,64]{4,3,2,1,0:T(8,128)S(1)}, f32[2,4,16,32,64]{4,3,2,1,0:T(8,128)}, u32[]{:S(2)}) copy-start(f32[2,4,16,32,64]{4,3,2,1,0:T(8,128)} %param.6) | copy-start | bytes 3145732
  3.3 30.3 %collective-permute-start.2 = (bf16[4,16,16,128]{3,1,2,0:T(8,128)(2,1)}, bf16[4,16,16,128]{3,1,2,0:T(8,128)(2,1)S(1)}, u32[]{:S(2)}, u32[]{:S(2)}) collective-permute-start(bf16[4,16,16,128]{3,1,2,0:T(8,128)(2,1)} %fusion.91), channel_id=1, source_target_pairs={{0,12},{4,0},{8,4},{12,8},{1,13},{5,1},{9,5},{13,9},{2,14},{6,2},{... | collective-permute-start | bytes 786440 | tf_op jit(solution)/shard_map/ppermute | solution.py:67
  8.3 25.3 %collective-permute-start.3 = (bf16[4,16,16,128]{3,1,2,0:T(8,128)(2,1)}, bf16[4,16,16,128]{3,1,2,0:T(8,128)(2,1)S(1)}, u32[]{:S(2)}, u32[]{:S(2)}) collective-permute-start(bf16[4,16,16,128]{3,1,2,0:T(8,128)(2,1)} %fusion.91), channel_id=1, source_target_pairs={{0,8},{4,12},{8,0},{12,4},{1,9},{5,13},{9,1},{13,5},{2,10},{6,14},... | collective-permute-start | bytes 786440 | tf_op jit(solution)/shard_map/ppermute | solution.py:67
  8.3 25.3 %collective-permute-start.4 = (bf16[4,16,16,128]{3,1,2,0:T(8,128)(2,1)}, bf16[4,16,16,128]{3,1,2,0:T(8,128)(2,1)S(1)}, u32[]{:S(2)}, u32[]{:S(2)}) collective-permute-start(bf16[4,16,16,128]{3,1,2,0:T(8,128)(2,1)} %fusion.91), channel_id=1, source_target_pairs={{0,4},{4,8},{8,12},{12,0},{1,5},{5,9},{9,13},{13,1},{2,6},{6,10},{... | collective-permute-start | bytes 786440 | tf_op jit(solution)/shard_map/ppermute | solution.py:67
  9.6 13.7 %copy-start.5 = (f32[1,64,64]{2,1,0:T(8,128)}, f32[1,64,64]{2,1,0:T(8,128)S(1)}, u32[]{:S(2)}) copy-start(f32[1,64,64]{2,1,0:T(8,128)S(1)} %get-tuple-element.12) | copy-start | bytes 49156
  9.6 13.7 %copy-start.7 = (f32[1,64,64]{2,1,0:T(8,128)}, f32[1,64,64]{2,1,0:T(8,128)S(1)}, u32[]{:S(2)}) copy-start(f32[1,64,64]{2,1,0:T(8,128)S(1)} %get-tuple-element.13) | copy-start | bytes 49156
  18.7 3.9 %copy-start.4 = (bf16[1,4,32,64,64]{4,3,2,1,0:T(8,128)(2,1)S(1)}, bf16[1,4,32,64,64]{4,3,2,1,0:T(8,128)(2,1)}, u32[]{:S(2)}) copy-start(bf16[1,4,32,64,64]{4,3,2,1,0:T(8,128)(2,1)} %param.5) | copy-start | bytes 3145732
  21.1 14.5 %collective-permute-start = (bf16[1,2,32,32,128]{4,2,3,1,0:T(8,128)(2,1)}, bf16[1,2,32,32,128]{4,2,3,1,0:T(8,128)(2,1)S(1)}, u32[]{:S(2)}, u32[]{:S(2)}) collective-permute-start(bf16[1,2,32,32,128]{4,2,3,1,0:T(8,128)(2,1)} %copy.15), channel_id=1, source_target_pairs={{0,2},{2,0},{1,3},{3,1},{4,6},{6,4},{5,7},{7,5},{8,10},{10,8},{9,1... | collective-permute-start | bytes 1572872 | tf_op jit(solution)/shard_map/ppermute | solution.py:84
  32.7 12.8 %collective-permute-start.1 = (bf16[1,2,32,32,128]{4,2,3,1,0:T(8,128)(2,1)}, bf16[1,2,32,32,128]{4,2,3,1,0:T(8,128)(2,1)S(1)}, u32[]{:S(2)}, u32[]{:S(2)}) collective-permute-start(bf16[1,2,32,32,128]{4,2,3,1,0:T(8,128)(2,1)} %copy.18), channel_id=1, source_target_pairs={{0,2},{2,0},{1,3},{3,1},{4,6},{6,4},{5,7},{7,5},{8,10},{10,8},{9,1... | collective-permute-start | bytes 1572872 | tf_op jit(solution)/shard_map/ppermute | solution.py:84
  35.4 18.4 %collective-permute-start.5 = (bf16[4,4,16,16,128]{4,2,3,1,0:T(8,128)(2,1)}, bf16[4,4,16,16,128]{4,2,3,1,0:T(8,128)(2,1)}, u32[]{:S(2)}, u32[]{:S(2)}) collective-permute-start(bf16[4,4,16,16,128]{4,2,3,1,0:T(8,128)(2,1)} %constant_dynamic-slice_fusion), channel_id=1, source_target_pairs={{0,1},{1,0},{2,3},{3,2},{4,5},{5,4},{6,7},{7,6},{8,9},{9,8},{10,11... | collective-permute-start | bytes 3145736 | tf_op jit(solution)/shard_map/ppermute | solution.py:67
  58.3 4.4 %copy-start.6 = (f32[1,64,64]{2,1,0:T(8,128)S(1)}, f32[1,64,64]{2,1,0:T(8,128)}, u32[]{:S(2)}) copy-start(f32[1,64,64]{2,1,0:T(8,128)} %copy-done.5) | copy-start | bytes 49156
  58.3 4.4 %copy-start.8 = (f32[1,64,64]{2,1,0:T(8,128)S(1)}, f32[1,64,64]{2,1,0:T(8,128)}, u32[]{:S(2)}) copy-start(f32[1,64,64]{2,1,0:T(8,128)} %copy-done.7) | copy-start | bytes 49156
  67.4 5.2 %copy-start.9 = (s32[1,1,1,8]{3,2,1,0:T(1,128)S(1)}, s32[1,1,1,8]{3,2,1,0:T(1,128)}, u32[]{:S(2)}) copy-start(s32[1,1,1,8]{3,2,1,0:T(1,128)} %param.7) | copy-start | bytes 100
  67.4 5.2 %copy-start.10 = (s32[1,1,1,8,1]{3,4,2,1,0:T(1,128)S(1)}, s32[1,1,1,8,1]{3,4,2,1,0:T(1,128)}, u32[]{:S(2)}) copy-start(s32[1,1,1,8,1]{3,4,2,1,0:T(1,128)} %param.8) | copy-start | bytes 100
  70.0 16.4 %copy-start.2 = (f32[1,64,32,128]{3,2,1,0:T(8,128)S(1)}, f32[1,64,32,128]{3,2,1,0:T(8,128)}, u32[]{:S(2)}) copy-start(f32[1,64,32,128]{3,2,1,0:T(8,128)} %shard_map.73) | copy-start | bytes 3145732
  71.2 13.2 %collective-permute-start.6 = (f32[32,1,32,128]{3,2,0,1:T(8,128)S(1)}, f32[32,1,32,128]{3,2,0,1:T(8,128)S(1)}, u32[]{:S(2)}, u32[]{:S(2)}) collective-permute-start(f32[32,1,32,128]{3,2,0,1:T(8,128)S(1)} %dynamic-slice_bitcast_fusion), channel_id=1, source_target_pairs={{0,2},{2,0},{1,3},{3,1},{4,6},{6,4},{5,7},{7,5},{8,10},{10,8},{9,1... | collective-permute-start | bytes 1572872 | tf_op jit(solution)/shard_map/ppermute | solution.py:84
  88.8 19.7 %copy-start.1 = (f32[2,4,16,32,64]{4,3,2,1,0:T(8,128)S(1)}, f32[2,4,16,32,64]{4,3,2,1,0:T(8,128)}, u32[]{:S(2)}) copy-start(f32[2,4,16,32,64]{4,3,2,1,0:T(8,128)} %param.6) | copy-start | bytes 3145732
  93.7 14.8 %copy-start.3 = (f32[32,64,64]{2,1,0:T(8,128)}, f32[32,64,64]{2,1,0:T(8,128)S(1)}, u32[]{:S(2)}) copy-start(f32[32,64,64]{2,1,0:T(8,128)S(1)} %convolution_multiply_fusion) | copy-start | bytes 1572868

commit v15 on v14

--- a/solution.py
+++ b/solution.py
@@ -93,6 +93,14 @@
             chosen = jnp.where(index == source, piece, chosen)
         ordered.append(chosen)
     return ordered
+
+
+def exact_times(spec, table, values):
+    high = table.astype(jnp.bfloat16)
+    low = (table - high.astype(jnp.float32)).astype(jnp.bfloat16)
+    return jnp.einsum(spec, high, values, preferred_element_type=jnp.float32) + jnp.einsum(
+        spec, low, values, preferred_element_type=jnp.float32
+    )
 
 
 def gather_receptor(receptor):
@@ -167,21 +175,17 @@
     part_terms = terms // chunks
     pair_x = pair.reshape(2, length, n_sub, x_local)
     z_table = jnp.concatenate([cos_table, -sin_table], axis=1)
-    values = ligand.astype(jnp.float32)
     spectra = []
     for chunk in range(chunks):
-        part = values[:, chunk * part_terms:(chunk + 1) * part_terms]
-        along_z = jnp.einsum("rtxyz,zl->rtxyl", part, z_table, precision=highest)
+        part = ligand[:, chunk * part_terms:(chunk + 1) * part_terms]
+        along_z = exact_times("zl,rtxyz->rtxyl", z_table, part)
         along_y = jnp.einsum("ejy,rtxyl->rtxejl", pair, along_z, precision=highest)
         sending = combine_call(
             along_y.reshape(-1, 2, ny, 2 * length), 1.0, -1.0, n_sub, jnp.bfloat16,
             lax.axis_index("sub"),
         ).reshape(n_sub, rots, part_terms, x_local, y_local, 2 * length)
         along_x = sum(
-            jnp.einsum(
-                "ekx,rtxjl->rtjekl", pair_x[:, :, source], piece.astype(jnp.float32),
-                precision=highest,
-            )
+            exact_times("ekx,rtxjl->rtjekl", pair_x[:, :, source], piece)
             for source, piece in enumerate(by_source(exchange(sending, "sub", rotated=True)))
         )
         spectrum = combine_call(

time: 109 us -> 128 us (1.17)
  matrix products: 30.1 us -> 41.6 us
  waiting for transfers between devices: 13.1 us -> 18.3 us
  local copies, waits for them, and re-layouts: 17.1 us -> 18.5 us
    dot_general x6 -> x12, matrix products: 12.5 us -> 22.2 us  [the longest x6 13.9 us: exact_times(): jnp.einsum(spec, high, values, preferred_element_type=jnp.float32)]
    ppermute x3, waiting for transfers between devices: 13.1 us -> 18.3 us  [exchange(): lax.ppermute(entry(shift), axis, pairs)]
    dot_general x2, matrix products: 7.45 us -> 9.07 us  [local(): along_y = jnp.einsum('ejy,rtxyl->rtxejl', pair, along_z, precision=highest)]
    unnamed x29 -> x31, local copies, waits for them, and re-layouts: 2.45 us -> 3.89 us
  transfers between devices with their start and end apart: 7 -> 7, of which waited for: 2 -> 2; matrix products, arithmetic and copies ran while one was open for 25% -> 30% of each run, Pallas kernels for 12% -> 11%
where the time goes in v15:
time: 128 us; the launch traced here: 127 us
  matrix products  41.6 us (32%)
  Pallas kernels  23.4 us (18%)
  local copies, waits for them, and re-layouts  18.5 us (14%)
  waiting for transfers between devices  18.3 us (14%)
  blocking collectives  10.2 us (8%)
  starting transfers between devices  9.41 us (7%)
  other arithmetic  4.63 us (4%)
    pallas_call x6, Pallas kernels, combine_call(): pl.pallas_call(functools.partial(combine_kernel, first=first, second=seco...  19 us
    ppermute x3, waiting for transfers between devices, exchange(): lax.ppermute(entry(shift), axis, pairs)  18.3 us
    dot_general x6, matrix products, exact_times(): jnp.einsum(spec, high, values, preferred_element_type=jnp.float32)  13.9 us
    all_to_all x1, blocking collectives, local(): lax.all_to_all(packed, ('rot', 'ref'), split_axis=0, concat_axis=0, tiled...  10.2 us
    dot_general x2, matrix products, local(): along_y = jnp.einsum('ejy,rtxyl->rtxejl', pair, along_z, precision=highest)  9.07 us
    dot_general x6, matrix products, exact_times(): jnp.einsum(spec, low, values, preferred_element_type=jnp.float32)  8.37 us
    ppermute x4, starting transfers between devices, gather_by_shifts(): pieces.append(lax.ppermute(piece, axis, pairs))  6.06 us
    dot_general x2, matrix products, local(): jnp.einsum('eyj,xrjl->rxeyl', pair_y[:, :, source], piece, precision=high...  4.58 us
  transfers between devices with their start and end apart: 7, of which 2 were waited for; matrix products, arithmetic and copies ran while one was open for 30% of the time, Pallas kernels for 11%

profile of v15, /device:TPU:0, one launch (start us, length us, event | category | flops | bytes accessed | tf_op | source)
XLA Modules:
  0.0 127.1 jit_solution(10985947614499576430)
XLA Ops:
  0.7 1.6 %copy-done = f32[2,4,16,32,64]{4,3,2,1,0:T(8,128)S(1)} copy-done((f32[2,4,16,32,64]{4,3,2,1,0:T(8,128)S(1)}, f32[2,4,16,32,64]{4,3,2,1,0:T(8,128)}, u32[]{:S(2)}) %copy-start) | copy-done | bytes 1048600
  3.3 5.0 %collective-permute-start.2 = (bf16[4,16,16,128]{3,1,2,0:T(8,128)(2,1)}, bf16[4,16,16,128]{3,1,2,0:T(8,128)(2,1)S(1)}, u32[]{:S(2)}, u32[]{:S(2)}) collective-permute-start(bf16[4,16,16,128]{3,1,2,0:T(8,128)(2,1)} %fusion.111), channel_id=1, source_target_pairs={{0,12},{4,0},{8,4},{12,8},{1,13},{5,1},{9,5},{13,9},{2,14},{6,2},{... | collective-permute-start | bytes 786440 | tf_op jit(solution)/shard_map/ppermute | solution.py:67
  9.5 1.7 %fusion.17 = f32[128,2,32,64]{0,3,2,1:T(8,128)S(1)} fusion(bf16[1,4,32,64,64]{4,3,2,1,0:T(8,128)(2,1)} %param.5, f32[64,64]{0,1:T(8,128)S(1)} %get-tuple-element.12, f32[64,64]{0,1:T(8,128)S(1)} %get-tuple-element.13), kind=kOutput, calls=%fused_computation.27 | convolution fusion | flops 67141632 | bytes 3178496 | tf_op jit(solution)/shard_map/zl,rtxyz->rtxyl/dot_general | solution.py:101
  11.1 3.0 %fusion.15 = f32[128,2,32,64]{0,3,2,1:T(8,128)} fusion(bf16[1,4,32,64,64]{4,3,2,1,0:T(8,128)(2,1)} %param.5, f32[64,64]{0,1:T(8,128)S(1)} %get-tuple-element.12, f32[64,64]{0,1:T(8,128)S(1)} %get-tuple-element.13), kind=kOutput, calls=%fused_computation.25 | convolution fusion | flops 67149824 | bytes 3178496 | tf_op jit(solution)/shard_map/zl,rtxyz->rtxyl/dot_general | solution.py:101
  14.3 5.3 %fusion.6 = f32[2,32,128,2,64]{2,4,3,1,0:T(8,128)} fusion(f32[128,2,32,64]{0,3,2,1:T(8,128)S(1)} %fusion.17, f32[128,2,32,64]{0,3,2,1:T(8,128)} %fusion.15, f32[1,64,64]{2,1,0:T(8,128)S(1)} %get-tuple-element.14, f32[1,64,64]{2,1,0:T(8,128)S(1)} %get-tuple-element.15), kind=kOutput, calls=%fused_computation.13 | convolution fusion | flops 403185664 | bytes 8421376 | tf_op jit(solution)/shard_map/ejy,rtxyl->rtxejl/dot_general | solution.py:182
  19.7 3.4 %shard_map.68 = bf16[2,64,32,128]{3,2,1,0:T(8,128)(2,1)} custom-call(s32[1]{0:T(128)} %bitcast.me_ref, f32[64,2,64,128]{3,2,1,0:T(8,128)} %bitcast.242), custom_call_target="tpu_custom_call" | custom-call | flops 1572864 | bytes 5242880 | tf_op jit(solution)/shard_map/pallas_call | solution.py:44
  23.0 1.4 %fusion.113 = (bf16[1,64,32,128]{3,2,1,0:T(8,128)(2,1)S(1)}, bf16[1,64,32,128]{3,2,1,0:T(8,128)(2,1)S(1)}) fusion(bf16[2,64,32,128]{3,2,1,0:T(8,128)(2,1)} %shard_map.68), kind=kLoop, calls=%fused_computation.161 | loop fusion | bytes 2097152 | tf_op jit(solution)/shard_map/slice | solution.py:78
  25.4 1.5 %collective-permute-start = (bf16[1,2,32,32,128]{4,2,3,1,0:T(8,128)(2,1)}, bf16[1,2,32,32,128]{4,2,3,1,0:T(8,128)(2,1)S(1)}, u32[]{:S(2)}, u32[]{:S(2)}) collective-permute-start(bf16[1,2,32,32,128]{4,2,3,1,0:T(8,128)(2,1)} %copy.15), channel_id=1, source_target_pairs={{0,2},{2,0},{1,3},{3,1},{4,6},{6,4},{5,7},{7,5},{8,10},{10,8},{9,1... | collective-permute-start | bytes 1572872 | tf_op jit(solution)/shard_map/ppermute | solution.py:84
  27.8 3.7 %fusion.4 = f32[2,32,128,2,64]{2,4,3,1,0:T(8,128)} fusion(f32[128,2,32,64]{0,3,2,1:T(8,128)S(1)} %fusion.13, f32[128,2,32,64]{0,3,2,1:T(8,128)S(1)} %fusion.11, f32[1,64,64]{2,1,0:T(8,128)S(1)} %get-tuple-element.14, f32[1,64,64]{2,1,0:T(8,128)S(1)} %get-tuple-element.15), kind=kOutput, calls=%fused_computation.11 | convolution fusion | flops 403185664 | bytes 8421376 | tf_op jit(solution)/shard_map/ejy,rtxyl->rtxejl/dot_general | solution.py:182
  31.6 3.4 %shard_map.70 = bf16[2,64,32,128]{3,2,1,0:T(8,128)(2,1)} custom-call(s32[1]{0:T(128)} %bitcast.me_ref, f32[64,2,64,128]{3,2,1,0:T(8,128)} %bitcast.243), custom_call_target="tpu_custom_call" | custom-call | flops 1572864 | bytes 5242880 | tf_op jit(solution)/shard_map/pallas_call | solution.py:44
  42.4 7.5 %collective-permute-done.1 = bf16[1,2,32,32,128]{4,2,3,1,0:T(8,128)(2,1)S(1)} collective-permute-done((bf16[1,2,32,32,128]{4,2,3,1,0:T(8,128)(2,1)}, bf16[1,2,32,32,128]{4,2,3,1,0:T(8,128)(2,1)S(1)}, u32[]{:S(2)}, u32[]{:S(2)}) %collective-permute-start.1) | collective-permute-done | bytes 524320 | tf_op jit(solution)/shard_map/ppermute | solution.py:84
  49.9 2.7 %fusion.26 = f32[2,32,128,2,64]{2,4,3,1,0:T(8,128)} fusion(bf16[1,2,32,32,128]{4,2,3,1,0:T(8,128)(2,1)S(1)} %collective-permute-done.1, pred[]{:T(512)S(6)} %eq.47, bf16[1,2,32,32,128]{4,3,2,1,0:T(8,128)(2,1)S(1)} %bitcast.236, f32[2,64,1,32]{1,3,0,2:T(8,128)S(1)} %get-tuple-element.9), kind=kOutput, calls=%fused_computation.39 | convolution fusion | flops 67387392 | bytes 5259265 | tf_op jit(solution)/shard_map/ekx,rtxjl->rtjekl/dot_general | solution.py:101
  52.6 3.0 %add_add_fusion.1 = f32[2,32,128,2,64]{2,4,3,1,0:T(8,128)} fusion(f32[2,32,128,2,64]{2,4,3,1,0:T(8,128)S(1)} %fusion.33, f32[2,32,128,2,64]{2,4,3,1,0:T(8,128)S(1)} %fusion.38, f32[2,32,128,2,64]{2,4,3,1,0:T(8,128)S(1)} %fusion.36, bf16[1,2,32,32,128]{4,2,3,1,0:T(8,128)(2,1)S(1)} %collective-permute-done, pred[]{:T(512)S(6)} %eq.47, ...), kind=kOutput, calls=%fused_computation.6 | convolution fusion | flops 70520832 | bytes 17842176 | tf_op jit(solution)/shard_map/ekx,rtxjl->rtjekl/dot_general | solution.py:101
  55.6 2.7 %fusion.31 = f32[2,32,128,2,64]{2,4,3,1,0:T(8,128)} fusion(bf16[1,2,32,32,128]{4,2,3,1,0:T(8,128)(2,1)S(1)} %collective-permute-done.1, pred[]{:T(512)S(6)} %eq.46, bf16[1,2,32,32,128]{4,3,2,1,0:T(8,128)(2,1)S(1)} %bitcast.237, f32[2,64,1,32]{1,3,0,2:T(8,128)S(1)} %get-tuple-element.8), kind=kOutput, calls=%fused_computation.44 | convolution fusion | flops 67375104 | bytes 5259265 | tf_op jit(solution)/shard_map/ekx,rtxjl->rtjekl/dot_general | solution.py:101
  58.4 3.4 %shard_map.69 = bf16[1,64,64,128]{3,2,1,0:T(8,128)(2,1)} custom-call(s32[1]{0:T(128)} %constant.80.clone.1.me_ref, f32[64,2,64,128]{3,2,1,0:T(8,128)} %bitcast.240), custom_call_target="tpu_custom_call" | custom-call | flops 1572864 | bytes 5242880 | tf_op jit(solution)/shard_map/pallas_call | solution.py:44
  62.5 1.4 %copy-done.2 = f32[2,32,128,2,64]{2,4,3,1,0:T(8,128)S(1)} copy-done((f32[2,32,128,2,64]{2,4,3,1,0:T(8,128)S(1)}, f32[2,32,128,2,64]{2,4,3,1,0:T(8,128)}, u32[]{:S(2)}) %copy-start.2) | copy-done | bytes 4194328
  63.9 5.2 %add_add_fusion = f32[2,32,128,2,64]{2,4,3,1,0:T(8,128)} fusion(f32[2,32,128,2,64]{2,4,3,1,0:T(8,128)S(1)} %copy-done.2, f32[2,32,128,2,64]{2,4,3,1,0:T(8,128)} %fusion.31, f32[2,32,128,2,64]{2,4,3,1,0:T(8,128)S(1)} %fusion.29, bf16[1,2,32,32,128]{4,2,3,1,0:T(8,128)(2,1)S(1)} %collective-permute-done.1, pred[]{:T(512)S(6)} %eq.47, ...), kind=kOutput, calls=%fused_computation.5 | convolution fusion | flops 70520832 | bytes 17842176 | tf_op jit(solution)/shard_map/ekx,rtxjl->rtjekl/dot_general | solution.py:101
  69.2 3.3 %shard_map.71 = bf16[1,64,64,128]{3,2,1,0:T(8,128)(2,1)} custom-call(s32[1]{0:T(128)} %constant.80.clone.1.me_ref, f32[64,2,64,128]{3,2,1,0:T(8,128)} %bitcast.241), custom_call_target="tpu_custom_call" | custom-call | flops 1572864 | bytes 5242880 | tf_op jit(solution)/shard_map/pallas_call | solution.py:44
  72.5 2.7 %fusion.3 = bf16[4,2,16,4,16,128]{5,2,4,0,3,1:T(8,128)(2,1)S(1)} fusion(s32[]{:T(128)S(6)} %select_n.146, bf16[1,4,4,16,16,128]{5,3,4,2,1,0:T(8,128)(2,1)} %bitcast.79, bf16[1,4,4,16,16,128]{5,3,4,2,1,0:T(8,128)(2,1)S(1)} %fusion.119), kind=kLoop, calls=%fused_computation.10 | loop fusion | flops 3145728 | bytes 4194308 | tf_op jit(solution)/shard_map/transpose | solution.py:116
  75.2 1.9 %copy.21 = bf16[4,2,16,4,16,128]{5,4,3,2,1,0:T(8,128)(2,1)} copy(bf16[4,2,16,4,16,128]{5,2,4,0,3,1:T(8,128)(2,1)S(1)} %fusion.3) | data formatting | bytes 4194304 | tf_op jit(solution)/shard_map/transpose | solution.py:116
  77.1 4.3 %shard_map.72 = f32[1,2048,128]{2,1,0:T(8,128)} custom-call(bf16[1,2,2048,128]{3,2,1,0:T(8,128)(2,1)} %bitcast.251, bf16[1,2,2048,128]{3,2,1,0:T(8,128)(2,1)} %bitcast.252, bf16[4,2048,128]{2,1,0:T(8,128)(2,1)} %bitcast.244), custom_call_target="tpu_custom_call" | custom-call | flops 8388608 | bytes 5242880 | tf_op jit(solution)/shard_map/pallas_call | solution.py:147
  81.4 2.2 %fusion.44 = f32[32,128,2,64]{1,3,2,0:T(8,128)S(1)} fusion(f32[32,64,128,1]{2,1,3,0:T(8,128)} %bitcast.249, f32[1,64,64]{2,1,0:T(8,128)S(1)} %copy-done.7, f32[1,64,64]{2,1,0:T(8,128)S(1)} %copy-done.9), kind=kOutput, calls=%fused_computation.77 | convolution fusion | flops 201334784 | bytes 3178496 | tf_op jit(solution)/shard_map/exk,rjkl->xrejl/dot_general | solution.py:199
  83.6 2.5 %copy.68 = f32[32,128,2,64]{1,0,2,3:T(8,128)} copy(f32[32,128,2,64]{1,3,2,0:T(8,128)S(1)} %fusion.44) | data formatting | bytes 4194304 | tf_op jit(solution)/shard_map/exk,rjkl->xrejl/dot_general | solution.py:199
  86.2 2.6 %shard_map.73 = f32[1,64,32,128]{3,2,1,0:T(8,128)} custom-call(s32[1]{0:T(128)} %constant.80.clone.1.me_ref, f32[64,2,32,128]{3,2,1,0:T(8,128)} %bitcast.245), custom_call_target="tpu_custom_call" | custom-call | flops 786432 | bytes 3145728 | tf_op jit(solution)/shard_map/pallas_call | solution.py:44
  91.5 10.8 %collective-permute-done.6 = f32[32,1,32,128]{3,2,0,1:T(8,128)} collective-permute-done((f32[32,1,32,128]{3,2,0,1:T(8,128)S(1)}, f32[32,1,32,128]{3,2,0,1:T(8,128)}, u32[]{:S(2)}, u32[]{:S(2)}) %collective-permute-start.6) | collective-permute-done | bytes 524320 | tf_op jit(solution)/shard_map/ppermute | solution.py:84
  102.2 2.2 %fusion.23 = f32[32,128,2,64]{1,3,2,0:T(8,128)S(1)} fusion(f32[32,1,32,128]{3,2,0,1:T(8,128)} %collective-permute-done.6, f32[2,32,1,32,128]{4,3,1,0,2:T(8,128)} %bitcast.247, s32[]{:T(128)S(6)} %select_n.150, pred[]{:T(512)S(6)} %eq.47, f32[2,64,1,32]{1,3,0,2:T(8,128)S(1)} %get-tuple-element.9), kind=kOutput, calls=%fused_computation.34 | convolution fusion | flops 100794368 | bytes 3162117 | tf_op jit(solution)/shard_map/eyj,xrjl->rxeyl/dot_general | solution.py:204
  104.5 2.4 %add_bitcast_fusion.in_ref = f32[32,2,64,128]{3,2,1,0:T(8,128)} fusion(f32[32,128,2,64]{1,3,2,0:T(8,128)S(1)} %fusion.23, f32[32,1,32,128]{3,2,0,1:T(8,128)} %collective-permute-done.6, f32[2,32,1,32,128]{4,3,1,0,2:T(8,128)S(1)} %bitcast.248, s32[]{:T(128)S(6)} %select_n.150, pred[]{:T(512)S(6)} %eq.46, f32[2,64,1,32]{1,3,0,2:T(8,128)S(1)} %get-tuple-element.8), kind=kOutput, calls=%fused_computation.16 | convolution fusion | flops 101318656 | bytes 5275653 | tf_op jit(solution)/shard_map/eyj,xrjl->rxeyl/dot_general | solution.py:204
  106.8 3.0 %shard_map.74 = f32[1,32,64,128]{3,2,1,0:T(8,128)} custom-call(s32[1]{0:T(128)} %constant.80.clone.1.me_ref, f32[32,2,64,128]{3,2,1,0:T(8,128)} %add_bitcast_fusion.in_ref), custom_call_target="tpu_custom_call" | custom-call | flops 786432 | bytes 3145728 | tf_op jit(solution)/shard_map/pallas_call | solution.py:44
  109.9 1.9 %convolution_multiply_fusion = f32[32,64,64]{2,1,0:T(8,128)S(1)} fusion(f32[1,32,64,128]{3,2,1,0:T(8,128)} %shard_map.74, f32[64,64]{0,1:T(8,128)S(1)} %get-tuple-element.12, f32[64,64]{0,1:T(8,128)S(1)} %get-tuple-element.13), kind=kOutput, calls=%fused_computation.19 | convolution fusion | flops 100802560 | bytes 1605632 | tf_op jit(solution)/shard_map/rxyl,lz->rxyz/dot_general | solution.py:210
  112.9 1.6 %gather_fusion = f32[8,512]{1,0:T(8,128)S(1)} fusion(f32[256,512]{1,0:T(8,128)} %reshape.333, s32[1024]{0:T(1024)S(1)} %pad_clamp_fusion), kind=kCustom, calls=%fused_computation | custom fusion | bytes 32800 | tf_op jit(solution)/shard_map/gather | solution.py:217
  114.5 1.6 %fusion.114 = f32[8,512]{1,0:T(8,128)S(1)} fusion(f32[8,512]{1,0:T(8,128)S(1)} %gather_fusion, f32[512,512]{1,0:T(8,128)} %param.9), kind=kOutput, calls=%fused_computation.162 | convolution fusion | flops 12582912 | bytes 1081344 | tf_op jit(solution)/shard_map/dot_general | solution.py:226
  116.3 10.2 %all_to_all.5 = f32[8,2,512]{2,1,0:T(2,128)S(1)} all-to-all(f32[8,2,512]{2,1,0:T(2,128)S(1)} %reshape.335), channel_id=1, replica_groups=mesh['grp'=2,'rot'=4,'sub'=2,'ref'=2] {'rot','ref'}, dimensions={0} | all-to-all | bytes 65536 | tf_op jit(solution)/shard_map/all_to_all | solution.py:228
  (68 shorter events, 16.9 us)
Async XLA Ops:
  0.6 1.6 %copy-start = (f32[2,4,16,32,64]{4,3,2,1,0:T(8,128)S(1)}, f32[2,4,16,32,64]{4,3,2,1,0:T(8,128)}, u32[]{:S(2)}) copy-start(f32[2,4,16,32,64]{4,3,2,1,0:T(8,128)} %param.6) | copy-start | bytes 3145732
  3.3 34.8 %collective-permute-start.2 = (bf16[4,16,16,128]{3,1,2,0:T(8,128)(2,1)}, bf16[4,16,16,128]{3,1,2,0:T(8,128)(2,1)S(1)}, u32[]{:S(2)}, u32[]{:S(2)}) collective-permute-start(bf16[4,16,16,128]{3,1,2,0:T(8,128)(2,1)} %fusion.111), channel_id=1, source_target_pairs={{0,12},{4,0},{8,4},{12,8},{1,13},{5,1},{9,5},{13,9},{2,14},{6,2},{... | collective-permute-start | bytes 786440 | tf_op jit(solution)/shard_map/ppermute | solution.py:67
  8.3 29.8 %collective-permute-start.3 = (bf16[4,16,16,128]{3,1,2,0:T(8,128)(2,1)}, bf16[4,16,16,128]{3,1,2,0:T(8,128)(2,1)S(1)}, u32[]{:S(2)}, u32[]{:S(2)}) collective-permute-start(bf16[4,16,16,128]{3,1,2,0:T(8,128)(2,1)} %fusion.111), channel_id=1, source_target_pairs={{0,8},{4,12},{8,0},{12,4},{1,9},{5,13},{9,1},{13,5},{2,10},{6,14},... | collective-permute-start | bytes 786440 | tf_op jit(solution)/shard_map/ppermute | solution.py:67
  8.3 29.8 %collective-permute-start.4 = (bf16[4,16,16,128]{3,1,2,0:T(8,128)(2,1)}, bf16[4,16,16,128]{3,1,2,0:T(8,128)(2,1)S(1)}, u32[]{:S(2)}, u32[]{:S(2)}) collective-permute-start(bf16[4,16,16,128]{3,1,2,0:T(8,128)(2,1)} %fusion.111), channel_id=1, source_target_pairs={{0,4},{4,8},{8,12},{12,0},{1,5},{5,9},{9,13},{13,1},{2,6},{6,10},{... | collective-permute-start | bytes 786440 | tf_op jit(solution)/shard_map/ppermute | solution.py:67
  14.3 13.5 %copy-start.6 = (f32[1,64,64]{2,1,0:T(8,128)}, f32[1,64,64]{2,1,0:T(8,128)S(1)}, u32[]{:S(2)}) copy-start(f32[1,64,64]{2,1,0:T(8,128)S(1)} %get-tuple-element.14) | copy-start | bytes 49156
  14.3 13.5 %copy-start.8 = (f32[1,64,64]{2,1,0:T(8,128)}, f32[1,64,64]{2,1,0:T(8,128)S(1)}, u32[]{:S(2)}) copy-start(f32[1,64,64]{2,1,0:T(8,128)S(1)} %get-tuple-element.15) | copy-start | bytes 49156
  23.0 3.9 %copy-start.3 = (bf16[1,4,32,64,64]{4,3,2,1,0:T(8,128)(2,1)S(1)}, bf16[1,4,32,64,64]{4,3,2,1,0:T(8,128)(2,1)}, u32[]{:S(2)}) copy-start(bf16[1,4,32,64,64]{4,3,2,1,0:T(8,128)(2,1)} %param.5) | copy-start | bytes 3145732
  25.4 14.7 %collective-permute-start = (bf16[1,2,32,32,128]{4,2,3,1,0:T(8,128)(2,1)}, bf16[1,2,32,32,128]{4,2,3,1,0:T(8,128)(2,1)S(1)}, u32[]{:S(2)}, u32[]{:S(2)}) collective-permute-start(bf16[1,2,32,32,128]{4,2,3,1,0:T(8,128)(2,1)} %copy.15), channel_id=1, source_target_pairs={{0,2},{2,0},{1,3},{3,1},{4,6},{6,4},{5,7},{7,5},{8,10},{10,8},{9,1... | collective-permute-start | bytes 1572872 | tf_op jit(solution)/shard_map/ppermute | solution.py:84
  37.2 12.7 %collective-permute-start.1 = (bf16[1,2,32,32,128]{4,2,3,1,0:T(8,128)(2,1)}, bf16[1,2,32,32,128]{4,2,3,1,0:T(8,128)(2,1)S(1)}, u32[]{:S(2)}, u32[]{:S(2)}) collective-permute-start(bf16[1,2,32,32,128]{4,2,3,1,0:T(8,128)(2,1)} %copy.18), channel_id=1, source_target_pairs={{0,2},{2,0},{1,3},{3,1},{4,6},{6,4},{5,7},{7,5},{8,10},{10,8},{9,1... | collective-permute-start | bytes 1572872 | tf_op jit(solution)/shard_map/ppermute | solution.py:84
  39.9 32.6 %collective-permute-start.5 = (bf16[4,4,16,16,128]{4,2,3,1,0:T(8,128)(2,1)}, bf16[4,4,16,16,128]{4,2,3,1,0:T(8,128)(2,1)}, u32[]{:S(2)}, u32[]{:S(2)}) collective-permute-start(bf16[4,4,16,16,128]{4,2,3,1,0:T(8,128)(2,1)} %constant_dynamic-slice_fusion), channel_id=1, source_target_pairs={{0,1},{1,0},{2,3},{3,2},{4,5},{5,4},{6,7},{7,6},{8,9},{9,8},{10,11... | collective-permute-start | bytes 3145736 | tf_op jit(solution)/shard_map/ppermute | solution.py:67
  61.8 2.2 %copy-start.2 = (f32[2,32,128,2,64]{2,4,3,1,0:T(8,128)S(1)}, f32[2,32,128,2,64]{2,4,3,1,0:T(8,128)}, u32[]{:S(2)}) copy-start(f32[2,32,128,2,64]{2,4,3,1,0:T(8,128)} %fusion.26) | copy-start | bytes 12582916
  77.1 4.4 %copy-start.7 = (f32[1,64,64]{2,1,0:T(8,128)S(1)}, f32[1,64,64]{2,1,0:T(8,128)}, u32[]{:S(2)}) copy-start(f32[1,64,64]{2,1,0:T(8,128)} %copy-done.6) | copy-start | bytes 49156
  77.1 4.4 %copy-start.9 = (f32[1,64,64]{2,1,0:T(8,128)S(1)}, f32[1,64,64]{2,1,0:T(8,128)}, u32[]{:S(2)}) copy-start(f32[1,64,64]{2,1,0:T(8,128)} %copy-done.8) | copy-start | bytes 49156
  86.2 5.1 %copy-start.10 = (s32[1,1,1,8]{3,2,1,0:T(1,128)S(1)}, s32[1,1,1,8]{3,2,1,0:T(1,128)}, u32[]{:S(2)}) copy-start(s32[1,1,1,8]{3,2,1,0:T(1,128)} %param.7) | copy-start | bytes 100
  86.2 5.1 %copy-start.11 = (s32[1,1,1,8,1]{3,4,2,1,0:T(1,128)S(1)}, s32[1,1,1,8,1]{3,4,2,1,0:T(1,128)}, u32[]{:S(2)}) copy-start(s32[1,1,1,8,1]{3,4,2,1,0:T(1,128)} %param.8) | copy-start | bytes 100
  88.8 15.7 %copy-start.4 = (f32[1,64,32,128]{3,2,1,0:T(8,128)S(1)}, f32[1,64,32,128]{3,2,1,0:T(8,128)}, u32[]{:S(2)}) copy-start(f32[1,64,32,128]{3,2,1,0:T(8,128)} %shard_map.73) | copy-start | bytes 3145732
  89.9 12.3 %collective-permute-start.6 = (f32[32,1,32,128]{3,2,0,1:T(8,128)S(1)}, f32[32,1,32,128]{3,2,0,1:T(8,128)}, u32[]{:S(2)}, u32[]{:S(2)}) collective-permute-start(f32[32,1,32,128]{3,2,0,1:T(8,128)S(1)} %dynamic-slice_bitcast_fusion), channel_id=1, source_target_pairs={{0,2},{2,0},{1,3},{3,1},{4,6},{6,4},{5,7},{7,5},{8,10},{10,8},{9,1... | collective-permute-start | bytes 1572872 | tf_op jit(solution)/shard_map/ppermute | solution.py:84
  106.8 20.3 %copy-start.1 = (f32[2,4,16,32,64]{4,3,2,1,0:T(8,128)S(1)}, f32[2,4,16,32,64]{4,3,2,1,0:T(8,128)}, u32[]{:S(2)}) copy-start(f32[2,4,16,32,64]{4,3,2,1,0:T(8,128)} %param.6) | copy-start | bytes 3145732
  111.8 15.3 %copy-start.5 = (f32[32,64,64]{2,1,0:T(8,128)}, f32[32,64,64]{2,1,0:T(8,128)S(1)}, u32[]{:S(2)}) copy-start(f32[32,64,64]{2,1,0:T(8,128)S(1)} %convolution_multiply_fusion) | copy-start | bytes 1572868

commit v16 on v14

--- a/solution.py
+++ b/solution.py
@@ -163,7 +163,7 @@
     cos_table, sin_table = make_tables(length)
     pair = jnp.stack([cos_table, sin_table])
 
-    chunks = 2 if terms % 2 == 0 else 1
+    chunks = 4 if terms % 4 == 0 else 1
     part_terms = terms // chunks
     pair_x = pair.reshape(2, length, n_sub, x_local)
     z_table = jnp.concatenate([cos_table, -sin_table], axis=1)

time: 109 us -> 131 us (1.20)
  Pallas kernels: 23.4 us -> 31.9 us
  matrix products: 30.1 us -> 36.9 us
  local copies, waits for them, and re-layouts: 17.1 us -> 20.6 us
  starting transfers between devices: 9.57 us -> 11.8 us
    pallas_call x6 -> x10, Pallas kernels: 19 us -> 27.5 us  [combine_call(): pl.pallas_call(functools.partial(combine_kernel, first=first, second=seco...]
    squeeze x2 -> x4, local copies, waits for them, and re-layouts: 2 us -> 6.71 us  [entry(): return sending[shift]]
    dot_general x2 -> x4, matrix products: 2.66 us -> 5.93 us  [local(): along_z = jnp.einsum('rtxyz,zl->rtxyl', part, z_table, precision=highest)]
    slice x2 -> x0, local copies, waits for them, and re-layouts: 2.69 us -> none  [entry(): return sending[shift]]
    ppermute x3 -> x5, starting transfers between devices: 3.5 us -> 5.73 us  [exchange(): lax.ppermute(entry(shift), axis, pairs)]
    dot_general x4 -> x8, matrix products: 9.81 us -> 11.6 us  [local(): jnp.einsum('ekx,rtxjl->rtjekl', pair_x[:, :, source], piece.astype(jnp.fl...]
    dot_general x2 -> x4, matrix products: 7.45 us -> 9.18 us  [local(): along_y = jnp.einsum('ejy,rtxyl->rtxejl', pair, along_z, precision=highest)]
    ppermute x3 -> x5, waiting for transfers between devices: 13.1 us -> 13.1 us  [exchange(): lax.ppermute(entry(shift), axis, pairs)]
  transfers between devices with their start and end apart: 7 -> 9, of which waited for: 2 -> 2; matrix products, arithmetic and copies ran while one was open for 25% -> 30% of each run, Pallas kernels for 12% -> 17%
where the time goes in v16:
time: 131 us; the launch traced here: 130 us
  matrix products  36.9 us (28%)
  Pallas kernels  31.9 us (24%)
  local copies, waits for them, and re-layouts  20.6 us (16%)
  waiting for transfers between devices  13.1 us (10%)
  starting transfers between devices  11.8 us (9%)
  blocking collectives  9.63 us (7%)
  other arithmetic  5.04 us (4%)
    pallas_call x10, Pallas kernels, combine_call(): pl.pallas_call(functools.partial(combine_kernel, first=first, second=seco...  27.5 us
    ppermute x5, waiting for transfers between devices, exchange(): lax.ppermute(entry(shift), axis, pairs)  13.1 us
    dot_general x8, matrix products, local(): jnp.einsum('ekx,rtxjl->rtjekl', pair_x[:, :, source], piece.astype(jnp.fl...  11.6 us
    all_to_all x1, blocking collectives, local(): lax.all_to_all(packed, ('rot', 'ref'), split_axis=0, concat_axis=0, tiled...  9.63 us
    dot_general x4, matrix products, local(): along_y = jnp.einsum('ejy,rtxyl->rtxejl', pair, along_z, precision=highest)  9.18 us
    squeeze x4, local copies, waits for them, and re-layouts, entry(): return sending[shift]  6.71 us
    ppermute x4, starting transfers between devices, gather_by_shifts(): pieces.append(lax.ppermute(piece, axis, pairs))  6.12 us
    dot_general x4, matrix products, local(): along_z = jnp.einsum('rtxyz,zl->rtxyl', part, z_table, precision=highest)  5.93 us
  transfers between devices with their start and end apart: 9, of which 2 were waited for; matrix products, arithmetic and copies ran while one was open for 30% of the time, Pallas kernels for 17%

profile of v16, /device:TPU:0, one launch (start us, length us, event | category | flops | bytes accessed | tf_op | source)
XLA Modules:
  0.0 130.1 jit_solution(6386382213285261442)
XLA Ops:
  2.6 5.1 %collective-permute-start.4 = (bf16[4,16,16,128]{3,1,2,0:T(8,128)(2,1)S(1)}, bf16[4,16,16,128]{3,1,2,0:T(8,128)(2,1)S(1)}, u32[]{:S(2)}, u32[]{:S(2)}) collective-permute-start(bf16[4,16,16,128]{3,1,2,0:T(8,128)(2,1)S(1)} %fusion.77), channel_id=1, source_target_pairs={{0,12},{4,0},{8,4},{12,8},{1,13},{5,1},{9,5},{13,9},{2,14},{6,2},{... | collective-permute-start | bytes 786440 | tf_op jit(solution)/shard_map/ppermute | solution.py:67
  10.5 2.3 %convolution_bitcast_fusion.1.in_ref = f32[32,2,64,128]{3,2,1,0:T(8,128)} fusion(f32[32,64,128,1]{2,1,3,0:T(8,128)S(1)} %convolution_bitcast_fusion.5, f32[1,64,64]{2,1,0:T(8,128)S(1)} %get-tuple-element.18, f32[1,64,64]{2,1,0:T(8,128)S(1)} %get-tuple-element.19), kind=kOutput, calls=%fused_computation.16 | convolution fusion | flops 201334784 | bytes 3178496 | tf_op jit(solution)/shard_map/ejy,rtxyl->rtxejl/dot_general | solution.py:175
  12.8 2.7 %shard_map.72 = bf16[2,32,32,128]{3,2,1,0:T(8,128)(2,1)} custom-call(s32[1]{0:T(128)} %bitcast.me_ref, f32[32,2,64,128]{3,2,1,0:T(8,128)} %convolution_bitcast_fusion.1.in_ref), custom_call_target="tpu_custom_call" | custom-call | flops 786432 | bytes 2621440 | tf_op jit(solution)/shard_map/pallas_call | solution.py:44
  15.5 1.7 %slice_bitcast_fusion.5 = bf16[1,1,32,32,128]{4,3,2,1,0:T(8,128)(2,1)} fusion(bf16[2,32,32,128]{3,2,1,0:T(8,128)(2,1)} %shard_map.72), kind=kLoop, calls=%fused_computation.47 | loop fusion | bytes 524288 | tf_op jit(solution)/shard_map/squeeze | solution.py:78
  20.2 2.3 %convolution_bitcast_fusion.in_ref = f32[32,2,64,128]{3,2,1,0:T(8,128)} fusion(f32[32,64,128,1]{2,1,3,0:T(8,128)S(1)} %convolution_bitcast_fusion.4, f32[1,64,64]{2,1,0:T(8,128)S(1)} %get-tuple-element.18, f32[1,64,64]{2,1,0:T(8,128)S(1)} %get-tuple-element.19), kind=kOutput, calls=%fused_computation.15 | convolution fusion | flops 201334784 | bytes 3178496 | tf_op jit(solution)/shard_map/ejy,rtxyl->rtxejl/dot_general | solution.py:175
  22.5 2.7 %shard_map.74 = bf16[2,32,32,128]{3,2,1,0:T(8,128)(2,1)} custom-call(s32[1]{0:T(128)} %bitcast.me_ref, f32[32,2,64,128]{3,2,1,0:T(8,128)} %convolution_bitcast_fusion.in_ref), custom_call_target="tpu_custom_call" | custom-call | flops 786432 | bytes 2621440 | tf_op jit(solution)/shard_map/pallas_call | solution.py:44
  30.4 2.3 %convolution_bitcast_fusion.2.in_ref = f32[32,2,64,128]{3,2,1,0:T(8,128)} fusion(f32[32,64,128,1]{2,1,3,0:T(8,128)S(1)} %convolution_bitcast_fusion.6, f32[1,64,64]{2,1,0:T(8,128)S(1)} %get-tuple-element.18, f32[1,64,64]{2,1,0:T(8,128)S(1)} %get-tuple-element.19), kind=kOutput, calls=%fused_computation.17 | convolution fusion | flops 201334784 | bytes 3178496 | tf_op jit(solution)/shard_map/ejy,rtxyl->rtxejl/dot_general | solution.py:175
  32.7 2.7 %shard_map.70 = bf16[2,32,32,128]{3,2,1,0:T(8,128)(2,1)} custom-call(s32[1]{0:T(128)} %bitcast.me_ref, f32[32,2,64,128]{3,2,1,0:T(8,128)} %convolution_bitcast_fusion.2.in_ref), custom_call_target="tpu_custom_call" | custom-call | flops 786432 | bytes 2621440 | tf_op jit(solution)/shard_map/pallas_call | solution.py:44
  37.1 2.3 %convolution_bitcast_fusion.3.in_ref = f32[32,2,64,128]{3,2,1,0:T(8,128)} fusion(f32[32,64,128,1]{2,1,3,0:T(8,128)S(1)} %convolution_bitcast_fusion.7, f32[1,64,64]{2,1,0:T(8,128)S(1)} %get-tuple-element.18, f32[1,64,64]{2,1,0:T(8,128)S(1)} %get-tuple-element.19), kind=kOutput, calls=%fused_computation.18 | convolution fusion | flops 201334784 | bytes 3178496 | tf_op jit(solution)/shard_map/ejy,rtxyl->rtxejl/dot_general | solution.py:175
  39.4 2.7 %shard_map.68 = bf16[2,32,32,128]{3,2,1,0:T(8,128)(2,1)} custom-call(s32[1]{0:T(128)} %bitcast.me_ref, f32[32,2,64,128]{3,2,1,0:T(8,128)} %convolution_bitcast_fusion.3.in_ref), custom_call_target="tpu_custom_call" | custom-call | flops 786432 | bytes 2621440 | tf_op jit(solution)/shard_map/pallas_call | solution.py:44
  42.1 1.7 %slice_bitcast_fusion.9 = bf16[1,1,32,32,128]{4,3,2,1,0:T(8,128)(2,1)} fusion(bf16[2,32,32,128]{3,2,1,0:T(8,128)(2,1)} %shard_map.68), kind=kLoop, calls=%fused_computation.51 | loop fusion | bytes 524288 | tf_op jit(solution)/shard_map/squeeze | solution.py:78
  50.1 3.5 %collective-permute-done.1 = bf16[1,1,32,32,128]{4,3,2,1,0:T(8,128)(2,1)S(1)} collective-permute-done((bf16[1,1,32,32,128]{4,3,2,1,0:T(8,128)(2,1)}, bf16[1,1,32,32,128]{4,3,2,1,0:T(8,128)(2,1)S(1)}, u32[]{:S(2)}, u32[]{:S(2)}) %collective-permute-start.1) | collective-permute-done | bytes 262176 | tf_op jit(solution)/shard_map/ppermute | solution.py:84
  54.4 2.2 %add_bitcast_fusion.2.in_ref = f32[32,2,64,128]{3,2,1,0:T(8,128)} fusion(f32[32,128,2,64]{1,3,2,0:T(8,128)S(1)} %fusion.21, f32[2,64,32,1]{1,2,0,3:T(8,128)S(1)} %get-tuple-element.12, bf16[32,32,128,1]{2,1,0,3:T(8,128)(2,1)S(1)} %get-tuple-element.4), kind=kOutput, calls=%fused_computation.12 | convolution fusion | flops 101187584 | bytes 4472832 | tf_op jit(solution)/shard_map/ekx,rtxjl->rtjekl/dot_general | solution.py:181
  56.6 2.1 %add_bitcast_fusion.1.in_ref = f32[32,2,64,128]{3,2,1,0:T(8,128)} fusion(f32[32,128,2,64]{1,3,2,0:T(8,128)S(1)} %fusion.18, f32[2,64,32,1]{1,2,0,3:T(8,128)S(1)} %get-tuple-element.12, bf16[32,32,128,1]{2,1,0,3:T(8,128)(2,1)S(1)} %get-tuple-element.2), kind=kOutput, calls=%fused_computation.11 | convolution fusion | flops 101187584 | bytes 4472832 | tf_op jit(solution)/shard_map/ekx,rtxjl->rtjekl/dot_general | solution.py:181
  58.7 2.3 %add_bitcast_fusion.3.in_ref = f32[32,2,64,128]{3,2,1,0:T(8,128)} fusion(f32[32,128,2,64]{1,3,2,0:T(8,128)S(1)} %fusion.24, f32[2,64,32,1]{1,2,0,3:T(8,128)S(1)} %get-tuple-element.12, bf16[32,32,128,1]{2,1,0,3:T(8,128)(2,1)S(1)} %get-tuple-element.6), kind=kOutput, calls=%fused_computation.13 | convolution fusion | flops 101187584 | bytes 4472832 | tf_op jit(solution)/shard_map/ekx,rtxjl->rtjekl/dot_general | solution.py:181
  60.9 2.8 %shard_map.73 = bf16[1,32,64,128]{3,2,1,0:T(8,128)(2,1)} custom-call(s32[1]{0:T(128)} %constant.84.clone.1.me_ref, f32[32,2,64,128]{3,2,1,0:T(8,128)} %add_bitcast_fusion.2.in_ref), custom_call_target="tpu_custom_call" | custom-call | flops 786432 | bytes 2621440 | tf_op jit(solution)/shard_map/pallas_call | solution.py:44
  63.7 2.8 %shard_map.75 = bf16[1,32,64,128]{3,2,1,0:T(8,128)(2,1)} custom-call(s32[1]{0:T(128)} %constant.84.clone.1.me_ref, f32[32,2,64,128]{3,2,1,0:T(8,128)} %add_bitcast_fusion.1.in_ref), custom_call_target="tpu_custom_call" | custom-call | flops 786432 | bytes 2621440 | tf_op jit(solution)/shard_map/pallas_call | solution.py:44
  66.5 2.7 %shard_map.71 = bf16[1,32,64,128]{3,2,1,0:T(8,128)(2,1)} custom-call(s32[1]{0:T(128)} %constant.84.clone.1.me_ref, f32[32,2,64,128]{3,2,1,0:T(8,128)} %add_bitcast_fusion.3.in_ref), custom_call_target="tpu_custom_call" | custom-call | flops 786432 | bytes 2621440 | tf_op jit(solution)/shard_map/pallas_call | solution.py:44
  71.0 2.1 %add_bitcast_fusion.4.in_ref = f32[32,2,64,128]{3,2,1,0:T(8,128)} fusion(f32[32,128,2,64]{1,3,2,0:T(8,128)S(1)} %fusion.27, f32[2,64,32,1]{1,2,0,3:T(8,128)S(1)} %get-tuple-element.12, bf16[32,32,128,1]{2,1,0,3:T(8,128)(2,1)S(1)} %get-tuple-element.8), kind=kOutput, calls=%fused_computation.14 | convolution fusion | flops 101187584 | bytes 4472832 | tf_op jit(solution)/shard_map/ekx,rtxjl->rtjekl/dot_general | solution.py:181
  73.0 2.7 %shard_map.69 = bf16[1,32,64,128]{3,2,1,0:T(8,128)(2,1)} custom-call(s32[1]{0:T(128)} %constant.84.clone.1.me_ref, f32[32,2,64,128]{3,2,1,0:T(8,128)} %add_bitcast_fusion.4.in_ref), custom_call_target="tpu_custom_call" | custom-call | flops 786432 | bytes 2621440 | tf_op jit(solution)/shard_map/pallas_call | solution.py:44
  77.2 2.7 %fusion.3 = bf16[4,2,16,4,16,128]{5,2,4,0,3,1:T(8,128)(2,1)S(1)} fusion(s32[]{:T(128)S(6)} %select_n.170, bf16[1,4,4,16,16,128]{5,3,4,2,1,0:T(8,128)(2,1)} %bitcast.82, bf16[1,4,4,16,16,128]{5,3,4,2,1,0:T(8,128)(2,1)S(1)} %fusion.97), kind=kLoop, calls=%fused_computation.8 | loop fusion | flops 3145728 | bytes 4194308 | tf_op jit(solution)/shard_map/transpose | solution.py:108
  79.9 1.9 %copy.25 = bf16[4,2,16,4,16,128]{5,4,3,2,1,0:T(8,128)(2,1)} copy(bf16[4,2,16,4,16,128]{5,2,4,0,3,1:T(8,128)(2,1)S(1)} %fusion.3) | data formatting | bytes 4194304 | tf_op jit(solution)/shard_map/transpose | solution.py:108
  81.8 4.3 %shard_map.76 = f32[1,2048,128]{2,1,0:T(8,128)} custom-call(bf16[1,1,2048,128]{3,2,1,0:T(8,128)(2,1)} %bitcast.281, bf16[1,1,2048,128]{3,2,1,0:T(8,128)(2,1)} %bitcast.280, bf16[1,1,2048,128]{3,2,1,0:T(8,128)(2,1)} %bitcast.278, bf16[1,1,2048,128]{3,2,1,0:T(8,128)(2,1)} %bitcast.279, bf16[4,2048,128]{2,1,0:T(8,128)(2,1)} %bitcast.271), custom_call_target="tpu_custom_call" | custom-call | flops 8388608 | bytes 5242880 | tf_op jit(solution)/shard_map/pallas_call | solution.py:139
  86.1 2.2 %fusion.55 = f32[32,128,2,64]{1,3,2,0:T(8,128)S(1)} fusion(f32[32,64,128,1]{2,1,3,0:T(8,128)} %bitcast.276, f32[1,64,64]{2,1,0:T(8,128)S(1)} %get-tuple-element.18, f32[1,64,64]{2,1,0:T(8,128)S(1)} %get-tuple-element.19), kind=kOutput, calls=%fused_computation.122 | convolution fusion | flops 201334784 | bytes 3178496 | tf_op jit(solution)/shard_map/exk,rjkl->xrejl/dot_general | solution.py:195
  88.3 2.5 %copy.75 = f32[32,128,2,64]{1,0,2,3:T(8,128)} copy(f32[32,128,2,64]{1,3,2,0:T(8,128)S(1)} %fusion.55) | data formatting | bytes 4194304 | tf_op jit(solution)/shard_map/exk,rjkl->xrejl/dot_general | solution.py:195
  90.9 2.6 %shard_map.77 = f32[1,64,32,128]{3,2,1,0:T(8,128)} custom-call(s32[1]{0:T(128)} %constant.84.clone.1.me_ref, f32[64,2,32,128]{3,2,1,0:T(8,128)} %bitcast.272), custom_call_target="tpu_custom_call" | custom-call | flops 786432 | bytes 3145728 | tf_op jit(solution)/shard_map/pallas_call | solution.py:44
  96.4 9.6 %collective-permute-done.8 = f32[32,1,32,128]{3,2,0,1:T(8,128)S(1)} collective-permute-done((f32[32,1,32,128]{3,2,0,1:T(8,128)S(1)}, f32[32,1,32,128]{3,2,0,1:T(8,128)S(1)}, u32[]{:S(2)}, u32[]{:S(2)}) %collective-permute-start.8) | collective-permute-done | bytes 524320 | tf_op jit(solution)/shard_map/ppermute | solution.py:84
  106.0 2.1 %fusion.5 = f32[32,128,2,64]{1,3,2,0:T(8,128)S(1)} fusion(f32[2,64,32,1]{1,2,0,3:T(8,128)S(1)} %get-tuple-element.13, f32[32,1,32,128]{3,2,0,1:T(8,128)S(1)} %collective-permute-done.8, f32[2,32,1,32,128]{4,3,1,0,2:T(8,128)} %bitcast.274, s32[]{:T(128)S(6)} %select_n.174, pred[]{:T(512)S(6)} %eq.53), kind=kOutput, calls=%fused_computation.26 | convolution fusion | flops 100794368 | bytes 3162117 | tf_op jit(solution)/shard_map/eyj,xrjl->rxeyl/dot_general | solution.py:200
  108.0 2.4 %add_bitcast_fusion.in_ref = f32[32,2,64,128]{3,2,1,0:T(8,128)} fusion(f32[32,128,2,64]{1,3,2,0:T(8,128)S(1)} %fusion.5, f32[2,64,32,1]{1,2,0,3:T(8,128)S(1)} %get-tuple-element.12, f32[32,1,32,128]{3,2,0,1:T(8,128)S(1)} %collective-permute-done.8, f32[2,32,1,32,128]{4,3,1,0,2:T(8,128)S(1)} %bitcast.275, s32[]{:T(128)S(6)} %select_n.174, pred[]{:T(512)S(6)} %eq.52), kind=kOutput, calls=%fused_computation.10 | convolution fusion | flops 101318656 | bytes 5275653 | tf_op jit(solution)/shard_map/eyj,xrjl->rxeyl/dot_general | solution.py:200
  110.4 3.0 %shard_map.78 = f32[1,32,64,128]{3,2,1,0:T(8,128)} custom-call(s32[1]{0:T(128)} %constant.84.clone.1.me_ref, f32[32,2,64,128]{3,2,1,0:T(8,128)} %add_bitcast_fusion.in_ref), custom_call_target="tpu_custom_call" | custom-call | flops 786432 | bytes 3145728 | tf_op jit(solution)/shard_map/pallas_call | solution.py:44
  113.5 1.9 %convolution_multiply_fusion = f32[32,64,64]{2,1,0:T(8,128)S(1)} fusion(f32[1,32,64,128]{3,2,1,0:T(8,128)} %shard_map.78, f32[64,64]{0,1:T(8,128)S(1)} %get-tuple-element.16, f32[64,64]{0,1:T(8,128)S(1)} %get-tuple-element.17), kind=kOutput, calls=%fused_computation.23 | convolution fusion | flops 100802560 | bytes 1605632 | tf_op jit(solution)/shard_map/rxyl,lz->rxyz/dot_general | solution.py:206
  119.8 9.6 %all_to_all.5 = f32[8,2,512]{2,1,0:T(2,128)S(1)} all-to-all(f32[8,2,512]{2,1,0:T(2,128)S(1)} %reshape.375), channel_id=1, replica_groups=mesh['grp'=2,'rot'=4,'sub'=2,'ref'=2] {'rot','ref'}, dimensions={0} | all-to-all | bytes 65536 | tf_op jit(solution)/shard_map/all_to_all | solution.py:224
  (80 shorter events, 32.6 us)
Async XLA Ops:
  0.6 1.6 %copy-start = (f32[2,4,16,32,64]{4,3,2,1,0:T(8,128)S(1)}, f32[2,4,16,32,64]{4,3,2,1,0:T(8,128)}, u32[]{:S(2)}) copy-start(f32[2,4,16,32,64]{4,3,2,1,0:T(8,128)} %param.6) | copy-start | bytes 3145732
  2.6 41.5 %collective-permute-start.4 = (bf16[4,16,16,128]{3,1,2,0:T(8,128)(2,1)S(1)}, bf16[4,16,16,128]{3,1,2,0:T(8,128)(2,1)S(1)}, u32[]{:S(2)}, u32[]{:S(2)}) collective-permute-start(bf16[4,16,16,128]{3,1,2,0:T(8,128)(2,1)S(1)} %fusion.77), channel_id=1, source_target_pairs={{0,12},{4,0},{8,4},{12,8},{1,13},{5,1},{9,5},{13,9},{2,14},{6,2},{... | collective-permute-start | bytes 786440 | tf_op jit(solution)/shard_map/ppermute | solution.py:67
  7.7 38.0 %collective-permute-start.5 = (bf16[4,16,16,128]{3,1,2,0:T(8,128)(2,1)S(1)}, bf16[4,16,16,128]{3,1,2,0:T(8,128)(2,1)S(1)}, u32[]{:S(2)}, u32[]{:S(2)}) collective-permute-start(bf16[4,16,16,128]{3,1,2,0:T(8,128)(2,1)S(1)} %fusion.77), channel_id=1, source_target_pairs={{0,8},{4,12},{8,0},{12,4},{1,9},{5,13},{9,1},{13,5},{2,10},{6,14},... | collective-permute-start | bytes 786440 | tf_op jit(solution)/shard_map/ppermute | solution.py:67
  7.7 38.7 %collective-permute-start.6 = (bf16[4,16,16,128]{3,1,2,0:T(8,128)(2,1)S(1)}, bf16[4,16,16,128]{3,1,2,0:T(8,128)(2,1)S(1)}, u32[]{:S(2)}, u32[]{:S(2)}) collective-permute-start(bf16[4,16,16,128]{3,1,2,0:T(8,128)(2,1)S(1)} %fusion.77), channel_id=1, source_target_pairs={{0,4},{4,8},{8,12},{12,0},{1,5},{5,9},{9,13},{13,1},{2,6},{6,10},{... | collective-permute-start | bytes 786440 | tf_op jit(solution)/shard_map/ppermute | solution.py:67
  17.2 31.1 %collective-permute-start.2 = (bf16[1,1,32,32,128]{4,3,2,1,0:T(8,128)(2,1)}, bf16[1,1,32,32,128]{4,3,2,1,0:T(8,128)(2,1)S(1)}, u32[]{:S(2)}, u32[]{:S(2)}) collective-permute-start(bf16[1,1,32,32,128]{4,3,2,1,0:T(8,128)(2,1)} %slice_bitcast_fusion.5), channel_id=1, source_target_pairs={{0,2},{2,0},{1,3},{3,1},{4,6},{6,4},{5,7},{7,5},{8,10},{10,8},{9,1... | collective-permute-start | bytes 786440 | tf_op jit(solution)/shard_map/ppermute | solution.py:84
  26.9 22.2 %collective-permute-start.3 = (bf16[1,1,32,32,128]{4,3,2,1,0:T(8,128)(2,1)}, bf16[1,1,32,32,128]{4,3,2,1,0:T(8,128)(2,1)S(1)}, u32[]{:S(2)}, u32[]{:S(2)}) collective-permute-start(bf16[1,1,32,32,128]{4,3,2,1,0:T(8,128)(2,1)} %slice_bitcast_fusion.3), channel_id=1, source_target_pairs={{0,2},{2,0},{1,3},{3,1},{4,6},{6,4},{5,7},{7,5},{8,10},{10,8},{9,1... | collective-permute-start | bytes 786440 | tf_op jit(solution)/shard_map/ppermute | solution.py:84
  44.1 9.5 %collective-permute-start.1 = (bf16[1,1,32,32,128]{4,3,2,1,0:T(8,128)(2,1)}, bf16[1,1,32,32,128]{4,3,2,1,0:T(8,128)(2,1)S(1)}, u32[]{:S(2)}, u32[]{:S(2)}) collective-permute-start(bf16[1,1,32,32,128]{4,3,2,1,0:T(8,128)(2,1)} %slice_bitcast_fusion.7), channel_id=1, source_target_pairs={{0,2},{2,0},{1,3},{3,1},{4,6},{6,4},{5,7},{7,5},{8,10},{10,8},{9,1... | collective-permute-start | bytes 786440 | tf_op jit(solution)/shard_map/ppermute | solution.py:84
  45.7 23.5 %collective-permute-start = (bf16[1,1,32,32,128]{4,3,2,1,0:T(8,128)(2,1)}, bf16[1,1,32,32,128]{4,3,2,1,0:T(8,128)(2,1)}, u32[]{:S(2)}, u32[]{:S(2)}) collective-permute-start(bf16[1,1,32,32,128]{4,3,2,1,0:T(8,128)(2,1)} %slice_bitcast_fusion.9), channel_id=1, source_target_pairs={{0,2},{2,0},{1,3},{3,1},{4,6},{6,4},{5,7},{7,5},{8,10},{10,8},{9,1... | collective-permute-start | bytes 786440 | tf_op jit(solution)/shard_map/ppermute | solution.py:84
  46.6 1.6 %copy-start.7 = (bf16[2,32,32,128]{3,2,1,0:T(8,128)(2,1)S(1)}, bf16[2,32,32,128]{3,2,1,0:T(8,128)(2,1)}, u32[]{:S(2)}) copy-start(bf16[2,32,32,128]{3,2,1,0:T(8,128)(2,1)} %shard_map.72) | copy-start | bytes 1572868
  46.9 2.2 %copy-start.4 = (bf16[8,4,16,16,128]{4,2,3,1,0:T(8,128)(2,1)}, bf16[8,4,16,16,128]{4,2,3,1,0:T(8,128)(2,1)S(1)}, u32[]{:S(2)}) copy-start(bf16[8,4,16,16,128]{4,2,3,1,0:T(8,128)(2,1)S(1)} %bitcast_dynamic-update-slice_fusion.1) | copy-start | bytes 6291460
  48.2 1.0 copy-start.6
  48.3 29.0 %collective-permute-start.7 = (bf16[4,4,16,16,128]{4,2,3,1,0:T(8,128)(2,1)}, bf16[4,4,16,16,128]{4,2,3,1,0:T(8,128)(2,1)}, u32[]{:S(2)}, u32[]{:S(2)}) collective-permute-start(bf16[4,4,16,16,128]{4,2,3,1,0:T(8,128)(2,1)} %constant_dynamic-slice_fusion), channel_id=1, source_target_pairs={{0,1},{1,0},{2,3},{3,2},{4,5},{5,4},{6,7},{7,6},{8,9},{9,8},{10,11... | collective-permute-start | bytes 3145736 | tf_op jit(solution)/shard_map/ppermute | solution.py:67
  49.1 4.5 %copy-start.8 = (bf16[2,32,32,128]{3,2,1,0:T(8,128)(2,1)S(1)}, bf16[2,32,32,128]{3,2,1,0:T(8,128)(2,1)}, u32[]{:S(2)}) copy-start(bf16[2,32,32,128]{3,2,1,0:T(8,128)(2,1)} %shard_map.70) | copy-start | bytes 1572868
  63.7 5.5 %copy-start.5 = (bf16[2,32,32,128]{3,2,1,0:T(8,128)(2,1)S(1)}, bf16[2,32,32,128]{3,2,1,0:T(8,128)(2,1)}, u32[]{:S(2)}) copy-start(bf16[2,32,32,128]{3,2,1,0:T(8,128)(2,1)} %shard_map.68) | copy-start | bytes 1572868
  90.9 5.3 %copy-start.9 = (s32[1,1,1,8]{3,2,1,0:T(1,128)S(1)}, s32[1,1,1,8]{3,2,1,0:T(1,128)}, u32[]{:S(2)}) copy-start(s32[1,1,1,8]{3,2,1,0:T(1,128)} %param.7) | copy-start | bytes 100
  90.9 5.3 %copy-start.10 = (s32[1,1,1,8,1]{3,4,2,1,0:T(1,128)S(1)}, s32[1,1,1,8,1]{3,4,2,1,0:T(1,128)}, u32[]{:S(2)}) copy-start(s32[1,1,1,8,1]{3,4,2,1,0:T(1,128)} %param.8) | copy-start | bytes 100
  93.4 14.6 %copy-start.2 = (f32[1,64,32,128]{3,2,1,0:T(8,128)S(1)}, f32[1,64,32,128]{3,2,1,0:T(8,128)}, u32[]{:S(2)}) copy-start(f32[1,64,32,128]{3,2,1,0:T(8,128)} %shard_map.77) | copy-start | bytes 3145732
  94.6 11.4 %collective-permute-start.8 = (f32[32,1,32,128]{3,2,0,1:T(8,128)S(1)}, f32[32,1,32,128]{3,2,0,1:T(8,128)S(1)}, u32[]{:S(2)}, u32[]{:S(2)}) collective-permute-start(f32[32,1,32,128]{3,2,0,1:T(8,128)S(1)} %dynamic-slice_bitcast_fusion), channel_id=1, source_target_pairs={{0,2},{2,0},{1,3},{3,1},{4,6},{6,4},{5,7},{7,5},{8,10},{10,8},{9,1... | collective-permute-start | bytes 1572872 | tf_op jit(solution)/shard_map/ppermute | solution.py:84
  110.4 19.7 %copy-start.1 = (f32[2,4,16,32,64]{4,3,2,1,0:T(8,128)S(1)}, f32[2,4,16,32,64]{4,3,2,1,0:T(8,128)}, u32[]{:S(2)}) copy-start(f32[2,4,16,32,64]{4,3,2,1,0:T(8,128)} %param.6) | copy-start | bytes 3145732
  115.3 14.8 %copy-start.3 = (f32[32,64,64]{2,1,0:T(8,128)}, f32[32,64,64]{2,1,0:T(8,128)S(1)}, u32[]{:S(2)}) copy-start(f32[32,64,64]{2,1,0:T(8,128)S(1)} %convolution_multiply_fusion) | copy-start | bytes 1572868

commit v17 on v14

--- a/solution.py
+++ b/solution.py
@@ -39,7 +39,7 @@
 
 def combine_call(stacked, first, second, split, dtype, me=0):
     batch, _, rows, lanes = stacked.shape
-    block = max(b for b in range(1, 33) if batch % b == 0)
+    block = max(b for b in range(1, min(32, max(batch // 2, 1)) + 1) if batch % b == 0)
     part = rows // split
     return pl.pallas_call(
         functools.partial(combine_kernel, first=first, second=second),

time: 109 us -> 109 us (level)
  no operation moved by 1% of the time
where the time goes in v17:
time: 109 us; the launch traced here: 108 us
  matrix products  30.1 us (28%)
  Pallas kernels  23 us (21%)
  local copies, waits for them, and re-layouts  17.1 us (16%)
  waiting for transfers between devices  13.1 us (12%)
  blocking collectives  9.63 us (9%)
  starting transfers between devices  9.57 us (9%)
  other arithmetic  4.63 us (4%)
    pallas_call x6, Pallas kernels, combine_call(): pl.pallas_call(functools.partial(combine_kernel, first=first, second=seco...  18.7 us
    ppermute x3, waiting for transfers between devices, exchange(): lax.ppermute(entry(shift), axis, pairs)  13.1 us
    dot_general x4, matrix products, local(): jnp.einsum('ekx,rtxjl->rtjekl', pair_x[:, :, source], piece.astype(jnp.fl...  9.81 us
    all_to_all x1, blocking collectives, local(): lax.all_to_all(packed, ('rot', 'ref'), split_axis=0, concat_axis=0, tiled...  9.63 us
    dot_general x2, matrix products, local(): along_y = jnp.einsum('ejy,rtxyl->rtxejl', pair, along_z, precision=highest)  7.45 us
    ppermute x4, starting transfers between devices, gather_by_shifts(): pieces.append(lax.ppermute(piece, axis, pairs))  6.06 us
    dot_general x2, matrix products, local(): jnp.einsum('eyj,xrjl->rxeyl', pair_y[:, :, source], piece, precision=high...  4.42 us
    pallas_call x1, Pallas kernels, correlate(): pl.pallas_call(product_kernel, grid=(rots, rows // block), in_specs=[pl.B...  4.35 us
  transfers between devices with their start and end apart: 7, of which 2 were waited for; matrix products, arithmetic and copies ran while one was open for 25% of the time, Pallas kernels for 12%

profile of v17, /device:TPU:0, one launch (start us, length us, event | category | flops | bytes accessed | tf_op | source)
XLA Modules:
  0.0 108.1 jit_solution(4728893297231473607)
XLA Ops:
  0.7 1.6 %copy-done = f32[2,4,16,32,64]{4,3,2,1,0:T(8,128)S(1)} copy-done((f32[2,4,16,32,64]{4,3,2,1,0:T(8,128)S(1)}, f32[2,4,16,32,64]{4,3,2,1,0:T(8,128)}, u32[]{:S(2)}) %copy-start) | copy-done | bytes 1048600
  3.3 5.0 %collective-permute-start.2 = (bf16[4,16,16,128]{3,1,2,0:T(8,128)(2,1)}, bf16[4,16,16,128]{3,1,2,0:T(8,128)(2,1)S(1)}, u32[]{:S(2)}, u32[]{:S(2)}) collective-permute-start(bf16[4,16,16,128]{3,1,2,0:T(8,128)(2,1)} %fusion.91), channel_id=1, source_target_pairs={{0,12},{4,0},{8,4},{12,8},{1,13},{5,1},{9,5},{13,9},{2,14},{6,2},{... | collective-permute-start | bytes 786440 | tf_op jit(solution)/shard_map/ppermute | solution.py:67
  9.7 2.0 %fusion.11 = f32[128,2,32,64]{0,3,2,1:T(8,128)S(1)} fusion(bf16[1,4,32,64,64]{4,3,2,1,0:T(8,128)(2,1)} %param.5, f32[64,64]{0,1:T(8,128)S(1)} %get-tuple-element.10, f32[64,64]{0,1:T(8,128)S(1)} %get-tuple-element.11), kind=kOutput, calls=%fused_computation.21 | convolution fusion | flops 201334784 | bytes 3178496 | tf_op jit(solution)/shard_map/rtxyz,zl->rtxyl/dot_general | solution.py:174
  11.6 3.7 %fusion.6 = f32[2,32,128,2,64]{2,4,3,1,0:T(8,128)} fusion(f32[128,2,32,64]{0,3,2,1:T(8,128)S(1)} %fusion.11, f32[1,64,64]{2,1,0:T(8,128)S(1)} %get-tuple-element.12, f32[1,64,64]{2,1,0:T(8,128)S(1)} %get-tuple-element.13), kind=kOutput, calls=%fused_computation.13 | convolution fusion | flops 402661376 | bytes 6324224 | tf_op jit(solution)/shard_map/ejy,rtxyl->rtxejl/dot_general | solution.py:175
  15.3 3.4 %shard_map.68 = bf16[2,64,32,128]{3,2,1,0:T(8,128)(2,1)} custom-call(s32[1]{0:T(128)} %bitcast.me_ref, f32[64,2,64,128]{3,2,1,0:T(8,128)} %bitcast.198), custom_call_target="tpu_custom_call" | custom-call | flops 1572864 | bytes 5242880 | tf_op jit(solution)/shard_map/pallas_call | solution.py:44
  18.7 1.4 %fusion.93 = (bf16[1,64,32,128]{3,2,1,0:T(8,128)(2,1)S(1)}, bf16[1,64,32,128]{3,2,1,0:T(8,128)(2,1)S(1)}) fusion(bf16[2,64,32,128]{3,2,1,0:T(8,128)(2,1)} %shard_map.68), kind=kLoop, calls=%fused_computation.139 | loop fusion | bytes 2097152 | tf_op jit(solution)/shard_map/slice | solution.py:78
  21.1 1.5 %collective-permute-start = (bf16[1,2,32,32,128]{4,2,3,1,0:T(8,128)(2,1)}, bf16[1,2,32,32,128]{4,2,3,1,0:T(8,128)(2,1)S(1)}, u32[]{:S(2)}, u32[]{:S(2)}) collective-permute-start(bf16[1,2,32,32,128]{4,2,3,1,0:T(8,128)(2,1)} %copy.15), channel_id=1, source_target_pairs={{0,2},{2,0},{1,3},{3,1},{4,6},{6,4},{5,7},{7,5},{8,10},{10,8},{9,1... | collective-permute-start | bytes 1572872 | tf_op jit(solution)/shard_map/ppermute | solution.py:84
  23.4 3.7 %fusion.4 = f32[2,32,128,2,64]{2,4,3,1,0:T(8,128)} fusion(f32[128,2,32,64]{0,3,2,1:T(8,128)S(1)} %fusion.9, f32[1,64,64]{2,1,0:T(8,128)S(1)} %get-tuple-element.12, f32[1,64,64]{2,1,0:T(8,128)S(1)} %get-tuple-element.13), kind=kOutput, calls=%fused_computation.11 | convolution fusion | flops 402661376 | bytes 6324224 | tf_op jit(solution)/shard_map/ejy,rtxyl->rtxejl/dot_general | solution.py:175
  27.1 3.4 %shard_map.70 = bf16[2,64,32,128]{3,2,1,0:T(8,128)(2,1)} custom-call(s32[1]{0:T(128)} %bitcast.me_ref, f32[64,2,64,128]{3,2,1,0:T(8,128)} %bitcast.199), custom_call_target="tpu_custom_call" | custom-call | flops 1572864 | bytes 5242880 | tf_op jit(solution)/shard_map/pallas_call | solution.py:44
  30.4 1.3 %fusion.92 = (bf16[1,64,32,128]{3,2,1,0:T(8,128)(2,1)S(1)}, bf16[1,64,32,128]{3,2,1,0:T(8,128)(2,1)S(1)}) fusion(bf16[2,64,32,128]{3,2,1,0:T(8,128)(2,1)} %shard_map.70), kind=kLoop, calls=%fused_computation.138 | loop fusion | bytes 2097152 | tf_op jit(solution)/shard_map/slice | solution.py:78
  35.6 1.3 %fusion.21 = f32[2,32,128,2,64]{2,4,3,1,0:T(8,128)S(1)} fusion(bf16[1,2,32,32,128]{4,2,3,1,0:T(8,128)(2,1)S(1)} %collective-permute-done, pred[]{:T(512)S(6)} %eq.47, bf16[1,2,32,32,128]{4,3,2,1,0:T(8,128)(2,1)S(1)} %bitcast.200, f32[1,64,2,32]{1,3,0,2:T(8,128)S(1)} %get-tuple-element.9, f32[1,64,2,32]{1,3,0,2:T(8,128)S(1)} %get-tuple-element.8), kind=kOutput, calls=%fused_computation.32 | convolution fusion | flops 201592832 | bytes 5275649 | tf_op jit(solution)/shard_map/ekx,rtxjl->rtjekl/dot_general | solution.py:181
  36.9 3.6 %convolution_add_fusion.1 = f32[2,32,128,2,64]{2,4,3,1,0:T(8,128)} fusion(f32[2,32,128,2,64]{2,4,3,1,0:T(8,128)S(1)} %fusion.21, bf16[1,2,32,32,128]{4,2,3,1,0:T(8,128)(2,1)S(1)} %collective-permute-done, pred[]{:T(512)S(6)} %eq.46, bf16[1,2,32,32,128]{4,3,2,1,0:T(8,128)(2,1)S(1)} %bitcast.201, f32[1,64,2,32]{1,3,0,2:T(8,128)S(1)} %get-tuple-element.8, ...), kind=kOutput, calls=%fused_computation.6 | convolution fusion | flops 202641408 | bytes 9469953 | tf_op jit(solution)/shard_map/ekx,rtxjl->rtjekl/dot_general | solution.py:181
  40.5 3.4 %shard_map.69 = bf16[1,64,64,128]{3,2,1,0:T(8,128)(2,1)} custom-call(s32[1]{0:T(128)} %constant.80.clone.1.me_ref, f32[64,2,64,128]{3,2,1,0:T(8,128)} %bitcast.196), custom_call_target="tpu_custom_call" | custom-call | flops 1572864 | bytes 5242880 | tf_op jit(solution)/shard_map/pallas_call | solution.py:44
  43.9 1.6 %collective-permute-done.1 = bf16[1,2,32,32,128]{4,2,3,1,0:T(8,128)(2,1)S(1)} collective-permute-done((bf16[1,2,32,32,128]{4,2,3,1,0:T(8,128)(2,1)}, bf16[1,2,32,32,128]{4,2,3,1,0:T(8,128)(2,1)S(1)}, u32[]{:S(2)}, u32[]{:S(2)}) %collective-permute-start.1) | collective-permute-done | bytes 524320 | tf_op jit(solution)/shard_map/ppermute | solution.py:84
  45.5 1.3 %fusion.18 = f32[2,32,128,2,64]{2,4,3,1,0:T(8,128)S(1)} fusion(bf16[1,2,32,32,128]{4,2,3,1,0:T(8,128)(2,1)S(1)} %collective-permute-done.1, pred[]{:T(512)S(6)} %eq.47, bf16[1,2,32,32,128]{4,3,2,1,0:T(8,128)(2,1)S(1)} %bitcast.202, f32[1,64,2,32]{1,3,0,2:T(8,128)S(1)} %get-tuple-element.9, f32[1,64,2,32]{1,3,0,2:T(8,128)S(1)} %get-tuple-element.8), kind=kOutput, calls=%fused_computation.29 | convolution fusion | flops 201592832 | bytes 5275649 | tf_op jit(solution)/shard_map/ekx,rtxjl->rtjekl/dot_general | solution.py:181
  46.8 3.6 %convolution_add_fusion = f32[2,32,128,2,64]{2,4,3,1,0:T(8,128)} fusion(f32[2,32,128,2,64]{2,4,3,1,0:T(8,128)S(1)} %fusion.18, bf16[1,2,32,32,128]{4,2,3,1,0:T(8,128)(2,1)S(1)} %collective-permute-done.1, pred[]{:T(512)S(6)} %eq.46, bf16[1,2,32,32,128]{4,3,2,1,0:T(8,128)(2,1)S(1)} %bitcast.203, f32[1,64,2,32]{1,3,0,2:T(8,128)S(1)} %get-tuple-element.8, ...), kind=kOutput, calls=%fused_computation.5 | convolution fusion | flops 202641408 | bytes 9469953 | tf_op jit(solution)/shard_map/ekx,rtxjl->rtjekl/dot_general | solution.py:181
  50.4 3.4 %shard_map.71 = bf16[1,64,64,128]{3,2,1,0:T(8,128)(2,1)} custom-call(s32[1]{0:T(128)} %constant.80.clone.1.me_ref, f32[64,2,64,128]{3,2,1,0:T(8,128)} %bitcast.197), custom_call_target="tpu_custom_call" | custom-call | flops 1572864 | bytes 5242880 | tf_op jit(solution)/shard_map/pallas_call | solution.py:44
  53.8 2.7 %fusion.3 = bf16[4,2,16,4,16,128]{5,2,4,0,3,1:T(8,128)(2,1)S(1)} fusion(s32[]{:T(128)S(6)} %select_n.146, bf16[1,4,4,16,16,128]{5,3,4,2,1,0:T(8,128)(2,1)} %bitcast.62, bf16[1,4,4,16,16,128]{5,3,4,2,1,0:T(8,128)(2,1)S(1)} %fusion.99), kind=kLoop, calls=%fused_computation.10 | loop fusion | flops 3145728 | bytes 4194308 | tf_op jit(solution)/shard_map/transpose | solution.py:108
  56.4 1.9 %copy.21 = bf16[4,2,16,4,16,128]{5,4,3,2,1,0:T(8,128)(2,1)} copy(bf16[4,2,16,4,16,128]{5,2,4,0,3,1:T(8,128)(2,1)S(1)} %fusion.3) | data formatting | bytes 4194304 | tf_op jit(solution)/shard_map/transpose | solution.py:108
  58.3 4.3 %shard_map.72 = f32[1,2048,128]{2,1,0:T(8,128)} custom-call(bf16[1,2,2048,128]{3,2,1,0:T(8,128)(2,1)} %bitcast.210, bf16[1,2,2048,128]{3,2,1,0:T(8,128)(2,1)} %bitcast.212, bf16[4,2048,128]{2,1,0:T(8,128)(2,1)} %bitcast.204), custom_call_target="tpu_custom_call" | custom-call | flops 8388608 | bytes 5242880 | tf_op jit(solution)/shard_map/pallas_call | solution.py:139
  62.7 2.2 %fusion.40 = f32[32,128,2,64]{1,3,2,0:T(8,128)S(1)} fusion(f32[32,64,128,1]{2,1,3,0:T(8,128)} %bitcast.209, f32[1,64,64]{2,1,0:T(8,128)S(1)} %copy-done.6, f32[1,64,64]{2,1,0:T(8,128)S(1)} %copy-done.8), kind=kOutput, calls=%fused_computation.69 | convolution fusion | flops 201334784 | bytes 3178496 | tf_op jit(solution)/shard_map/exk,rjkl->xrejl/dot_general | solution.py:195
  64.9 2.5 %copy.53 = f32[32,128,2,64]{1,0,2,3:T(8,128)} copy(f32[32,128,2,64]{1,3,2,0:T(8,128)S(1)} %fusion.40) | data formatting | bytes 4194304 | tf_op jit(solution)/shard_map/exk,rjkl->xrejl/dot_general | solution.py:195
  67.4 2.6 %shard_map.73 = f32[1,64,32,128]{3,2,1,0:T(8,128)} custom-call(s32[1]{0:T(128)} %constant.80.clone.1.me_ref, f32[64,2,32,128]{3,2,1,0:T(8,128)} %bitcast.205), custom_call_target="tpu_custom_call" | custom-call | flops 786432 | bytes 3145728 | tf_op jit(solution)/shard_map/pallas_call | solution.py:44
  71.2 1.5 %collective-permute-start.6 = (f32[32,1,32,128]{3,2,0,1:T(8,128)S(1)}, f32[32,1,32,128]{3,2,0,1:T(8,128)S(1)}, u32[]{:S(2)}, u32[]{:S(2)}) collective-permute-start(f32[32,1,32,128]{3,2,0,1:T(8,128)S(1)} %dynamic-slice_bitcast_fusion), channel_id=1, source_target_pairs={{0,2},{2,0},{1,3},{3,1},{4,6},{6,4},{5,7},{7,5},{8,10},{10,8},{9,1... | collective-permute-start | bytes 1572872 | tf_op jit(solution)/shard_map/ppermute | solution.py:84
  72.8 11.5 %collective-permute-done.6 = f32[32,1,32,128]{3,2,0,1:T(8,128)S(1)} collective-permute-done((f32[32,1,32,128]{3,2,0,1:T(8,128)S(1)}, f32[32,1,32,128]{3,2,0,1:T(8,128)S(1)}, u32[]{:S(2)}, u32[]{:S(2)}) %collective-permute-start.6) | collective-permute-done | bytes 524320 | tf_op jit(solution)/shard_map/ppermute | solution.py:84
  84.4 2.1 %fusion.15 = f32[32,128,2,64]{1,3,2,0:T(8,128)S(1)} fusion(f32[32,1,32,128]{3,2,0,1:T(8,128)S(1)} %collective-permute-done.6, f32[2,32,1,32,128]{4,3,1,0,2:T(8,128)} %bitcast.207, s32[]{:T(128)S(6)} %select_n.150, pred[]{:T(512)S(6)} %eq.47, f32[1,64,2,32]{1,3,0,2:T(8,128)S(1)} %get-tuple-element.9, f32[1,64,2,32]{1,3,0,2:T(8,128)S(1)} %get-tuple-element.8), kind=kOutput, calls=%fused_computation.26 | convolution fusion | flops 100798464 | bytes 3178501 | tf_op jit(solution)/shard_map/eyj,xrjl->rxeyl/dot_general | solution.py:200
  86.4 2.4 %add_bitcast_fusion.in_ref = f32[32,2,64,128]{3,2,1,0:T(8,128)} fusion(f32[32,128,2,64]{1,3,2,0:T(8,128)S(1)} %fusion.15, f32[32,1,32,128]{3,2,0,1:T(8,128)S(1)} %collective-permute-done.6, f32[2,32,1,32,128]{4,3,1,0,2:T(8,128)S(1)} %bitcast.208, s32[]{:T(128)S(6)} %select_n.150, pred[]{:T(512)S(6)} %eq.46, f32[1,64,2,32]{1,3,0,2:T(8,128)S(1)} %get-tuple-element.8, ...), kind=kOutput, calls=%fused_computation.16 | convolution fusion | flops 101322752 | bytes 5308421 | tf_op jit(solution)/shard_map/eyj,xrjl->rxeyl/dot_general | solution.py:200
  88.8 2.7 %shard_map.74 = f32[1,32,64,128]{3,2,1,0:T(8,128)} custom-call(s32[1]{0:T(128)} %constant.80.clone.1.me_ref, f32[32,2,64,128]{3,2,1,0:T(8,128)} %add_bitcast_fusion.in_ref), custom_call_target="tpu_custom_call" | custom-call | flops 786432 | bytes 3145728 | tf_op jit(solution)/shard_map/pallas_call | solution.py:44
  91.5 1.9 %convolution_multiply_fusion = f32[32,64,64]{2,1,0:T(8,128)S(1)} fusion(f32[1,32,64,128]{3,2,1,0:T(8,128)} %shard_map.74, f32[64,64]{0,1:T(8,128)S(1)} %get-tuple-element.10, f32[64,64]{0,1:T(8,128)S(1)} %get-tuple-element.11), kind=kOutput, calls=%fused_computation.17 | convolution fusion | flops 100802560 | bytes 1605632 | tf_op jit(solution)/shard_map/rxyl,lz->rxyz/dot_general | solution.py:206
  94.5 1.6 %gather_fusion = f32[8,512]{1,0:T(8,128)S(1)} fusion(f32[256,512]{1,0:T(8,128)} %reshape.307, s32[1024]{0:T(1024)S(1)} %pad_clamp_fusion), kind=kCustom, calls=%fused_computation | custom fusion | bytes 32800 | tf_op jit(solution)/shard_map/gather | solution.py:213
  96.1 1.6 %fusion.94 = f32[8,512]{1,0:T(8,128)S(1)} fusion(f32[8,512]{1,0:T(8,128)S(1)} %gather_fusion, f32[512,512]{1,0:T(8,128)} %param.9), kind=kOutput, calls=%fused_computation.140 | convolution fusion | flops 12582912 | bytes 1081344 | tf_op jit(solution)/shard_map/dot_general | solution.py:222
  97.9 9.6 %all_to_all.5 = f32[8,2,512]{2,1,0:T(2,128)S(1)} all-to-all(f32[8,2,512]{2,1,0:T(2,128)S(1)} %reshape.309), channel_id=1, replica_groups=mesh['grp'=2,'rot'=4,'sub'=2,'ref'=2] {'rot','ref'}, dimensions={0} | all-to-all | bytes 65536 | tf_op jit(solution)/shard_map/all_to_all | solution.py:224
  (59 shorter events, 11.1 us)
Async XLA Ops:
  0.6 1.6 %copy-start = (f32[2,4,16,32,64]{4,3,2,1,0:T(8,128)S(1)}, f32[2,4,16,32,64]{4,3,2,1,0:T(8,128)}, u32[]{:S(2)}) copy-start(f32[2,4,16,32,64]{4,3,2,1,0:T(8,128)} %param.6) | copy-start | bytes 3145732
  3.3 30.3 %collective-permute-start.2 = (bf16[4,16,16,128]{3,1,2,0:T(8,128)(2,1)}, bf16[4,16,16,128]{3,1,2,0:T(8,128)(2,1)S(1)}, u32[]{:S(2)}, u32[]{:S(2)}) collective-permute-start(bf16[4,16,16,128]{3,1,2,0:T(8,128)(2,1)} %fusion.91), channel_id=1, source_target_pairs={{0,12},{4,0},{8,4},{12,8},{1,13},{5,1},{9,5},{13,9},{2,14},{6,2},{... | collective-permute-start | bytes 786440 | tf_op jit(solution)/shard_map/ppermute | solution.py:67
  8.3 25.3 %collective-permute-start.3 = (bf16[4,16,16,128]{3,1,2,0:T(8,128)(2,1)}, bf16[4,16,16,128]{3,1,2,0:T(8,128)(2,1)S(1)}, u32[]{:S(2)}, u32[]{:S(2)}) collective-permute-start(bf16[4,16,16,128]{3,1,2,0:T(8,128)(2,1)} %fusion.91), channel_id=1, source_target_pairs={{0,8},{4,12},{8,0},{12,4},{1,9},{5,13},{9,1},{13,5},{2,10},{6,14},... | collective-permute-start | bytes 786440 | tf_op jit(solution)/shard_map/ppermute | solution.py:67
  8.3 25.3 %collective-permute-start.4 = (bf16[4,16,16,128]{3,1,2,0:T(8,128)(2,1)}, bf16[4,16,16,128]{3,1,2,0:T(8,128)(2,1)S(1)}, u32[]{:S(2)}, u32[]{:S(2)}) collective-permute-start(bf16[4,16,16,128]{3,1,2,0:T(8,128)(2,1)} %fusion.91), channel_id=1, source_target_pairs={{0,4},{4,8},{8,12},{12,0},{1,5},{5,9},{9,13},{13,1},{2,6},{6,10},{... | collective-permute-start | bytes 786440 | tf_op jit(solution)/shard_map/ppermute | solution.py:67
  9.6 13.7 %copy-start.5 = (f32[1,64,64]{2,1,0:T(8,128)}, f32[1,64,64]{2,1,0:T(8,128)S(1)}, u32[]{:S(2)}) copy-start(f32[1,64,64]{2,1,0:T(8,128)S(1)} %get-tuple-element.12) | copy-start | bytes 49156
  9.6 13.7 %copy-start.7 = (f32[1,64,64]{2,1,0:T(8,128)}, f32[1,64,64]{2,1,0:T(8,128)S(1)}, u32[]{:S(2)}) copy-start(f32[1,64,64]{2,1,0:T(8,128)S(1)} %get-tuple-element.13) | copy-start | bytes 49156
  18.7 3.9 %copy-start.4 = (bf16[1,4,32,64,64]{4,3,2,1,0:T(8,128)(2,1)S(1)}, bf16[1,4,32,64,64]{4,3,2,1,0:T(8,128)(2,1)}, u32[]{:S(2)}) copy-start(bf16[1,4,32,64,64]{4,3,2,1,0:T(8,128)(2,1)} %param.5) | copy-start | bytes 3145732
  21.1 14.5 %collective-permute-start = (bf16[1,2,32,32,128]{4,2,3,1,0:T(8,128)(2,1)}, bf16[1,2,32,32,128]{4,2,3,1,0:T(8,128)(2,1)S(1)}, u32[]{:S(2)}, u32[]{:S(2)}) collective-permute-start(bf16[1,2,32,32,128]{4,2,3,1,0:T(8,128)(2,1)} %copy.15), channel_id=1, source_target_pairs={{0,2},{2,0},{1,3},{3,1},{4,6},{6,4},{5,7},{7,5},{8,10},{10,8},{9,1... | collective-permute-start | bytes 1572872 | tf_op jit(solution)/shard_map/ppermute | solution.py:84
  32.7 12.8 %collective-permute-start.1 = (bf16[1,2,32,32,128]{4,2,3,1,0:T(8,128)(2,1)}, bf16[1,2,32,32,128]{4,2,3,1,0:T(8,128)(2,1)S(1)}, u32[]{:S(2)}, u32[]{:S(2)}) collective-permute-start(bf16[1,2,32,32,128]{4,2,3,1,0:T(8,128)(2,1)} %copy.18), channel_id=1, source_target_pairs={{0,2},{2,0},{1,3},{3,1},{4,6},{6,4},{5,7},{7,5},{8,10},{10,8},{9,1... | collective-permute-start | bytes 1572872 | tf_op jit(solution)/shard_map/ppermute | solution.py:84
  35.4 18.4 %collective-permute-start.5 = (bf16[4,4,16,16,128]{4,2,3,1,0:T(8,128)(2,1)}, bf16[4,4,16,16,128]{4,2,3,1,0:T(8,128)(2,1)}, u32[]{:S(2)}, u32[]{:S(2)}) collective-permute-start(bf16[4,4,16,16,128]{4,2,3,1,0:T(8,128)(2,1)} %constant_dynamic-slice_fusion), channel_id=1, source_target_pairs={{0,1},{1,0},{2,3},{3,2},{4,5},{5,4},{6,7},{7,6},{8,9},{9,8},{10,11... | collective-permute-start | bytes 3145736 | tf_op jit(solution)/shard_map/ppermute | solution.py:67
  58.3 4.4 %copy-start.6 = (f32[1,64,64]{2,1,0:T(8,128)S(1)}, f32[1,64,64]{2,1,0:T(8,128)}, u32[]{:S(2)}) copy-start(f32[1,64,64]{2,1,0:T(8,128)} %copy-done.5) | copy-start | bytes 49156
  58.3 4.4 %copy-start.8 = (f32[1,64,64]{2,1,0:T(8,128)S(1)}, f32[1,64,64]{2,1,0:T(8,128)}, u32[]{:S(2)}) copy-start(f32[1,64,64]{2,1,0:T(8,128)} %copy-done.7) | copy-start | bytes 49156
  67.4 5.2 %copy-start.9 = (s32[1,1,1,8]{3,2,1,0:T(1,128)S(1)}, s32[1,1,1,8]{3,2,1,0:T(1,128)}, u32[]{:S(2)}) copy-start(s32[1,1,1,8]{3,2,1,0:T(1,128)} %param.7) | copy-start | bytes 100
  67.4 5.2 %copy-start.10 = (s32[1,1,1,8,1]{3,4,2,1,0:T(1,128)S(1)}, s32[1,1,1,8,1]{3,4,2,1,0:T(1,128)}, u32[]{:S(2)}) copy-start(s32[1,1,1,8,1]{3,4,2,1,0:T(1,128)} %param.8) | copy-start | bytes 100
  70.0 16.4 %copy-start.2 = (f32[1,64,32,128]{3,2,1,0:T(8,128)S(1)}, f32[1,64,32,128]{3,2,1,0:T(8,128)}, u32[]{:S(2)}) copy-start(f32[1,64,32,128]{3,2,1,0:T(8,128)} %shard_map.73) | copy-start | bytes 3145732
  71.2 13.2 %collective-permute-start.6 = (f32[32,1,32,128]{3,2,0,1:T(8,128)S(1)}, f32[32,1,32,128]{3,2,0,1:T(8,128)S(1)}, u32[]{:S(2)}, u32[]{:S(2)}) collective-permute-start(f32[32,1,32,128]{3,2,0,1:T(8,128)S(1)} %dynamic-slice_bitcast_fusion), channel_id=1, source_target_pairs={{0,2},{2,0},{1,3},{3,1},{4,6},{6,4},{5,7},{7,5},{8,10},{10,8},{9,1... | collective-permute-start | bytes 1572872 | tf_op jit(solution)/shard_map/ppermute | solution.py:84
  88.8 19.3 %copy-start.1 = (f32[2,4,16,32,64]{4,3,2,1,0:T(8,128)S(1)}, f32[2,4,16,32,64]{4,3,2,1,0:T(8,128)}, u32[]{:S(2)}) copy-start(f32[2,4,16,32,64]{4,3,2,1,0:T(8,128)} %param.6) | copy-start | bytes 3145732
  93.4 14.8 %copy-start.3 = (f32[32,64,64]{2,1,0:T(8,128)}, f32[32,64,64]{2,1,0:T(8,128)S(1)}, u32[]{:S(2)}) copy-start(f32[32,64,64]{2,1,0:T(8,128)S(1)} %convolution_multiply_fusion) | copy-start | bytes 1572868

commit v18 on v17

--- a/solution.py
+++ b/solution.py
@@ -39,7 +39,7 @@
 
 def combine_call(stacked, first, second, split, dtype, me=0):
     batch, _, rows, lanes = stacked.shape
-    block = max(b for b in range(1, min(32, max(batch // 2, 1)) + 1) if batch % b == 0)
+    block = max(b for b in range(1, min(16, max(batch // 2, 1)) + 1) if batch % b == 0)
     part = rows // split
     return pl.pallas_call(
         functools.partial(combine_kernel, first=first, second=second),

time: 109 us -> 114 us (1.046)
  Pallas kernels: 23 us -> 28.2 us
    pallas_call x6, Pallas kernels: 18.7 us -> 23.9 us  [combine_call(): pl.pallas_call(functools.partial(combine_kernel, first=first, second=seco...]
  transfers between devices with their start and end apart: 7 -> 7, of which waited for: 2 -> 2; matrix products, arithmetic and copies ran while one was open for 25% -> 24% of each run, Pallas kernels for 12% -> 15%
where the time goes in v18:
time: 114 us; the launch traced here: 113 us
  matrix products  30.1 us (26%)
  Pallas kernels  28.2 us (25%)
  local copies, waits for them, and re-layouts  17.1 us (15%)
  waiting for transfers between devices  13.6 us (12%)
  blocking collectives  9.63 us (8%)
  starting transfers between devices  9.07 us (8%)
  other arithmetic  4.63 us (4%)
    pallas_call x6, Pallas kernels, combine_call(): pl.pallas_call(functools.partial(combine_kernel, first=first, second=seco...  23.9 us
    ppermute x3, waiting for transfers between devices, exchange(): lax.ppermute(entry(shift), axis, pairs)  13.6 us
    dot_general x4, matrix products, local(): jnp.einsum('ekx,rtxjl->rtjekl', pair_x[:, :, source], piece.astype(jnp.fl...  9.8 us
    all_to_all x1, blocking collectives, local(): lax.all_to_all(packed, ('rot', 'ref'), split_axis=0, concat_axis=0, tiled...  9.63 us
    dot_general x2, matrix products, local(): along_y = jnp.einsum('ejy,rtxyl->rtxejl', pair, along_z, precision=highest)  7.46 us
    ppermute x4, starting transfers between devices, gather_by_shifts(): pieces.append(lax.ppermute(piece, axis, pairs))  6.06 us
    dot_general x2, matrix products, local(): jnp.einsum('eyj,xrjl->rxeyl', pair_y[:, :, source], piece, precision=high...  4.43 us
    pallas_call x1, Pallas kernels, correlate(): pl.pallas_call(product_kernel, grid=(rots, rows // block), in_specs=[pl.B...  4.35 us
  transfers between devices with their start and end apart: 7, of which 2 were waited for; matrix products, arithmetic and copies ran while one was open for 24% of the time, Pallas kernels for 15%

profile of v18, /device:TPU:0, one launch (start us, length us, event | category | flops | bytes accessed | tf_op | source)
XLA Modules:
  0.0 113.3 jit_solution(11035357046264341912)
XLA Ops:
  0.7 1.6 %copy-done = f32[2,4,16,32,64]{4,3,2,1,0:T(8,128)S(1)} copy-done((f32[2,4,16,32,64]{4,3,2,1,0:T(8,128)S(1)}, f32[2,4,16,32,64]{4,3,2,1,0:T(8,128)}, u32[]{:S(2)}) %copy-start) | copy-done | bytes 1048600
  3.3 5.0 %collective-permute-start.2 = (bf16[4,16,16,128]{3,1,2,0:T(8,128)(2,1)}, bf16[4,16,16,128]{3,1,2,0:T(8,128)(2,1)S(1)}, u32[]{:S(2)}, u32[]{:S(2)}) collective-permute-start(bf16[4,16,16,128]{3,1,2,0:T(8,128)(2,1)} %fusion.91), channel_id=1, source_target_pairs={{0,12},{4,0},{8,4},{12,8},{1,13},{5,1},{9,5},{13,9},{2,14},{6,2},{... | collective-permute-start | bytes 786440 | tf_op jit(solution)/shard_map/ppermute | solution.py:67
  9.7 2.0 %fusion.11 = f32[128,2,32,64]{0,3,2,1:T(8,128)S(1)} fusion(bf16[1,4,32,64,64]{4,3,2,1,0:T(8,128)(2,1)} %param.5, f32[64,64]{0,1:T(8,128)S(1)} %get-tuple-element.10, f32[64,64]{0,1:T(8,128)S(1)} %get-tuple-element.11), kind=kOutput, calls=%fused_computation.21 | convolution fusion | flops 201334784 | bytes 3178496 | tf_op jit(solution)/shard_map/rtxyz,zl->rtxyl/dot_general | solution.py:174
  11.6 3.7 %fusion.6 = f32[2,32,128,2,64]{2,4,3,1,0:T(8,128)} fusion(f32[128,2,32,64]{0,3,2,1:T(8,128)S(1)} %fusion.11, f32[1,64,64]{2,1,0:T(8,128)S(1)} %get-tuple-element.12, f32[1,64,64]{2,1,0:T(8,128)S(1)} %get-tuple-element.13), kind=kOutput, calls=%fused_computation.13 | convolution fusion | flops 402661376 | bytes 6324224 | tf_op jit(solution)/shard_map/ejy,rtxyl->rtxejl/dot_general | solution.py:175
  15.3 4.3 %shard_map.68 = bf16[2,64,32,128]{3,2,1,0:T(8,128)(2,1)} custom-call(s32[1]{0:T(128)} %bitcast.me_ref, f32[64,2,64,128]{3,2,1,0:T(8,128)} %bitcast.198), custom_call_target="tpu_custom_call" | custom-call | flops 1572864 | bytes 5242880 | tf_op jit(solution)/shard_map/pallas_call | solution.py:44
  19.7 1.4 %fusion.93 = (bf16[1,64,32,128]{3,2,1,0:T(8,128)(2,1)S(1)}, bf16[1,64,32,128]{3,2,1,0:T(8,128)(2,1)S(1)}) fusion(bf16[2,64,32,128]{3,2,1,0:T(8,128)(2,1)} %shard_map.68), kind=kLoop, calls=%fused_computation.139 | loop fusion | bytes 2097152 | tf_op jit(solution)/shard_map/slice | solution.py:78
  22.1 1.5 %collective-permute-start = (bf16[1,2,32,32,128]{4,2,3,1,0:T(8,128)(2,1)}, bf16[1,2,32,32,128]{4,2,3,1,0:T(8,128)(2,1)S(1)}, u32[]{:S(2)}, u32[]{:S(2)}) collective-permute-start(bf16[1,2,32,32,128]{4,2,3,1,0:T(8,128)(2,1)} %copy.15), channel_id=1, source_target_pairs={{0,2},{2,0},{1,3},{3,1},{4,6},{6,4},{5,7},{7,5},{8,10},{10,8},{9,1... | collective-permute-start | bytes 1572872 | tf_op jit(solution)/shard_map/ppermute | solution.py:84
  24.3 3.7 %fusion.4 = f32[2,32,128,2,64]{2,4,3,1,0:T(8,128)} fusion(f32[128,2,32,64]{0,3,2,1:T(8,128)S(1)} %fusion.9, f32[1,64,64]{2,1,0:T(8,128)S(1)} %get-tuple-element.12, f32[1,64,64]{2,1,0:T(8,128)S(1)} %get-tuple-element.13), kind=kOutput, calls=%fused_computation.11 | convolution fusion | flops 402661376 | bytes 6324224 | tf_op jit(solution)/shard_map/ejy,rtxyl->rtxejl/dot_general | solution.py:175
  28.1 4.3 %shard_map.70 = bf16[2,64,32,128]{3,2,1,0:T(8,128)(2,1)} custom-call(s32[1]{0:T(128)} %bitcast.me_ref, f32[64,2,64,128]{3,2,1,0:T(8,128)} %bitcast.199), custom_call_target="tpu_custom_call" | custom-call | flops 1572864 | bytes 5242880 | tf_op jit(solution)/shard_map/pallas_call | solution.py:44
  32.4 1.3 %fusion.92 = (bf16[1,64,32,128]{3,2,1,0:T(8,128)(2,1)S(1)}, bf16[1,64,32,128]{3,2,1,0:T(8,128)(2,1)S(1)}) fusion(bf16[2,64,32,128]{3,2,1,0:T(8,128)(2,1)} %shard_map.70), kind=kLoop, calls=%fused_computation.138 | loop fusion | bytes 2097152 | tf_op jit(solution)/shard_map/slice | solution.py:78
  36.2 1.2 %constant_dynamic-slice_fusion = bf16[4,4,16,16,128]{4,2,3,1,0:T(8,128)(2,1)} fusion(bf16[8,4,16,16,128]{4,2,3,1,0:T(8,128)(2,1)S(1)} %bitcast_dynamic-update-slice_fusion.1, s32[]{:T(128)S(6)} %select_n.144), kind=kLoop, calls=%fused_computation.127 | loop fusion | bytes 2097156 | tf_op jit(solution)/shard_map/dynamic_slice | solution.py:69
  37.6 1.3 %fusion.21 = f32[2,32,128,2,64]{2,4,3,1,0:T(8,128)S(1)} fusion(bf16[1,2,32,32,128]{4,2,3,1,0:T(8,128)(2,1)S(1)} %collective-permute-done, pred[]{:T(512)S(6)} %eq.47, bf16[1,2,32,32,128]{4,3,2,1,0:T(8,128)(2,1)S(1)} %bitcast.200, f32[1,64,2,32]{1,3,0,2:T(8,128)S(1)} %get-tuple-element.9, f32[1,64,2,32]{1,3,0,2:T(8,128)S(1)} %get-tuple-element.8), kind=kOutput, calls=%fused_computation.32 | convolution fusion | flops 201592832 | bytes 5275649 | tf_op jit(solution)/shard_map/ekx,rtxjl->rtjekl/dot_general | solution.py:181
  38.9 3.6 %convolution_add_fusion.1 = f32[2,32,128,2,64]{2,4,3,1,0:T(8,128)} fusion(f32[2,32,128,2,64]{2,4,3,1,0:T(8,128)S(1)} %fusion.21, bf16[1,2,32,32,128]{4,2,3,1,0:T(8,128)(2,1)S(1)} %collective-permute-done, pred[]{:T(512)S(6)} %eq.46, bf16[1,2,32,32,128]{4,3,2,1,0:T(8,128)(2,1)S(1)} %bitcast.201, f32[1,64,2,32]{1,3,0,2:T(8,128)S(1)} %get-tuple-element.8, ...), kind=kOutput, calls=%fused_computation.6 | convolution fusion | flops 202641408 | bytes 9469953 | tf_op jit(solution)/shard_map/ekx,rtxjl->rtjekl/dot_general | solution.py:181
  42.5 4.3 %shard_map.69 = bf16[1,64,64,128]{3,2,1,0:T(8,128)(2,1)} custom-call(s32[1]{0:T(128)} %constant.80.clone.1.me_ref, f32[64,2,64,128]{3,2,1,0:T(8,128)} %bitcast.196), custom_call_target="tpu_custom_call" | custom-call | flops 1572864 | bytes 5242880 | tf_op jit(solution)/shard_map/pallas_call | solution.py:44
  47.5 1.3 %fusion.18 = f32[2,32,128,2,64]{2,4,3,1,0:T(8,128)S(1)} fusion(bf16[1,2,32,32,128]{4,2,3,1,0:T(8,128)(2,1)S(1)} %collective-permute-done.1, pred[]{:T(512)S(6)} %eq.47, bf16[1,2,32,32,128]{4,3,2,1,0:T(8,128)(2,1)S(1)} %bitcast.202, f32[1,64,2,32]{1,3,0,2:T(8,128)S(1)} %get-tuple-element.9, f32[1,64,2,32]{1,3,0,2:T(8,128)S(1)} %get-tuple-element.8), kind=kOutput, calls=%fused_computation.29 | convolution fusion | flops 201592832 | bytes 5275649 | tf_op jit(solution)/shard_map/ekx,rtxjl->rtjekl/dot_general | solution.py:181
  48.8 3.6 %convolution_add_fusion = f32[2,32,128,2,64]{2,4,3,1,0:T(8,128)} fusion(f32[2,32,128,2,64]{2,4,3,1,0:T(8,128)S(1)} %fusion.18, bf16[1,2,32,32,128]{4,2,3,1,0:T(8,128)(2,1)S(1)} %collective-permute-done.1, pred[]{:T(512)S(6)} %eq.46, bf16[1,2,32,32,128]{4,3,2,1,0:T(8,128)(2,1)S(1)} %bitcast.203, f32[1,64,2,32]{1,3,0,2:T(8,128)S(1)} %get-tuple-element.8, ...), kind=kOutput, calls=%fused_computation.5 | convolution fusion | flops 202641408 | bytes 9469953 | tf_op jit(solution)/shard_map/ekx,rtxjl->rtjekl/dot_general | solution.py:181
  52.4 4.3 %shard_map.71 = bf16[1,64,64,128]{3,2,1,0:T(8,128)(2,1)} custom-call(s32[1]{0:T(128)} %constant.80.clone.1.me_ref, f32[64,2,64,128]{3,2,1,0:T(8,128)} %bitcast.197), custom_call_target="tpu_custom_call" | custom-call | flops 1572864 | bytes 5242880 | tf_op jit(solution)/shard_map/pallas_call | solution.py:44
  56.7 2.7 %fusion.3 = bf16[4,2,16,4,16,128]{5,2,4,0,3,1:T(8,128)(2,1)S(1)} fusion(s32[]{:T(128)S(6)} %select_n.146, bf16[1,4,4,16,16,128]{5,3,4,2,1,0:T(8,128)(2,1)} %bitcast.62, bf16[1,4,4,16,16,128]{5,3,4,2,1,0:T(8,128)(2,1)S(1)} %fusion.99), kind=kLoop, calls=%fused_computation.10 | loop fusion | flops 3145728 | bytes 4194308 | tf_op jit(solution)/shard_map/transpose | solution.py:108
  59.4 1.9 %copy.21 = bf16[4,2,16,4,16,128]{5,4,3,2,1,0:T(8,128)(2,1)} copy(bf16[4,2,16,4,16,128]{5,2,4,0,3,1:T(8,128)(2,1)S(1)} %fusion.3) | data formatting | bytes 4194304 | tf_op jit(solution)/shard_map/transpose | solution.py:108
  61.3 4.3 %shard_map.72 = f32[1,2048,128]{2,1,0:T(8,128)} custom-call(bf16[1,2,2048,128]{3,2,1,0:T(8,128)(2,1)} %bitcast.210, bf16[1,2,2048,128]{3,2,1,0:T(8,128)(2,1)} %bitcast.212, bf16[4,2048,128]{2,1,0:T(8,128)(2,1)} %bitcast.204), custom_call_target="tpu_custom_call" | custom-call | flops 8388608 | bytes 5242880 | tf_op jit(solution)/shard_map/pallas_call | solution.py:139
  65.6 2.2 %fusion.40 = f32[32,128,2,64]{1,3,2,0:T(8,128)S(1)} fusion(f32[32,64,128,1]{2,1,3,0:T(8,128)} %bitcast.209, f32[1,64,64]{2,1,0:T(8,128)S(1)} %copy-done.6, f32[1,64,64]{2,1,0:T(8,128)S(1)} %copy-done.8), kind=kOutput, calls=%fused_computation.69 | convolution fusion | flops 201334784 | bytes 3178496 | tf_op jit(solution)/shard_map/exk,rjkl->xrejl/dot_general | solution.py:195
  67.8 2.5 %copy.53 = f32[32,128,2,64]{1,0,2,3:T(8,128)} copy(f32[32,128,2,64]{1,3,2,0:T(8,128)S(1)} %fusion.40) | data formatting | bytes 4194304 | tf_op jit(solution)/shard_map/exk,rjkl->xrejl/dot_general | solution.py:195
  70.4 3.8 %shard_map.73 = f32[1,64,32,128]{3,2,1,0:T(8,128)} custom-call(s32[1]{0:T(128)} %constant.80.clone.1.me_ref, f32[64,2,32,128]{3,2,1,0:T(8,128)} %bitcast.205), custom_call_target="tpu_custom_call" | custom-call | flops 786432 | bytes 3145728 | tf_op jit(solution)/shard_map/pallas_call | solution.py:44
  74.2 1.2 %dynamic-slice_bitcast_fusion = f32[32,1,32,128]{3,2,0,1:T(8,128)S(1)} fusion(f32[2,32,1,32,128]{4,3,1,0,2:T(8,128)} %bitcast.206, s32[]{:T(128)S(6)} %select_n.148), kind=kLoop, calls=%fused_computation.37 | loop fusion | bytes 1048580 | tf_op jit(solution)/shard_map/jit(dynamic_index_in_dim)/squeeze | solution.py:79
  76.6 13.0 %collective-permute-done.6 = f32[32,1,32,128]{3,2,0,1:T(8,128)S(1)} collective-permute-done((f32[32,1,32,128]{3,2,0,1:T(8,128)S(1)}, f32[32,1,32,128]{3,2,0,1:T(8,128)S(1)}, u32[]{:S(2)}, u32[]{:S(2)}) %collective-permute-start.6) | collective-permute-done | bytes 524320 | tf_op jit(solution)/shard_map/ppermute | solution.py:84
  89.6 2.1 %fusion.15 = f32[32,128,2,64]{1,3,2,0:T(8,128)S(1)} fusion(f32[32,1,32,128]{3,2,0,1:T(8,128)S(1)} %collective-permute-done.6, f32[2,32,1,32,128]{4,3,1,0,2:T(8,128)} %bitcast.207, s32[]{:T(128)S(6)} %select_n.150, pred[]{:T(512)S(6)} %eq.47, f32[1,64,2,32]{1,3,0,2:T(8,128)S(1)} %get-tuple-element.9, f32[1,64,2,32]{1,3,0,2:T(8,128)S(1)} %get-tuple-element.8), kind=kOutput, calls=%fused_computation.26 | convolution fusion | flops 100798464 | bytes 3178501 | tf_op jit(solution)/shard_map/eyj,xrjl->rxeyl/dot_general | solution.py:200
  91.6 2.4 %add_bitcast_fusion.in_ref = f32[32,2,64,128]{3,2,1,0:T(8,128)} fusion(f32[32,128,2,64]{1,3,2,0:T(8,128)S(1)} %fusion.15, f32[32,1,32,128]{3,2,0,1:T(8,128)S(1)} %collective-permute-done.6, f32[2,32,1,32,128]{4,3,1,0,2:T(8,128)S(1)} %bitcast.208, s32[]{:T(128)S(6)} %select_n.150, pred[]{:T(512)S(6)} %eq.46, f32[1,64,2,32]{1,3,0,2:T(8,128)S(1)} %get-tuple-element.8, ...), kind=kOutput, calls=%fused_computation.16 | convolution fusion | flops 101322752 | bytes 5308421 | tf_op jit(solution)/shard_map/eyj,xrjl->rxeyl/dot_general | solution.py:200
  94.0 2.7 %shard_map.74 = f32[1,32,64,128]{3,2,1,0:T(8,128)} custom-call(s32[1]{0:T(128)} %constant.80.clone.1.me_ref, f32[32,2,64,128]{3,2,1,0:T(8,128)} %add_bitcast_fusion.in_ref), custom_call_target="tpu_custom_call" | custom-call | flops 786432 | bytes 3145728 | tf_op jit(solution)/shard_map/pallas_call | solution.py:44
  96.7 1.9 %convolution_multiply_fusion = f32[32,64,64]{2,1,0:T(8,128)S(1)} fusion(f32[1,32,64,128]{3,2,1,0:T(8,128)} %shard_map.74, f32[64,64]{0,1:T(8,128)S(1)} %get-tuple-element.10, f32[64,64]{0,1:T(8,128)S(1)} %get-tuple-element.11), kind=kOutput, calls=%fused_computation.17 | convolution fusion | flops 100802560 | bytes 1605632 | tf_op jit(solution)/shard_map/rxyl,lz->rxyz/dot_general | solution.py:206
  99.7 1.6 %gather_fusion = f32[8,512]{1,0:T(8,128)S(1)} fusion(f32[256,512]{1,0:T(8,128)} %reshape.307, s32[1024]{0:T(1024)S(1)} %pad_clamp_fusion), kind=kCustom, calls=%fused_computation | custom fusion | bytes 32800 | tf_op jit(solution)/shard_map/gather | solution.py:213
  101.3 1.6 %fusion.94 = f32[8,512]{1,0:T(8,128)S(1)} fusion(f32[8,512]{1,0:T(8,128)S(1)} %gather_fusion, f32[512,512]{1,0:T(8,128)} %param.9), kind=kOutput, calls=%fused_computation.140 | convolution fusion | flops 12582912 | bytes 1081344 | tf_op jit(solution)/shard_map/dot_general | solution.py:222
  103.1 9.6 %all_to_all.5 = f32[8,2,512]{2,1,0:T(2,128)S(1)} all-to-all(f32[8,2,512]{2,1,0:T(2,128)S(1)} %reshape.309), channel_id=1, replica_groups=mesh['grp'=2,'rot'=4,'sub'=2,'ref'=2] {'rot','ref'}, dimensions={0} | all-to-all | bytes 65536 | tf_op jit(solution)/shard_map/all_to_all | solution.py:224
  (59 shorter events, 10.4 us)
Async XLA Ops:
  0.6 1.6 %copy-start = (f32[2,4,16,32,64]{4,3,2,1,0:T(8,128)S(1)}, f32[2,4,16,32,64]{4,3,2,1,0:T(8,128)}, u32[]{:S(2)}) copy-start(f32[2,4,16,32,64]{4,3,2,1,0:T(8,128)} %param.6) | copy-start | bytes 3145732
  3.3 32.3 %collective-permute-start.2 = (bf16[4,16,16,128]{3,1,2,0:T(8,128)(2,1)}, bf16[4,16,16,128]{3,1,2,0:T(8,128)(2,1)S(1)}, u32[]{:S(2)}, u32[]{:S(2)}) collective-permute-start(bf16[4,16,16,128]{3,1,2,0:T(8,128)(2,1)} %fusion.91), channel_id=1, source_target_pairs={{0,12},{4,0},{8,4},{12,8},{1,13},{5,1},{9,5},{13,9},{2,14},{6,2},{... | collective-permute-start | bytes 786440 | tf_op jit(solution)/shard_map/ppermute | solution.py:67
  8.3 27.2 %collective-permute-start.3 = (bf16[4,16,16,128]{3,1,2,0:T(8,128)(2,1)}, bf16[4,16,16,128]{3,1,2,0:T(8,128)(2,1)S(1)}, u32[]{:S(2)}, u32[]{:S(2)}) collective-permute-start(bf16[4,16,16,128]{3,1,2,0:T(8,128)(2,1)} %fusion.91), channel_id=1, source_target_pairs={{0,8},{4,12},{8,0},{12,4},{1,9},{5,13},{9,1},{13,5},{2,10},{6,14},... | collective-permute-start | bytes 786440 | tf_op jit(solution)/shard_map/ppermute | solution.py:67
  8.3 27.3 %collective-permute-start.4 = (bf16[4,16,16,128]{3,1,2,0:T(8,128)(2,1)}, bf16[4,16,16,128]{3,1,2,0:T(8,128)(2,1)S(1)}, u32[]{:S(2)}, u32[]{:S(2)}) collective-permute-start(bf16[4,16,16,128]{3,1,2,0:T(8,128)(2,1)} %fusion.91), channel_id=1, source_target_pairs={{0,4},{4,8},{8,12},{12,0},{1,5},{5,9},{9,13},{13,1},{2,6},{6,10},{... | collective-permute-start | bytes 786440 | tf_op jit(solution)/shard_map/ppermute | solution.py:67
  9.6 14.7 %copy-start.5 = (f32[1,64,64]{2,1,0:T(8,128)}, f32[1,64,64]{2,1,0:T(8,128)S(1)}, u32[]{:S(2)}) copy-start(f32[1,64,64]{2,1,0:T(8,128)S(1)} %get-tuple-element.12) | copy-start | bytes 49156
  9.6 14.7 %copy-start.7 = (f32[1,64,64]{2,1,0:T(8,128)}, f32[1,64,64]{2,1,0:T(8,128)S(1)}, u32[]{:S(2)}) copy-start(f32[1,64,64]{2,1,0:T(8,128)S(1)} %get-tuple-element.13) | copy-start | bytes 49156
  19.7 3.9 %copy-start.4 = (bf16[1,4,32,64,64]{4,3,2,1,0:T(8,128)(2,1)S(1)}, bf16[1,4,32,64,64]{4,3,2,1,0:T(8,128)(2,1)}, u32[]{:S(2)}) copy-start(bf16[1,4,32,64,64]{4,3,2,1,0:T(8,128)(2,1)} %param.5) | copy-start | bytes 3145732
  22.1 15.5 %collective-permute-start = (bf16[1,2,32,32,128]{4,2,3,1,0:T(8,128)(2,1)}, bf16[1,2,32,32,128]{4,2,3,1,0:T(8,128)(2,1)S(1)}, u32[]{:S(2)}, u32[]{:S(2)}) collective-permute-start(bf16[1,2,32,32,128]{4,2,3,1,0:T(8,128)(2,1)} %copy.15), channel_id=1, source_target_pairs={{0,2},{2,0},{1,3},{3,1},{4,6},{6,4},{5,7},{7,5},{8,10},{10,8},{9,1... | collective-permute-start | bytes 1572872 | tf_op jit(solution)/shard_map/ppermute | solution.py:84
  34.7 12.7 %collective-permute-start.1 = (bf16[1,2,32,32,128]{4,2,3,1,0:T(8,128)(2,1)}, bf16[1,2,32,32,128]{4,2,3,1,0:T(8,128)(2,1)S(1)}, u32[]{:S(2)}, u32[]{:S(2)}) collective-permute-start(bf16[1,2,32,32,128]{4,2,3,1,0:T(8,128)(2,1)} %copy.18), channel_id=1, source_target_pairs={{0,2},{2,0},{1,3},{3,1},{4,6},{6,4},{5,7},{7,5},{8,10},{10,8},{9,1... | collective-permute-start | bytes 1572872 | tf_op jit(solution)/shard_map/ppermute | solution.py:84
  37.4 19.4 %collective-permute-start.5 = (bf16[4,4,16,16,128]{4,2,3,1,0:T(8,128)(2,1)}, bf16[4,4,16,16,128]{4,2,3,1,0:T(8,128)(2,1)}, u32[]{:S(2)}, u32[]{:S(2)}) collective-permute-start(bf16[4,4,16,16,128]{4,2,3,1,0:T(8,128)(2,1)} %constant_dynamic-slice_fusion), channel_id=1, source_target_pairs={{0,1},{1,0},{2,3},{3,2},{4,5},{5,4},{6,7},{7,6},{8,9},{9,8},{10,11... | collective-permute-start | bytes 3145736 | tf_op jit(solution)/shard_map/ppermute | solution.py:67
  61.3 4.4 %copy-start.6 = (f32[1,64,64]{2,1,0:T(8,128)S(1)}, f32[1,64,64]{2,1,0:T(8,128)}, u32[]{:S(2)}) copy-start(f32[1,64,64]{2,1,0:T(8,128)} %copy-done.5) | copy-start | bytes 49156
  61.3 4.4 %copy-start.8 = (f32[1,64,64]{2,1,0:T(8,128)S(1)}, f32[1,64,64]{2,1,0:T(8,128)}, u32[]{:S(2)}) copy-start(f32[1,64,64]{2,1,0:T(8,128)} %copy-done.7) | copy-start | bytes 49156
  70.4 6.0 %copy-start.9 = (s32[1,1,1,8]{3,2,1,0:T(1,128)S(1)}, s32[1,1,1,8]{3,2,1,0:T(1,128)}, u32[]{:S(2)}) copy-start(s32[1,1,1,8]{3,2,1,0:T(1,128)} %param.7) | copy-start | bytes 100
  70.4 6.0 %copy-start.10 = (s32[1,1,1,8,1]{3,4,2,1,0:T(1,128)S(1)}, s32[1,1,1,8,1]{3,4,2,1,0:T(1,128)}, u32[]{:S(2)}) copy-start(s32[1,1,1,8,1]{3,4,2,1,0:T(1,128)} %param.8) | copy-start | bytes 100
  74.2 17.4 %copy-start.2 = (f32[1,64,32,128]{3,2,1,0:T(8,128)S(1)}, f32[1,64,32,128]{3,2,1,0:T(8,128)}, u32[]{:S(2)}) copy-start(f32[1,64,32,128]{3,2,1,0:T(8,128)} %shard_map.73) | copy-start | bytes 3145732
  75.4 14.2 %collective-permute-start.6 = (f32[32,1,32,128]{3,2,0,1:T(8,128)S(1)}, f32[32,1,32,128]{3,2,0,1:T(8,128)S(1)}, u32[]{:S(2)}, u32[]{:S(2)}) collective-permute-start(f32[32,1,32,128]{3,2,0,1:T(8,128)S(1)} %dynamic-slice_bitcast_fusion), channel_id=1, source_target_pairs={{0,2},{2,0},{1,3},{3,1},{4,6},{6,4},{5,7},{7,5},{8,10},{10,8},{9,1... | collective-permute-start | bytes 1572872 | tf_op jit(solution)/shard_map/ppermute | solution.py:84
  94.0 19.3 %copy-start.1 = (f32[2,4,16,32,64]{4,3,2,1,0:T(8,128)S(1)}, f32[2,4,16,32,64]{4,3,2,1,0:T(8,128)}, u32[]{:S(2)}) copy-start(f32[2,4,16,32,64]{4,3,2,1,0:T(8,128)} %param.6) | copy-start | bytes 3145732
  98.6 14.8 %copy-start.3 = (f32[32,64,64]{2,1,0:T(8,128)}, f32[32,64,64]{2,1,0:T(8,128)S(1)}, u32[]{:S(2)}) copy-start(f32[32,64,64]{2,1,0:T(8,128)S(1)} %convolution_multiply_fusion) | copy-start | bytes 1572868

commit v19 on v17

--- a/solution.py
+++ b/solution.py
@@ -133,7 +133,7 @@
     rots, _, kx, ky, lanes = spectra[0].shape
     terms = receptor.shape[0]
     rows = kx * ky
-    block = min(rows, 1024)
+    block = min(rows, 256)
     specs = [part.reshape(rots, part.shape[1], rows, lanes) for part in spectra]
     rec = receptor.reshape(terms, rows, lanes)
     out = pl.pallas_call(

time: 109 us -> 111 us (1.018)
  Pallas kernels: 23 us -> 25.5 us
    pallas_call x1, Pallas kernels: 4.35 us -> 6.82 us  [correlate(): pl.pallas_call(product_kernel, grid=(rots, rows // block), in_specs=[pl.B...]
where the time goes in v19:
time: 111 us
  matrix products  30.1 us (27%)
  Pallas kernels  25.5 us (23%)
  local copies, waits for them, and re-layouts  17.1 us (15%)
  waiting for transfers between devices  13.1 us (12%)
  blocking collectives  9.63 us (9%)
  starting transfers between devices  9.57 us (9%)
  other arithmetic  4.63 us (4%)
    pallas_call x6, Pallas kernels, combine_call(): pl.pallas_call(functools.partial(combine_kernel, first=first, second=seco...  18.7 us
    ppermute x3, waiting for transfers between devices, exchange(): lax.ppermute(entry(shift), axis, pairs)  13.1 us
    dot_general x4, matrix products, local(): jnp.einsum('ekx,rtxjl->rtjekl', pair_x[:, :, source], piece.astype(jnp.fl...  9.81 us
    all_to_all x1, blocking collectives, local(): lax.all_to_all(packed, ('rot', 'ref'), split_axis=0, concat_axis=0, tiled...  9.63 us
    dot_general x2, matrix products, local(): along_y = jnp.einsum('ejy,rtxyl->rtxejl', pair, along_z, precision=highest)  7.45 us
    pallas_call x1, Pallas kernels, correlate(): pl.pallas_call(product_kernel, grid=(rots, rows // block), in_specs=[pl.B...  6.82 us
    ppermute x4, starting transfers between devices, gather_by_shifts(): pieces.append(lax.ppermute(piece, axis, pairs))  6.06 us
    dot_general x2, matrix products, local(): jnp.einsum('eyj,xrjl->rxeyl', pair_y[:, :, source], piece, precision=high...  4.43 us
  transfers between devices with their start and end apart: 7, of which 2 were waited for; matrix products, arithmetic and copies ran while one was open for 25% of the time, Pallas kernels for 12%

profile of v19, /device:TPU:0, one launch (start us, length us, event | category | flops | bytes accessed | tf_op | source)
XLA Modules:
  0.0 110.6 jit_solution(6587717793257198345)
XLA Ops:
  0.7 1.6 %copy-done = f32[2,4,16,32,64]{4,3,2,1,0:T(8,128)S(1)} copy-done((f32[2,4,16,32,64]{4,3,2,1,0:T(8,128)S(1)}, f32[2,4,16,32,64]{4,3,2,1,0:T(8,128)}, u32[]{:S(2)}) %copy-start) | copy-done | bytes 1048600
  3.3 5.0 %collective-permute-start.2 = (bf16[4,16,16,128]{3,1,2,0:T(8,128)(2,1)}, bf16[4,16,16,128]{3,1,2,0:T(8,128)(2,1)S(1)}, u32[]{:S(2)}, u32[]{:S(2)}) collective-permute-start(bf16[4,16,16,128]{3,1,2,0:T(8,128)(2,1)} %fusion.91), channel_id=1, source_target_pairs={{0,12},{4,0},{8,4},{12,8},{1,13},{5,1},{9,5},{13,9},{2,14},{6,2},{... | collective-permute-start | bytes 786440 | tf_op jit(solution)/shard_map/ppermute | solution.py:67
  9.7 2.0 %fusion.11 = f32[128,2,32,64]{0,3,2,1:T(8,128)S(1)} fusion(bf16[1,4,32,64,64]{4,3,2,1,0:T(8,128)(2,1)} %param.5, f32[64,64]{0,1:T(8,128)S(1)} %get-tuple-element.10, f32[64,64]{0,1:T(8,128)S(1)} %get-tuple-element.11), kind=kOutput, calls=%fused_computation.21 | convolution fusion | flops 201334784 | bytes 3178496 | tf_op jit(solution)/shard_map/rtxyz,zl->rtxyl/dot_general | solution.py:174
  11.6 3.7 %fusion.6 = f32[2,32,128,2,64]{2,4,3,1,0:T(8,128)} fusion(f32[128,2,32,64]{0,3,2,1:T(8,128)S(1)} %fusion.11, f32[1,64,64]{2,1,0:T(8,128)S(1)} %get-tuple-element.12, f32[1,64,64]{2,1,0:T(8,128)S(1)} %get-tuple-element.13), kind=kOutput, calls=%fused_computation.13 | convolution fusion | flops 402661376 | bytes 6324224 | tf_op jit(solution)/shard_map/ejy,rtxyl->rtxejl/dot_general | solution.py:175
  15.3 3.4 %shard_map.68 = bf16[2,64,32,128]{3,2,1,0:T(8,128)(2,1)} custom-call(s32[1]{0:T(128)} %bitcast.me_ref, f32[64,2,64,128]{3,2,1,0:T(8,128)} %bitcast.198), custom_call_target="tpu_custom_call" | custom-call | flops 1572864 | bytes 5242880 | tf_op jit(solution)/shard_map/pallas_call | solution.py:44
  18.7 1.4 %fusion.93 = (bf16[1,64,32,128]{3,2,1,0:T(8,128)(2,1)S(1)}, bf16[1,64,32,128]{3,2,1,0:T(8,128)(2,1)S(1)}) fusion(bf16[2,64,32,128]{3,2,1,0:T(8,128)(2,1)} %shard_map.68), kind=kLoop, calls=%fused_computation.139 | loop fusion | bytes 2097152 | tf_op jit(solution)/shard_map/slice | solution.py:78
  21.1 1.5 %collective-permute-start = (bf16[1,2,32,32,128]{4,2,3,1,0:T(8,128)(2,1)}, bf16[1,2,32,32,128]{4,2,3,1,0:T(8,128)(2,1)S(1)}, u32[]{:S(2)}, u32[]{:S(2)}) collective-permute-start(bf16[1,2,32,32,128]{4,2,3,1,0:T(8,128)(2,1)} %copy.15), channel_id=1, source_target_pairs={{0,2},{2,0},{1,3},{3,1},{4,6},{6,4},{5,7},{7,5},{8,10},{10,8},{9,1... | collective-permute-start | bytes 1572872 | tf_op jit(solution)/shard_map/ppermute | solution.py:84
  23.4 3.7 %fusion.4 = f32[2,32,128,2,64]{2,4,3,1,0:T(8,128)} fusion(f32[128,2,32,64]{0,3,2,1:T(8,128)S(1)} %fusion.9, f32[1,64,64]{2,1,0:T(8,128)S(1)} %get-tuple-element.12, f32[1,64,64]{2,1,0:T(8,128)S(1)} %get-tuple-element.13), kind=kOutput, calls=%fused_computation.11 | convolution fusion | flops 402661376 | bytes 6324224 | tf_op jit(solution)/shard_map/ejy,rtxyl->rtxejl/dot_general | solution.py:175
  27.1 3.4 %shard_map.70 = bf16[2,64,32,128]{3,2,1,0:T(8,128)(2,1)} custom-call(s32[1]{0:T(128)} %bitcast.me_ref, f32[64,2,64,128]{3,2,1,0:T(8,128)} %bitcast.199), custom_call_target="tpu_custom_call" | custom-call | flops 1572864 | bytes 5242880 | tf_op jit(solution)/shard_map/pallas_call | solution.py:44
  30.4 1.3 %fusion.92 = (bf16[1,64,32,128]{3,2,1,0:T(8,128)(2,1)S(1)}, bf16[1,64,32,128]{3,2,1,0:T(8,128)(2,1)S(1)}) fusion(bf16[2,64,32,128]{3,2,1,0:T(8,128)(2,1)} %shard_map.70), kind=kLoop, calls=%fused_computation.138 | loop fusion | bytes 2097152 | tf_op jit(solution)/shard_map/slice | solution.py:78
  35.6 1.3 %fusion.21 = f32[2,32,128,2,64]{2,4,3,1,0:T(8,128)S(1)} fusion(bf16[1,2,32,32,128]{4,2,3,1,0:T(8,128)(2,1)S(1)} %collective-permute-done, pred[]{:T(512)S(6)} %eq.47, bf16[1,2,32,32,128]{4,3,2,1,0:T(8,128)(2,1)S(1)} %bitcast.200, f32[1,64,2,32]{1,3,0,2:T(8,128)S(1)} %get-tuple-element.9, f32[1,64,2,32]{1,3,0,2:T(8,128)S(1)} %get-tuple-element.8), kind=kOutput, calls=%fused_computation.32 | convolution fusion | flops 201592832 | bytes 5275649 | tf_op jit(solution)/shard_map/ekx,rtxjl->rtjekl/dot_general | solution.py:181
  36.9 3.6 %convolution_add_fusion.1 = f32[2,32,128,2,64]{2,4,3,1,0:T(8,128)} fusion(f32[2,32,128,2,64]{2,4,3,1,0:T(8,128)S(1)} %fusion.21, bf16[1,2,32,32,128]{4,2,3,1,0:T(8,128)(2,1)S(1)} %collective-permute-done, pred[]{:T(512)S(6)} %eq.46, bf16[1,2,32,32,128]{4,3,2,1,0:T(8,128)(2,1)S(1)} %bitcast.201, f32[1,64,2,32]{1,3,0,2:T(8,128)S(1)} %get-tuple-element.8, ...), kind=kOutput, calls=%fused_computation.6 | convolution fusion | flops 202641408 | bytes 9469953 | tf_op jit(solution)/shard_map/ekx,rtxjl->rtjekl/dot_general | solution.py:181
  40.5 3.4 %shard_map.69 = bf16[1,64,64,128]{3,2,1,0:T(8,128)(2,1)} custom-call(s32[1]{0:T(128)} %constant.80.clone.1.me_ref, f32[64,2,64,128]{3,2,1,0:T(8,128)} %bitcast.196), custom_call_target="tpu_custom_call" | custom-call | flops 1572864 | bytes 5242880 | tf_op jit(solution)/shard_map/pallas_call | solution.py:44
  43.9 1.6 %collective-permute-done.1 = bf16[1,2,32,32,128]{4,2,3,1,0:T(8,128)(2,1)S(1)} collective-permute-done((bf16[1,2,32,32,128]{4,2,3,1,0:T(8,128)(2,1)}, bf16[1,2,32,32,128]{4,2,3,1,0:T(8,128)(2,1)S(1)}, u32[]{:S(2)}, u32[]{:S(2)}) %collective-permute-start.1) | collective-permute-done | bytes 524320 | tf_op jit(solution)/shard_map/ppermute | solution.py:84
  45.5 1.3 %fusion.18 = f32[2,32,128,2,64]{2,4,3,1,0:T(8,128)S(1)} fusion(bf16[1,2,32,32,128]{4,2,3,1,0:T(8,128)(2,1)S(1)} %collective-permute-done.1, pred[]{:T(512)S(6)} %eq.47, bf16[1,2,32,32,128]{4,3,2,1,0:T(8,128)(2,1)S(1)} %bitcast.202, f32[1,64,2,32]{1,3,0,2:T(8,128)S(1)} %get-tuple-element.9, f32[1,64,2,32]{1,3,0,2:T(8,128)S(1)} %get-tuple-element.8), kind=kOutput, calls=%fused_computation.29 | convolution fusion | flops 201592832 | bytes 5275649 | tf_op jit(solution)/shard_map/ekx,rtxjl->rtjekl/dot_general | solution.py:181
  46.8 3.6 %convolution_add_fusion = f32[2,32,128,2,64]{2,4,3,1,0:T(8,128)} fusion(f32[2,32,128,2,64]{2,4,3,1,0:T(8,128)S(1)} %fusion.18, bf16[1,2,32,32,128]{4,2,3,1,0:T(8,128)(2,1)S(1)} %collective-permute-done.1, pred[]{:T(512)S(6)} %eq.46, bf16[1,2,32,32,128]{4,3,2,1,0:T(8,128)(2,1)S(1)} %bitcast.203, f32[1,64,2,32]{1,3,0,2:T(8,128)S(1)} %get-tuple-element.8, ...), kind=kOutput, calls=%fused_computation.5 | convolution fusion | flops 202641408 | bytes 9469953 | tf_op jit(solution)/shard_map/ekx,rtxjl->rtjekl/dot_general | solution.py:181
  50.4 3.4 %shard_map.71 = bf16[1,64,64,128]{3,2,1,0:T(8,128)(2,1)} custom-call(s32[1]{0:T(128)} %constant.80.clone.1.me_ref, f32[64,2,64,128]{3,2,1,0:T(8,128)} %bitcast.197), custom_call_target="tpu_custom_call" | custom-call | flops 1572864 | bytes 5242880 | tf_op jit(solution)/shard_map/pallas_call | solution.py:44
  53.8 2.7 %fusion.3 = bf16[4,2,16,4,16,128]{5,2,4,0,3,1:T(8,128)(2,1)S(1)} fusion(s32[]{:T(128)S(6)} %select_n.146, bf16[1,4,4,16,16,128]{5,3,4,2,1,0:T(8,128)(2,1)} %bitcast.62, bf16[1,4,4,16,16,128]{5,3,4,2,1,0:T(8,128)(2,1)S(1)} %fusion.99), kind=kLoop, calls=%fused_computation.10 | loop fusion | flops 3145728 | bytes 4194308 | tf_op jit(solution)/shard_map/transpose | solution.py:108
  56.4 1.9 %copy.21 = bf16[4,2,16,4,16,128]{5,4,3,2,1,0:T(8,128)(2,1)} copy(bf16[4,2,16,4,16,128]{5,2,4,0,3,1:T(8,128)(2,1)S(1)} %fusion.3) | data formatting | bytes 4194304 | tf_op jit(solution)/shard_map/transpose | solution.py:108
  58.3 6.8 %shard_map.72 = f32[1,2048,128]{2,1,0:T(8,128)} custom-call(bf16[1,2,2048,128]{3,2,1,0:T(8,128)(2,1)} %bitcast.210, bf16[1,2,2048,128]{3,2,1,0:T(8,128)(2,1)} %bitcast.212, bf16[4,2048,128]{2,1,0:T(8,128)(2,1)} %bitcast.204), custom_call_target="tpu_custom_call" | custom-call | flops 8388608 | bytes 5242880 | tf_op jit(solution)/shard_map/pallas_call | solution.py:139
  65.1 2.2 %fusion.40 = f32[32,128,2,64]{1,3,2,0:T(8,128)S(1)} fusion(f32[32,64,128,1]{2,1,3,0:T(8,128)} %bitcast.209, f32[1,64,64]{2,1,0:T(8,128)S(1)} %copy-done.6, f32[1,64,64]{2,1,0:T(8,128)S(1)} %copy-done.8), kind=kOutput, calls=%fused_computation.69 | convolution fusion | flops 201334784 | bytes 3178496 | tf_op jit(solution)/shard_map/exk,rjkl->xrejl/dot_general | solution.py:195
  67.3 2.5 %copy.53 = f32[32,128,2,64]{1,0,2,3:T(8,128)} copy(f32[32,128,2,64]{1,3,2,0:T(8,128)S(1)} %fusion.40) | data formatting | bytes 4194304 | tf_op jit(solution)/shard_map/exk,rjkl->xrejl/dot_general | solution.py:195
  69.9 2.6 %shard_map.73 = f32[1,64,32,128]{3,2,1,0:T(8,128)} custom-call(s32[1]{0:T(128)} %constant.80.clone.1.me_ref, f32[64,2,32,128]{3,2,1,0:T(8,128)} %bitcast.205), custom_call_target="tpu_custom_call" | custom-call | flops 786432 | bytes 3145728 | tf_op jit(solution)/shard_map/pallas_call | solution.py:44
  73.6 1.5 %collective-permute-start.6 = (f32[32,1,32,128]{3,2,0,1:T(8,128)S(1)}, f32[32,1,32,128]{3,2,0,1:T(8,128)S(1)}, u32[]{:S(2)}, u32[]{:S(2)}) collective-permute-start(f32[32,1,32,128]{3,2,0,1:T(8,128)S(1)} %dynamic-slice_bitcast_fusion), channel_id=1, source_target_pairs={{0,2},{2,0},{1,3},{3,1},{4,6},{6,4},{5,7},{7,5},{8,10},{10,8},{9,1... | collective-permute-start | bytes 1572872 | tf_op jit(solution)/shard_map/ppermute | solution.py:84
  75.3 11.5 %collective-permute-done.6 = f32[32,1,32,128]{3,2,0,1:T(8,128)S(1)} collective-permute-done((f32[32,1,32,128]{3,2,0,1:T(8,128)S(1)}, f32[32,1,32,128]{3,2,0,1:T(8,128)S(1)}, u32[]{:S(2)}, u32[]{:S(2)}) %collective-permute-start.6) | collective-permute-done | bytes 524320 | tf_op jit(solution)/shard_map/ppermute | solution.py:84
  86.8 2.1 %fusion.15 = f32[32,128,2,64]{1,3,2,0:T(8,128)S(1)} fusion(f32[32,1,32,128]{3,2,0,1:T(8,128)S(1)} %collective-permute-done.6, f32[2,32,1,32,128]{4,3,1,0,2:T(8,128)} %bitcast.207, s32[]{:T(128)S(6)} %select_n.150, pred[]{:T(512)S(6)} %eq.47, f32[1,64,2,32]{1,3,0,2:T(8,128)S(1)} %get-tuple-element.9, f32[1,64,2,32]{1,3,0,2:T(8,128)S(1)} %get-tuple-element.8), kind=kOutput, calls=%fused_computation.26 | convolution fusion | flops 100798464 | bytes 3178501 | tf_op jit(solution)/shard_map/eyj,xrjl->rxeyl/dot_general | solution.py:200
  88.9 2.4 %add_bitcast_fusion.in_ref = f32[32,2,64,128]{3,2,1,0:T(8,128)} fusion(f32[32,128,2,64]{1,3,2,0:T(8,128)S(1)} %fusion.15, f32[32,1,32,128]{3,2,0,1:T(8,128)S(1)} %collective-permute-done.6, f32[2,32,1,32,128]{4,3,1,0,2:T(8,128)S(1)} %bitcast.208, s32[]{:T(128)S(6)} %select_n.150, pred[]{:T(512)S(6)} %eq.46, f32[1,64,2,32]{1,3,0,2:T(8,128)S(1)} %get-tuple-element.8, ...), kind=kOutput, calls=%fused_computation.16 | convolution fusion | flops 101322752 | bytes 5308421 | tf_op jit(solution)/shard_map/eyj,xrjl->rxeyl/dot_general | solution.py:200
  91.3 2.7 %shard_map.74 = f32[1,32,64,128]{3,2,1,0:T(8,128)} custom-call(s32[1]{0:T(128)} %constant.80.clone.1.me_ref, f32[32,2,64,128]{3,2,1,0:T(8,128)} %add_bitcast_fusion.in_ref), custom_call_target="tpu_custom_call" | custom-call | flops 786432 | bytes 3145728 | tf_op jit(solution)/shard_map/pallas_call | solution.py:44
  94.0 1.9 %convolution_multiply_fusion = f32[32,64,64]{2,1,0:T(8,128)S(1)} fusion(f32[1,32,64,128]{3,2,1,0:T(8,128)} %shard_map.74, f32[64,64]{0,1:T(8,128)S(1)} %get-tuple-element.10, f32[64,64]{0,1:T(8,128)S(1)} %get-tuple-element.11), kind=kOutput, calls=%fused_computation.17 | convolution fusion | flops 100802560 | bytes 1605632 | tf_op jit(solution)/shard_map/rxyl,lz->rxyz/dot_general | solution.py:206
  97.0 1.6 %gather_fusion = f32[8,512]{1,0:T(8,128)S(1)} fusion(f32[256,512]{1,0:T(8,128)} %reshape.307, s32[1024]{0:T(1024)S(1)} %pad_clamp_fusion), kind=kCustom, calls=%fused_computation | custom fusion | bytes 32800 | tf_op jit(solution)/shard_map/gather | solution.py:213
  98.6 1.6 %fusion.94 = f32[8,512]{1,0:T(8,128)S(1)} fusion(f32[8,512]{1,0:T(8,128)S(1)} %gather_fusion, f32[512,512]{1,0:T(8,128)} %param.9), kind=kOutput, calls=%fused_computation.140 | convolution fusion | flops 12582912 | bytes 1081344 | tf_op jit(solution)/shard_map/dot_general | solution.py:222
  100.3 9.6 %all_to_all.5 = f32[8,2,512]{2,1,0:T(2,128)S(1)} all-to-all(f32[8,2,512]{2,1,0:T(2,128)S(1)} %reshape.309), channel_id=1, replica_groups=mesh['grp'=2,'rot'=4,'sub'=2,'ref'=2] {'rot','ref'}, dimensions={0} | all-to-all | bytes 65536 | tf_op jit(solution)/shard_map/all_to_all | solution.py:224
  (59 shorter events, 11.1 us)
Async XLA Ops:
  0.6 1.6 %copy-start = (f32[2,4,16,32,64]{4,3,2,1,0:T(8,128)S(1)}, f32[2,4,16,32,64]{4,3,2,1,0:T(8,128)}, u32[]{:S(2)}) copy-start(f32[2,4,16,32,64]{4,3,2,1,0:T(8,128)} %param.6) | copy-start | bytes 3145732
  3.3 30.3 %collective-permute-start.2 = (bf16[4,16,16,128]{3,1,2,0:T(8,128)(2,1)}, bf16[4,16,16,128]{3,1,2,0:T(8,128)(2,1)S(1)}, u32[]{:S(2)}, u32[]{:S(2)}) collective-permute-start(bf16[4,16,16,128]{3,1,2,0:T(8,128)(2,1)} %fusion.91), channel_id=1, source_target_pairs={{0,12},{4,0},{8,4},{12,8},{1,13},{5,1},{9,5},{13,9},{2,14},{6,2},{... | collective-permute-start | bytes 786440 | tf_op jit(solution)/shard_map/ppermute | solution.py:67
  8.3 25.3 %collective-permute-start.3 = (bf16[4,16,16,128]{3,1,2,0:T(8,128)(2,1)}, bf16[4,16,16,128]{3,1,2,0:T(8,128)(2,1)S(1)}, u32[]{:S(2)}, u32[]{:S(2)}) collective-permute-start(bf16[4,16,16,128]{3,1,2,0:T(8,128)(2,1)} %fusion.91), channel_id=1, source_target_pairs={{0,8},{4,12},{8,0},{12,4},{1,9},{5,13},{9,1},{13,5},{2,10},{6,14},... | collective-permute-start | bytes 786440 | tf_op jit(solution)/shard_map/ppermute | solution.py:67
  8.3 25.3 %collective-permute-start.4 = (bf16[4,16,16,128]{3,1,2,0:T(8,128)(2,1)}, bf16[4,16,16,128]{3,1,2,0:T(8,128)(2,1)S(1)}, u32[]{:S(2)}, u32[]{:S(2)}) collective-permute-start(bf16[4,16,16,128]{3,1,2,0:T(8,128)(2,1)} %fusion.91), channel_id=1, source_target_pairs={{0,4},{4,8},{8,12},{12,0},{1,5},{5,9},{9,13},{13,1},{2,6},{6,10},{... | collective-permute-start | bytes 786440 | tf_op jit(solution)/shard_map/ppermute | solution.py:67
  9.6 13.7 %copy-start.5 = (f32[1,64,64]{2,1,0:T(8,128)}, f32[1,64,64]{2,1,0:T(8,128)S(1)}, u32[]{:S(2)}) copy-start(f32[1,64,64]{2,1,0:T(8,128)S(1)} %get-tuple-element.12) | copy-start | bytes 49156
  9.6 13.7 %copy-start.7 = (f32[1,64,64]{2,1,0:T(8,128)}, f32[1,64,64]{2,1,0:T(8,128)S(1)}, u32[]{:S(2)}) copy-start(f32[1,64,64]{2,1,0:T(8,128)S(1)} %get-tuple-element.13) | copy-start | bytes 49156
  18.7 3.9 %copy-start.4 = (bf16[1,4,32,64,64]{4,3,2,1,0:T(8,128)(2,1)S(1)}, bf16[1,4,32,64,64]{4,3,2,1,0:T(8,128)(2,1)}, u32[]{:S(2)}) copy-start(bf16[1,4,32,64,64]{4,3,2,1,0:T(8,128)(2,1)} %param.5) | copy-start | bytes 3145732
  21.1 14.5 %collective-permute-start = (bf16[1,2,32,32,128]{4,2,3,1,0:T(8,128)(2,1)}, bf16[1,2,32,32,128]{4,2,3,1,0:T(8,128)(2,1)S(1)}, u32[]{:S(2)}, u32[]{:S(2)}) collective-permute-start(bf16[1,2,32,32,128]{4,2,3,1,0:T(8,128)(2,1)} %copy.15), channel_id=1, source_target_pairs={{0,2},{2,0},{1,3},{3,1},{4,6},{6,4},{5,7},{7,5},{8,10},{10,8},{9,1... | collective-permute-start | bytes 1572872 | tf_op jit(solution)/shard_map/ppermute | solution.py:84
  32.7 12.8 %collective-permute-start.1 = (bf16[1,2,32,32,128]{4,2,3,1,0:T(8,128)(2,1)}, bf16[1,2,32,32,128]{4,2,3,1,0:T(8,128)(2,1)S(1)}, u32[]{:S(2)}, u32[]{:S(2)}) collective-permute-start(bf16[1,2,32,32,128]{4,2,3,1,0:T(8,128)(2,1)} %copy.18), channel_id=1, source_target_pairs={{0,2},{2,0},{1,3},{3,1},{4,6},{6,4},{5,7},{7,5},{8,10},{10,8},{9,1... | collective-permute-start | bytes 1572872 | tf_op jit(solution)/shard_map/ppermute | solution.py:84
  35.4 18.4 %collective-permute-start.5 = (bf16[4,4,16,16,128]{4,2,3,1,0:T(8,128)(2,1)}, bf16[4,4,16,16,128]{4,2,3,1,0:T(8,128)(2,1)}, u32[]{:S(2)}, u32[]{:S(2)}) collective-permute-start(bf16[4,4,16,16,128]{4,2,3,1,0:T(8,128)(2,1)} %constant_dynamic-slice_fusion), channel_id=1, source_target_pairs={{0,1},{1,0},{2,3},{3,2},{4,5},{5,4},{6,7},{7,6},{8,9},{9,8},{10,11... | collective-permute-start | bytes 3145736 | tf_op jit(solution)/shard_map/ppermute | solution.py:67
  58.3 6.8 %copy-start.6 = (f32[1,64,64]{2,1,0:T(8,128)S(1)}, f32[1,64,64]{2,1,0:T(8,128)}, u32[]{:S(2)}) copy-start(f32[1,64,64]{2,1,0:T(8,128)} %copy-done.5) | copy-start | bytes 49156
  58.3 6.8 %copy-start.8 = (f32[1,64,64]{2,1,0:T(8,128)S(1)}, f32[1,64,64]{2,1,0:T(8,128)}, u32[]{:S(2)}) copy-start(f32[1,64,64]{2,1,0:T(8,128)} %copy-done.7) | copy-start | bytes 49156
  69.9 5.2 %copy-start.9 = (s32[1,1,1,8]{3,2,1,0:T(1,128)S(1)}, s32[1,1,1,8]{3,2,1,0:T(1,128)}, u32[]{:S(2)}) copy-start(s32[1,1,1,8]{3,2,1,0:T(1,128)} %param.7) | copy-start | bytes 100
  69.9 5.2 %copy-start.10 = (s32[1,1,1,8,1]{3,4,2,1,0:T(1,128)S(1)}, s32[1,1,1,8,1]{3,4,2,1,0:T(1,128)}, u32[]{:S(2)}) copy-start(s32[1,1,1,8,1]{3,4,2,1,0:T(1,128)} %param.8) | copy-start | bytes 100
  72.5 16.4 %copy-start.2 = (f32[1,64,32,128]{3,2,1,0:T(8,128)S(1)}, f32[1,64,32,128]{3,2,1,0:T(8,128)}, u32[]{:S(2)}) copy-start(f32[1,64,32,128]{3,2,1,0:T(8,128)} %shard_map.73) | copy-start | bytes 3145732
  73.6 13.2 %collective-permute-start.6 = (f32[32,1,32,128]{3,2,0,1:T(8,128)S(1)}, f32[32,1,32,128]{3,2,0,1:T(8,128)S(1)}, u32[]{:S(2)}, u32[]{:S(2)}) collective-permute-start(f32[32,1,32,128]{3,2,0,1:T(8,128)S(1)} %dynamic-slice_bitcast_fusion), channel_id=1, source_target_pairs={{0,2},{2,0},{1,3},{3,1},{4,6},{6,4},{5,7},{7,5},{8,10},{10,8},{9,1... | collective-permute-start | bytes 1572872 | tf_op jit(solution)/shard_map/ppermute | solution.py:84
  91.3 19.3 %copy-start.1 = (f32[2,4,16,32,64]{4,3,2,1,0:T(8,128)S(1)}, f32[2,4,16,32,64]{4,3,2,1,0:T(8,128)}, u32[]{:S(2)}) copy-start(f32[2,4,16,32,64]{4,3,2,1,0:T(8,128)} %param.6) | copy-start | bytes 3145732
  95.8 14.8 %copy-start.3 = (f32[32,64,64]{2,1,0:T(8,128)}, f32[32,64,64]{2,1,0:T(8,128)S(1)}, u32[]{:S(2)}) copy-start(f32[32,64,64]{2,1,0:T(8,128)S(1)} %convolution_multiply_fusion) | copy-start | bytes 1572868
